TPU v7x, 128 devices: a whole 4x4x4 slice. The times are simulated.
128 devices in a mesh: row: 8 (over x, core), cent: 16 (over y, z).
Axes of the slice: x: 4, y: 4, z: 4, core: 2. Of those that a mesh axis runs over, the one named last changes fastest.
Arguments:
- vectors: bfloat16 [16384, 768], P('row', 'cent'), may hold values from -6 to 6
- centroids: bfloat16 [16384, 768], P('cent'), may hold values from -6 to 6
- weights: float32 [16384], P('row'), may hold values from 1 to 270, as said below
Outputs:
- new_centroids: float32 [768, 16384], P('row', 'cent')
- row_log: float32 [16384], P('row')
- col_log: float32 [16384], P('cent')
Inputs may be any that keep to these rules, and one draw needn't show every extreme that they name: Positive sample weights.
All inputs are finite; a program needn't handle non-finite values.
Results may differ from a plain program's by a relative error of at most 0.00082.
Values may be sent and summed in bfloat16 or wider, within the bound.
No kernel may reach another device: no remote copies, remote signals or barrier semaphores. Data moves between devices by JAX's collectives and lax.ppermute only.
A program may use at most 64 MiB of HBM per device.

v0:
```python
import math

import jax
import jax.numpy as jnp
from jax import lax
from jax.sharding import PartitionSpec as P

ITERS = 3


entropic_smoothing = 0.02


def row_step(kernel, col_scale, weights):
    partial_mass = jnp.sum(kernel.astype(jnp.float32) * col_scale[None, :], axis=1)
    masses = lax.psum(partial_mass, "cent")
    return weights / masses


def per_device(vectors, centroids, weights):
    full_rows = lax.all_gather(vectors, "cent", axis=1, tiled=True)
    local_rows = full_rows.shape[0]
    feature_dimension = full_rows.shape[1]
    local_centres = centroids.shape[0]
    centre_total = local_centres * lax.axis_size("cent")
    block_rows = math.gcd(local_rows, 512)
    block_count = local_rows // block_rows
    reciprocal_vector_magnitudes = lax.rsqrt(
        jnp.mean(jnp.square(full_rows.astype(jnp.float32)), axis=1) + 1e-06
    )
    reciprocal_centroid_magnitudes = lax.rsqrt(
        jnp.mean(jnp.square(centroids.astype(jnp.float32)), axis=1) + 1e-06
    )

    def kernel_rows(inputs):
        vec_block, reciprocal_magnitude_tile = inputs
        similarity_matrix = jnp.dot(vec_block, centroids.T, preferred_element_type=jnp.float32)
        sharpened_similarity = (
            similarity_matrix
            * reciprocal_magnitude_tile[:, None]
            * reciprocal_centroid_magnitudes[None, :]
            / (feature_dimension * entropic_smoothing)
        )
        return jnp.exp(sharpened_similarity).astype(jnp.bfloat16)

    kernel = lax.map(
        kernel_rows,
        (
            full_rows.reshape(block_count, block_rows, feature_dimension),
            reciprocal_vector_magnitudes.reshape(block_count, block_rows),
        ),
    )
    kernel = kernel.reshape(local_rows, local_centres)
    weight_sum = lax.psum(jnp.sum(weights), "row")
    col_scale = jnp.full((local_centres,), 1.0, jnp.float32) / centre_total
    row_scale = row_step(kernel, col_scale, weights)
    for sweep in range(ITERS):
        partial_cols = jnp.sum(kernel.astype(jnp.float32) * row_scale[:, None], axis=0)
        col_mass = lax.psum(partial_cols, "row")
        col_scale = weight_sum / centre_total / col_mass
        row_scale = row_step(kernel, col_scale, weights)
    transport = (row_scale[:, None] * kernel.astype(jnp.float32) * col_scale[None, :]).astype(
        jnp.bfloat16
    )
    own_dims = feature_dimension // lax.axis_size("row")
    term = lax.dot_general(
        full_rows, transport, (((0,), (0,)), ((), ())), preferred_element_type=jnp.float32
    )
    summed = lax.psum(term, "row")
    sharpened_similarity = summed * lax.rsqrt(jnp.mean(summed * summed, axis=0) + 1e-06)[None, :]
    new_centroids = lax.dynamic_slice_in_dim(
        sharpened_similarity, lax.axis_index("row") * own_dims, own_dims, 0
    )
    return (new_centroids, jnp.log(row_scale), jnp.log(centre_total * col_scale))


def solution(mesh):
    return jax.shard_map(
        per_device,
        mesh=mesh,
        in_specs=(P("row", "cent"), P("cent", None), P("row")),
        out_specs=(P("row", "cent"), P("row"), P("cent")),
        check_vma=False,
    )
```

profile of v0, /device:TPU:0, one launch (start us, length us, event | category | flops | bytes accessed | tf_op | source)
XLA Modules:
  0.0 376.4 jit_solution(15189755268320284470)
XLA Ops:
  7.2 0.0 all-gather.2.cloned.1.call-start
  7.2 0.7 all-gather.2.cloned.1.call-update
  7.9 0.0 all-reduce.3.cloned.1.call-start
  8.0 1.8 multiply_reduce_fusion.2
  9.8 50.9 %all-gather.2.cloned.1.call-done = bf16[2048,768]{0,1:T(8,128)(2,1)} async-done(((bf16[2048,48]{0,1:T(8,128)(2,1)}), bf16[2048,768]{0,1:T(8,128)(2,1)}) %all-gather.2.cloned.1.call-update) | async-done | bytes 3145744 | tf_op jit(solution)/shard_map/all_gather | solution.py:21
  60.7 0.0 copy-start
  60.7 2.7 multiply_reduce_fusion
  63.4 0.1 copy-done
  63.5 2.8 copy.6
  66.3 14.9 %while.10 = (s32[]{:T(128)}, bf16[4,512,1024]{2,1,0:T(8,128)(2,1)}, bf16[4,512,768]{2,1,0:T(8,128)(2,1)}, bf16[1024,768]{1,0:T(8,128)(2,1)}, f32[4,512]{1,0:T(4,128)S(1)}, /*index=5*/f32[1024]{0:T(1024)S(1)}, s32[]{:T(128)}) while((s32[]{:T(128)}, bf16[4,512,1024]{2,1,0:T(8,128)(2,1)}, bf16[4,512,768]{2,1,0:T(8,128)(2,1)}, ...), condition=%wide.region_3.4_spmd, body=%wide.region_2.3_spmd.sunk | while | flops 807403520 | bytes 3419217 | solution.py:46
  66.3 3.7 fusion.24
  70.1 3.8 %fusion.24 = bf16[4,512,1024]{2,1,0:T(8,128)(2,1)} fusion(bf16[4,512,1024]{2,1,0:T(8,128)(2,1)} %get-tuple-element.104, s32[]{:T(128)} %get-tuple-element.103, bf16[1024,768]{1,0:T(8,128)(2,1)} %get-tuple-element.113, f32[1024]{0:T(1024)S(1)} %get-tuple-element.115, f32[512]{0:T(512)S(1)} %bitcast.37, bf16[4,512,768]{2,1,0:T(8,128)(2,1)} %get-tuple-element.112), kind=kOutput, calls=%fused_computation.2.clone.1 | convolution fusion | flops 807403520 | bytes 3415040 | tf_op jit(solution)/shard_map/while/body/eval_jaxpr/dot_general | solution.py:37
  73.8 3.7 fusion.24
  77.6 3.7 fusion.24
  81.3 0.0 copy-start.1
  81.3 3.1 fusion.5
  84.4 38.6 %psum.64 = f32[2048]{0:T(1024)S(1)} all-reduce(f32[2048]{0:T(1024)S(1)} %bitcast.42), channel_id=1, replica_groups=mesh['row'=8,'cent'=16] {'cent'}, use_global_device_ids=true, to_apply=%region_7.8 | all-reduce | flops 2048 | bytes 16384 | tf_op jit(solution)/shard_map/psum | solution.py:16
  123.0 0.0 copy-done.1
  123.0 0.6 fusion.15
  123.6 3.1 fusion.6
  126.7 13.3 %all-reduce = (f32[1024]{0:T(1024)S(1)}, f32[]{:T(128)}) all-reduce(f32[1024]{0:T(1024)S(1)} %fusion.6, f32[]{:T(128)} %get-tuple-element.57), channel_id=1, replica_groups=mesh['row'=8,'cent'=16] {'row'}, use_global_device_ids=true, to_apply=%region_9.10 | all-reduce | flops 1025 | bytes 8200 | tf_op jit(solution)/shard_map/psum | solution.py:59
  140.7 3.1 fusion.7
  143.8 36.0 %psum.66 = f32[2048]{0:T(1024)S(1)} all-reduce(f32[2048]{0:T(1024)S(1)} %bitcast.43), channel_id=1, replica_groups=mesh['row'=8,'cent'=16] {'cent'}, use_global_device_ids=true, to_apply=%region_11.12 | all-reduce | flops 2048 | bytes 16384 | tf_op jit(solution)/shard_map/psum | solution.py:16
  179.8 3.1 fusion.8
  182.9 12.4 %psum.67 = f32[1024]{0:T(1024)S(1)} all-reduce(f32[1024]{0:T(1024)S(1)} %fusion.8), channel_id=1, replica_groups=mesh['row'=8,'cent'=16] {'row'}, use_global_device_ids=true, to_apply=%region_13.14 | all-reduce | flops 1024 | bytes 8192 | tf_op jit(solution)/shard_map/psum | solution.py:59
  195.3 3.1 fusion.9
  198.4 38.0 %psum.68 = f32[2048]{0:T(1024)S(1)} all-reduce(f32[2048]{0:T(1024)S(1)} %bitcast.44), channel_id=1, replica_groups=mesh['row'=8,'cent'=16] {'cent'}, use_global_device_ids=true, to_apply=%region_15.16 | all-reduce | flops 2048 | bytes 16384 | tf_op jit(solution)/shard_map/psum | solution.py:16
  236.4 3.1 fusion.10
  239.5 12.4 %psum.69 = f32[1024]{0:T(1024)S(1)} all-reduce(f32[1024]{0:T(1024)S(1)} %fusion.10), channel_id=1, replica_groups=mesh['row'=8,'cent'=16] {'row'}, use_global_device_ids=true, to_apply=%region_17.18 | all-reduce | flops 1024 | bytes 8192 | tf_op jit(solution)/shard_map/psum | solution.py:59
  251.9 0.6 multiply_log_fusion
  252.5 3.1 fusion.11
  255.6 36.2 %psum.70 = f32[2048]{0:T(1024)S(1)} all-reduce(f32[2048]{0:T(1024)S(1)} %bitcast.45), channel_id=1, replica_groups=mesh['row'=8,'cent'=16] {'cent'}, use_global_device_ids=true, to_apply=%region_19.20 | all-reduce | flops 2048 | bytes 16384 | tf_op jit(solution)/shard_map/psum | solution.py:16
  291.8 0.6 fusion.14
  292.4 2.8 fusion.13
  295.2 5.2 %convolution_bitcast_fusion = f32[768,1024]{0,1:T(8,128)} fusion(bf16[2048,1024]{1,0:T(8,128)(2,1)S(1)} %fusion.13, bf16[2048,768]{0,1:T(8,128)(2,1)S(1)} %copy-done), kind=kOutput, calls=%fused_computation.27 | convolution fusion | flops 3221225472 | bytes 10485760 | tf_op jit(solution)/shard_map/dot_general | solution.py:66
  300.4 0.0 all-reduce.3.cloned.1.call-update
  300.5 64.4 %all-reduce.3.cloned.1.call-done = f32[768,1024]{0,1:T(8,128)} async-done(((f32[768,1024]{0,1:T(8,128)}), f32[768,1024]{0,1:T(8,128)}) %all-reduce.3.cloned.1.call-update) | async-done | bytes 3145744 | tf_op jit(solution)/shard_map/psum | solution.py:69
  364.8 2.2 multiply_reduce_fusion.1
  367.0 1.6 dynamic-slice_multiply_fusion
  368.6 0.9 copy.7
  (20 shorter events, 0.1 us)
Async XLA Ops:
  7.2 53.5 %all-gather.2.cloned.1.call-start = ((), (), s32[]{:S(2)}) async-start(), calls=%async_computation | async-start | bytes 3342336 | tf_op jit(solution)/shard_map/all_gather | solution.py:21
  7.9 356.9 %all-reduce.3.cloned.1.call-start = ((), (), s32[]{:S(2)}) async-start(), calls=%async_computation.1 | async-start | bytes 6291456 | tf_op jit(solution)/shard_map/psum | solution.py:69
  60.7 2.8 copy-start
  81.3 41.8 %copy-start.1 = (f32[2048]{0:T(1024)S(1)}, f32[2048]{0:T(1024)}, u32[]{:S(2)}) copy-start(f32[2048]{0:T(1024)} %param.7) | copy-start | bytes 24580
Sparse Core Ops, SparseCore 0:
  10.2 50.4 all-gather.1
  300.6 64.2 all-reduce.2
where the time goes:
time: 377 us; the launch traced here: 376 us
  blocking collectives  187 us (50%)
  waiting for transfers between devices  116 us (31%)
  other arithmetic  34.5 us (9%)
  matrix products  20.1 us (5%)
  between operations  14.9 us (4%)
  local copies, waits for them, and re-layouts  3.97 us (1%)
    psum x4, blocking collectives, row_step(): masses = lax.psum(partial_mass, 'cent')  149 us
    psum x1, waiting for transfers between devices, per_device(): summed = lax.psum(term, 'row')  64.4 us
    all_gather x1, waiting for transfers between devices, per_device(): full_rows = lax.all_gather(vectors, 'cent', axis=1, tiled=True)  50.9 us
    psum x3, blocking collectives, per_device(): col_mass = lax.psum(partial_cols, 'row')  38.2 us
    dot_general x4, matrix products, kernel_rows(): jnp.dot(vec_block, centroids.T, preferred_element_type=jnp.float32)  14.9 us
    reduce_sum x4, other arithmetic, row_step(): jnp.sum(kernel.astype(jnp.float32) * col_scale[None, :], axis=1)  12.4 us
    reduce_sum x3, other arithmetic, per_device(): jnp.sum(kernel.astype(jnp.float32) * row_scale[:, None], axis=0)  9.23 us
  transfers between devices with their start and end apart: 2, of which 2 were waited for; matrix products, arithmetic and copies ran while one was open for 0% of the time, Pallas kernels for 0%

commit v1 on v0

v1 whole, which is shorter than its diff:
```python
import math

import jax
import jax.numpy as jnp
from jax import lax
from jax.sharding import Mesh
from jax.sharding import PartitionSpec as P

ITERS = 3


entropic_smoothing = 0.02

ROW = ("rx", "rc")
CENT = ("cy", "cz")


def shifted_sum(x, axis):
    n = lax.axis_size(axis)
    total = x
    for k in range(1, n):
        total = total + lax.ppermute(x, axis, [(i, (i + k) % n) for i in range(n)])
    return total


def reduce_cent(x):
    return shifted_sum(shifted_sum(x, "cz"), "cy")


def reduce_row(x):
    return shifted_sum(shifted_sum(x, "rc"), "rx")


def scatter_row(x):
    n = lax.axis_size(ROW)
    me = lax.axis_index(ROW)
    blocks = x.reshape(n, x.shape[0] // n, *x.shape[1:])
    total = lax.dynamic_index_in_dim(blocks, me, 0, keepdims=False)
    for k in range(1, n):
        piece = lax.dynamic_index_in_dim(blocks, (me + k) % n, 0, keepdims=False)
        total = total + lax.ppermute(piece, ROW, [(i, (i + k) % n) for i in range(n)])
    return total


def row_step(kernel, col_scale, weights):
    partial_mass = jnp.sum(kernel.astype(jnp.float32) * col_scale[None, :], axis=1)
    masses = reduce_cent(partial_mass)
    return weights / masses


def per_device(vectors, centroids, weights):
    full_rows = lax.all_gather(vectors, CENT, axis=1, tiled=True)
    local_rows = full_rows.shape[0]
    feature_dimension = full_rows.shape[1]
    local_centres = centroids.shape[0]
    centre_total = local_centres * lax.axis_size(CENT)
    block_rows = math.gcd(local_rows, 512)
    block_count = local_rows // block_rows
    reciprocal_vector_magnitudes = lax.rsqrt(
        jnp.mean(jnp.square(full_rows.astype(jnp.float32)), axis=1) + 1e-06
    )
    reciprocal_centroid_magnitudes = lax.rsqrt(
        jnp.mean(jnp.square(centroids.astype(jnp.float32)), axis=1) + 1e-06
    )

    def kernel_rows(inputs):
        vec_block, reciprocal_magnitude_tile = inputs
        similarity_matrix = jnp.dot(vec_block, centroids.T, preferred_element_type=jnp.float32)
        sharpened_similarity = (
            similarity_matrix
            * reciprocal_magnitude_tile[:, None]
            * reciprocal_centroid_magnitudes[None, :]
            / (feature_dimension * entropic_smoothing)
        )
        return jnp.exp(sharpened_similarity).astype(jnp.bfloat16)

    kernel = lax.map(
        kernel_rows,
        (
            full_rows.reshape(block_count, block_rows, feature_dimension),
            reciprocal_vector_magnitudes.reshape(block_count, block_rows),
        ),
    )
    kernel = kernel.reshape(local_rows, local_centres)
    weight_sum = reduce_row(jnp.sum(weights))
    col_scale = jnp.full((local_centres,), 1.0, jnp.float32) / centre_total
    row_scale = row_step(kernel, col_scale, weights)
    for sweep in range(ITERS):
        partial_cols = jnp.sum(kernel.astype(jnp.float32) * row_scale[:, None], axis=0)
        col_mass = reduce_row(partial_cols)
        col_scale = weight_sum / centre_total / col_mass
        row_scale = row_step(kernel, col_scale, weights)
    transport = (row_scale[:, None] * kernel.astype(jnp.float32) * col_scale[None, :]).astype(
        jnp.bfloat16
    )
    term = lax.dot_general(
        full_rows, transport, (((0,), (0,)), ((), ())), preferred_element_type=jnp.float32
    )
    own_summed = scatter_row(term)
    square_sum = reduce_row(jnp.sum(own_summed * own_summed, axis=0))
    new_centroids = own_summed * lax.rsqrt(square_sum / feature_dimension + 1e-06)[None, :]
    return (new_centroids, jnp.log(row_scale), jnp.log(centre_total * col_scale))


def solution(mesh):
    rows, cents = mesh.devices.shape
    split = Mesh(mesh.devices.reshape(rows // 2, 2, 4, cents // 4), ROW + CENT)
    return jax.shard_map(
        per_device,
        mesh=split,
        in_specs=(P(ROW, CENT), P(CENT, None), P(ROW)),
        out_specs=(P(ROW, CENT), P(ROW), P(CENT)),
        check_vma=False,
    )
```

time: 377 us -> 260 us (0.69)
  blocking collectives: 187 us -> 0 us
  starting transfers between devices: 0.08 us -> 74.5 us
  other arithmetic: 34.5 us -> 29.1 us
    psum x7 -> x0, blocking collectives: 187 us -> none  [the longest x4 149 us: row_step(): masses = lax.psum(partial_mass, 'cent')]
    ppermute x0 -> x51, starting transfers between devices: none -> 74.4 us  [the longest x44 61.7 us: shifted_sum(): total = total + lax.ppermute(x, axis, [(i, (i + k) % n) for i in range(n)])]
    psum x1 -> x0, waiting for transfers between devices: 64.4 us -> none  [per_device(): summed = lax.psum(term, 'row')]
    ppermute x0 -> x51, waiting for transfers between devices: none -> 63.4 us  [the longest x44 38.3 us: shifted_sum(): total = total + lax.ppermute(x, axis, [(i, (i + k) % n) for i in range(n)])]
    reduce_sum x4, other arithmetic: 12.4 us -> 7.98 us  [row_step(): jnp.sum(kernel.astype(jnp.float32) * col_scale[None, :], axis=1)]
  transfers between devices with their start and end apart: 2 -> 52, of which waited for: 2 -> 45; matrix products, arithmetic and copies ran while one was open for 0% -> 1% of each run, Pallas kernels for 0% -> 0%
where the time goes in v1:
time: 260 us; the launch traced here: 259 us
  waiting for transfers between devices  115 us (44%)
  starting transfers between devices  74.5 us (29%)
  other arithmetic  29.1 us (11%)
  matrix products  18.3 us (7%)
  between operations  17.4 us (7%)
  local copies, waits for them, and re-layouts  4.86 us (2%)
    ppermute x44, starting transfers between devices, shifted_sum(): total = total + lax.ppermute(x, axis, [(i, (i + k) % n) for i in range(n)])  61.7 us
    all_gather x1, waiting for transfers between devices, per_device(): full_rows = lax.all_gather(vectors, CENT, axis=1, tiled=True)  50.9 us
    ppermute x44, waiting for transfers between devices, shifted_sum(): total = total + lax.ppermute(x, axis, [(i, (i + k) % n) for i in range(n)])  38.3 us
    ppermute x7, waiting for transfers between devices, scatter_row(): lax.ppermute(piece, ROW, [(i, (i + k) % n) for i in range(n)])  25.1 us
    dot_general x4, matrix products, kernel_rows(): jnp.dot(vec_block, centroids.T, preferred_element_type=jnp.float32)  14.8 us
    ppermute x7, starting transfers between devices, scatter_row(): lax.ppermute(piece, ROW, [(i, (i + k) % n) for i in range(n)])  12.7 us
    reduce_sum x3, other arithmetic, per_device(): jnp.sum(kernel.astype(jnp.float32) * row_scale[:, None], axis=0)  9.53 us
    reduce_sum x4, other arithmetic, row_step(): jnp.sum(kernel.astype(jnp.float32) * col_scale[None, :], axis=1)  7.98 us
  transfers between devices with their start and end apart: 52, of which 45 were waited for; matrix products, arithmetic and copies ran while one was open for 1% of the time, Pallas kernels for 0%

profile of v1, /device:TPU:0, one launch (start us, length us, event | category | flops | bytes accessed | tf_op | source)
XLA Modules:
  0.0 259.3 jit_solution(12651149162503111064)
XLA Ops:
  7.9 1.8 multiply_reduce_fusion.1
  9.7 50.9 %all-gather.2.cloned.1.call-done = bf16[2048,768]{0,1:T(8,128)(2,1)} async-done(((bf16[2048,48]{0,1:T(8,128)(2,1)}), bf16[2048,768]{0,1:T(8,128)(2,1)}) %all-gather.2.cloned.1.call-update) | async-done | bytes 3145744 | tf_op jit(solution)/shard_map/all_gather | solution.py:52
  60.7 2.7 %multiply_reduce_fusion = f32[2048]{0:T(1024)S(1)} fusion(bf16[2048,768]{0,1:T(8,128)(2,1)} %all-gather.2.cloned.1.call-done), kind=kLoop, calls=%fused_computation.24 | loop fusion | flops 4716544 | bytes 3153920 | tf_op jit(solution)/shard_map/reduce_sum | solution.py:60
  63.5 2.8 %copy.6 = bf16[2048,768]{1,0:T(8,128)(2,1)} copy(bf16[2048,768]{0,1:T(8,128)(2,1)S(1)} %copy-done.2) | data formatting | bytes 6291456 | tf_op jit(solution)/shard_map/all_gather | solution.py:52
  66.3 14.9 %while.10 = (s32[]{:T(128)}, bf16[4,512,1024]{2,1,0:T(8,128)(2,1)}, bf16[4,512,768]{2,1,0:T(8,128)(2,1)}, bf16[1024,768]{1,0:T(8,128)(2,1)}, f32[4,512]{1,0:T(4,128)S(1)}, /*index=5*/f32[1024]{0:T(1024)S(1)}, s32[]{:T(128)}) while((s32[]{:T(128)}, bf16[4,512,1024]{2,1,0:T(8,128)(2,1)}, bf16[4,512,768]{2,1,0:T(8,128)(2,1)}, ...), condition=%wide.region_3.4_spmd, body=%wide.region_2.3_spmd.sunk | while | flops 807403520 | bytes 3419217 | solution.py:77
  66.3 3.7 %fusion.32 = bf16[4,512,1024]{2,1,0:T(8,128)(2,1)} fusion(bf16[4,512,1024]{2,1,0:T(8,128)(2,1)} %get-tuple-element.108, s32[]{:T(128)} %get-tuple-element.107, bf16[1024,768]{1,0:T(8,128)(2,1)} %get-tuple-element.117, f32[1024]{0:T(1024)S(1)} %get-tuple-element.119, f32[512]{0:T(512)S(1)} %bitcast.69, bf16[4,512,768]{2,1,0:T(8,128)(2,1)} %get-tuple-element.116), kind=kOutput, calls=%fused_computation.2.clone.1 | convolution fusion | flops 807403520 | bytes 3415040 | tf_op jit(solution)/shard_map/while/body/eval_jaxpr/dot_general | solution.py:68
  70.1 3.7 %fusion.32 = bf16[4,512,1024]{2,1,0:T(8,128)(2,1)} fusion(bf16[4,512,1024]{2,1,0:T(8,128)(2,1)} %get-tuple-element.108, s32[]{:T(128)} %get-tuple-element.107, bf16[1024,768]{1,0:T(8,128)(2,1)} %get-tuple-element.117, f32[1024]{0:T(1024)S(1)} %get-tuple-element.119, f32[512]{0:T(512)S(1)} %bitcast.69, bf16[4,512,768]{2,1,0:T(8,128)(2,1)} %get-tuple-element.116), kind=kOutput, calls=%fused_computation.2.clone.1 | convolution fusion | flops 807403520 | bytes 3415040 | tf_op jit(solution)/shard_map/while/body/eval_jaxpr/dot_general | solution.py:68
  73.8 3.7 %fusion.32 = bf16[4,512,1024]{2,1,0:T(8,128)(2,1)} fusion(bf16[4,512,1024]{2,1,0:T(8,128)(2,1)} %get-tuple-element.108, s32[]{:T(128)} %get-tuple-element.107, bf16[1024,768]{1,0:T(8,128)(2,1)} %get-tuple-element.117, f32[1024]{0:T(1024)S(1)} %get-tuple-element.119, f32[512]{0:T(512)S(1)} %bitcast.69, bf16[4,512,768]{2,1,0:T(8,128)(2,1)} %get-tuple-element.116), kind=kOutput, calls=%fused_computation.2.clone.1 | convolution fusion | flops 807403520 | bytes 3415040 | tf_op jit(solution)/shard_map/while/body/eval_jaxpr/dot_general | solution.py:68
  77.5 3.7 %fusion.32 = bf16[4,512,1024]{2,1,0:T(8,128)(2,1)} fusion(bf16[4,512,1024]{2,1,0:T(8,128)(2,1)} %get-tuple-element.108, s32[]{:T(128)} %get-tuple-element.107, bf16[1024,768]{1,0:T(8,128)(2,1)} %get-tuple-element.117, f32[1024]{0:T(1024)S(1)} %get-tuple-element.119, f32[512]{0:T(512)S(1)} %bitcast.69, bf16[4,512,768]{2,1,0:T(8,128)(2,1)} %get-tuple-element.116), kind=kOutput, calls=%fused_computation.2.clone.1 | convolution fusion | flops 807403520 | bytes 3415040 | tf_op jit(solution)/shard_map/while/body/eval_jaxpr/dot_general | solution.py:68
  81.2 3.1 %fusion.5 = f32[4,512]{1,0:T(4,128)S(1)} fusion(bf16[4,512,1024]{2,1,0:T(8,128)(2,1)} %get-tuple-element.35), kind=kLoop, calls=%fused_computation.14 | loop fusion | flops 6289408 | bytes 4202496 | tf_op jit(solution)/shard_map/reduce_sum | solution.py:46
  84.9 2.7 %collective-permute-start.5 = (f32[2048]{0:T(1024)S(1)}, f32[2048]{0:T(1024)S(1)}, u32[]{:S(2)}, u32[]{:S(2)}) collective-permute-start(f32[2048]{0:T(1024)S(1)} %bitcast.75), channel_id=1, source_target_pairs={{0,2},{1,3},{2,0},{3,1},{4,6},{5,7},{6,4},{7,5},{8,10},{9,11},{10,... | collective-permute-start | bytes 24584 | tf_op jit(solution)/shard_map/ppermute | solution.py:22
  91.5 2.7 %collective-permute-start.8 = (f32[2048]{0:T(1024)S(1)}, f32[2048]{0:T(1024)S(1)}, u32[]{:S(2)}, u32[]{:S(2)}) collective-permute-start(f32[2048]{0:T(1024)S(1)} %add_add_fusion.3), channel_id=1, source_target_pairs={{0,8},{4,12},{8,0},{12,4},{1,9},{5,13},{9,1},{13,5},{2,10},{6,14},... | collective-permute-start | bytes 24584 | tf_op jit(solution)/shard_map/ppermute | solution.py:22
  94.2 1.4 collective-permute-start.9
  98.5 3.1 %fusion.6 = f32[1024]{0:T(1024)S(1)} fusion(bf16[4,512,1024]{2,1,0:T(8,128)(2,1)} %get-tuple-element.35, f32[4,512]{1,0:T(4,128)S(1)} %mul.123), kind=kLoop, calls=%fused_computation.15 | loop fusion | flops 6290432 | bytes 4206592 | tf_op jit(solution)/shard_map/reduce_sum | solution.py:89
  102.8 1.5 collective-permute-start.11
  104.3 2.7 %collective-permute-start.12 = (f32[1024]{0:T(1024)S(1)}, f32[1024]{0:T(1024)S(1)}, u32[]{:S(2)}, u32[]{:S(2)}) collective-permute-start(f32[1024]{0:T(1024)S(1)} %add.254), channel_id=1, source_target_pairs={{0,64},{32,96},{64,0},{96,32},{1,65},{33,97},{65,1},{97,33},{2,66}... | collective-permute-start | bytes 12296 | tf_op jit(solution)/shard_map/ppermute | solution.py:22
  106.9 1.5 collective-permute-start.13
  108.4 1.3 collective-permute-done
  111.0 1.9 collective-permute-start.1
  112.9 2.2 collective-permute-start.2
  115.8 2.4 collective-permute-start.3
  120.1 3.1 %fusion.7 = f32[4,512]{1,0:T(4,128)S(1)} fusion(bf16[4,512,1024]{2,1,0:T(8,128)(2,1)} %get-tuple-element.35, f32[1024]{0:T(1024)S(1)} %add_divide_fusion.6), kind=kLoop, calls=%fused_computation.16 | loop fusion | flops 6289408 | bytes 4206592 | tf_op jit(solution)/shard_map/reduce_sum | solution.py:46
  124.4 2.9 %collective-permute-start.15 = (f32[2048]{0:T(1024)S(1)}, f32[2048]{0:T(1024)S(1)}, u32[]{:S(2)}, u32[]{:S(2)}) collective-permute-start(f32[2048]{0:T(1024)S(1)} %bitcast.79), channel_id=1, source_target_pairs={{0,2},{1,3},{2,0},{3,1},{4,6},{5,7},{6,4},{7,5},{8,10},{9,11},{10,... | collective-permute-start | bytes 24584 | tf_op jit(solution)/shard_map/ppermute | solution.py:22
  128.1 1.4 collective-permute-done.15
  129.5 1.4 collective-permute-done.16
  131.9 2.9 %collective-permute-start.18 = (f32[2048]{0:T(1024)S(1)}, f32[2048]{0:T(1024)S(1)}, u32[]{:S(2)}, u32[]{:S(2)}) collective-permute-start(f32[2048]{0:T(1024)S(1)} %add_add_fusion.2), channel_id=1, source_target_pairs={{0,8},{4,12},{8,0},{12,4},{1,9},{5,13},{9,1},{13,5},{2,10},{6,14},... | collective-permute-start | bytes 24584 | tf_op jit(solution)/shard_map/ppermute | solution.py:22
  135.8 1.2 collective-permute-done.18
  137.1 1.4 collective-permute-done.19
  138.5 3.2 %fusion.8 = f32[1024]{0:T(1024)S(1)} fusion(bf16[4,512,1024]{2,1,0:T(8,128)(2,1)} %get-tuple-element.35, f32[4,512]{1,0:T(4,128)S(1)} %mul.128), kind=kLoop, calls=%fused_computation.17 | loop fusion | flops 6290432 | bytes 4206592 | tf_op jit(solution)/shard_map/reduce_sum | solution.py:89
  143.0 1.9 collective-permute-start.21
  144.9 1.8 collective-permute-start.22
  146.7 1.8 collective-permute-start.23
  148.5 1.5 collective-permute-done.22
  151.6 2.8 %collective-permute-start.25 = (f32[2048]{0:T(1024)S(1)}, f32[2048]{0:T(1024)S(1)}, u32[]{:S(2)}, u32[]{:S(2)}) collective-permute-start(f32[2048]{0:T(1024)S(1)} %bitcast.83), channel_id=1, source_target_pairs={{0,2},{1,3},{2,0},{3,1},{4,6},{5,7},{6,4},{7,5},{8,10},{9,11},{10,... | collective-permute-start | bytes 24584 | tf_op jit(solution)/shard_map/ppermute | solution.py:22
  156.8 1.3 collective-permute-done.26
  158.1 2.7 %collective-permute-start.28 = (f32[2048]{0:T(1024)S(1)}, f32[2048]{0:T(1024)S(1)}, u32[]{:S(2)}, u32[]{:S(2)}) collective-permute-start(f32[2048]{0:T(1024)S(1)} %add_add_fusion.1), channel_id=1, source_target_pairs={{0,8},{4,12},{8,0},{12,4},{1,9},{5,13},{9,1},{13,5},{2,10},{6,14},... | collective-permute-start | bytes 24584 | tf_op jit(solution)/shard_map/ppermute | solution.py:22
  160.8 1.4 collective-permute-start.29
  164.5 3.2 %fusion.10 = f32[1024]{0:T(1024)S(1)} fusion(bf16[4,512,1024]{2,1,0:T(8,128)(2,1)} %get-tuple-element.35, f32[4,512]{1,0:T(4,128)S(1)} %mul.133), kind=kLoop, calls=%fused_computation.19 | loop fusion | flops 6290432 | bytes 4206592 | tf_op jit(solution)/shard_map/reduce_sum | solution.py:89
  169.6 3.8 %collective-permute-start.32 = (f32[1024]{0:T(1024)S(1)}, f32[1024]{0:T(1024)S(1)}, u32[]{:S(2)}, u32[]{:S(2)}) collective-permute-start(f32[1024]{0:T(1024)S(1)} %add.274), channel_id=1, source_target_pairs={{0,64},{32,96},{64,0},{96,32},{1,65},{33,97},{65,1},{97,33},{2,66}... | collective-permute-start | bytes 12296 | tf_op jit(solution)/shard_map/ppermute | solution.py:22
  173.8 1.3 collective-permute-done.32
  175.1 2.0 collective-permute-done.33
  178.6 1.3 collective-permute-start.34
  179.9 2.8 %collective-permute-start.35 = (f32[2048]{0:T(1024)S(1)}, f32[2048]{0:T(1024)S(1)}, u32[]{:S(2)}, u32[]{:S(2)}) collective-permute-start(f32[2048]{0:T(1024)S(1)} %bitcast.87), channel_id=1, source_target_pairs={{0,2},{1,3},{2,0},{3,1},{4,6},{5,7},{6,4},{7,5},{8,10},{9,11},{10,... | collective-permute-start | bytes 24584 | tf_op jit(solution)/shard_map/ppermute | solution.py:22
  183.5 1.5 collective-permute-done.35
  185.1 1.3 collective-permute-done.36
  187.5 2.7 %collective-permute-start.38 = (f32[2048]{0:T(1024)S(1)}, f32[2048]{0:T(1024)S(1)}, u32[]{:S(2)}, u32[]{:S(2)}) collective-permute-start(f32[2048]{0:T(1024)S(1)} %add_add_fusion), channel_id=1, source_target_pairs={{0,8},{4,12},{8,0},{12,4},{1,9},{5,13},{9,1},{13,5},{2,10},{6,14},... | collective-permute-start | bytes 24584 | tf_op jit(solution)/shard_map/ppermute | solution.py:22
  191.2 1.4 collective-permute-done.38
  192.6 1.2 collective-permute-done.39
  194.5 2.8 %fusion.13 = bf16[2048,1024]{1,0:T(8,128)(2,1)S(1)} fusion(bf16[4,512,1024]{2,1,0:T(8,128)(2,1)} %get-tuple-element.35, f32[1024]{0:T(1024)S(1)} %get-tuple-element.49, f32[2048]{0:T(1024)S(1)} %get-tuple-element.51), kind=kLoop, calls=%fused_computation.23 | loop fusion | flops 8388608 | bytes 8400896 | tf_op jit(solution)/shard_map/convert_element_type | solution.py:93
  197.3 3.5 %fusion.23 = f32[1024,768]{0,1:T(8,128)S(1)} fusion(bf16[2048,768]{0,1:T(8,128)(2,1)S(1)} %copy-done.2, bf16[2048,1024]{1,0:T(8,128)(2,1)S(1)} %fusion.13), kind=kOutput, calls=%fused_computation.59 | convolution fusion | flops 3221225472 | bytes 10485760 | tf_op jit(solution)/shard_map/dot_general | solution.py:96
  200.7 1.6 copy-done.3
  202.6 2.0 collective-permute-start.42
  204.6 2.3 collective-permute-start.43
  207.0 1.3 collective-permute-start.44
  208.3 6.2 %collective-permute-done.40 = f32[96,1024]{1,0:T(8,128)S(1)} collective-permute-done((f32[96,1024]{1,0:T(8,128)S(1)}, f32[96,1024]{1,0:T(8,128)S(1)}, u32[]{:S(2)}, u32[]{:S(2)}) %collective-permute-start.40) | collective-permute-done | bytes 393248 | tf_op jit(solution)/shard_map/ppermute | solution.py:41
  214.5 1.3 collective-permute-done.41
  215.8 6.9 %collective-permute-start.46 = (f32[96,1024]{1,0:T(8,128)S(1)}, f32[96,1024]{1,0:T(8,128)}, u32[]{:S(2)}, u32[]{:S(2)}) collective-permute-start(f32[96,1024]{1,0:T(8,128)S(1)} %get-tuple-element.55), channel_id=1, source_target_pairs={{0,112},{16,0},{32,16},{48,32},{64,48},{80,64},{96,80},{112,96},{1... | collective-permute-start | bytes 1179656 | tf_op jit(solution)/shard_map/ppermute | solution.py:41
  222.8 8.1 %collective-permute-done.42 = f32[96,1024]{1,0:T(8,128)S(1)} collective-permute-done((f32[96,1024]{1,0:T(8,128)S(1)}, f32[96,1024]{1,0:T(8,128)S(1)}, u32[]{:S(2)}, u32[]{:S(2)}) %collective-permute-start.42) | collective-permute-done | bytes 393248 | tf_op jit(solution)/shard_map/ppermute | solution.py:41
  230.9 1.3 collective-permute-done.43
  232.2 4.3 %collective-permute-done.44 = f32[96,1024]{1,0:T(8,128)} collective-permute-done((f32[96,1024]{1,0:T(8,128)S(1)}, f32[96,1024]{1,0:T(8,128)}, u32[]{:S(2)}, u32[]{:S(2)}) %collective-permute-start.44) | collective-permute-done | bytes 393248 | tf_op jit(solution)/shard_map/ppermute | solution.py:41
  236.6 3.8 %collective-permute-done.46 = f32[96,1024]{1,0:T(8,128)} collective-permute-done((f32[96,1024]{1,0:T(8,128)S(1)}, f32[96,1024]{1,0:T(8,128)}, u32[]{:S(2)}, u32[]{:S(2)}) %collective-permute-start.46) | collective-permute-done | bytes 393248 | tf_op jit(solution)/shard_map/ppermute | solution.py:41
  240.4 1.6 multiply_reduce_fusion.2
  244.8 3.2 %collective-permute-start.49 = (f32[1024]{0:T(1024)S(1)}, f32[1024]{0:T(1024)S(1)}, u32[]{:S(2)}, u32[]{:S(2)}) collective-permute-start(f32[1024]{0:T(1024)S(1)} %add.314), channel_id=1, source_target_pairs={{0,64},{32,96},{64,0},{96,32},{1,65},{33,97},{65,1},{97,33},{2,66}... | collective-permute-start | bytes 12296 | tf_op jit(solution)/shard_map/ppermute | solution.py:22
  249.9 1.7 collective-permute-done.50
  (102 shorter events, 34.7 us)
Async XLA Ops:
  7.2 53.5 %all-gather.2.cloned.1.call-start = ((), (), s32[]{:S(2)}) async-start(), calls=%async_computation | async-start | bytes 3342336 | tf_op jit(solution)/shard_map/all_gather | solution.py:52
  60.7 2.8 %copy-start.2 = (bf16[2048,768]{0,1:T(8,128)(2,1)S(1)}, bf16[2048,768]{0,1:T(8,128)(2,1)}, u32[]{:S(2)}) copy-start(bf16[2048,768]{0,1:T(8,128)(2,1)} %all-gather.2.cloned.1.call-done) | copy-start | bytes 9437188
  81.2 16.6 %copy-start.4 = (f32[2048]{0:T(1024)S(1)}, f32[2048]{0:T(1024)}, u32[]{:S(2)}) copy-start(f32[2048]{0:T(1024)} %param.7) | copy-start | bytes 24580
  84.3 4.9 %collective-permute-start.4 = (f32[2048]{0:T(1024)S(1)}, f32[2048]{0:T(1024)S(1)}, u32[]{:S(2)}, u32[]{:S(2)}) collective-permute-start(f32[2048]{0:T(1024)S(1)} %bitcast.74), channel_id=1, source_target_pairs={{0,1},{1,2},{2,3},{3,0},{4,5},{5,6},{6,7},{7,4},{8,9},{9,10},{10,1... | collective-permute-start | bytes 24584 | tf_op jit(solution)/shard_map/ppermute | solution.py:22
  84.9 5.2 %collective-permute-start.5 = (f32[2048]{0:T(1024)S(1)}, f32[2048]{0:T(1024)S(1)}, u32[]{:S(2)}, u32[]{:S(2)}) collective-permute-start(f32[2048]{0:T(1024)S(1)} %bitcast.75), channel_id=1, source_target_pairs={{0,2},{1,3},{2,0},{3,1},{4,6},{5,7},{6,4},{7,5},{8,10},{9,11},{10,... | collective-permute-start | bytes 24584 | tf_op jit(solution)/shard_map/ppermute | solution.py:22
  87.5 3.7 %collective-permute-start.6 = (f32[2048]{0:T(1024)S(1)}, f32[2048]{0:T(1024)S(1)}, u32[]{:S(2)}, u32[]{:S(2)}) collective-permute-start(f32[2048]{0:T(1024)S(1)} %bitcast.76), channel_id=1, source_target_pairs={{0,3},{1,0},{2,1},{3,2},{4,7},{5,4},{6,5},{7,6},{8,11},{9,8},{10,9... | collective-permute-start | bytes 24584 | tf_op jit(solution)/shard_map/ppermute | solution.py:22
  91.2 4.9 %collective-permute-start.7 = (f32[2048]{0:T(1024)S(1)}, f32[2048]{0:T(1024)S(1)}, u32[]{:S(2)}, u32[]{:S(2)}) collective-permute-start(f32[2048]{0:T(1024)S(1)} %add_add_fusion.3), channel_id=1, source_target_pairs={{0,4},{4,8},{8,12},{12,0},{1,5},{5,9},{9,13},{13,1},{2,6},{6,10},{... | collective-permute-start | bytes 24584 | tf_op jit(solution)/shard_map/ppermute | solution.py:22
  91.5 5.2 %collective-permute-start.8 = (f32[2048]{0:T(1024)S(1)}, f32[2048]{0:T(1024)S(1)}, u32[]{:S(2)}, u32[]{:S(2)}) collective-permute-start(f32[2048]{0:T(1024)S(1)} %add_add_fusion.3), channel_id=1, source_target_pairs={{0,8},{4,12},{8,0},{12,4},{1,9},{5,13},{9,1},{13,5},{2,10},{6,14},... | collective-permute-start | bytes 24584 | tf_op jit(solution)/shard_map/ppermute | solution.py:22
  94.2 3.7 %collective-permute-start.9 = (f32[2048]{0:T(1024)S(1)}, f32[2048]{0:T(1024)S(1)}, u32[]{:S(2)}, u32[]{:S(2)}) collective-permute-start(f32[2048]{0:T(1024)S(1)} %add_add_fusion.3), channel_id=1, source_target_pairs={{0,12},{4,0},{8,4},{12,8},{1,13},{5,1},{9,5},{13,9},{2,14},{6,2},{... | collective-permute-start | bytes 24584 | tf_op jit(solution)/shard_map/ppermute | solution.py:22
  101.5 1.2 collective-permute-start.10
  102.8 17.3 %collective-permute-start.11 = (f32[1024]{0:T(1024)S(1)}, f32[1024]{0:T(1024)S(1)}, u32[]{:S(2)}, u32[]{:S(2)}) collective-permute-start(f32[1024]{0:T(1024)S(1)} %add.254), channel_id=1, source_target_pairs={{0,32},{32,64},{64,96},{96,0},{1,33},{33,65},{65,97},{97,1},{2,34}... | collective-permute-start | bytes 12296 | tf_op jit(solution)/shard_map/ppermute | solution.py:22
  104.3 15.8 %collective-permute-start.12 = (f32[1024]{0:T(1024)S(1)}, f32[1024]{0:T(1024)S(1)}, u32[]{:S(2)}, u32[]{:S(2)}) collective-permute-start(f32[1024]{0:T(1024)S(1)} %add.254), channel_id=1, source_target_pairs={{0,64},{32,96},{64,0},{96,32},{1,65},{33,97},{65,1},{97,33},{2,66}... | collective-permute-start | bytes 12296 | tf_op jit(solution)/shard_map/ppermute | solution.py:22
  106.9 13.1 %collective-permute-start.13 = (f32[1024]{0:T(1024)S(1)}, f32[1024]{0:T(1024)S(1)}, u32[]{:S(2)}, u32[]{:S(2)}) collective-permute-start(f32[1024]{0:T(1024)S(1)} %add.254), channel_id=1, source_target_pairs={{0,96},{32,0},{64,32},{96,64},{1,97},{33,1},{65,33},{97,65},{2,98}... | collective-permute-start | bytes 12296 | tf_op jit(solution)/shard_map/ppermute | solution.py:22
  108.4 1.3 collective-permute-start
  111.0 4.8 %collective-permute-start.1 = (f32[]{:T(128)}, f32[]{:T(128)}, u32[]{:S(2)}, u32[]{:S(2)}) collective-permute-start(f32[]{:T(128)} %add.244), channel_id=1, source_target_pairs={{0,32},{32,64},{64,96},{96,0},{1,33},{33,65},{65,97},{97,1},{2,34}... | collective-permute-start | bytes 20 | tf_op jit(solution)/shard_map/ppermute | solution.py:22
  112.9 5.9 %collective-permute-start.2 = (f32[]{:T(128)}, f32[]{:T(128)}, u32[]{:S(2)}, u32[]{:S(2)}) collective-permute-start(f32[]{:T(128)} %add.244), channel_id=1, source_target_pairs={{0,64},{32,96},{64,0},{96,32},{1,65},{33,97},{65,1},{97,33},{2,66}... | collective-permute-start | bytes 20 | tf_op jit(solution)/shard_map/ppermute | solution.py:22
  115.8 3.7 %collective-permute-start.3 = (f32[]{:T(128)}, f32[]{:T(128)}, u32[]{:S(2)}, u32[]{:S(2)}) collective-permute-start(f32[]{:T(128)} %add.244), channel_id=1, source_target_pairs={{0,96},{32,0},{64,32},{96,64},{1,97},{33,1},{65,33},{97,65},{2,98}... | collective-permute-start | bytes 20 | tf_op jit(solution)/shard_map/ppermute | solution.py:22
  123.2 4.9 %collective-permute-start.14 = (f32[2048]{0:T(1024)S(1)}, f32[2048]{0:T(1024)S(1)}, u32[]{:S(2)}, u32[]{:S(2)}) collective-permute-start(f32[2048]{0:T(1024)S(1)} %bitcast.78), channel_id=1, source_target_pairs={{0,1},{1,2},{2,3},{3,0},{4,5},{5,6},{6,7},{7,4},{8,9},{9,10},{10,1... | collective-permute-start | bytes 24584 | tf_op jit(solution)/shard_map/ppermute | solution.py:22
  124.4 5.2 %collective-permute-start.15 = (f32[2048]{0:T(1024)S(1)}, f32[2048]{0:T(1024)S(1)}, u32[]{:S(2)}, u32[]{:S(2)}) collective-permute-start(f32[2048]{0:T(1024)S(1)} %bitcast.79), channel_id=1, source_target_pairs={{0,2},{1,3},{2,0},{3,1},{4,6},{5,7},{6,4},{7,5},{8,10},{9,11},{10,... | collective-permute-start | bytes 24584 | tf_op jit(solution)/shard_map/ppermute | solution.py:22
  127.3 3.7 %collective-permute-start.16 = (f32[2048]{0:T(1024)S(1)}, f32[2048]{0:T(1024)S(1)}, u32[]{:S(2)}, u32[]{:S(2)}) collective-permute-start(f32[2048]{0:T(1024)S(1)} %bitcast.80), channel_id=1, source_target_pairs={{0,3},{1,0},{2,1},{3,2},{4,7},{5,4},{6,5},{7,6},{8,11},{9,8},{10,9... | collective-permute-start | bytes 24584 | tf_op jit(solution)/shard_map/ppermute | solution.py:22
  131.0 4.9 %collective-permute-start.17 = (f32[2048]{0:T(1024)S(1)}, f32[2048]{0:T(1024)S(1)}, u32[]{:S(2)}, u32[]{:S(2)}) collective-permute-start(f32[2048]{0:T(1024)S(1)} %add_add_fusion.2), channel_id=1, source_target_pairs={{0,4},{4,8},{8,12},{12,0},{1,5},{5,9},{9,13},{13,1},{2,6},{6,10},{... | collective-permute-start | bytes 24584 | tf_op jit(solution)/shard_map/ppermute | solution.py:22
  131.9 5.2 %collective-permute-start.18 = (f32[2048]{0:T(1024)S(1)}, f32[2048]{0:T(1024)S(1)}, u32[]{:S(2)}, u32[]{:S(2)}) collective-permute-start(f32[2048]{0:T(1024)S(1)} %add_add_fusion.2), channel_id=1, source_target_pairs={{0,8},{4,12},{8,0},{12,4},{1,9},{5,13},{9,1},{13,5},{2,10},{6,14},... | collective-permute-start | bytes 24584 | tf_op jit(solution)/shard_map/ppermute | solution.py:22
  134.8 3.7 %collective-permute-start.19 = (f32[2048]{0:T(1024)S(1)}, f32[2048]{0:T(1024)S(1)}, u32[]{:S(2)}, u32[]{:S(2)}) collective-permute-start(f32[2048]{0:T(1024)S(1)} %add_add_fusion.2), channel_id=1, source_target_pairs={{0,12},{4,0},{8,4},{12,8},{1,13},{5,1},{9,5},{13,9},{2,14},{6,2},{... | collective-permute-start | bytes 24584 | tf_op jit(solution)/shard_map/ppermute | solution.py:22
  138.5 11.8 %copy-start = (bf16[4,512,1024]{2,1,0:T(8,128)(2,1)S(1)}, bf16[4,512,1024]{2,1,0:T(8,128)(2,1)}, u32[]{:S(2)}) copy-start(bf16[4,512,1024]{2,1,0:T(8,128)(2,1)} %get-tuple-element.35) | copy-start | bytes 12582916
  141.7 1.2 collective-permute-start.20
  143.0 5.5 %collective-permute-start.21 = (f32[1024]{0:T(1024)S(1)}, f32[1024]{0:T(1024)S(1)}, u32[]{:S(2)}, u32[]{:S(2)}) collective-permute-start(f32[1024]{0:T(1024)S(1)} %add.264), channel_id=1, source_target_pairs={{0,32},{32,64},{64,96},{96,0},{1,33},{33,65},{65,97},{97,1},{2,34}... | collective-permute-start | bytes 12296 | tf_op jit(solution)/shard_map/ppermute | solution.py:22
  144.9 5.1 %collective-permute-start.22 = (f32[1024]{0:T(1024)S(1)}, f32[1024]{0:T(1024)S(1)}, u32[]{:S(2)}, u32[]{:S(2)}) collective-permute-start(f32[1024]{0:T(1024)S(1)} %add.264), channel_id=1, source_target_pairs={{0,64},{32,96},{64,0},{96,32},{1,65},{33,97},{65,1},{97,33},{2,66}... | collective-permute-start | bytes 12296 | tf_op jit(solution)/shard_map/ppermute | solution.py:22
  146.7 3.6 %collective-permute-start.23 = (f32[1024]{0:T(1024)S(1)}, f32[1024]{0:T(1024)S(1)}, u32[]{:S(2)}, u32[]{:S(2)}) collective-permute-start(f32[1024]{0:T(1024)S(1)} %add.264), channel_id=1, source_target_pairs={{0,96},{32,0},{64,32},{96,64},{1,97},{33,1},{65,33},{97,65},{2,98}... | collective-permute-start | bytes 12296 | tf_op jit(solution)/shard_map/ppermute | solution.py:22
  151.3 4.9 %collective-permute-start.24 = (f32[2048]{0:T(1024)S(1)}, f32[2048]{0:T(1024)S(1)}, u32[]{:S(2)}, u32[]{:S(2)}) collective-permute-start(f32[2048]{0:T(1024)S(1)} %bitcast.82), channel_id=1, source_target_pairs={{0,1},{1,2},{2,3},{3,0},{4,5},{5,6},{6,7},{7,4},{8,9},{9,10},{10,1... | collective-permute-start | bytes 24584 | tf_op jit(solution)/shard_map/ppermute | solution.py:22
  151.6 5.2 %collective-permute-start.25 = (f32[2048]{0:T(1024)S(1)}, f32[2048]{0:T(1024)S(1)}, u32[]{:S(2)}, u32[]{:S(2)}) collective-permute-start(f32[2048]{0:T(1024)S(1)} %bitcast.83), channel_id=1, source_target_pairs={{0,2},{1,3},{2,0},{3,1},{4,6},{5,7},{6,4},{7,5},{8,10},{9,11},{10,... | collective-permute-start | bytes 24584 | tf_op jit(solution)/shard_map/ppermute | solution.py:22
  154.4 3.7 %collective-permute-start.26 = (f32[2048]{0:T(1024)S(1)}, f32[2048]{0:T(1024)S(1)}, u32[]{:S(2)}, u32[]{:S(2)}) collective-permute-start(f32[2048]{0:T(1024)S(1)} %bitcast.84), channel_id=1, source_target_pairs={{0,3},{1,0},{2,1},{3,2},{4,7},{5,4},{6,5},{7,6},{8,11},{9,8},{10,9... | collective-permute-start | bytes 24584 | tf_op jit(solution)/shard_map/ppermute | solution.py:22
  158.1 4.9 %collective-permute-start.27 = (f32[2048]{0:T(1024)S(1)}, f32[2048]{0:T(1024)S(1)}, u32[]{:S(2)}, u32[]{:S(2)}) collective-permute-start(f32[2048]{0:T(1024)S(1)} %add_add_fusion.1), channel_id=1, source_target_pairs={{0,4},{4,8},{8,12},{12,0},{1,5},{5,9},{9,13},{13,1},{2,6},{6,10},{... | collective-permute-start | bytes 24584 | tf_op jit(solution)/shard_map/ppermute | solution.py:22
  158.1 5.2 %collective-permute-start.28 = (f32[2048]{0:T(1024)S(1)}, f32[2048]{0:T(1024)S(1)}, u32[]{:S(2)}, u32[]{:S(2)}) collective-permute-start(f32[2048]{0:T(1024)S(1)} %add_add_fusion.1), channel_id=1, source_target_pairs={{0,8},{4,12},{8,0},{12,4},{1,9},{5,13},{9,1},{13,5},{2,10},{6,14},... | collective-permute-start | bytes 24584 | tf_op jit(solution)/shard_map/ppermute | solution.py:22
  160.8 3.7 %collective-permute-start.29 = (f32[2048]{0:T(1024)S(1)}, f32[2048]{0:T(1024)S(1)}, u32[]{:S(2)}, u32[]{:S(2)}) collective-permute-start(f32[2048]{0:T(1024)S(1)} %add_add_fusion.1), channel_id=1, source_target_pairs={{0,12},{4,0},{8,4},{12,8},{1,13},{5,1},{9,5},{13,9},{2,14},{6,2},{... | collective-permute-start | bytes 24584 | tf_op jit(solution)/shard_map/ppermute | solution.py:22
  164.5 13.2 %copy-start.1 = (bf16[4,512,1024]{2,1,0:T(8,128)(2,1)S(1)}, bf16[4,512,1024]{2,1,0:T(8,128)(2,1)}, u32[]{:S(2)}) copy-start(bf16[4,512,1024]{2,1,0:T(8,128)(2,1)} %get-tuple-element.35) | copy-start | bytes 12582916
  167.7 1.2 collective-permute-start.30
  169.0 4.8 %collective-permute-start.31 = (f32[1024]{0:T(1024)S(1)}, f32[1024]{0:T(1024)S(1)}, u32[]{:S(2)}, u32[]{:S(2)}) collective-permute-start(f32[1024]{0:T(1024)S(1)} %add.274), channel_id=1, source_target_pairs={{0,32},{32,64},{64,96},{96,0},{1,33},{33,65},{65,97},{97,1},{2,34}... | collective-permute-start | bytes 12296 | tf_op jit(solution)/shard_map/ppermute | solution.py:22
  169.6 5.5 %collective-permute-start.32 = (f32[1024]{0:T(1024)S(1)}, f32[1024]{0:T(1024)S(1)}, u32[]{:S(2)}, u32[]{:S(2)}) collective-permute-start(f32[1024]{0:T(1024)S(1)} %add.274), channel_id=1, source_target_pairs={{0,64},{32,96},{64,0},{96,32},{1,65},{33,97},{65,1},{97,33},{2,66}... | collective-permute-start | bytes 12296 | tf_op jit(solution)/shard_map/ppermute | solution.py:22
  173.4 3.6 %collective-permute-start.33 = (f32[1024]{0:T(1024)S(1)}, f32[1024]{0:T(1024)S(1)}, u32[]{:S(2)}, u32[]{:S(2)}) collective-permute-start(f32[1024]{0:T(1024)S(1)} %add.274), channel_id=1, source_target_pairs={{0,96},{32,0},{64,32},{96,64},{1,97},{33,1},{65,33},{97,65},{2,98}... | collective-permute-start | bytes 12296 | tf_op jit(solution)/shard_map/ppermute | solution.py:22
  178.6 4.9 %collective-permute-start.34 = (f32[2048]{0:T(1024)S(1)}, f32[2048]{0:T(1024)S(1)}, u32[]{:S(2)}, u32[]{:S(2)}) collective-permute-start(f32[2048]{0:T(1024)S(1)} %bitcast.86), channel_id=1, source_target_pairs={{0,1},{1,2},{2,3},{3,0},{4,5},{5,6},{6,7},{7,4},{8,9},{9,10},{10,1... | collective-permute-start | bytes 24584 | tf_op jit(solution)/shard_map/ppermute | solution.py:22
  179.9 5.2 %collective-permute-start.35 = (f32[2048]{0:T(1024)S(1)}, f32[2048]{0:T(1024)S(1)}, u32[]{:S(2)}, u32[]{:S(2)}) collective-permute-start(f32[2048]{0:T(1024)S(1)} %bitcast.87), channel_id=1, source_target_pairs={{0,2},{1,3},{2,0},{3,1},{4,6},{5,7},{6,4},{7,5},{8,10},{9,11},{10,... | collective-permute-start | bytes 24584 | tf_op jit(solution)/shard_map/ppermute | solution.py:22
  182.7 3.7 %collective-permute-start.36 = (f32[2048]{0:T(1024)S(1)}, f32[2048]{0:T(1024)S(1)}, u32[]{:S(2)}, u32[]{:S(2)}) collective-permute-start(f32[2048]{0:T(1024)S(1)} %bitcast.88), channel_id=1, source_target_pairs={{0,3},{1,0},{2,1},{3,2},{4,7},{5,4},{6,5},{7,6},{8,11},{9,8},{10,9... | collective-permute-start | bytes 24584 | tf_op jit(solution)/shard_map/ppermute | solution.py:22
  186.3 4.9 %collective-permute-start.37 = (f32[2048]{0:T(1024)S(1)}, f32[2048]{0:T(1024)S(1)}, u32[]{:S(2)}, u32[]{:S(2)}) collective-permute-start(f32[2048]{0:T(1024)S(1)} %add_add_fusion), channel_id=1, source_target_pairs={{0,4},{4,8},{8,12},{12,0},{1,5},{5,9},{9,13},{13,1},{2,6},{6,10},{... | collective-permute-start | bytes 24584 | tf_op jit(solution)/shard_map/ppermute | solution.py:22
  187.5 5.2 %collective-permute-start.38 = (f32[2048]{0:T(1024)S(1)}, f32[2048]{0:T(1024)S(1)}, u32[]{:S(2)}, u32[]{:S(2)}) collective-permute-start(f32[2048]{0:T(1024)S(1)} %add_add_fusion), channel_id=1, source_target_pairs={{0,8},{4,12},{8,0},{12,4},{1,9},{5,13},{9,1},{13,5},{2,10},{6,14},... | collective-permute-start | bytes 24584 | tf_op jit(solution)/shard_map/ppermute | solution.py:22
  190.2 3.7 %collective-permute-start.39 = (f32[2048]{0:T(1024)S(1)}, f32[2048]{0:T(1024)S(1)}, u32[]{:S(2)}, u32[]{:S(2)}) collective-permute-start(f32[2048]{0:T(1024)S(1)} %add_add_fusion), channel_id=1, source_target_pairs={{0,12},{4,0},{8,4},{12,8},{1,13},{5,1},{9,5},{13,9},{2,14},{6,2},{... | collective-permute-start | bytes 24584 | tf_op jit(solution)/shard_map/ppermute | solution.py:22
  200.7 1.6 copy-start.3
  202.5 12.0 %collective-permute-start.40 = (f32[96,1024]{1,0:T(8,128)S(1)}, f32[96,1024]{1,0:T(8,128)S(1)}, u32[]{:S(2)}, u32[]{:S(2)}) collective-permute-start(f32[96,1024]{1,0:T(8,128)S(1)} %get-tuple-element.54), channel_id=1, source_target_pairs={{0,16},{16,32},{32,48},{48,64},{64,80},{80,96},{96,112},{112,0},{1... | collective-permute-start | bytes 1179656 | tf_op jit(solution)/shard_map/ppermute | solution.py:41
  202.6 13.3 %collective-permute-start.41 = (f32[96,1024]{1,0:T(8,128)S(1)}, f32[96,1024]{1,0:T(8,128)S(1)}, u32[]{:S(2)}, u32[]{:S(2)}) collective-permute-start(f32[96,1024]{1,0:T(8,128)S(1)} %get-tuple-element.60), channel_id=1, source_target_pairs={{0,32},{16,48},{32,64},{48,80},{64,96},{80,112},{96,0},{112,16},{1... | collective-permute-start | bytes 1179656 | tf_op jit(solution)/shard_map/ppermute | solution.py:41
  202.6 28.3 %collective-permute-start.42 = (f32[96,1024]{1,0:T(8,128)S(1)}, f32[96,1024]{1,0:T(8,128)S(1)}, u32[]{:S(2)}, u32[]{:S(2)}) collective-permute-start(f32[96,1024]{1,0:T(8,128)S(1)} %get-tuple-element.59), channel_id=1, source_target_pairs={{0,48},{16,64},{32,80},{48,96},{64,112},{80,0},{96,16},{112,32},{1... | collective-permute-start | bytes 1179656 | tf_op jit(solution)/shard_map/ppermute | solution.py:41
  204.6 27.6 %collective-permute-start.43 = (f32[96,1024]{1,0:T(8,128)S(1)}, f32[96,1024]{1,0:T(8,128)S(1)}, u32[]{:S(2)}, u32[]{:S(2)}) collective-permute-start(f32[96,1024]{1,0:T(8,128)S(1)} %get-tuple-element.58), channel_id=1, source_target_pairs={{0,64},{16,80},{32,96},{48,112},{64,0},{80,16},{96,32},{112,48},{1... | collective-permute-start | bytes 1179656 | tf_op jit(solution)/shard_map/ppermute | solution.py:41
  207.0 29.6 %collective-permute-start.44 = (f32[96,1024]{1,0:T(8,128)S(1)}, f32[96,1024]{1,0:T(8,128)}, u32[]{:S(2)}, u32[]{:S(2)}) collective-permute-start(f32[96,1024]{1,0:T(8,128)S(1)} %get-tuple-element.57), channel_id=1, source_target_pairs={{0,80},{16,96},{32,112},{48,0},{64,16},{80,32},{96,48},{112,64},{1... | collective-permute-start | bytes 1179656 | tf_op jit(solution)/shard_map/ppermute | solution.py:41
  214.5 22.0 %collective-permute-start.45 = (f32[96,1024]{1,0:T(8,128)S(1)}, f32[96,1024]{1,0:T(8,128)}, u32[]{:S(2)}, u32[]{:S(2)}) collective-permute-start(f32[96,1024]{1,0:T(8,128)S(1)} %get-tuple-element.56), channel_id=1, source_target_pairs={{0,96},{16,112},{32,0},{48,16},{64,32},{80,48},{96,64},{112,80},{1... | collective-permute-start | bytes 1179656 | tf_op jit(solution)/shard_map/ppermute | solution.py:41
  215.8 24.5 %collective-permute-start.46 = (f32[96,1024]{1,0:T(8,128)S(1)}, f32[96,1024]{1,0:T(8,128)}, u32[]{:S(2)}, u32[]{:S(2)}) collective-permute-start(f32[96,1024]{1,0:T(8,128)S(1)} %get-tuple-element.55), channel_id=1, source_target_pairs={{0,112},{16,0},{32,16},{48,32},{64,48},{80,64},{96,80},{112,96},{1... | collective-permute-start | bytes 1179656 | tf_op jit(solution)/shard_map/ppermute | solution.py:41
  242.0 1.9 collective-permute-start.47
  243.9 4.8 %collective-permute-start.48 = (f32[1024]{0:T(1024)S(1)}, f32[1024]{0:T(1024)S(1)}, u32[]{:S(2)}, u32[]{:S(2)}) collective-permute-start(f32[1024]{0:T(1024)S(1)} %add.314), channel_id=1, source_target_pairs={{0,32},{32,64},{64,96},{96,0},{1,33},{33,65},{65,97},{97,1},{2,34}... | collective-permute-start | bytes 12296 | tf_op jit(solution)/shard_map/ppermute | solution.py:22
  244.8 5.1 %collective-permute-start.49 = (f32[1024]{0:T(1024)S(1)}, f32[1024]{0:T(1024)S(1)}, u32[]{:S(2)}, u32[]{:S(2)}) collective-permute-start(f32[1024]{0:T(1024)S(1)} %add.314), channel_id=1, source_target_pairs={{0,64},{32,96},{64,0},{96,32},{1,65},{33,97},{65,1},{97,33},{2,66}... | collective-permute-start | bytes 12296 | tf_op jit(solution)/shard_map/ppermute | solution.py:22
  248.0 3.6 %collective-permute-start.50 = (f32[1024]{0:T(1024)S(1)}, f32[1024]{0:T(1024)S(1)}, u32[]{:S(2)}, u32[]{:S(2)}) collective-permute-start(f32[1024]{0:T(1024)S(1)} %add.314), channel_id=1, source_target_pairs={{0,96},{32,0},{64,32},{96,64},{1,97},{33,1},{65,33},{97,65},{2,98}... | collective-permute-start | bytes 12296 | tf_op jit(solution)/shard_map/ppermute | solution.py:22
Sparse Core Ops, SparseCore 0:
  10.2 50.4 all-gather.1

commit v2 on v1

--- a/solution.py
+++ b/solution.py
@@ -1,5 +1,3 @@
-import math
-
 import jax
 import jax.numpy as jnp
 from jax import lax
@@ -32,13 +30,17 @@
 
 
 def scatter_row(x):
-    n = lax.axis_size(ROW)
-    me = lax.axis_index(ROW)
-    blocks = x.reshape(n, x.shape[0] // n, *x.shape[1:])
-    total = lax.dynamic_index_in_dim(blocks, me, 0, keepdims=False)
-    for k in range(1, n):
-        piece = lax.dynamic_index_in_dim(blocks, (me + k) % n, 0, keepdims=False)
-        total = total + lax.ppermute(piece, ROW, [(i, (i + k) % n) for i in range(n)])
+    chips, cores = lax.axis_size("rx"), lax.axis_size("rc")
+    rx, rc = lax.axis_index("rx"), lax.axis_index("rc")
+    blocks = x.reshape(chips, cores, x.shape[0] // (chips * cores), *x.shape[1:])
+    half = lax.dynamic_index_in_dim(blocks, rc, 1, keepdims=False)
+    for k in range(1, cores):
+        piece = lax.dynamic_index_in_dim(blocks, (rc + k) % cores, 1, keepdims=False)
+        half = half + lax.ppermute(piece, "rc", [(i, (i + k) % cores) for i in range(cores)])
+    total = lax.dynamic_index_in_dim(half, rx, 0, keepdims=False)
+    for k in range(1, chips):
+        piece = lax.dynamic_index_in_dim(half, (rx + k) % chips, 0, keepdims=False)
+        total = total + lax.ppermute(piece, "rx", [(i, (i + k) % chips) for i in range(chips)])
     return total
 
 
@@ -54,34 +56,20 @@
     feature_dimension = full_rows.shape[1]
     local_centres = centroids.shape[0]
     centre_total = local_centres * lax.axis_size(CENT)
-    block_rows = math.gcd(local_rows, 512)
-    block_count = local_rows // block_rows
     reciprocal_vector_magnitudes = lax.rsqrt(
         jnp.mean(jnp.square(full_rows.astype(jnp.float32)), axis=1) + 1e-06
     )
     reciprocal_centroid_magnitudes = lax.rsqrt(
         jnp.mean(jnp.square(centroids.astype(jnp.float32)), axis=1) + 1e-06
     )
-
-    def kernel_rows(inputs):
-        vec_block, reciprocal_magnitude_tile = inputs
-        similarity_matrix = jnp.dot(vec_block, centroids.T, preferred_element_type=jnp.float32)
-        sharpened_similarity = (
-            similarity_matrix
-            * reciprocal_magnitude_tile[:, None]
-            * reciprocal_centroid_magnitudes[None, :]
-            / (feature_dimension * entropic_smoothing)
-        )
-        return jnp.exp(sharpened_similarity).astype(jnp.bfloat16)
-
-    kernel = lax.map(
-        kernel_rows,
-        (
-            full_rows.reshape(block_count, block_rows, feature_dimension),
-            reciprocal_vector_magnitudes.reshape(block_count, block_rows),
-        ),
+    similarity_matrix = jnp.dot(full_rows, centroids.T, preferred_element_type=jnp.float32)
+    sharpened_similarity = (
+        similarity_matrix
+        * reciprocal_vector_magnitudes[:, None]
+        * reciprocal_centroid_magnitudes[None, :]
+        / (feature_dimension * entropic_smoothing)
     )
-    kernel = kernel.reshape(local_rows, local_centres)
+    kernel = jnp.exp(sharpened_similarity).astype(jnp.bfloat16)
     weight_sum = reduce_row(jnp.sum(weights))
     col_scale = jnp.full((local_centres,), 1.0, jnp.float32) / centre_total
     row_scale = row_step(kernel, col_scale, weights)

time: 260 us -> 226 us (0.87)
  other arithmetic: 29.1 us -> 17.5 us
  starting transfers between devices: 74.5 us -> 64.7 us
  matrix products: 18.3 us -> 12.3 us
  waiting for transfers between devices: 115 us -> 111 us
  local copies, waits for them, and re-layouts: 4.86 us -> 1.93 us
    ppermute x7 -> x4, starting transfers between devices: 12.7 us -> 4.28 us  [the longest x3 4.2 us: scatter_row(): lax.ppermute(piece, 'rx', [(i, (i + k) % chips) for i in range(chips)])]
    dot_general x4 -> x1, matrix products: 14.8 us -> 6.6 us  [per_device(): jnp.dot(full_rows, centroids.T, preferred_element_type=jnp.float32)]
    reduce_sum x3, other arithmetic: 9.53 us -> 2.67 us  [per_device(): jnp.sum(kernel.astype(jnp.float32) * row_scale[:, None], axis=0)]
    ppermute x7 -> x4, waiting for transfers between devices: 25.1 us -> 20.7 us  [the longest x3 17.4 us: scatter_row(): lax.ppermute(piece, 'rx', [(i, (i + k) % chips) for i in range(chips)])]
    reduce_sum x4 -> x3, other arithmetic: 7.98 us -> 5 us  [row_step(): jnp.sum(kernel.astype(jnp.float32) * col_scale[None, :], axis=1)]
    all_gather x1 -> x0, local copies, waits for them, and re-layouts: 2.84 us -> none  [per_device(): full_rows = lax.all_gather(vectors, CENT, axis=1, tiled=True)]
    convert_element_type x1 -> x0, other arithmetic: 2.79 us -> none  [per_device(): (row_scale[:, None] * kernel.astype(jnp.float32) * col_scale[None, :]).as...]
  transfers between devices with their start and end apart: 52 -> 49, of which waited for: 45 -> 43; matrix products, arithmetic and copies ran while one was open for 1% -> 1% of each run, Pallas kernels for 0% -> 0%
where the time goes in v2:
time: 226 us; the launch traced here: 225 us
  waiting for transfers between devices  111 us (49%)
  starting transfers between devices  64.7 us (29%)
  other arithmetic  17.5 us (8%)
  between operations  17.5 us (8%)
  matrix products  12.3 us (5%)
    ppermute x44, starting transfers between devices, shifted_sum(): total = total + lax.ppermute(x, axis, [(i, (i + k) % n) for i in range(n)])  60.4 us
    all_gather x1, waiting for transfers between devices, per_device(): full_rows = lax.all_gather(vectors, CENT, axis=1, tiled=True)  51 us
    ppermute x44, waiting for transfers between devices, shifted_sum(): total = total + lax.ppermute(x, axis, [(i, (i + k) % n) for i in range(n)])  39.1 us
    ppermute x3, waiting for transfers between devices, scatter_row(): lax.ppermute(piece, 'rx', [(i, (i + k) % chips) for i in range(chips)])  17.4 us
    dot_general x1, matrix products, per_device(): jnp.dot(full_rows, centroids.T, preferred_element_type=jnp.float32)  6.6 us
    dot_general x1, matrix products, per_device(): lax.dot_general(full_rows, transport, (((0,), (0,)), ((), ())), preferred...  5.69 us
    reduce_sum x3, other arithmetic, row_step(): jnp.sum(kernel.astype(jnp.float32) * col_scale[None, :], axis=1)  5 us
  transfers between devices with their start and end apart: 49, of which 43 were waited for; matrix products, arithmetic and copies ran while one was open for 1% of the time, Pallas kernels for 0%

profile of v2, /device:TPU:0, one launch (start us, length us, event | category | flops | bytes accessed | tf_op | source)
XLA Modules:
  0.0 225.5 jit_solution(10450461926518699902)
XLA Ops:
  7.9 1.8 multiply_reduce_fusion.1
  9.7 51.0 %all-gather.2.cloned.1.call-done = bf16[2048,768]{0,1:T(8,128)(2,1)} async-done(((bf16[2048,48]{0,1:T(8,128)(2,1)}), bf16[2048,768]{0,1:T(8,128)(2,1)}) %all-gather.2.cloned.1.call-update) | async-done | bytes 3145744 | tf_op jit(solution)/shard_map/all_gather | solution.py:54
  60.7 2.6 %multiply_reduce_fusion = f32[2048]{0:T(1024)S(1)} fusion(bf16[2048,768]{0,1:T(8,128)(2,1)} %all-gather.2.cloned.1.call-done), kind=kLoop, calls=%fused_computation.18 | loop fusion | flops 4716544 | bytes 3153920 | tf_op jit(solution)/shard_map/reduce_sum | solution.py:60
  63.2 6.6 %fusion = (f32[2048]{0:T(1024)S(1)}, bf16[2048,1024]{0,1:T(8,128)(2,1)S(1)}) fusion(f32[1024]{0:T(1024)S(1)} %add_rsqrt_fusion.2, f32[2048]{0:T(1024)S(1)} %add_rsqrt_fusion, bf16[1024,768]{1,0:T(8,128)(2,1)S(1)} %copy-done.4, bf16[2048,768]{0,1:T(8,128)(2,1)} %all-gather.2.cloned.1.call-done), kind=kOutput, calls=%fused_computation.8 | convolution fusion | flops 3235903488 | bytes 8933376 | tf_op jit(solution)/shard_map/dot_general | solution.py:65
  70.4 2.7 %collective-permute-start.5 = (f32[2048]{0:T(1024)S(1)}, f32[2048]{0:T(1024)S(1)}, u32[]{:S(2)}, u32[]{:S(2)}) collective-permute-start(f32[2048]{0:T(1024)S(1)} %get-tuple-element.14), channel_id=1, source_target_pairs={{0,2},{1,3},{2,0},{3,1},{4,6},{5,7},{6,4},{7,5},{8,10},{9,11},{10,... | collective-permute-start | bytes 24584 | tf_op jit(solution)/shard_map/ppermute | solution.py:20
  73.1 1.2 collective-permute-start.6
  75.6 1.2 collective-permute-done.6
  77.1 2.7 %collective-permute-start.8 = (f32[2048]{0:T(1024)S(1)}, f32[2048]{0:T(1024)S(1)}, u32[]{:S(2)}, u32[]{:S(2)}) collective-permute-start(f32[2048]{0:T(1024)S(1)} %add_add_fusion.3), channel_id=1, source_target_pairs={{0,8},{4,12},{8,0},{12,4},{1,9},{5,13},{9,1},{13,5},{2,10},{6,14},... | collective-permute-start | bytes 24584 | tf_op jit(solution)/shard_map/ppermute | solution.py:20
  79.7 1.4 collective-permute-start.9
  82.2 1.2 collective-permute-done.9
  84.0 0.9 fusion.1
  85.0 1.2 collective-permute-done.10
  86.2 1.5 collective-permute-start.11
  87.6 2.7 %collective-permute-start.12 = (f32[1024]{0:T(1024)S(1)}, f32[1024]{0:T(1024)S(1)}, u32[]{:S(2)}, u32[]{:S(2)}) collective-permute-start(f32[1024]{0:T(1024)S(1)} %add.222), channel_id=1, source_target_pairs={{0,64},{32,96},{64,0},{96,32},{1,65},{33,97},{65,1},{97,33},{2,66}... | collective-permute-start | bytes 12296 | tf_op jit(solution)/shard_map/ppermute | solution.py:20
  90.3 1.5 collective-permute-start.13
  91.8 1.4 collective-permute-done
  94.5 1.9 collective-permute-start.1
  96.4 2.2 collective-permute-start.2
  99.4 2.3 collective-permute-start.3
  103.8 3.2 %fusion.2 = f32[2048]{0:T(1024)S(1)} fusion(bf16[2048,1024]{0,1:T(8,128)(2,1)} %copy-done, f32[1024]{0:T(1024)S(1)} %add_divide_fusion.6), kind=kLoop, calls=%fused_computation.10 | loop fusion | flops 6289408 | bytes 4206592 | tf_op jit(solution)/shard_map/reduce_sum | solution.py:48
  107.0 1.2 collective-permute-start.14
  108.2 2.9 %collective-permute-start.15 = (f32[2048]{0:T(1024)S(1)}, f32[2048]{0:T(1024)S(1)}, u32[]{:S(2)}, u32[]{:S(2)}) collective-permute-start(f32[2048]{0:T(1024)S(1)} %fusion.2), channel_id=1, source_target_pairs={{0,2},{1,3},{2,0},{3,1},{4,6},{5,7},{6,4},{7,5},{8,10},{9,11},{10,... | collective-permute-start | bytes 24584 | tf_op jit(solution)/shard_map/ppermute | solution.py:20
  112.0 1.4 collective-permute-done.15
  113.4 1.4 collective-permute-done.16
  114.8 0.9 collective-permute-start.17
  115.7 2.9 %collective-permute-start.18 = (f32[2048]{0:T(1024)S(1)}, f32[2048]{0:T(1024)S(1)}, u32[]{:S(2)}, u32[]{:S(2)}) collective-permute-start(f32[2048]{0:T(1024)S(1)} %add_add_fusion.2), channel_id=1, source_target_pairs={{0,8},{4,12},{8,0},{12,4},{1,9},{5,13},{9,1},{13,5},{2,10},{6,14},... | collective-permute-start | bytes 24584 | tf_op jit(solution)/shard_map/ppermute | solution.py:20
  119.7 1.2 collective-permute-done.18
  120.9 1.4 collective-permute-done.19
  123.3 1.2 collective-permute-done.20
  124.5 1.8 collective-permute-start.21
  126.3 1.8 collective-permute-start.22
  128.1 1.8 collective-permute-start.23
  129.9 1.5 collective-permute-done.22
  131.7 0.9 fusion.4
  133.0 2.8 %collective-permute-start.25 = (f32[2048]{0:T(1024)S(1)}, f32[2048]{0:T(1024)S(1)}, u32[]{:S(2)}, u32[]{:S(2)}) collective-permute-start(f32[2048]{0:T(1024)S(1)} %fusion.4), channel_id=1, source_target_pairs={{0,2},{1,3},{2,0},{3,1},{4,6},{5,7},{6,4},{7,5},{8,10},{9,11},{10,... | collective-permute-start | bytes 24584 | tf_op jit(solution)/shard_map/ppermute | solution.py:20
  135.8 1.1 collective-permute-start.26
  138.2 1.3 collective-permute-done.26
  139.4 2.7 %collective-permute-start.28 = (f32[2048]{0:T(1024)S(1)}, f32[2048]{0:T(1024)S(1)}, u32[]{:S(2)}, u32[]{:S(2)}) collective-permute-start(f32[2048]{0:T(1024)S(1)} %add_add_fusion.1), channel_id=1, source_target_pairs={{0,8},{4,12},{8,0},{12,4},{1,9},{5,13},{9,1},{13,5},{2,10},{6,14},... | collective-permute-start | bytes 24584 | tf_op jit(solution)/shard_map/ppermute | solution.py:20
  142.1 1.4 collective-permute-start.29
  144.7 1.1 collective-permute-done.29
  146.8 1.2 collective-permute-done.30
  148.6 3.8 %collective-permute-start.32 = (f32[1024]{0:T(1024)S(1)}, f32[1024]{0:T(1024)S(1)}, u32[]{:S(2)}, u32[]{:S(2)}) collective-permute-start(f32[1024]{0:T(1024)S(1)} %add.242), channel_id=1, source_target_pairs={{0,64},{32,96},{64,0},{96,32},{1,65},{33,97},{65,1},{97,33},{2,66}... | collective-permute-start | bytes 12296 | tf_op jit(solution)/shard_map/ppermute | solution.py:20
  152.8 1.3 collective-permute-done.32
  154.0 2.0 collective-permute-done.33
  157.5 1.3 collective-permute-start.34
  158.8 2.8 %collective-permute-start.35 = (f32[2048]{0:T(1024)S(1)}, f32[2048]{0:T(1024)S(1)}, u32[]{:S(2)}, u32[]{:S(2)}) collective-permute-start(f32[2048]{0:T(1024)S(1)} %fusion.6), channel_id=1, source_target_pairs={{0,2},{1,3},{2,0},{3,1},{4,6},{5,7},{6,4},{7,5},{8,10},{9,11},{10,... | collective-permute-start | bytes 24584 | tf_op jit(solution)/shard_map/ppermute | solution.py:20
  162.4 1.5 collective-permute-done.35
  164.0 1.3 collective-permute-done.36
  165.3 1.1 collective-permute-start.37
  166.4 2.7 %collective-permute-start.38 = (f32[2048]{0:T(1024)S(1)}, f32[2048]{0:T(1024)S(1)}, u32[]{:S(2)}, u32[]{:S(2)}) collective-permute-start(f32[2048]{0:T(1024)S(1)} %add_add_fusion), channel_id=1, source_target_pairs={{0,8},{4,12},{8,0},{12,4},{1,9},{5,13},{9,1},{13,5},{2,10},{6,14},... | collective-permute-start | bytes 24584 | tf_op jit(solution)/shard_map/ppermute | solution.py:20
  170.1 1.4 collective-permute-done.38
  171.6 1.2 collective-permute-done.39
  173.4 5.7 %fusion.9 = f32[1024,768]{0,1:T(8,128)S(1)} fusion(bf16[2048,768]{0,1:T(8,128)(2,1)S(1)} %copy-done.2, bf16[2048,1024]{0,1:T(8,128)(2,1)} %copy-done, f32[2048]{0:T(1024)S(1)} %get-tuple-element.6, f32[1024]{0:T(1024)S(1)} %get-tuple-element.4), kind=kOutput, calls=%fused_computation.19 | convolution fusion | flops 3229614080 | bytes 10498048 | tf_op jit(solution)/shard_map/dot_general | solution.py:84
  179.1 1.6 copy-done.3
  181.0 3.4 %collective-permute-done.40 = f32[4,96,1024]{2,1,0:T(8,128)S(1)} collective-permute-done((f32[4,96,1024]{2,1,0:T(8,128)S(1)}, f32[4,96,1024]{2,1,0:T(8,128)S(1)}, u32[]{:S(2)}, u32[]{:S(2)}) %collective-permute-start.40) | collective-permute-done | bytes 1572896 | tf_op jit(solution)/shard_map/ppermute | solution.py:39
  184.4 1.7 bitcast_add_fusion
  186.3 2.7 %collective-permute-start.42 = (f32[96,1024]{1,0:T(8,128)S(1)}, f32[96,1024]{1,0:T(8,128)S(1)}, u32[]{:S(2)}, u32[]{:S(2)}) collective-permute-start(f32[96,1024]{1,0:T(8,128)S(1)} %get-tuple-element.11), channel_id=1, source_target_pairs={{0,64},{32,96},{64,0},{96,32},{1,65},{33,97},{65,1},{97,33},{2,66}... | collective-permute-start | bytes 1179656 | tf_op jit(solution)/shard_map/ppermute | solution.py:43
  188.9 1.5 collective-permute-start.43
  190.4 16.7 %collective-permute-done.41 = f32[96,1024]{1,0:T(8,128)S(1)} collective-permute-done((f32[96,1024]{1,0:T(8,128)S(1)}, f32[96,1024]{1,0:T(8,128)S(1)}, u32[]{:S(2)}, u32[]{:S(2)}) %collective-permute-start.41) | collective-permute-done | bytes 393248 | tf_op jit(solution)/shard_map/ppermute | solution.py:43
  207.8 1.1 multiply_reduce_fusion.2
  209.0 1.2 collective-permute-done.44
  211.0 3.2 %collective-permute-start.46 = (f32[1024]{0:T(1024)S(1)}, f32[1024]{0:T(1024)S(1)}, u32[]{:S(2)}, u32[]{:S(2)}) collective-permute-start(f32[1024]{0:T(1024)S(1)} %add.270), channel_id=1, source_target_pairs={{0,64},{32,96},{64,0},{96,32},{1,65},{33,97},{65,1},{97,33},{2,66}... | collective-permute-start | bytes 12296 | tf_op jit(solution)/shard_map/ppermute | solution.py:20
  214.9 1.2 collective-permute-done.46
  216.1 1.7 collective-permute-done.47
  (80 shorter events, 21.1 us)
Async XLA Ops:
  7.2 56.1 %copy-start.4 = (bf16[1024,768]{1,0:T(8,128)(2,1)S(1)}, bf16[1024,768]{1,0:T(8,128)(2,1)}, u32[]{:S(2)}) copy-start(bf16[1024,768]{1,0:T(8,128)(2,1)} %param.4) | copy-start | bytes 4718596
  7.2 53.5 %all-gather.2.cloned.1.call-start = ((), (), s32[]{:S(2)}) async-start(), calls=%async_computation | async-start | bytes 3342336 | tf_op jit(solution)/shard_map/all_gather | solution.py:54
  63.2 20.2 %copy-start.5 = (f32[2048]{0:T(1024)S(1)}, f32[2048]{0:T(1024)}, u32[]{:S(2)}) copy-start(f32[2048]{0:T(1024)} %param.5) | copy-start | bytes 24580
  69.9 14.1 %copy-start = (bf16[2048,1024]{0,1:T(8,128)(2,1)}, bf16[2048,1024]{0,1:T(8,128)(2,1)S(1)}, u32[]{:S(2)}) copy-start(bf16[2048,1024]{0,1:T(8,128)(2,1)S(1)} %get-tuple-element.15) | copy-start | bytes 12582916
  69.9 4.9 %collective-permute-start.4 = (f32[2048]{0:T(1024)S(1)}, f32[2048]{0:T(1024)S(1)}, u32[]{:S(2)}, u32[]{:S(2)}) collective-permute-start(f32[2048]{0:T(1024)S(1)} %get-tuple-element.14), channel_id=1, source_target_pairs={{0,1},{1,2},{2,3},{3,0},{4,5},{5,6},{6,7},{7,4},{8,9},{9,10},{10,1... | collective-permute-start | bytes 24584 | tf_op jit(solution)/shard_map/ppermute | solution.py:20
  70.4 5.2 %collective-permute-start.5 = (f32[2048]{0:T(1024)S(1)}, f32[2048]{0:T(1024)S(1)}, u32[]{:S(2)}, u32[]{:S(2)}) collective-permute-start(f32[2048]{0:T(1024)S(1)} %get-tuple-element.14), channel_id=1, source_target_pairs={{0,2},{1,3},{2,0},{3,1},{4,6},{5,7},{6,4},{7,5},{8,10},{9,11},{10,... | collective-permute-start | bytes 24584 | tf_op jit(solution)/shard_map/ppermute | solution.py:20
  73.1 3.7 %collective-permute-start.6 = (f32[2048]{0:T(1024)S(1)}, f32[2048]{0:T(1024)S(1)}, u32[]{:S(2)}, u32[]{:S(2)}) collective-permute-start(f32[2048]{0:T(1024)S(1)} %get-tuple-element.14), channel_id=1, source_target_pairs={{0,3},{1,0},{2,1},{3,2},{4,7},{5,4},{6,5},{7,6},{8,11},{9,8},{10,9... | collective-permute-start | bytes 24584 | tf_op jit(solution)/shard_map/ppermute | solution.py:20
  76.8 4.9 %collective-permute-start.7 = (f32[2048]{0:T(1024)S(1)}, f32[2048]{0:T(1024)S(1)}, u32[]{:S(2)}, u32[]{:S(2)}) collective-permute-start(f32[2048]{0:T(1024)S(1)} %add_add_fusion.3), channel_id=1, source_target_pairs={{0,4},{4,8},{8,12},{12,0},{1,5},{5,9},{9,13},{13,1},{2,6},{6,10},{... | collective-permute-start | bytes 24584 | tf_op jit(solution)/shard_map/ppermute | solution.py:20
  77.1 5.2 %collective-permute-start.8 = (f32[2048]{0:T(1024)S(1)}, f32[2048]{0:T(1024)S(1)}, u32[]{:S(2)}, u32[]{:S(2)}) collective-permute-start(f32[2048]{0:T(1024)S(1)} %add_add_fusion.3), channel_id=1, source_target_pairs={{0,8},{4,12},{8,0},{12,4},{1,9},{5,13},{9,1},{13,5},{2,10},{6,14},... | collective-permute-start | bytes 24584 | tf_op jit(solution)/shard_map/ppermute | solution.py:20
  79.7 3.7 %collective-permute-start.9 = (f32[2048]{0:T(1024)S(1)}, f32[2048]{0:T(1024)S(1)}, u32[]{:S(2)}, u32[]{:S(2)}) collective-permute-start(f32[2048]{0:T(1024)S(1)} %add_add_fusion.3), channel_id=1, source_target_pairs={{0,12},{4,0},{8,4},{12,8},{1,13},{5,1},{9,5},{13,9},{2,14},{6,2},{... | collective-permute-start | bytes 24584 | tf_op jit(solution)/shard_map/ppermute | solution.py:20
  84.9 1.2 collective-permute-start.10
  86.2 17.6 %collective-permute-start.11 = (f32[1024]{0:T(1024)S(1)}, f32[1024]{0:T(1024)S(1)}, u32[]{:S(2)}, u32[]{:S(2)}) collective-permute-start(f32[1024]{0:T(1024)S(1)} %add.222), channel_id=1, source_target_pairs={{0,32},{32,64},{64,96},{96,0},{1,33},{33,65},{65,97},{97,1},{2,34}... | collective-permute-start | bytes 12296 | tf_op jit(solution)/shard_map/ppermute | solution.py:20
  87.6 16.2 %collective-permute-start.12 = (f32[1024]{0:T(1024)S(1)}, f32[1024]{0:T(1024)S(1)}, u32[]{:S(2)}, u32[]{:S(2)}) collective-permute-start(f32[1024]{0:T(1024)S(1)} %add.222), channel_id=1, source_target_pairs={{0,64},{32,96},{64,0},{96,32},{1,65},{33,97},{65,1},{97,33},{2,66}... | collective-permute-start | bytes 12296 | tf_op jit(solution)/shard_map/ppermute | solution.py:20
  90.3 13.5 %collective-permute-start.13 = (f32[1024]{0:T(1024)S(1)}, f32[1024]{0:T(1024)S(1)}, u32[]{:S(2)}, u32[]{:S(2)}) collective-permute-start(f32[1024]{0:T(1024)S(1)} %add.222), channel_id=1, source_target_pairs={{0,96},{32,0},{64,32},{96,64},{1,97},{33,1},{65,33},{97,65},{2,98}... | collective-permute-start | bytes 12296 | tf_op jit(solution)/shard_map/ppermute | solution.py:20
  91.8 1.4 collective-permute-start
  94.5 5.0 %collective-permute-start.1 = (f32[]{:T(128)}, f32[]{:T(128)}, u32[]{:S(2)}, u32[]{:S(2)}) collective-permute-start(f32[]{:T(128)} %add.212), channel_id=1, source_target_pairs={{0,32},{32,64},{64,96},{96,0},{1,33},{33,65},{65,97},{97,1},{2,34}... | collective-permute-start | bytes 20 | tf_op jit(solution)/shard_map/ppermute | solution.py:20
  96.4 5.9 %collective-permute-start.2 = (f32[]{:T(128)}, f32[]{:T(128)}, u32[]{:S(2)}, u32[]{:S(2)}) collective-permute-start(f32[]{:T(128)} %add.212), channel_id=1, source_target_pairs={{0,64},{32,96},{64,0},{96,32},{1,65},{33,97},{65,1},{97,33},{2,66}... | collective-permute-start | bytes 20 | tf_op jit(solution)/shard_map/ppermute | solution.py:20
  99.4 3.7 %collective-permute-start.3 = (f32[]{:T(128)}, f32[]{:T(128)}, u32[]{:S(2)}, u32[]{:S(2)}) collective-permute-start(f32[]{:T(128)} %add.212), channel_id=1, source_target_pairs={{0,96},{32,0},{64,32},{96,64},{1,97},{33,1},{65,33},{97,65},{2,98}... | collective-permute-start | bytes 20 | tf_op jit(solution)/shard_map/ppermute | solution.py:20
  103.7 18.6 %copy-start.1 = (bf16[2048,1024]{0,1:T(8,128)(2,1)S(1)}, bf16[2048,1024]{0,1:T(8,128)(2,1)}, u32[]{:S(2)}) copy-start(bf16[2048,1024]{0,1:T(8,128)(2,1)} %copy-done) | copy-start | bytes 12582916
  107.0 4.9 %collective-permute-start.14 = (f32[2048]{0:T(1024)S(1)}, f32[2048]{0:T(1024)S(1)}, u32[]{:S(2)}, u32[]{:S(2)}) collective-permute-start(f32[2048]{0:T(1024)S(1)} %fusion.2), channel_id=1, source_target_pairs={{0,1},{1,2},{2,3},{3,0},{4,5},{5,6},{6,7},{7,4},{8,9},{9,10},{10,1... | collective-permute-start | bytes 24584 | tf_op jit(solution)/shard_map/ppermute | solution.py:20
  108.2 5.2 %collective-permute-start.15 = (f32[2048]{0:T(1024)S(1)}, f32[2048]{0:T(1024)S(1)}, u32[]{:S(2)}, u32[]{:S(2)}) collective-permute-start(f32[2048]{0:T(1024)S(1)} %fusion.2), channel_id=1, source_target_pairs={{0,2},{1,3},{2,0},{3,1},{4,6},{5,7},{6,4},{7,5},{8,10},{9,11},{10,... | collective-permute-start | bytes 24584 | tf_op jit(solution)/shard_map/ppermute | solution.py:20
  111.1 3.7 %collective-permute-start.16 = (f32[2048]{0:T(1024)S(1)}, f32[2048]{0:T(1024)S(1)}, u32[]{:S(2)}, u32[]{:S(2)}) collective-permute-start(f32[2048]{0:T(1024)S(1)} %fusion.2), channel_id=1, source_target_pairs={{0,3},{1,0},{2,1},{3,2},{4,7},{5,4},{6,5},{7,6},{8,11},{9,8},{10,9... | collective-permute-start | bytes 24584 | tf_op jit(solution)/shard_map/ppermute | solution.py:20
  114.8 4.9 %collective-permute-start.17 = (f32[2048]{0:T(1024)S(1)}, f32[2048]{0:T(1024)S(1)}, u32[]{:S(2)}, u32[]{:S(2)}) collective-permute-start(f32[2048]{0:T(1024)S(1)} %add_add_fusion.2), channel_id=1, source_target_pairs={{0,4},{4,8},{8,12},{12,0},{1,5},{5,9},{9,13},{13,1},{2,6},{6,10},{... | collective-permute-start | bytes 24584 | tf_op jit(solution)/shard_map/ppermute | solution.py:20
  115.7 5.2 %collective-permute-start.18 = (f32[2048]{0:T(1024)S(1)}, f32[2048]{0:T(1024)S(1)}, u32[]{:S(2)}, u32[]{:S(2)}) collective-permute-start(f32[2048]{0:T(1024)S(1)} %add_add_fusion.2), channel_id=1, source_target_pairs={{0,8},{4,12},{8,0},{12,4},{1,9},{5,13},{9,1},{13,5},{2,10},{6,14},... | collective-permute-start | bytes 24584 | tf_op jit(solution)/shard_map/ppermute | solution.py:20
  118.6 3.7 %collective-permute-start.19 = (f32[2048]{0:T(1024)S(1)}, f32[2048]{0:T(1024)S(1)}, u32[]{:S(2)}, u32[]{:S(2)}) collective-permute-start(f32[2048]{0:T(1024)S(1)} %add_add_fusion.2), channel_id=1, source_target_pairs={{0,12},{4,0},{8,4},{12,8},{1,13},{5,1},{9,5},{13,9},{2,14},{6,2},{... | collective-permute-start | bytes 24584 | tf_op jit(solution)/shard_map/ppermute | solution.py:20
  123.2 1.2 collective-permute-start.20
  124.5 5.4 %collective-permute-start.21 = (f32[1024]{0:T(1024)S(1)}, f32[1024]{0:T(1024)S(1)}, u32[]{:S(2)}, u32[]{:S(2)}) collective-permute-start(f32[1024]{0:T(1024)S(1)} %add.232), channel_id=1, source_target_pairs={{0,32},{32,64},{64,96},{96,0},{1,33},{33,65},{65,97},{97,1},{2,34}... | collective-permute-start | bytes 12296 | tf_op jit(solution)/shard_map/ppermute | solution.py:20
  126.3 5.1 %collective-permute-start.22 = (f32[1024]{0:T(1024)S(1)}, f32[1024]{0:T(1024)S(1)}, u32[]{:S(2)}, u32[]{:S(2)}) collective-permute-start(f32[1024]{0:T(1024)S(1)} %add.232), channel_id=1, source_target_pairs={{0,64},{32,96},{64,0},{96,32},{1,65},{33,97},{65,1},{97,33},{2,66}... | collective-permute-start | bytes 12296 | tf_op jit(solution)/shard_map/ppermute | solution.py:20
  128.1 3.6 %collective-permute-start.23 = (f32[1024]{0:T(1024)S(1)}, f32[1024]{0:T(1024)S(1)}, u32[]{:S(2)}, u32[]{:S(2)}) collective-permute-start(f32[1024]{0:T(1024)S(1)} %add.232), channel_id=1, source_target_pairs={{0,96},{32,0},{64,32},{96,64},{1,97},{33,1},{65,33},{97,65},{2,98}... | collective-permute-start | bytes 12296 | tf_op jit(solution)/shard_map/ppermute | solution.py:20
  132.6 4.9 %collective-permute-start.24 = (f32[2048]{0:T(1024)S(1)}, f32[2048]{0:T(1024)S(1)}, u32[]{:S(2)}, u32[]{:S(2)}) collective-permute-start(f32[2048]{0:T(1024)S(1)} %fusion.4), channel_id=1, source_target_pairs={{0,1},{1,2},{2,3},{3,0},{4,5},{5,6},{6,7},{7,4},{8,9},{9,10},{10,1... | collective-permute-start | bytes 24584 | tf_op jit(solution)/shard_map/ppermute | solution.py:20
  133.0 5.2 %collective-permute-start.25 = (f32[2048]{0:T(1024)S(1)}, f32[2048]{0:T(1024)S(1)}, u32[]{:S(2)}, u32[]{:S(2)}) collective-permute-start(f32[2048]{0:T(1024)S(1)} %fusion.4), channel_id=1, source_target_pairs={{0,2},{1,3},{2,0},{3,1},{4,6},{5,7},{6,4},{7,5},{8,10},{9,11},{10,... | collective-permute-start | bytes 24584 | tf_op jit(solution)/shard_map/ppermute | solution.py:20
  135.8 3.7 %collective-permute-start.26 = (f32[2048]{0:T(1024)S(1)}, f32[2048]{0:T(1024)S(1)}, u32[]{:S(2)}, u32[]{:S(2)}) collective-permute-start(f32[2048]{0:T(1024)S(1)} %fusion.4), channel_id=1, source_target_pairs={{0,3},{1,0},{2,1},{3,2},{4,7},{5,4},{6,5},{7,6},{8,11},{9,8},{10,9... | collective-permute-start | bytes 24584 | tf_op jit(solution)/shard_map/ppermute | solution.py:20
  139.4 4.9 %collective-permute-start.27 = (f32[2048]{0:T(1024)S(1)}, f32[2048]{0:T(1024)S(1)}, u32[]{:S(2)}, u32[]{:S(2)}) collective-permute-start(f32[2048]{0:T(1024)S(1)} %add_add_fusion.1), channel_id=1, source_target_pairs={{0,4},{4,8},{8,12},{12,0},{1,5},{5,9},{9,13},{13,1},{2,6},{6,10},{... | collective-permute-start | bytes 24584 | tf_op jit(solution)/shard_map/ppermute | solution.py:20
  139.4 5.2 %collective-permute-start.28 = (f32[2048]{0:T(1024)S(1)}, f32[2048]{0:T(1024)S(1)}, u32[]{:S(2)}, u32[]{:S(2)}) collective-permute-start(f32[2048]{0:T(1024)S(1)} %add_add_fusion.1), channel_id=1, source_target_pairs={{0,8},{4,12},{8,0},{12,4},{1,9},{5,13},{9,1},{13,5},{2,10},{6,14},... | collective-permute-start | bytes 24584 | tf_op jit(solution)/shard_map/ppermute | solution.py:20
  142.1 3.7 %collective-permute-start.29 = (f32[2048]{0:T(1024)S(1)}, f32[2048]{0:T(1024)S(1)}, u32[]{:S(2)}, u32[]{:S(2)}) collective-permute-start(f32[2048]{0:T(1024)S(1)} %add_add_fusion.1), channel_id=1, source_target_pairs={{0,12},{4,0},{8,4},{12,8},{1,13},{5,1},{9,5},{13,9},{2,14},{6,2},{... | collective-permute-start | bytes 24584 | tf_op jit(solution)/shard_map/ppermute | solution.py:20
  145.8 27.6 %copy-start.2 = (bf16[2048,768]{0,1:T(8,128)(2,1)S(1)}, bf16[2048,768]{0,1:T(8,128)(2,1)}, u32[]{:S(2)}) copy-start(bf16[2048,768]{0,1:T(8,128)(2,1)} %all-gather.2.cloned.1.call-done) | copy-start | bytes 9437188
  146.7 1.2 collective-permute-start.30
  148.0 4.8 %collective-permute-start.31 = (f32[1024]{0:T(1024)S(1)}, f32[1024]{0:T(1024)S(1)}, u32[]{:S(2)}, u32[]{:S(2)}) collective-permute-start(f32[1024]{0:T(1024)S(1)} %add.242), channel_id=1, source_target_pairs={{0,32},{32,64},{64,96},{96,0},{1,33},{33,65},{65,97},{97,1},{2,34}... | collective-permute-start | bytes 12296 | tf_op jit(solution)/shard_map/ppermute | solution.py:20
  148.6 5.5 %collective-permute-start.32 = (f32[1024]{0:T(1024)S(1)}, f32[1024]{0:T(1024)S(1)}, u32[]{:S(2)}, u32[]{:S(2)}) collective-permute-start(f32[1024]{0:T(1024)S(1)} %add.242), channel_id=1, source_target_pairs={{0,64},{32,96},{64,0},{96,32},{1,65},{33,97},{65,1},{97,33},{2,66}... | collective-permute-start | bytes 12296 | tf_op jit(solution)/shard_map/ppermute | solution.py:20
  152.4 3.6 %collective-permute-start.33 = (f32[1024]{0:T(1024)S(1)}, f32[1024]{0:T(1024)S(1)}, u32[]{:S(2)}, u32[]{:S(2)}) collective-permute-start(f32[1024]{0:T(1024)S(1)} %add.242), channel_id=1, source_target_pairs={{0,96},{32,0},{64,32},{96,64},{1,97},{33,1},{65,33},{97,65},{2,98}... | collective-permute-start | bytes 12296 | tf_op jit(solution)/shard_map/ppermute | solution.py:20
  157.5 4.9 %collective-permute-start.34 = (f32[2048]{0:T(1024)S(1)}, f32[2048]{0:T(1024)S(1)}, u32[]{:S(2)}, u32[]{:S(2)}) collective-permute-start(f32[2048]{0:T(1024)S(1)} %fusion.6), channel_id=1, source_target_pairs={{0,1},{1,2},{2,3},{3,0},{4,5},{5,6},{6,7},{7,4},{8,9},{9,10},{10,1... | collective-permute-start | bytes 24584 | tf_op jit(solution)/shard_map/ppermute | solution.py:20
  158.8 5.2 %collective-permute-start.35 = (f32[2048]{0:T(1024)S(1)}, f32[2048]{0:T(1024)S(1)}, u32[]{:S(2)}, u32[]{:S(2)}) collective-permute-start(f32[2048]{0:T(1024)S(1)} %fusion.6), channel_id=1, source_target_pairs={{0,2},{1,3},{2,0},{3,1},{4,6},{5,7},{6,4},{7,5},{8,10},{9,11},{10,... | collective-permute-start | bytes 24584 | tf_op jit(solution)/shard_map/ppermute | solution.py:20
  161.6 3.7 %collective-permute-start.36 = (f32[2048]{0:T(1024)S(1)}, f32[2048]{0:T(1024)S(1)}, u32[]{:S(2)}, u32[]{:S(2)}) collective-permute-start(f32[2048]{0:T(1024)S(1)} %fusion.6), channel_id=1, source_target_pairs={{0,3},{1,0},{2,1},{3,2},{4,7},{5,4},{6,5},{7,6},{8,11},{9,8},{10,9... | collective-permute-start | bytes 24584 | tf_op jit(solution)/shard_map/ppermute | solution.py:20
  165.3 4.9 %collective-permute-start.37 = (f32[2048]{0:T(1024)S(1)}, f32[2048]{0:T(1024)S(1)}, u32[]{:S(2)}, u32[]{:S(2)}) collective-permute-start(f32[2048]{0:T(1024)S(1)} %add_add_fusion), channel_id=1, source_target_pairs={{0,4},{4,8},{8,12},{12,0},{1,5},{5,9},{9,13},{13,1},{2,6},{6,10},{... | collective-permute-start | bytes 24584 | tf_op jit(solution)/shard_map/ppermute | solution.py:20
  166.4 5.2 %collective-permute-start.38 = (f32[2048]{0:T(1024)S(1)}, f32[2048]{0:T(1024)S(1)}, u32[]{:S(2)}, u32[]{:S(2)}) collective-permute-start(f32[2048]{0:T(1024)S(1)} %add_add_fusion), channel_id=1, source_target_pairs={{0,8},{4,12},{8,0},{12,4},{1,9},{5,13},{9,1},{13,5},{2,10},{6,14},... | collective-permute-start | bytes 24584 | tf_op jit(solution)/shard_map/ppermute | solution.py:20
  169.1 3.7 %collective-permute-start.39 = (f32[2048]{0:T(1024)S(1)}, f32[2048]{0:T(1024)S(1)}, u32[]{:S(2)}, u32[]{:S(2)}) collective-permute-start(f32[2048]{0:T(1024)S(1)} %add_add_fusion), channel_id=1, source_target_pairs={{0,12},{4,0},{8,4},{12,8},{1,13},{5,1},{9,5},{13,9},{2,14},{6,2},{... | collective-permute-start | bytes 24584 | tf_op jit(solution)/shard_map/ppermute | solution.py:20
  179.1 1.6 copy-start.3
  180.9 3.5 %collective-permute-start.40 = (f32[4,96,1024]{2,1,0:T(8,128)S(1)}, f32[4,96,1024]{2,1,0:T(8,128)S(1)}, u32[]{:S(2)}, u32[]{:S(2)}) collective-permute-start(f32[4,96,1024]{2,1,0:T(8,128)S(1)} %dynamic-slice_bitcast_fusion), channel_id=1, source_target_pairs={{0,16},{16,0},{1,17},{17,1},{2,18},{18,2},{3,19},{19,3},{4,20},{20... | collective-permute-start | bytes 4718600 | tf_op jit(solution)/shard_map/ppermute | solution.py:39
  186.2 20.9 %collective-permute-start.41 = (f32[96,1024]{1,0:T(8,128)S(1)}, f32[96,1024]{1,0:T(8,128)S(1)}, u32[]{:S(2)}, u32[]{:S(2)}) collective-permute-start(f32[96,1024]{1,0:T(8,128)S(1)} %get-tuple-element.9), channel_id=1, source_target_pairs={{0,32},{32,64},{64,96},{96,0},{1,33},{33,65},{65,97},{97,1},{2,34}... | collective-permute-start | bytes 1179656 | tf_op jit(solution)/shard_map/ppermute | solution.py:43
  186.3 20.8 %collective-permute-start.42 = (f32[96,1024]{1,0:T(8,128)S(1)}, f32[96,1024]{1,0:T(8,128)S(1)}, u32[]{:S(2)}, u32[]{:S(2)}) collective-permute-start(f32[96,1024]{1,0:T(8,128)S(1)} %get-tuple-element.11), channel_id=1, source_target_pairs={{0,64},{32,96},{64,0},{96,32},{1,65},{33,97},{65,1},{97,33},{2,66}... | collective-permute-start | bytes 1179656 | tf_op jit(solution)/shard_map/ppermute | solution.py:43
  188.9 18.8 %collective-permute-start.43 = (f32[96,1024]{1,0:T(8,128)S(1)}, f32[96,1024]{1,0:T(8,128)}, u32[]{:S(2)}, u32[]{:S(2)}) collective-permute-start(f32[96,1024]{1,0:T(8,128)S(1)} %get-tuple-element.10), channel_id=1, source_target_pairs={{0,96},{32,0},{64,32},{96,64},{1,97},{33,1},{65,33},{97,65},{2,98}... | collective-permute-start | bytes 1179656 | tf_op jit(solution)/shard_map/ppermute | solution.py:43
  208.9 1.2 collective-permute-start.44
  210.1 4.8 %collective-permute-start.45 = (f32[1024]{0:T(1024)S(1)}, f32[1024]{0:T(1024)S(1)}, u32[]{:S(2)}, u32[]{:S(2)}) collective-permute-start(f32[1024]{0:T(1024)S(1)} %add.270), channel_id=1, source_target_pairs={{0,32},{32,64},{64,96},{96,0},{1,33},{33,65},{65,97},{97,1},{2,34}... | collective-permute-start | bytes 12296 | tf_op jit(solution)/shard_map/ppermute | solution.py:20
  211.0 5.1 %collective-permute-start.46 = (f32[1024]{0:T(1024)S(1)}, f32[1024]{0:T(1024)S(1)}, u32[]{:S(2)}, u32[]{:S(2)}) collective-permute-start(f32[1024]{0:T(1024)S(1)} %add.270), channel_id=1, source_target_pairs={{0,64},{32,96},{64,0},{96,32},{1,65},{33,97},{65,1},{97,33},{2,66}... | collective-permute-start | bytes 12296 | tf_op jit(solution)/shard_map/ppermute | solution.py:20
  214.2 3.6 %collective-permute-start.47 = (f32[1024]{0:T(1024)S(1)}, f32[1024]{0:T(1024)S(1)}, u32[]{:S(2)}, u32[]{:S(2)}) collective-permute-start(f32[1024]{0:T(1024)S(1)} %add.270), channel_id=1, source_target_pairs={{0,96},{32,0},{64,32},{96,64},{1,97},{33,1},{65,33},{97,65},{2,98}... | collective-permute-start | bytes 12296 | tf_op jit(solution)/shard_map/ppermute | solution.py:20
Sparse Core Ops, SparseCore 0:
  10.2 50.4 all-gather.1

commit v3 on v2

--- a/solution.py
+++ b/solution.py
@@ -22,7 +22,9 @@
 
 
 def reduce_cent(x):
-    return shifted_sum(shifted_sum(x, "cz"), "cy")
+    n = lax.axis_size(CENT)
+    copies = lax.all_to_all(jnp.broadcast_to(x, (n, *x.shape)), CENT, 0, 0, tiled=False)
+    return jnp.sum(copies, axis=0)
 
 
 def reduce_row(x):

time: 226 us -> 223 us (0.987)
  blocking collectives: 0 us -> 34.4 us
  starting transfers between devices: 64.7 us -> 34.1 us
  waiting for transfers between devices: 111 us -> 95.8 us
  other arithmetic: 17.5 us -> 24.5 us
    ppermute x44 -> x20, starting transfers between devices: 60.4 us -> 25.6 us  [shifted_sum(): total = total + lax.ppermute(x, axis, [(i, (i + k) % n) for i in range(n)])]
    all_to_all x0 -> x3, blocking collectives: none -> 34.4 us  [reduce_cent(): lax.all_to_all(jnp.broadcast_to(x, (n, *x.shape)), CENT, 0, 0, tiled=False)]
    ppermute x44 -> x20, waiting for transfers between devices: 39.1 us -> 16.1 us  [shifted_sum(): total = total + lax.ppermute(x, axis, [(i, (i + k) % n) for i in range(n)])]
    all_to_all x0 -> x1, waiting for transfers between devices: none -> 7.82 us  [reduce_cent(): lax.all_to_all(jnp.broadcast_to(x, (n, *x.shape)), CENT, 0, 0, tiled=False)]
    reduce_sum x3, other arithmetic: 2.67 us -> 9.52 us  [per_device(): jnp.sum(kernel.astype(jnp.float32) * row_scale[:, None], axis=0)]
    all_to_all x0 -> x1, starting transfers between devices: none -> 3.6 us  [reduce_cent(): lax.all_to_all(jnp.broadcast_to(x, (n, *x.shape)), CENT, 0, 0, tiled=False)]
  transfers between devices with their start and end apart: 49 -> 26, of which waited for: 43 -> 19; matrix products, arithmetic and copies ran while one was open for 1% -> 1% of each run, Pallas kernels for 0% -> 0%
where the time goes in v3:
time: 223 us
  waiting for transfers between devices  95.8 us (43%)
  blocking collectives  34.4 us (15%)
  starting transfers between devices  34.1 us (15%)
  other arithmetic  24.5 us (11%)
  between operations  17.6 us (8%)
  matrix products  13.6 us (6%)
  local copies, waits for them, and re-layouts  2.9 us (1%)
    all_gather x1, waiting for transfers between devices, per_device(): full_rows = lax.all_gather(vectors, CENT, axis=1, tiled=True)  51 us
    all_to_all x3, blocking collectives, reduce_cent(): lax.all_to_all(jnp.broadcast_to(x, (n, *x.shape)), CENT, 0, 0, tiled=False)  34.4 us
    ppermute x20, starting transfers between devices, shifted_sum(): total = total + lax.ppermute(x, axis, [(i, (i + k) % n) for i in range(n)])  25.6 us
    ppermute x3, waiting for transfers between devices, scatter_row(): lax.ppermute(piece, 'rx', [(i, (i + k) % chips) for i in range(chips)])  16.9 us
    ppermute x20, waiting for transfers between devices, shifted_sum(): total = total + lax.ppermute(x, axis, [(i, (i + k) % n) for i in range(n)])  16.1 us
    reduce_sum x3, other arithmetic, per_device(): jnp.sum(kernel.astype(jnp.float32) * row_scale[:, None], axis=0)  9.52 us
    dot_general x1, matrix products, per_device(): jnp.dot(full_rows, centroids.T, preferred_element_type=jnp.float32)  7.88 us
    all_to_all x1, waiting for transfers between devices, reduce_cent(): lax.all_to_all(jnp.broadcast_to(x, (n, *x.shape)), CENT, 0, 0, tiled=False)  7.82 us
  transfers between devices with their start and end apart: 26, of which 19 were waited for; matrix products, arithmetic and copies ran while one was open for 1% of the time, Pallas kernels for 0%

profile of v3, /device:TPU:0, one launch (start us, length us, event | category | flops | bytes accessed | tf_op | source)
XLA Modules:
  0.0 222.9 jit_solution(11298160007546934467)
XLA Ops:
  7.2 0.7 all-gather.2.cloned.1.call-update
  7.9 1.8 multiply_reduce_fusion.1
  9.7 51.0 %all-gather.2.cloned.1.call-done = bf16[2048,768]{0,1:T(8,128)(2,1)} async-done(((bf16[2048,48]{0,1:T(8,128)(2,1)}), bf16[2048,768]{0,1:T(8,128)(2,1)}) %all-gather.2.cloned.1.call-update) | async-done | bytes 3145744 | tf_op jit(solution)/shard_map/all_gather | solution.py:56
  60.7 2.6 %multiply_reduce_fusion = f32[2048]{0:T(1024)S(1)} fusion(bf16[2048,768]{0,1:T(8,128)(2,1)} %all-gather.2.cloned.1.call-done), kind=kLoop, calls=%fused_computation.18 | loop fusion | flops 4716544 | bytes 3153920 | tf_op jit(solution)/shard_map/reduce_sum | solution.py:62
  63.2 7.9 %fusion = (f32[2048]{0:T(1024)S(1)}, bf16[2048,1024]{0,1:T(8,128)(2,1)}) fusion(f32[1024]{0:T(1024)S(1)} %add_rsqrt_fusion.2, f32[2048]{0:T(1024)S(1)} %add_rsqrt_fusion, bf16[1024,768]{1,0:T(8,128)(2,1)S(1)} %copy-done.4, bf16[2048,768]{0,1:T(8,128)(2,1)} %all-gather.2.cloned.1.call-done), kind=kOutput, calls=%fused_computation.8 | convolution fusion | flops 3235903488 | bytes 8933376 | tf_op jit(solution)/shard_map/dot_general | solution.py:67
  71.2 12.0 %all_to_all.24 = f32[16,1,2048]{2,1,0:T(1,128)S(1)} all-to-all(f32[16,1,2048]{2,1,0:T(1,128)S(1)} %broadcast_in_dim.8), channel_id=1, replica_groups=mesh['rx'=4,'rc'=2,'cy'=4,'cz'=4] {'cy','cz'}, dimensions={0} | all-to-all | bytes 262144 | tf_op jit(solution)/shard_map/all_to_all | solution.py:26
  83.2 0.1 reduce_sum.139
  83.3 0.6 fusion.17
  83.9 3.1 %fusion.1 = f32[1024]{0:T(1024)S(1)} fusion(bf16[2048,1024]{0,1:T(8,128)(2,1)} %get-tuple-element.15, f32[2048]{0:T(1024)S(1)} %get-tuple-element.13), kind=kLoop, calls=%fused_computation.9 | loop fusion | flops 6290432 | bytes 4206592 | tf_op jit(solution)/shard_map/reduce_sum | solution.py:79
  87.0 1.2 collective-permute-done.4
  88.2 1.5 collective-permute-start.5
  89.7 2.7 %collective-permute-start.6 = (f32[1024]{0:T(1024)S(1)}, f32[1024]{0:T(1024)S(1)}, u32[]{:S(2)}, u32[]{:S(2)}) collective-permute-start(f32[1024]{0:T(1024)S(1)} %add.144), channel_id=1, source_target_pairs={{0,64},{32,96},{64,0},{96,32},{1,65},{33,97},{65,1},{97,33},{2,66}... | collective-permute-start | bytes 12296 | tf_op jit(solution)/shard_map/ppermute | solution.py:20
  92.3 1.5 collective-permute-start.7
  93.8 1.3 collective-permute-done
  96.4 1.9 collective-permute-start.1
  98.3 2.2 collective-permute-start.2
  100.5 0.7 collective-permute-done.1
  101.2 2.4 %collective-permute-start.3 = (f32[]{:T(128)}, f32[]{:T(128)}, u32[]{:S(2)}, u32[]{:S(2)}) collective-permute-start(f32[]{:T(128)} %add.140), channel_id=1, source_target_pairs={{0,96},{32,0},{64,32},{96,64},{1,97},{33,1},{65,33},{97,65},{2,98}... | collective-permute-start | bytes 20 | tf_op jit(solution)/shard_map/ppermute | solution.py:20
  105.6 3.1 %fusion.2 = f32[2048]{0:T(1024)S(1)} fusion(bf16[2048,1024]{0,1:T(8,128)(2,1)} %get-tuple-element.15, f32[1024]{0:T(1024)S(1)} %add_divide_fusion.2), kind=kLoop, calls=%fused_computation.10 | loop fusion | flops 6289408 | bytes 4206592 | tf_op jit(solution)/shard_map/reduce_sum | solution.py:50
  108.7 11.2 %all_to_all.25 = f32[16,1,2048]{2,1,0:T(1,128)S(1)} all-to-all(f32[16,1,2048]{2,1,0:T(1,128)S(1)} %broadcast_in_dim.9), channel_id=1, replica_groups=mesh['rx'=4,'rc'=2,'cy'=4,'cz'=4] {'cy','cz'}, dimensions={0} | all-to-all | bytes 262144 | tf_op jit(solution)/shard_map/all_to_all | solution.py:26
  120.0 0.1 reduce_sum.142
  120.1 3.2 %fusion.3 = f32[1024]{0:T(1024)S(1)} fusion(bf16[2048,1024]{0,1:T(8,128)(2,1)} %get-tuple-element.15, f32[2048]{0:T(1024)S(1)} %div.58), kind=kLoop, calls=%fused_computation.11 | loop fusion | flops 6290432 | bytes 4206592 | tf_op jit(solution)/shard_map/reduce_sum | solution.py:79
  123.4 1.2 collective-permute-done.8
  124.6 2.9 %collective-permute-start.10 = (f32[1024]{0:T(1024)S(1)}, f32[1024]{0:T(1024)S(1)}, u32[]{:S(2)}, u32[]{:S(2)}) collective-permute-start(f32[1024]{0:T(1024)S(1)} %add.148), channel_id=1, source_target_pairs={{0,64},{32,96},{64,0},{96,32},{1,65},{33,97},{65,1},{97,33},{2,66}... | collective-permute-start | bytes 12296 | tf_op jit(solution)/shard_map/ppermute | solution.py:20
  127.5 1.5 collective-permute-start.11
  129.0 0.5 collective-permute-start.9
  129.5 0.2 collective-permute-done.10
  129.7 1.4 collective-permute-done.11
  131.1 2.8 %collective-permute-done.9 = f32[1024]{0:T(1024)S(1)} collective-permute-done((f32[1024]{0:T(1024)S(1)}, f32[1024]{0:T(1024)S(1)}, u32[]{:S(2)}, u32[]{:S(2)}) %collective-permute-start.9) | collective-permute-done | bytes 4128 | tf_op jit(solution)/shard_map/ppermute | solution.py:20
  133.8 0.9 fusion.4
  134.8 11.2 %all_to_all.26 = f32[16,1,2048]{2,1,0:T(1,128)S(1)} all-to-all(f32[16,1,2048]{2,1,0:T(1,128)S(1)} %broadcast_in_dim.10), channel_id=1, replica_groups=mesh['rx'=4,'rc'=2,'cy'=4,'cz'=4] {'cy','cz'}, dimensions={0} | all-to-all | bytes 262144 | tf_op jit(solution)/shard_map/all_to_all | solution.py:26
  146.1 0.1 reduce_sum.145
  146.2 3.2 %fusion.5 = f32[1024]{0:T(1024)S(1)} fusion(bf16[2048,1024]{0,1:T(8,128)(2,1)} %get-tuple-element.15, f32[2048]{0:T(1024)S(1)} %div.60), kind=kLoop, calls=%fused_computation.13 | loop fusion | flops 6290432 | bytes 4206592 | tf_op jit(solution)/shard_map/reduce_sum | solution.py:79
  149.5 1.2 collective-permute-done.12
  150.7 1.5 collective-permute-start.14
  152.1 1.8 collective-permute-start.15
  153.9 1.6 collective-permute-done.13
  155.5 0.3 collective-permute-done.14
  155.8 0.6 collective-permute-done.15
  156.4 0.6 multiply_log_fusion
  157.0 0.9 fusion.6
  157.9 0.7 broadcast_in_dim.11
  158.6 3.6 %all-to-all-start.3 = ((f32[16,1,2048]{2,1,0:T(1,128)}), f32[16,1,2048]{2,1,0:T(1,128)S(1)}, u32[]{:S(2)}, u32[]{:S(2)}) async-start(f32[16,1,2048]{2,1,0:T(1,128)} %broadcast_in_dim.11), calls=%async_computation.3 | async-start | bytes 262144 | tf_op jit(solution)/shard_map/all_to_all | solution.py:26
  162.2 7.8 %all-to-all-done.3 = f32[16,1,2048]{2,1,0:T(1,128)S(1)} async-done(((f32[16,1,2048]{2,1,0:T(1,128)}), f32[16,1,2048]{2,1,0:T(1,128)S(1)}, u32[]{:S(2)}, u32[]{:S(2)}) %all-to-all-start.3) | async-done | bytes 131104 | tf_op jit(solution)/shard_map/all_to_all | solution.py:26
  170.2 0.6 fusion.15
  170.8 5.7 %fusion.9 = f32[1024,768]{0,1:T(8,128)S(1)} fusion(bf16[2048,768]{0,1:T(8,128)(2,1)S(1)} %copy-done.2, bf16[2048,1024]{0,1:T(8,128)(2,1)} %get-tuple-element.15, f32[2048]{0:T(1024)S(1)} %get-tuple-element.6, f32[1024]{0:T(1024)S(1)} %get-tuple-element.4), kind=kOutput, calls=%fused_computation.19 | convolution fusion | flops 3229614080 | bytes 10498048 | tf_op jit(solution)/shard_map/dot_general | solution.py:86
  176.5 1.7 copy-done.3
  178.1 0.2 dynamic-slice_bitcast_fusion
  178.4 3.4 %collective-permute-done.16 = f32[4,96,1024]{2,1,0:T(8,128)S(1)} collective-permute-done((f32[4,96,1024]{2,1,0:T(8,128)S(1)}, f32[4,96,1024]{2,1,0:T(8,128)S(1)}, u32[]{:S(2)}, u32[]{:S(2)}) %collective-permute-start.16) | collective-permute-done | bytes 1572896 | tf_op jit(solution)/shard_map/ppermute | solution.py:41
  181.8 1.7 bitcast_add_fusion
  183.5 0.1 dynamic-slice_bitcast_fusion.3
  183.6 2.0 collective-permute-start.17
  185.6 2.1 collective-permute-start.18
  187.8 0.7 collective-permute-start.19
  188.4 7.6 %collective-permute-done.17 = f32[96,1024]{1,0:T(8,128)S(1)} collective-permute-done((f32[96,1024]{1,0:T(8,128)S(1)}, f32[96,1024]{1,0:T(8,128)S(1)}, u32[]{:S(2)}, u32[]{:S(2)}) %collective-permute-start.17) | collective-permute-done | bytes 393248 | tf_op jit(solution)/shard_map/ppermute | solution.py:45
  196.0 9.3 %collective-permute-done.18 = f32[96,1024]{1,0:T(8,128)S(1)} collective-permute-done((f32[96,1024]{1,0:T(8,128)S(1)}, f32[96,1024]{1,0:T(8,128)S(1)}, u32[]{:S(2)}, u32[]{:S(2)}) %collective-permute-start.18) | collective-permute-done | bytes 393248 | tf_op jit(solution)/shard_map/ppermute | solution.py:45
  205.3 1.1 multiply_reduce_fusion.2
  206.5 1.2 collective-permute-done.20
  207.7 1.6 collective-permute-start.21
  209.3 2.4 %collective-permute-start.22 = (f32[1024]{0:T(1024)S(1)}, f32[1024]{0:T(1024)S(1)}, u32[]{:S(2)}, u32[]{:S(2)}) collective-permute-start(f32[1024]{0:T(1024)S(1)} %add.174), channel_id=1, source_target_pairs={{0,64},{32,96},{64,0},{96,32},{1,65},{33,97},{65,1},{97,33},{2,66}... | collective-permute-start | bytes 12296 | tf_op jit(solution)/shard_map/ppermute | solution.py:20
  211.6 0.9 collective-permute-start.23
  212.6 1.8 collective-permute-done.22
  214.4 0.9 collective-permute-done.23
  215.3 0.8 broadcast_multiply_fusion
  (41 shorter events, 0.9 us)
Async XLA Ops:
  7.2 56.1 %copy-start.4 = (bf16[1024,768]{1,0:T(8,128)(2,1)S(1)}, bf16[1024,768]{1,0:T(8,128)(2,1)}, u32[]{:S(2)}) copy-start(bf16[1024,768]{1,0:T(8,128)(2,1)} %param.4) | copy-start | bytes 4718596
  7.2 53.5 %all-gather.2.cloned.1.call-start = ((), (), s32[]{:S(2)}) async-start(), calls=%async_computation.4 | async-start | bytes 3342336 | tf_op jit(solution)/shard_map/all_gather | solution.py:56
  63.2 20.0 %copy-start.5 = (f32[2048]{0:T(1024)S(1)}, f32[2048]{0:T(1024)}, u32[]{:S(2)}) copy-start(f32[2048]{0:T(1024)} %param.5) | copy-start | bytes 24580
  86.9 1.2 collective-permute-start.4
  88.2 17.3 %collective-permute-start.5 = (f32[1024]{0:T(1024)S(1)}, f32[1024]{0:T(1024)S(1)}, u32[]{:S(2)}, u32[]{:S(2)}) collective-permute-start(f32[1024]{0:T(1024)S(1)} %add.144), channel_id=1, source_target_pairs={{0,32},{32,64},{64,96},{96,0},{1,33},{33,65},{65,97},{97,1},{2,34}... | collective-permute-start | bytes 12296 | tf_op jit(solution)/shard_map/ppermute | solution.py:20
  89.7 15.9 %collective-permute-start.6 = (f32[1024]{0:T(1024)S(1)}, f32[1024]{0:T(1024)S(1)}, u32[]{:S(2)}, u32[]{:S(2)}) collective-permute-start(f32[1024]{0:T(1024)S(1)} %add.144), channel_id=1, source_target_pairs={{0,64},{32,96},{64,0},{96,32},{1,65},{33,97},{65,1},{97,33},{2,66}... | collective-permute-start | bytes 12296 | tf_op jit(solution)/shard_map/ppermute | solution.py:20
  92.3 13.2 %collective-permute-start.7 = (f32[1024]{0:T(1024)S(1)}, f32[1024]{0:T(1024)S(1)}, u32[]{:S(2)}, u32[]{:S(2)}) collective-permute-start(f32[1024]{0:T(1024)S(1)} %add.144), channel_id=1, source_target_pairs={{0,96},{32,0},{64,32},{96,64},{1,97},{33,1},{65,33},{97,65},{2,98}... | collective-permute-start | bytes 12296 | tf_op jit(solution)/shard_map/ppermute | solution.py:20
  93.8 1.3 collective-permute-start
  96.4 4.8 %collective-permute-start.1 = (f32[]{:T(128)}, f32[]{:T(128)}, u32[]{:S(2)}, u32[]{:S(2)}) collective-permute-start(f32[]{:T(128)} %add.140), channel_id=1, source_target_pairs={{0,32},{32,64},{64,96},{96,0},{1,33},{33,65},{65,97},{97,1},{2,34}... | collective-permute-start | bytes 20 | tf_op jit(solution)/shard_map/ppermute | solution.py:20
  98.3 6.0 %collective-permute-start.2 = (f32[]{:T(128)}, f32[]{:T(128)}, u32[]{:S(2)}, u32[]{:S(2)}) collective-permute-start(f32[]{:T(128)} %add.140), channel_id=1, source_target_pairs={{0,64},{32,96},{64,0},{96,32},{1,65},{33,97},{65,1},{97,33},{2,66}... | collective-permute-start | bytes 20 | tf_op jit(solution)/shard_map/ppermute | solution.py:20
  101.2 3.7 %collective-permute-start.3 = (f32[]{:T(128)}, f32[]{:T(128)}, u32[]{:S(2)}, u32[]{:S(2)}) collective-permute-start(f32[]{:T(128)} %add.140), channel_id=1, source_target_pairs={{0,96},{32,0},{64,32},{96,64},{1,97},{33,1},{65,33},{97,65},{2,98}... | collective-permute-start | bytes 20 | tf_op jit(solution)/shard_map/ppermute | solution.py:20
  120.1 13.8 %copy-start = (bf16[2048,1024]{0,1:T(8,128)(2,1)S(1)}, bf16[2048,1024]{0,1:T(8,128)(2,1)}, u32[]{:S(2)}) copy-start(bf16[2048,1024]{0,1:T(8,128)(2,1)} %get-tuple-element.15) | copy-start | bytes 12582916
  123.3 1.2 collective-permute-start.8
  124.6 5.1 %collective-permute-start.10 = (f32[1024]{0:T(1024)S(1)}, f32[1024]{0:T(1024)S(1)}, u32[]{:S(2)}, u32[]{:S(2)}) collective-permute-start(f32[1024]{0:T(1024)S(1)} %add.148), channel_id=1, source_target_pairs={{0,64},{32,96},{64,0},{96,32},{1,65},{33,97},{65,1},{97,33},{2,66}... | collective-permute-start | bytes 12296 | tf_op jit(solution)/shard_map/ppermute | solution.py:20
  127.5 3.6 %collective-permute-start.11 = (f32[1024]{0:T(1024)S(1)}, f32[1024]{0:T(1024)S(1)}, u32[]{:S(2)}, u32[]{:S(2)}) collective-permute-start(f32[1024]{0:T(1024)S(1)} %add.148), channel_id=1, source_target_pairs={{0,96},{32,0},{64,32},{96,64},{1,97},{33,1},{65,33},{97,65},{2,98}... | collective-permute-start | bytes 12296 | tf_op jit(solution)/shard_map/ppermute | solution.py:20
  129.0 4.8 %collective-permute-start.9 = (f32[1024]{0:T(1024)S(1)}, f32[1024]{0:T(1024)S(1)}, u32[]{:S(2)}, u32[]{:S(2)}) collective-permute-start(f32[1024]{0:T(1024)S(1)} %add.148), channel_id=1, source_target_pairs={{0,32},{32,64},{64,96},{96,0},{1,33},{33,65},{65,97},{97,1},{2,34}... | collective-permute-start | bytes 12296 | tf_op jit(solution)/shard_map/ppermute | solution.py:20
  146.2 10.8 %copy-start.1 = (bf16[2048,1024]{0,1:T(8,128)(2,1)S(1)}, bf16[2048,1024]{0,1:T(8,128)(2,1)}, u32[]{:S(2)}) copy-start(bf16[2048,1024]{0,1:T(8,128)(2,1)} %get-tuple-element.15) | copy-start | bytes 12582916
  146.2 24.6 %copy-start.2 = (bf16[2048,768]{0,1:T(8,128)(2,1)S(1)}, bf16[2048,768]{0,1:T(8,128)(2,1)}, u32[]{:S(2)}) copy-start(bf16[2048,768]{0,1:T(8,128)(2,1)} %all-gather.2.cloned.1.call-done) | copy-start | bytes 9437188
  149.4 1.2 collective-permute-start.12
  150.7 4.8 %collective-permute-start.13 = (f32[1024]{0:T(1024)S(1)}, f32[1024]{0:T(1024)S(1)}, u32[]{:S(2)}, u32[]{:S(2)}) collective-permute-start(f32[1024]{0:T(1024)S(1)} %add.152), channel_id=1, source_target_pairs={{0,32},{32,64},{64,96},{96,0},{1,33},{33,65},{65,97},{97,1},{2,34}... | collective-permute-start | bytes 12296 | tf_op jit(solution)/shard_map/ppermute | solution.py:20
  150.7 5.1 %collective-permute-start.14 = (f32[1024]{0:T(1024)S(1)}, f32[1024]{0:T(1024)S(1)}, u32[]{:S(2)}, u32[]{:S(2)}) collective-permute-start(f32[1024]{0:T(1024)S(1)} %add.152), channel_id=1, source_target_pairs={{0,64},{32,96},{64,0},{96,32},{1,65},{33,97},{65,1},{97,33},{2,66}... | collective-permute-start | bytes 12296 | tf_op jit(solution)/shard_map/ppermute | solution.py:20
  152.1 4.2 %collective-permute-start.15 = (f32[1024]{0:T(1024)S(1)}, f32[1024]{0:T(1024)S(1)}, u32[]{:S(2)}, u32[]{:S(2)}) collective-permute-start(f32[1024]{0:T(1024)S(1)} %add.152), channel_id=1, source_target_pairs={{0,96},{32,0},{64,32},{96,64},{1,97},{33,1},{65,33},{97,65},{2,98}... | collective-permute-start | bytes 12296 | tf_op jit(solution)/shard_map/ppermute | solution.py:20
  158.6 11.4 %all-to-all-start.3 = ((f32[16,1,2048]{2,1,0:T(1,128)}), f32[16,1,2048]{2,1,0:T(1,128)S(1)}, u32[]{:S(2)}, u32[]{:S(2)}) async-start(f32[16,1,2048]{2,1,0:T(1,128)} %broadcast_in_dim.11), calls=%async_computation.3 | async-start | bytes 262144 | tf_op jit(solution)/shard_map/all_to_all | solution.py:26
  176.5 1.7 copy-start.3
  178.3 3.5 %collective-permute-start.16 = (f32[4,96,1024]{2,1,0:T(8,128)S(1)}, f32[4,96,1024]{2,1,0:T(8,128)S(1)}, u32[]{:S(2)}, u32[]{:S(2)}) collective-permute-start(f32[4,96,1024]{2,1,0:T(8,128)S(1)} %dynamic-slice_bitcast_fusion), channel_id=1, source_target_pairs={{0,16},{16,0},{1,17},{17,1},{2,18},{18,2},{3,19},{19,3},{4,20},{20... | collective-permute-start | bytes 4718600 | tf_op jit(solution)/shard_map/ppermute | solution.py:41
  183.6 12.4 %collective-permute-start.17 = (f32[96,1024]{1,0:T(8,128)S(1)}, f32[96,1024]{1,0:T(8,128)S(1)}, u32[]{:S(2)}, u32[]{:S(2)}) collective-permute-start(f32[96,1024]{1,0:T(8,128)S(1)} %get-tuple-element.9), channel_id=1, source_target_pairs={{0,32},{32,64},{64,96},{96,0},{1,33},{33,65},{65,97},{97,1},{2,34}... | collective-permute-start | bytes 1179656 | tf_op jit(solution)/shard_map/ppermute | solution.py:45
  185.6 19.7 %collective-permute-start.18 = (f32[96,1024]{1,0:T(8,128)S(1)}, f32[96,1024]{1,0:T(8,128)S(1)}, u32[]{:S(2)}, u32[]{:S(2)}) collective-permute-start(f32[96,1024]{1,0:T(8,128)S(1)} %get-tuple-element.11), channel_id=1, source_target_pairs={{0,64},{32,96},{64,0},{96,32},{1,65},{33,97},{65,1},{97,33},{2,66}... | collective-permute-start | bytes 1179656 | tf_op jit(solution)/shard_map/ppermute | solution.py:45
  187.8 17.6 %collective-permute-start.19 = (f32[96,1024]{1,0:T(8,128)S(1)}, f32[96,1024]{1,0:T(8,128)}, u32[]{:S(2)}, u32[]{:S(2)}) collective-permute-start(f32[96,1024]{1,0:T(8,128)S(1)} %get-tuple-element.10), channel_id=1, source_target_pairs={{0,96},{32,0},{64,32},{96,64},{1,97},{33,1},{65,33},{97,65},{2,98}... | collective-permute-start | bytes 1179656 | tf_op jit(solution)/shard_map/ppermute | solution.py:45
  206.4 1.2 collective-permute-start.20
  207.7 4.9 %collective-permute-start.21 = (f32[1024]{0:T(1024)S(1)}, f32[1024]{0:T(1024)S(1)}, u32[]{:S(2)}, u32[]{:S(2)}) collective-permute-start(f32[1024]{0:T(1024)S(1)} %add.174), channel_id=1, source_target_pairs={{0,32},{32,64},{64,96},{96,0},{1,33},{33,65},{65,97},{97,1},{2,34}... | collective-permute-start | bytes 12296 | tf_op jit(solution)/shard_map/ppermute | solution.py:20
  209.3 5.1 %collective-permute-start.22 = (f32[1024]{0:T(1024)S(1)}, f32[1024]{0:T(1024)S(1)}, u32[]{:S(2)}, u32[]{:S(2)}) collective-permute-start(f32[1024]{0:T(1024)S(1)} %add.174), channel_id=1, source_target_pairs={{0,64},{32,96},{64,0},{96,32},{1,65},{33,97},{65,1},{97,33},{2,66}... | collective-permute-start | bytes 12296 | tf_op jit(solution)/shard_map/ppermute | solution.py:20
  211.6 3.6 %collective-permute-start.23 = (f32[1024]{0:T(1024)S(1)}, f32[1024]{0:T(1024)S(1)}, u32[]{:S(2)}, u32[]{:S(2)}) collective-permute-start(f32[1024]{0:T(1024)S(1)} %add.174), channel_id=1, source_target_pairs={{0,96},{32,0},{64,32},{96,64},{1,97},{33,1},{65,33},{97,65},{2,98}... | collective-permute-start | bytes 12296 | tf_op jit(solution)/shard_map/ppermute | solution.py:20
Sparse Core Ops, SparseCore 0:
  10.2 50.4 all-gather.1

commit v4 on v3

--- a/solution.py
+++ b/solution.py
@@ -72,12 +72,16 @@
         / (feature_dimension * entropic_smoothing)
     )
     kernel = jnp.exp(sharpened_similarity).astype(jnp.bfloat16)
-    weight_sum = reduce_row(jnp.sum(weights))
     col_scale = jnp.full((local_centres,), 1.0, jnp.float32) / centre_total
     row_scale = row_step(kernel, col_scale, weights)
+    weight_sum = None
     for sweep in range(ITERS):
         partial_cols = jnp.sum(kernel.astype(jnp.float32) * row_scale[:, None], axis=0)
-        col_mass = reduce_row(partial_cols)
+        if weight_sum is None:
+            both = reduce_row(jnp.concatenate([partial_cols, jnp.sum(weights)[None]]))
+            col_mass, weight_sum = both[:local_centres], both[local_centres]
+        else:
+            col_mass = reduce_row(partial_cols)
         col_scale = weight_sum / centre_total / col_mass
         row_scale = row_step(kernel, col_scale, weights)
     transport = (row_scale[:, None] * kernel.astype(jnp.float32) * col_scale[None, :]).astype(

time: 223 us -> 215 us (0.964)
  starting transfers between devices: 34.1 us -> 24.7 us
  waiting for transfers between devices: 95.8 us -> 99 us
  between operations: 17.6 us -> 15 us
    ppermute x20 -> x16, starting transfers between devices: 25.6 us -> 17.7 us  [shifted_sum(): total = total + lax.ppermute(x, axis, [(i, (i + k) % n) for i in range(n)])]
    ppermute x20 -> x16, waiting for transfers between devices: 16.1 us -> 17.9 us  [shifted_sum(): total = total + lax.ppermute(x, axis, [(i, (i + k) % n) for i in range(n)])]
  transfers between devices with their start and end apart: 26 -> 22, of which waited for: 19 -> 19; matrix products, arithmetic and copies ran while one was open for 1% -> 1% of each run, Pallas kernels for 0% -> 0%
where the time goes in v4:
time: 215 us; the launch traced here: 214 us
  waiting for transfers between devices  99 us (46%)
  blocking collectives  34.4 us (16%)
  starting transfers between devices  24.7 us (11%)
  other arithmetic  23.9 us (11%)
  between operations  15 us (7%)
  matrix products  13.6 us (6%)
  local copies, waits for them, and re-layouts  3.42 us (2%)
    all_gather x1, waiting for transfers between devices, per_device(): full_rows = lax.all_gather(vectors, CENT, axis=1, tiled=True)  51 us
    all_to_all x3, blocking collectives, reduce_cent(): lax.all_to_all(jnp.broadcast_to(x, (n, *x.shape)), CENT, 0, 0, tiled=False)  34.4 us
    ppermute x3, waiting for transfers between devices, scatter_row(): lax.ppermute(piece, 'rx', [(i, (i + k) % chips) for i in range(chips)])  18.3 us
    ppermute x16, waiting for transfers between devices, shifted_sum(): total = total + lax.ppermute(x, axis, [(i, (i + k) % n) for i in range(n)])  17.9 us
    ppermute x16, starting transfers between devices, shifted_sum(): total = total + lax.ppermute(x, axis, [(i, (i + k) % n) for i in range(n)])  17.7 us
    reduce_sum x3, other arithmetic, per_device(): jnp.sum(kernel.astype(jnp.float32) * row_scale[:, None], axis=0)  9.83 us
    dot_general x1, matrix products, per_device(): jnp.dot(full_rows, centroids.T, preferred_element_type=jnp.float32)  7.88 us
    all_to_all x1, waiting for transfers between devices, reduce_cent(): lax.all_to_all(jnp.broadcast_to(x, (n, *x.shape)), CENT, 0, 0, tiled=False)  7.82 us
  transfers between devices with their start and end apart: 22, of which 19 were waited for; matrix products, arithmetic and copies ran while one was open for 1% of the time, Pallas kernels for 0%

profile of v4, /device:TPU:0, one launch (start us, length us, event | category | flops | bytes accessed | tf_op | source)
XLA Modules:
  0.0 214.1 jit_solution(12845187041566993706)
XLA Ops:
  7.2 0.7 all-gather.2.cloned.1.call-update
  7.9 1.8 multiply_reduce_fusion.1
  9.7 51.0 %all-gather.2.cloned.1.call-done = bf16[2048,768]{0,1:T(8,128)(2,1)} async-done(((bf16[2048,48]{0,1:T(8,128)(2,1)}), bf16[2048,768]{0,1:T(8,128)(2,1)}) %all-gather.2.cloned.1.call-update) | async-done | bytes 3145744 | tf_op jit(solution)/shard_map/all_gather | solution.py:56
  60.7 2.6 %multiply_reduce_fusion = f32[2048]{0:T(1024)S(1)} fusion(bf16[2048,768]{0,1:T(8,128)(2,1)} %all-gather.2.cloned.1.call-done), kind=kLoop, calls=%fused_computation.18 | loop fusion | flops 4716544 | bytes 3153920 | tf_op jit(solution)/shard_map/reduce_sum | solution.py:62
  63.2 7.9 %fusion = (f32[2048]{0:T(1024)S(1)}, bf16[2048,1024]{0,1:T(8,128)(2,1)}) fusion(f32[1024]{0:T(1024)S(1)} %add_rsqrt_fusion.2, f32[2048]{0:T(1024)S(1)} %add_rsqrt_fusion, bf16[1024,768]{1,0:T(8,128)(2,1)S(1)} %copy-done.5, bf16[2048,768]{0,1:T(8,128)(2,1)} %all-gather.2.cloned.1.call-done), kind=kOutput, calls=%fused_computation.8 | convolution fusion | flops 3235903488 | bytes 8933376 | tf_op jit(solution)/shard_map/dot_general | solution.py:67
  71.2 12.0 %all_to_all.24 = f32[16,1,2048]{2,1,0:T(1,128)S(1)} all-to-all(f32[16,1,2048]{2,1,0:T(1,128)S(1)} %broadcast_in_dim.10), channel_id=1, replica_groups=mesh['rx'=4,'rc'=2,'cy'=4,'cz'=4] {'cy','cz'}, dimensions={0} | all-to-all | bytes 262144 | tf_op jit(solution)/shard_map/all_to_all | solution.py:26
  83.2 0.1 reduce_sum.138
  83.3 0.6 fusion.18
  83.9 3.4 %fusion.1 = f32[1024]{0:T(1024)S(1)} fusion(bf16[2048,1024]{0,1:T(8,128)(2,1)} %get-tuple-element.15, f32[2048]{0:T(1024)S(1)} %get-tuple-element.12), kind=kLoop, calls=%fused_computation.9 | loop fusion | flops 6290432 | bytes 4206592 | tf_op jit(solution)/shard_map/reduce_sum | solution.py:79
  87.3 0.7 pad_maximum_fusion
  88.0 1.2 collective-permute-done
  89.2 0.7 fusion.15
  89.8 1.5 collective-permute-start.1
  91.4 2.7 %collective-permute-start.2 = (f32[1025]{0:T(1024)S(1)}, f32[1025]{0:T(1024)S(1)}, u32[]{:S(2)}, u32[]{:S(2)}) collective-permute-start(f32[1025]{0:T(1024)S(1)} %fusion.15), channel_id=1, source_target_pairs={{0,64},{32,96},{64,0},{96,32},{1,65},{33,97},{65,1},{97,33},{2,66}... | collective-permute-start | bytes 12308 | tf_op jit(solution)/shard_map/ppermute | solution.py:20
  94.0 1.5 collective-permute-start.3
  95.5 1.0 collective-permute-done.2
  96.5 1.2 collective-permute-done.3
  97.7 0.5 slice.8
  98.9 0.9 fusion.2
  99.9 11.2 %all_to_all.25 = f32[16,1,2048]{2,1,0:T(1,128)S(1)} all-to-all(f32[16,1,2048]{2,1,0:T(1,128)S(1)} %broadcast_in_dim.12), channel_id=1, replica_groups=mesh['rx'=4,'rc'=2,'cy'=4,'cz'=4] {'cy','cz'}, dimensions={0} | all-to-all | bytes 262144 | tf_op jit(solution)/shard_map/all_to_all | solution.py:26
  111.1 0.1 reduce_sum.142
  111.2 3.2 %fusion.3 = f32[1024]{0:T(1024)S(1)} fusion(bf16[2048,1024]{0,1:T(8,128)(2,1)} %get-tuple-element.15, f32[2048]{0:T(1024)S(1)} %div.61), kind=kLoop, calls=%fused_computation.11 | loop fusion | flops 6290432 | bytes 4206592 | tf_op jit(solution)/shard_map/reduce_sum | solution.py:79
  114.5 1.2 collective-permute-done.4
  115.7 0.3 collective-permute-start.5
  116.0 3.8 %collective-permute-start.6 = (f32[1024]{0:T(1024)S(1)}, f32[1024]{0:T(1024)S(1)}, u32[]{:S(2)}, u32[]{:S(2)}) collective-permute-start(f32[1024]{0:T(1024)S(1)} %add.132), channel_id=1, source_target_pairs={{0,64},{32,96},{64,0},{96,32},{1,65},{33,97},{65,1},{97,33},{2,66}... | collective-permute-start | bytes 12296 | tf_op jit(solution)/shard_map/ppermute | solution.py:20
  119.8 0.7 collective-permute-done.5
  120.5 0.9 collective-permute-done.6
  121.5 2.0 collective-permute-done.7
  123.4 0.9 fusion.4
  124.4 11.2 %all_to_all.26 = f32[16,1,2048]{2,1,0:T(1,128)S(1)} all-to-all(f32[16,1,2048]{2,1,0:T(1,128)S(1)} %broadcast_in_dim.13), channel_id=1, replica_groups=mesh['rx'=4,'rc'=2,'cy'=4,'cz'=4] {'cy','cz'}, dimensions={0} | all-to-all | bytes 262144 | tf_op jit(solution)/shard_map/all_to_all | solution.py:26
  135.7 0.1 reduce_sum.145
  135.8 3.2 %fusion.5 = f32[1024]{0:T(1024)S(1)} fusion(bf16[2048,1024]{0,1:T(8,128)(2,1)} %get-tuple-element.15, f32[2048]{0:T(1024)S(1)} %div.63), kind=kLoop, calls=%fused_computation.13 | loop fusion | flops 6290432 | bytes 4206592 | tf_op jit(solution)/shard_map/reduce_sum | solution.py:79
  139.0 0.3 collective-permute-start.8
  139.3 1.2 collective-permute-done.8
  140.4 1.5 collective-permute-start.10
  142.0 1.1 collective-permute-start.11
  143.1 0.9 collective-permute-start.9
  144.0 1.6 collective-permute-done.10
  145.6 2.3 %collective-permute-done.9 = f32[1024]{0:T(1024)S(1)} collective-permute-done((f32[1024]{0:T(1024)S(1)}, f32[1024]{0:T(1024)S(1)}, u32[]{:S(2)}, u32[]{:S(2)}) %collective-permute-start.9) | collective-permute-done | bytes 4128 | tf_op jit(solution)/shard_map/ppermute | solution.py:20
  147.9 0.6 multiply_log_fusion
  148.5 0.9 fusion.6
  149.4 0.7 broadcast_in_dim.14
  150.1 3.6 %all-to-all-start.3 = ((f32[16,1,2048]{2,1,0:T(1,128)}), f32[16,1,2048]{2,1,0:T(1,128)S(1)}, u32[]{:S(2)}, u32[]{:S(2)}) async-start(f32[16,1,2048]{2,1,0:T(1,128)} %broadcast_in_dim.14), calls=%async_computation.3 | async-start | bytes 262144 | tf_op jit(solution)/shard_map/all_to_all | solution.py:26
  153.8 7.8 %all-to-all-done.3 = f32[16,1,2048]{2,1,0:T(1,128)S(1)} async-done(((f32[16,1,2048]{2,1,0:T(1,128)}), f32[16,1,2048]{2,1,0:T(1,128)S(1)}, u32[]{:S(2)}, u32[]{:S(2)}) %all-to-all-start.3) | async-done | bytes 131104 | tf_op jit(solution)/shard_map/all_to_all | solution.py:26
  161.6 0.1 reduce_sum.148
  161.7 0.6 fusion.16
  162.3 5.7 %fusion.9 = f32[1024,768]{0,1:T(8,128)S(1)} fusion(bf16[2048,768]{0,1:T(8,128)(2,1)S(1)} %copy-done.3, bf16[2048,1024]{0,1:T(8,128)(2,1)} %get-tuple-element.15, f32[2048]{0:T(1024)S(1)} %get-tuple-element.6, f32[1024]{0:T(1024)S(1)} %get-tuple-element.4), kind=kOutput, calls=%fused_computation.19 | convolution fusion | flops 3229614080 | bytes 10498048 | tf_op jit(solution)/shard_map/dot_general | solution.py:90
  168.0 1.7 copy-done.4
  169.6 0.2 dynamic-slice_bitcast_fusion
  170.0 3.4 %collective-permute-done.12 = f32[4,96,1024]{2,1,0:T(8,128)S(1)} collective-permute-done((f32[4,96,1024]{2,1,0:T(8,128)S(1)}, f32[4,96,1024]{2,1,0:T(8,128)S(1)}, u32[]{:S(2)}, u32[]{:S(2)}) %collective-permute-start.12) | collective-permute-done | bytes 1572896 | tf_op jit(solution)/shard_map/ppermute | solution.py:41
  173.3 1.7 bitcast_add_fusion
  175.0 0.1 dynamic-slice_bitcast_fusion.3
  175.2 1.7 collective-permute-start.14
  176.9 1.5 collective-permute-start.15
  178.4 17.6 %collective-permute-done.13 = f32[96,1024]{1,0:T(8,128)S(1)} collective-permute-done((f32[96,1024]{1,0:T(8,128)S(1)}, f32[96,1024]{1,0:T(8,128)S(1)}, u32[]{:S(2)}, u32[]{:S(2)}) %collective-permute-start.13) | collective-permute-done | bytes 393248 | tf_op jit(solution)/shard_map/ppermute | solution.py:45
  196.0 0.7 collective-permute-done.15
  196.7 1.1 multiply_reduce_fusion.2
  197.9 1.2 collective-permute-done.16
  199.1 0.2 collective-permute-start.17
  199.3 3.6 %collective-permute-start.18 = (f32[1024]{0:T(1024)S(1)}, f32[1024]{0:T(1024)S(1)}, u32[]{:S(2)}, u32[]{:S(2)}) collective-permute-start(f32[1024]{0:T(1024)S(1)} %add.158), channel_id=1, source_target_pairs={{0,64},{32,96},{64,0},{96,32},{1,65},{33,97},{65,1},{97,33},{2,66}... | collective-permute-start | bytes 12296 | tf_op jit(solution)/shard_map/ppermute | solution.py:20
  202.9 1.0 collective-permute-done.17
  203.9 0.6 collective-permute-done.18
  204.5 2.0 collective-permute-done.19
  206.5 0.8 broadcast_multiply_fusion
  (38 shorter events, 0.8 us)
Async XLA Ops:
  7.2 56.1 %copy-start.5 = (bf16[1024,768]{1,0:T(8,128)(2,1)S(1)}, bf16[1024,768]{1,0:T(8,128)(2,1)}, u32[]{:S(2)}) copy-start(bf16[1024,768]{1,0:T(8,128)(2,1)} %param.4) | copy-start | bytes 4718596
  7.2 53.5 %all-gather.2.cloned.1.call-start = ((), (), s32[]{:S(2)}) async-start(), calls=%async_computation.4 | async-start | bytes 3342336 | tf_op jit(solution)/shard_map/all_gather | solution.py:56
  63.2 20.0 %copy-start.6 = (f32[2048]{0:T(1024)S(1)}, f32[2048]{0:T(1024)}, u32[]{:S(2)}) copy-start(f32[2048]{0:T(1024)} %param.5) | copy-start | bytes 24580
  83.3 15.6 %copy-start = (bf16[2048,1024]{0,1:T(8,128)(2,1)S(1)}, bf16[2048,1024]{0,1:T(8,128)(2,1)}, u32[]{:S(2)}) copy-start(bf16[2048,1024]{0,1:T(8,128)(2,1)} %get-tuple-element.15) | copy-start | bytes 12582916
  87.9 1.3 collective-permute-start
  89.8 5.7 %collective-permute-start.1 = (f32[1025]{0:T(1024)S(1)}, f32[1025]{0:T(1024)S(1)}, u32[]{:S(2)}, u32[]{:S(2)}) collective-permute-start(f32[1025]{0:T(1024)S(1)} %fusion.15), channel_id=1, source_target_pairs={{0,32},{32,64},{64,96},{96,0},{1,33},{33,65},{65,97},{97,1},{2,34}... | collective-permute-start | bytes 12308 | tf_op jit(solution)/shard_map/ppermute | solution.py:20
  91.4 5.2 %collective-permute-start.2 = (f32[1025]{0:T(1024)S(1)}, f32[1025]{0:T(1024)S(1)}, u32[]{:S(2)}, u32[]{:S(2)}) collective-permute-start(f32[1025]{0:T(1024)S(1)} %fusion.15), channel_id=1, source_target_pairs={{0,64},{32,96},{64,0},{96,32},{1,65},{33,97},{65,1},{97,33},{2,66}... | collective-permute-start | bytes 12308 | tf_op jit(solution)/shard_map/ppermute | solution.py:20
  94.0 3.7 %collective-permute-start.3 = (f32[1025]{0:T(1024)S(1)}, f32[1025]{0:T(1024)S(1)}, u32[]{:S(2)}, u32[]{:S(2)}) collective-permute-start(f32[1025]{0:T(1024)S(1)} %fusion.15), channel_id=1, source_target_pairs={{0,96},{32,0},{64,32},{96,64},{1,97},{33,1},{65,33},{97,65},{2,98}... | collective-permute-start | bytes 12308 | tf_op jit(solution)/shard_map/ppermute | solution.py:20
  111.2 12.2 %copy-start.1 = (bf16[2048,1024]{0,1:T(8,128)(2,1)S(1)}, bf16[2048,1024]{0,1:T(8,128)(2,1)}, u32[]{:S(2)}) copy-start(bf16[2048,1024]{0,1:T(8,128)(2,1)} %get-tuple-element.15) | copy-start | bytes 12582916
  114.4 1.2 collective-permute-start.4
  115.7 4.8 %collective-permute-start.5 = (f32[1024]{0:T(1024)S(1)}, f32[1024]{0:T(1024)S(1)}, u32[]{:S(2)}, u32[]{:S(2)}) collective-permute-start(f32[1024]{0:T(1024)S(1)} %add.132), channel_id=1, source_target_pairs={{0,32},{32,64},{64,96},{96,0},{1,33},{33,65},{65,97},{97,1},{2,34}... | collective-permute-start | bytes 12296 | tf_op jit(solution)/shard_map/ppermute | solution.py:20
  116.0 5.5 %collective-permute-start.6 = (f32[1024]{0:T(1024)S(1)}, f32[1024]{0:T(1024)S(1)}, u32[]{:S(2)}, u32[]{:S(2)}) collective-permute-start(f32[1024]{0:T(1024)S(1)} %add.132), channel_id=1, source_target_pairs={{0,64},{32,96},{64,0},{96,32},{1,65},{33,97},{65,1},{97,33},{2,66}... | collective-permute-start | bytes 12296 | tf_op jit(solution)/shard_map/ppermute | solution.py:20
  119.8 3.6 %collective-permute-start.7 = (f32[1024]{0:T(1024)S(1)}, f32[1024]{0:T(1024)S(1)}, u32[]{:S(2)}, u32[]{:S(2)}) collective-permute-start(f32[1024]{0:T(1024)S(1)} %add.132), channel_id=1, source_target_pairs={{0,96},{32,0},{64,32},{96,64},{1,97},{33,1},{65,33},{97,65},{2,98}... | collective-permute-start | bytes 12296 | tf_op jit(solution)/shard_map/ppermute | solution.py:20
  135.8 12.8 %copy-start.2 = (bf16[2048,1024]{0,1:T(8,128)(2,1)S(1)}, bf16[2048,1024]{0,1:T(8,128)(2,1)}, u32[]{:S(2)}) copy-start(bf16[2048,1024]{0,1:T(8,128)(2,1)} %get-tuple-element.15) | copy-start | bytes 12582916
  135.8 26.5 %copy-start.3 = (bf16[2048,768]{0,1:T(8,128)(2,1)S(1)}, bf16[2048,768]{0,1:T(8,128)(2,1)}, u32[]{:S(2)}) copy-start(bf16[2048,768]{0,1:T(8,128)(2,1)} %all-gather.2.cloned.1.call-done) | copy-start | bytes 9437188
  139.0 1.4 collective-permute-start.8
  140.4 5.1 %collective-permute-start.10 = (f32[1024]{0:T(1024)S(1)}, f32[1024]{0:T(1024)S(1)}, u32[]{:S(2)}, u32[]{:S(2)}) collective-permute-start(f32[1024]{0:T(1024)S(1)} %add.136), channel_id=1, source_target_pairs={{0,64},{32,96},{64,0},{96,32},{1,65},{33,97},{65,1},{97,33},{2,66}... | collective-permute-start | bytes 12296 | tf_op jit(solution)/shard_map/ppermute | solution.py:20
  142.0 3.6 %collective-permute-start.11 = (f32[1024]{0:T(1024)S(1)}, f32[1024]{0:T(1024)S(1)}, u32[]{:S(2)}, u32[]{:S(2)}) collective-permute-start(f32[1024]{0:T(1024)S(1)} %add.136), channel_id=1, source_target_pairs={{0,96},{32,0},{64,32},{96,64},{1,97},{33,1},{65,33},{97,65},{2,98}... | collective-permute-start | bytes 12296 | tf_op jit(solution)/shard_map/ppermute | solution.py:20
  143.1 4.8 %collective-permute-start.9 = (f32[1024]{0:T(1024)S(1)}, f32[1024]{0:T(1024)S(1)}, u32[]{:S(2)}, u32[]{:S(2)}) collective-permute-start(f32[1024]{0:T(1024)S(1)} %add.136), channel_id=1, source_target_pairs={{0,32},{32,64},{64,96},{96,0},{1,33},{33,65},{65,97},{97,1},{2,34}... | collective-permute-start | bytes 12296 | tf_op jit(solution)/shard_map/ppermute | solution.py:20
  150.1 11.4 %all-to-all-start.3 = ((f32[16,1,2048]{2,1,0:T(1,128)}), f32[16,1,2048]{2,1,0:T(1,128)S(1)}, u32[]{:S(2)}, u32[]{:S(2)}) async-start(f32[16,1,2048]{2,1,0:T(1,128)} %broadcast_in_dim.14), calls=%async_computation.3 | async-start | bytes 262144 | tf_op jit(solution)/shard_map/all_to_all | solution.py:26
  168.0 1.7 copy-start.4
  169.8 3.5 %collective-permute-start.12 = (f32[4,96,1024]{2,1,0:T(8,128)S(1)}, f32[4,96,1024]{2,1,0:T(8,128)S(1)}, u32[]{:S(2)}, u32[]{:S(2)}) collective-permute-start(f32[4,96,1024]{2,1,0:T(8,128)S(1)} %dynamic-slice_bitcast_fusion), channel_id=1, source_target_pairs={{0,16},{16,0},{1,17},{17,1},{2,18},{18,2},{3,19},{19,3},{4,20},{20... | collective-permute-start | bytes 4718600 | tf_op jit(solution)/shard_map/ppermute | solution.py:41
  175.1 20.9 %collective-permute-start.13 = (f32[96,1024]{1,0:T(8,128)S(1)}, f32[96,1024]{1,0:T(8,128)S(1)}, u32[]{:S(2)}, u32[]{:S(2)}) collective-permute-start(f32[96,1024]{1,0:T(8,128)S(1)} %get-tuple-element.9), channel_id=1, source_target_pairs={{0,32},{32,64},{64,96},{96,0},{1,33},{33,65},{65,97},{97,1},{2,34}... | collective-permute-start | bytes 1179656 | tf_op jit(solution)/shard_map/ppermute | solution.py:45
  175.2 20.8 %collective-permute-start.14 = (f32[96,1024]{1,0:T(8,128)S(1)}, f32[96,1024]{1,0:T(8,128)S(1)}, u32[]{:S(2)}, u32[]{:S(2)}) collective-permute-start(f32[96,1024]{1,0:T(8,128)S(1)} %get-tuple-element.11), channel_id=1, source_target_pairs={{0,64},{32,96},{64,0},{96,32},{1,65},{33,97},{65,1},{97,33},{2,66}... | collective-permute-start | bytes 1179656 | tf_op jit(solution)/shard_map/ppermute | solution.py:45
  176.9 19.8 %collective-permute-start.15 = (f32[96,1024]{1,0:T(8,128)S(1)}, f32[96,1024]{1,0:T(8,128)}, u32[]{:S(2)}, u32[]{:S(2)}) collective-permute-start(f32[96,1024]{1,0:T(8,128)S(1)} %get-tuple-element.10), channel_id=1, source_target_pairs={{0,96},{32,0},{64,32},{96,64},{1,97},{33,1},{65,33},{97,65},{2,98}... | collective-permute-start | bytes 1179656 | tf_op jit(solution)/shard_map/ppermute | solution.py:45
  197.8 1.2 collective-permute-start.16
  199.1 4.8 %collective-permute-start.17 = (f32[1024]{0:T(1024)S(1)}, f32[1024]{0:T(1024)S(1)}, u32[]{:S(2)}, u32[]{:S(2)}) collective-permute-start(f32[1024]{0:T(1024)S(1)} %add.158), channel_id=1, source_target_pairs={{0,32},{32,64},{64,96},{96,0},{1,33},{33,65},{65,97},{97,1},{2,34}... | collective-permute-start | bytes 12296 | tf_op jit(solution)/shard_map/ppermute | solution.py:20
  199.3 5.2 %collective-permute-start.18 = (f32[1024]{0:T(1024)S(1)}, f32[1024]{0:T(1024)S(1)}, u32[]{:S(2)}, u32[]{:S(2)}) collective-permute-start(f32[1024]{0:T(1024)S(1)} %add.158), channel_id=1, source_target_pairs={{0,64},{32,96},{64,0},{96,32},{1,65},{33,97},{65,1},{97,33},{2,66}... | collective-permute-start | bytes 12296 | tf_op jit(solution)/shard_map/ppermute | solution.py:20
  202.9 3.6 %collective-permute-start.19 = (f32[1024]{0:T(1024)S(1)}, f32[1024]{0:T(1024)S(1)}, u32[]{:S(2)}, u32[]{:S(2)}) collective-permute-start(f32[1024]{0:T(1024)S(1)} %add.158), channel_id=1, source_target_pairs={{0,96},{32,0},{64,32},{96,64},{1,97},{33,1},{65,33},{97,65},{2,98}... | collective-permute-start | bytes 12296 | tf_op jit(solution)/shard_map/ppermute | solution.py:20
Sparse Core Ops, SparseCore 0:
  10.2 50.4 all-gather.1

commit v5 on v4

--- a/solution.py
+++ b/solution.py
@@ -84,15 +84,21 @@
             col_mass = reduce_row(partial_cols)
         col_scale = weight_sum / centre_total / col_mass
         row_scale = row_step(kernel, col_scale, weights)
-    transport = (row_scale[:, None] * kernel.astype(jnp.float32) * col_scale[None, :]).astype(
-        jnp.bfloat16
-    )
-    term = lax.dot_general(
-        full_rows, transport, (((0,), (0,)), ((), ())), preferred_element_type=jnp.float32
-    )
-    own_summed = scatter_row(term)
-    square_sum = reduce_row(jnp.sum(own_summed * own_summed, axis=0))
-    new_centroids = own_summed * lax.rsqrt(square_sum / feature_dimension + 1e-06)[None, :]
+    halves = 2
+    width = local_centres // halves
+    pieces = []
+    for half in range(halves):
+        columns = slice(half * width, (half + 1) * width)
+        transport = (
+            row_scale[:, None] * kernel[:, columns].astype(jnp.float32) * col_scale[None, columns]
+        ).astype(jnp.bfloat16)
+        term = lax.dot_general(
+            full_rows, transport, (((0,), (0,)), ((), ())), preferred_element_type=jnp.float32
+        )
+        own_summed = scatter_row(term)
+        square_sum = reduce_row(jnp.sum(own_summed * own_summed, axis=0))
+        pieces.append(own_summed * lax.rsqrt(square_sum / feature_dimension + 1e-06)[None, :])
+    new_centroids = jnp.concatenate(pieces, axis=1)
     return (new_centroids, jnp.log(row_scale), jnp.log(centre_total * col_scale))
 
 

time: 215 us -> 231 us (1.074)
  local copies, waits for them, and re-layouts: 3.42 us -> 9.18 us
  starting transfers between devices: 24.7 us -> 30.2 us
  matrix products: 13.6 us -> 18.2 us
  other arithmetic: 23.9 us -> 28 us
  waiting for transfers between devices: 99 us -> 95.2 us
    ppermute x3 -> x6, waiting for transfers between devices: 18.3 us -> 11.8 us  [scatter_row(): lax.ppermute(piece, 'rx', [(i, (i + k) % chips) for i in range(chips)])]
    dot_general x1 -> x2, matrix products: 5.68 us -> 10.3 us  [per_device(): lax.dot_general(full_rows, transport, (((0,), (0,)), ((), ())), preferred...]
    dot_general x0 -> x2, local copies, waits for them, and re-layouts: none -> 3.74 us  [per_device(): lax.dot_general(full_rows, transport, (((0,), (0,)), ((), ())), preferred...]
    ppermute x3 -> x6, starting transfers between devices: 3.3 us -> 6.81 us  [scatter_row(): lax.ppermute(piece, 'rx', [(i, (i + k) % chips) for i in range(chips)])]
    ppermute x16 -> x20, waiting for transfers between devices: 17.9 us -> 20.7 us  [shifted_sum(): total = total + lax.ppermute(x, axis, [(i, (i + k) % n) for i in range(n)])]
    ppermute x16 -> x20, starting transfers between devices: 17.7 us -> 19.2 us  [shifted_sum(): total = total + lax.ppermute(x, axis, [(i, (i + k) % n) for i in range(n)])]
  transfers between devices with their start and end apart: 22 -> 30, of which waited for: 19 -> 19; matrix products, arithmetic and copies ran while one was open for 1% -> 2% of each run, Pallas kernels for 0% -> 0%
where the time goes in v5:
time: 231 us; the launch traced here: 230 us
  waiting for transfers between devices  95.2 us (41%)
  blocking collectives  34.4 us (15%)
  starting transfers between devices  30.2 us (13%)
  other arithmetic  28 us (12%)
  matrix products  18.2 us (8%)
  between operations  15 us (6%)
  local copies, waits for them, and re-layouts  9.18 us (4%)
    all_gather x1, waiting for transfers between devices, per_device(): full_rows = lax.all_gather(vectors, CENT, axis=1, tiled=True)  51 us
    all_to_all x3, blocking collectives, reduce_cent(): lax.all_to_all(jnp.broadcast_to(x, (n, *x.shape)), CENT, 0, 0, tiled=False)  34.4 us
    ppermute x20, waiting for transfers between devices, shifted_sum(): total = total + lax.ppermute(x, axis, [(i, (i + k) % n) for i in range(n)])  20.7 us
    ppermute x20, starting transfers between devices, shifted_sum(): total = total + lax.ppermute(x, axis, [(i, (i + k) % n) for i in range(n)])  19.2 us
    ppermute x6, waiting for transfers between devices, scatter_row(): lax.ppermute(piece, 'rx', [(i, (i + k) % chips) for i in range(chips)])  11.8 us
    dot_general x2, matrix products, per_device(): lax.dot_general(full_rows, transport, (((0,), (0,)), ((), ())), preferred...  10.3 us
    reduce_sum x3, other arithmetic, per_device(): jnp.sum(kernel.astype(jnp.float32) * row_scale[:, None], axis=0)  9.83 us
    dot_general x1, matrix products, per_device(): jnp.dot(full_rows, centroids.T, preferred_element_type=jnp.float32)  7.89 us
  transfers between devices with their start and end apart: 30, of which 19 were waited for; matrix products, arithmetic and copies ran while one was open for 2% of the time, Pallas kernels for 0%

profile of v5, /device:TPU:0, one launch (start us, length us, event | category | flops | bytes accessed | tf_op | source)
XLA Modules:
  0.0 230.2 jit_solution(12231079368385152222)
XLA Ops:
  7.2 0.7 all-gather.2.cloned.1.call-update
  7.9 1.8 multiply_reduce_fusion.1
  9.7 51.0 %all-gather.2.cloned.1.call-done = bf16[2048,768]{0,1:T(8,128)(2,1)} async-done(((bf16[2048,48]{0,1:T(8,128)(2,1)}), bf16[2048,768]{0,1:T(8,128)(2,1)}) %all-gather.2.cloned.1.call-update) | async-done | bytes 3145744 | tf_op jit(solution)/shard_map/all_gather | solution.py:56
  60.7 2.6 %multiply_reduce_fusion = f32[2048]{0:T(1024)S(1)} fusion(bf16[2048,768]{0,1:T(8,128)(2,1)} %all-gather.2.cloned.1.call-done), kind=kLoop, calls=%fused_computation.15 | loop fusion | flops 4716544 | bytes 3153920 | tf_op jit(solution)/shard_map/reduce_sum | solution.py:62
  63.2 7.9 %fusion = (f32[2048]{0:T(1024)S(1)}, bf16[2048,1024]{0,1:T(8,128)(2,1)}) fusion(f32[1024]{0:T(1024)S(1)} %add_rsqrt_fusion.1, f32[2048]{0:T(1024)S(1)} %add_rsqrt_fusion, bf16[1024,768]{1,0:T(8,128)(2,1)S(1)} %copy-done.4, bf16[2048,768]{0,1:T(8,128)(2,1)} %all-gather.2.cloned.1.call-done), kind=kOutput, calls=%fused_computation.7 | convolution fusion | flops 3235903488 | bytes 8933376 | tf_op jit(solution)/shard_map/dot_general | solution.py:67
  71.2 12.0 %all_to_all.24 = f32[16,1,2048]{2,1,0:T(1,128)S(1)} all-to-all(f32[16,1,2048]{2,1,0:T(1,128)S(1)} %broadcast_in_dim.10), channel_id=1, replica_groups=mesh['rx'=4,'rc'=2,'cy'=4,'cz'=4] {'cy','cz'}, dimensions={0} | all-to-all | bytes 262144 | tf_op jit(solution)/shard_map/all_to_all | solution.py:26
  83.3 0.6 fusion.25
  83.9 3.4 %fusion.1 = f32[1024]{0:T(1024)S(1)} fusion(bf16[2048,1024]{0,1:T(8,128)(2,1)} %get-tuple-element.22, f32[2048]{0:T(1024)S(1)} %get-tuple-element.17), kind=kLoop, calls=%fused_computation.8 | loop fusion | flops 6290432 | bytes 4206592 | tf_op jit(solution)/shard_map/reduce_sum | solution.py:79
  87.3 0.7 pad_maximum_fusion.1
  88.0 1.2 collective-permute-done
  89.2 0.7 fusion.21
  89.8 2.8 %collective-permute-start.3 = (f32[1025]{0:T(1024)S(1)}, f32[1025]{0:T(1024)S(1)}, u32[]{:S(2)}, u32[]{:S(2)}) collective-permute-start(f32[1025]{0:T(1024)S(1)} %fusion.21), channel_id=1, source_target_pairs={{0,96},{32,0},{64,32},{96,64},{1,97},{33,1},{65,33},{97,65},{2,98}... | collective-permute-start | bytes 12308 | tf_op jit(solution)/shard_map/ppermute | solution.py:20
  92.6 0.8 collective-permute-start.2
  93.4 0.9 collective-permute-start.1
  94.3 3.4 %collective-permute-done.2 = f32[1025]{0:T(1024)S(1)} collective-permute-done((f32[1025]{0:T(1024)S(1)}, f32[1025]{0:T(1024)S(1)}, u32[]{:S(2)}, u32[]{:S(2)}) %collective-permute-start.2) | collective-permute-done | bytes 4132 | tf_op jit(solution)/shard_map/ppermute | solution.py:20
  99.5 0.9 fusion.2
  100.5 11.2 %all_to_all.25 = f32[16,1,2048]{2,1,0:T(1,128)S(1)} all-to-all(f32[16,1,2048]{2,1,0:T(1,128)S(1)} %broadcast_in_dim.12), channel_id=1, replica_groups=mesh['rx'=4,'rc'=2,'cy'=4,'cz'=4] {'cy','cz'}, dimensions={0} | all-to-all | bytes 262144 | tf_op jit(solution)/shard_map/all_to_all | solution.py:26
  111.8 3.2 %fusion.3 = f32[1024]{0:T(1024)S(1)} fusion(bf16[2048,1024]{0,1:T(8,128)(2,1)} %get-tuple-element.22, f32[2048]{0:T(1024)S(1)} %div.68), kind=kLoop, calls=%fused_computation.10 | loop fusion | flops 6290432 | bytes 4206592 | tf_op jit(solution)/shard_map/reduce_sum | solution.py:79
  115.1 1.2 collective-permute-done.4
  116.6 1.4 collective-permute-start.6
  118.0 1.2 collective-permute-start.5
  119.2 0.7 collective-permute-done.7
  119.9 1.8 collective-permute-done.6
  121.7 1.1 collective-permute-done.5
  122.9 0.9 fusion.4
  123.8 11.2 %all_to_all.26 = f32[16,1,2048]{2,1,0:T(1,128)S(1)} all-to-all(f32[16,1,2048]{2,1,0:T(1,128)S(1)} %broadcast_in_dim.13), channel_id=1, replica_groups=mesh['rx'=4,'rc'=2,'cy'=4,'cz'=4] {'cy','cz'}, dimensions={0} | all-to-all | bytes 262144 | tf_op jit(solution)/shard_map/all_to_all | solution.py:26
  135.2 3.2 %fusion.5 = f32[1024]{0:T(1024)S(1)} fusion(bf16[2048,1024]{0,1:T(8,128)(2,1)} %get-tuple-element.22, f32[2048]{0:T(1024)S(1)} %div.70), kind=kLoop, calls=%fused_computation.12 | loop fusion | flops 6290432 | bytes 4206592 | tf_op jit(solution)/shard_map/reduce_sum | solution.py:79
  138.7 1.2 collective-permute-done.8
  139.8 1.8 collective-permute-start.11
  141.6 0.9 collective-permute-start.10
  142.5 0.9 collective-permute-done.11
  143.4 3.3 %collective-permute-done.10 = f32[1024]{0:T(1024)S(1)} collective-permute-done((f32[1024]{0:T(1024)S(1)}, f32[1024]{0:T(1024)S(1)}, u32[]{:S(2)}, u32[]{:S(2)}) %collective-permute-start.10) | collective-permute-done | bytes 4128 | tf_op jit(solution)/shard_map/ppermute | solution.py:20
  146.7 0.6 collective-permute-done.9
  147.3 0.6 multiply_log_fusion
  147.9 3.1 %fusion.6 = f32[2048]{0:T(1024)S(1)} fusion(bf16[2048,1024]{0,1:T(8,128)(2,1)} %get-tuple-element.22, f32[1024]{0:T(1024)S(1)} %get-tuple-element.4), kind=kLoop, calls=%fused_computation.13 | loop fusion | flops 6289408 | bytes 4206592 | tf_op jit(solution)/shard_map/reduce_sum | solution.py:50
  151.0 0.7 broadcast_in_dim.14
  151.7 3.6 %all-to-all-start.3 = ((f32[16,1,2048]{2,1,0:T(1,128)}), f32[16,1,2048]{2,1,0:T(1,128)S(1)}, u32[]{:S(2)}, u32[]{:S(2)}) async-start(f32[16,1,2048]{2,1,0:T(1,128)} %broadcast_in_dim.14), calls=%async_computation.3 | async-start | bytes 262144 | tf_op jit(solution)/shard_map/all_to_all | solution.py:26
  155.4 7.8 %all-to-all-done.3 = f32[16,1,2048]{2,1,0:T(1,128)S(1)} async-done(((f32[16,1,2048]{2,1,0:T(1,128)}), f32[16,1,2048]{2,1,0:T(1,128)S(1)}, u32[]{:S(2)}, u32[]{:S(2)}) %all-to-all-start.3) | async-done | bytes 131104 | tf_op jit(solution)/shard_map/all_to_all | solution.py:26
  163.3 0.6 fusion.22
  163.9 4.7 %fusion.16 = f32[768,512]{0,1:T(8,128)} fusion(bf16[2048,768]{0,1:T(8,128)(2,1)S(1)} %copy-done.3, bf16[2048,1024]{0,1:T(8,128)(2,1)} %get-tuple-element.22, f32[512]{0:T(512)S(1)} %get-tuple-element.19, f32[2048]{0:T(1024)S(1)} %get-tuple-element.6), kind=kOutput, calls=%fused_computation.28 | convolution fusion | flops 1614807040 | bytes 6825984 | tf_op jit(solution)/shard_map/dot_general | solution.py:95
  168.6 1.9 copy.14
  170.5 5.6 %fusion.15 = f32[768,512]{0,1:T(8,128)} fusion(bf16[2048,768]{0,1:T(8,128)(2,1)} %all-gather.2.cloned.1.call-done, bf16[2048,1024]{0,1:T(8,128)(2,1)} %get-tuple-element.22, f32[512]{0:T(512)S(1)} %get-tuple-element.20, f32[2048]{0:T(1024)S(1)} %get-tuple-element.6), kind=kOutput, calls=%fused_computation.27 | convolution fusion | flops 1614807040 | bytes 6825984 | tf_op jit(solution)/shard_map/dot_general | solution.py:95
  176.1 1.9 copy.15
  178.0 0.9 dynamic-slice_bitcast_fusion
  178.9 0.9 dynamic-slice_bitcast_fusion.1
  180.3 2.1 collective-permute-done.12
  182.5 1.1 collective-permute-done.20
  183.6 2.6 %bitcast_add_fusion = (f32[4,96,512]{2,1,0:T(8,128)S(1)}, f32[4,96,512]{2,1,0:T(8,128)}) fusion(f32[4,96,512]{2,1,0:T(8,128)} %collective-permute-done.20, f32[4,2,96,512]{3,2,1,0:T(8,128)S(1)} %bitcast.49, s32[]{:T(128)S(6)} %select_n.53, f32[4,96,512]{2,1,0:T(8,128)} %collective-permute-done.12, f32[4,2,96,512]{3,2,1,0:T(8,128)S(1)} %bitcast.47), kind=kLoop, calls=%fused_computation.29 | loop fusion | flops 393216 | bytes 4718596 | tf_op jit(solution)/shard_map/add | solution.py:41
  186.2 0.9 copy-done.2
  187.2 3.2 %collective-permute-start.23 = (f32[96,512]{1,0:T(8,128)S(1)}, f32[96,512]{1,0:T(8,128)S(1)}, u32[]{:S(2)}, u32[]{:S(2)}) collective-permute-start(f32[96,512]{1,0:T(8,128)S(1)} %get-tuple-element.15), channel_id=1, source_target_pairs={{0,96},{32,0},{64,32},{96,64},{1,97},{33,1},{65,33},{97,65},{2,98}... | collective-permute-start | bytes 589832 | tf_op jit(solution)/shard_map/ppermute | solution.py:45
  190.6 1.2 dynamic-slice_bitcast_fusion.7
  191.8 0.7 collective-permute-start.13
  192.5 2.6 %collective-permute-start.15 = (f32[96,512]{1,0:T(8,128)S(1)}, f32[96,512]{1,0:T(8,128)S(1)}, u32[]{:S(2)}, u32[]{:S(2)}) collective-permute-start(f32[96,512]{1,0:T(8,128)S(1)} %get-tuple-element.12), channel_id=1, source_target_pairs={{0,96},{32,0},{64,32},{96,64},{1,97},{33,1},{65,33},{97,65},{2,98}... | collective-permute-start | bytes 589832 | tf_op jit(solution)/shard_map/ppermute | solution.py:45
  195.1 5.3 %collective-permute-done.21 = f32[96,512]{1,0:T(8,128)S(1)} collective-permute-done((f32[96,512]{1,0:T(8,128)S(1)}, f32[96,512]{1,0:T(8,128)S(1)}, u32[]{:S(2)}, u32[]{:S(2)}) %collective-permute-start.21) | collective-permute-done | bytes 196640 | tf_op jit(solution)/shard_map/ppermute | solution.py:45
  200.4 1.0 multiply_reduce_fusion.2
  201.5 6.5 %collective-permute-done.13 = f32[96,512]{1,0:T(8,128)S(1)} collective-permute-done((f32[96,512]{1,0:T(8,128)S(1)}, f32[96,512]{1,0:T(8,128)S(1)}, u32[]{:S(2)}, u32[]{:S(2)}) %collective-permute-start.13) | collective-permute-done | bytes 196640 | tf_op jit(solution)/shard_map/ppermute | solution.py:45
  208.0 1.0 multiply_reduce_fusion.3
  209.1 3.0 %collective-permute-start.27 = (f32[512]{0:T(512)S(1)}, f32[512]{0:T(512)S(1)}, u32[]{:S(2)}, u32[]{:S(2)}) collective-permute-start(f32[512]{0:T(512)S(1)} %add.212), channel_id=1, source_target_pairs={{0,96},{32,0},{64,32},{96,64},{1,97},{33,1},{65,33},{97,65},{2,98}... | collective-permute-start | bytes 6152 | tf_op jit(solution)/shard_map/ppermute | solution.py:20
  212.2 0.9 collective-permute-start.25
  213.1 2.3 collective-permute-start.19
  215.4 2.3 %collective-permute-start.18 = (f32[512]{0:T(512)S(1)}, f32[512]{0:T(512)S(1)}, u32[]{:S(2)}, u32[]{:S(2)}) collective-permute-start(f32[512]{0:T(512)S(1)} %add.203), channel_id=1, source_target_pairs={{0,64},{32,96},{64,0},{96,32},{1,65},{33,97},{65,1},{97,33},{2,66}... | collective-permute-start | bytes 6152 | tf_op jit(solution)/shard_map/ppermute | solution.py:20
  217.8 2.7 %collective-permute-done.18 = f32[512]{0:T(512)S(1)} collective-permute-done((f32[512]{0:T(512)S(1)}, f32[512]{0:T(512)S(1)}, u32[]{:S(2)}, u32[]{:S(2)}) %collective-permute-start.18) | collective-permute-done | bytes 2080 | tf_op jit(solution)/shard_map/ppermute | solution.py:20
  220.5 2.0 collective-permute-done.17
  222.5 0.8 pad_maximum_fusion
  (63 shorter events, 3.6 us)
Async XLA Ops:
  7.2 56.1 %copy-start.4 = (bf16[1024,768]{1,0:T(8,128)(2,1)S(1)}, bf16[1024,768]{1,0:T(8,128)(2,1)}, u32[]{:S(2)}) copy-start(bf16[1024,768]{1,0:T(8,128)(2,1)} %param.4) | copy-start | bytes 4718596
  7.2 53.5 %all-gather.2.cloned.1.call-start = ((), (), s32[]{:S(2)}) async-start(), calls=%async_computation.4 | async-start | bytes 3342336 | tf_op jit(solution)/shard_map/all_gather | solution.py:56
  63.2 20.0 %copy-start.5 = (f32[2048]{0:T(1024)S(1)}, f32[2048]{0:T(1024)}, u32[]{:S(2)}) copy-start(f32[2048]{0:T(1024)} %param.5) | copy-start | bytes 24580
  83.3 16.2 %copy-start = (bf16[2048,1024]{0,1:T(8,128)(2,1)S(1)}, bf16[2048,1024]{0,1:T(8,128)(2,1)}, u32[]{:S(2)}) copy-start(bf16[2048,1024]{0,1:T(8,128)(2,1)} %get-tuple-element.22) | copy-start | bytes 12582916
  87.9 1.3 collective-permute-start
  89.8 4.5 %collective-permute-start.3 = (f32[1025]{0:T(1024)S(1)}, f32[1025]{0:T(1024)S(1)}, u32[]{:S(2)}, u32[]{:S(2)}) collective-permute-start(f32[1025]{0:T(1024)S(1)} %fusion.21), channel_id=1, source_target_pairs={{0,96},{32,0},{64,32},{96,64},{1,97},{33,1},{65,33},{97,65},{2,98}... | collective-permute-start | bytes 12308 | tf_op jit(solution)/shard_map/ppermute | solution.py:20
  92.6 5.2 %collective-permute-start.2 = (f32[1025]{0:T(1024)S(1)}, f32[1025]{0:T(1024)S(1)}, u32[]{:S(2)}, u32[]{:S(2)}) collective-permute-start(f32[1025]{0:T(1024)S(1)} %fusion.21), channel_id=1, source_target_pairs={{0,64},{32,96},{64,0},{96,32},{1,65},{33,97},{65,1},{97,33},{2,66}... | collective-permute-start | bytes 12308 | tf_op jit(solution)/shard_map/ppermute | solution.py:20
  93.4 4.9 %collective-permute-start.1 = (f32[1025]{0:T(1024)S(1)}, f32[1025]{0:T(1024)S(1)}, u32[]{:S(2)}, u32[]{:S(2)}) collective-permute-start(f32[1025]{0:T(1024)S(1)} %fusion.21), channel_id=1, source_target_pairs={{0,32},{32,64},{64,96},{96,0},{1,33},{33,65},{65,97},{97,1},{2,34}... | collective-permute-start | bytes 12308 | tf_op jit(solution)/shard_map/ppermute | solution.py:20
  111.8 11.0 %copy-start.1 = (bf16[2048,1024]{0,1:T(8,128)(2,1)S(1)}, bf16[2048,1024]{0,1:T(8,128)(2,1)}, u32[]{:S(2)}) copy-start(bf16[2048,1024]{0,1:T(8,128)(2,1)} %get-tuple-element.22) | copy-start | bytes 12582916
  115.0 1.2 collective-permute-start.4
  116.3 3.6 %collective-permute-start.7 = (f32[1024]{0:T(1024)S(1)}, f32[1024]{0:T(1024)S(1)}, u32[]{:S(2)}, u32[]{:S(2)}) collective-permute-start(f32[1024]{0:T(1024)S(1)} %add.177), channel_id=1, source_target_pairs={{0,96},{32,0},{64,32},{96,64},{1,97},{33,1},{65,33},{97,65},{2,98}... | collective-permute-start | bytes 12296 | tf_op jit(solution)/shard_map/ppermute | solution.py:20
  116.6 5.1 %collective-permute-start.6 = (f32[1024]{0:T(1024)S(1)}, f32[1024]{0:T(1024)S(1)}, u32[]{:S(2)}, u32[]{:S(2)}) collective-permute-start(f32[1024]{0:T(1024)S(1)} %add.177), channel_id=1, source_target_pairs={{0,64},{32,96},{64,0},{96,32},{1,65},{33,97},{65,1},{97,33},{2,66}... | collective-permute-start | bytes 12296 | tf_op jit(solution)/shard_map/ppermute | solution.py:20
  118.0 4.8 %collective-permute-start.5 = (f32[1024]{0:T(1024)S(1)}, f32[1024]{0:T(1024)S(1)}, u32[]{:S(2)}, u32[]{:S(2)}) collective-permute-start(f32[1024]{0:T(1024)S(1)} %add.177), channel_id=1, source_target_pairs={{0,32},{32,64},{64,96},{96,0},{1,33},{33,65},{65,97},{97,1},{2,34}... | collective-permute-start | bytes 12296 | tf_op jit(solution)/shard_map/ppermute | solution.py:20
  135.2 28.7 %copy-start.3 = (bf16[2048,768]{0,1:T(8,128)(2,1)S(1)}, bf16[2048,768]{0,1:T(8,128)(2,1)}, u32[]{:S(2)}) copy-start(bf16[2048,768]{0,1:T(8,128)(2,1)} %all-gather.2.cloned.1.call-done) | copy-start | bytes 9437188
  138.4 1.4 collective-permute-start.8
  139.8 3.6 %collective-permute-start.11 = (f32[1024]{0:T(1024)S(1)}, f32[1024]{0:T(1024)S(1)}, u32[]{:S(2)}, u32[]{:S(2)}) collective-permute-start(f32[1024]{0:T(1024)S(1)} %add.181), channel_id=1, source_target_pairs={{0,96},{32,0},{64,32},{96,64},{1,97},{33,1},{65,33},{97,65},{2,98}... | collective-permute-start | bytes 12296 | tf_op jit(solution)/shard_map/ppermute | solution.py:20
  141.6 5.1 %collective-permute-start.10 = (f32[1024]{0:T(1024)S(1)}, f32[1024]{0:T(1024)S(1)}, u32[]{:S(2)}, u32[]{:S(2)}) collective-permute-start(f32[1024]{0:T(1024)S(1)} %add.181), channel_id=1, source_target_pairs={{0,64},{32,96},{64,0},{96,32},{1,65},{33,97},{65,1},{97,33},{2,66}... | collective-permute-start | bytes 12296 | tf_op jit(solution)/shard_map/ppermute | solution.py:20
  142.5 4.8 %collective-permute-start.9 = (f32[1024]{0:T(1024)S(1)}, f32[1024]{0:T(1024)S(1)}, u32[]{:S(2)}, u32[]{:S(2)}) collective-permute-start(f32[1024]{0:T(1024)S(1)} %add.181), channel_id=1, source_target_pairs={{0,32},{32,64},{64,96},{96,0},{1,33},{33,65},{65,97},{97,1},{2,34}... | collective-permute-start | bytes 12296 | tf_op jit(solution)/shard_map/ppermute | solution.py:20
  151.7 11.4 %all-to-all-start.3 = ((f32[16,1,2048]{2,1,0:T(1,128)}), f32[16,1,2048]{2,1,0:T(1,128)S(1)}, u32[]{:S(2)}, u32[]{:S(2)}) async-start(f32[16,1,2048]{2,1,0:T(1,128)} %broadcast_in_dim.14), calls=%async_computation.3 | async-start | bytes 262144 | tf_op jit(solution)/shard_map/all_to_all | solution.py:26
  179.8 2.6 %collective-permute-start.12 = (f32[4,96,512]{2,1,0:T(8,128)}, f32[4,96,512]{2,1,0:T(8,128)}, u32[]{:S(2)}, u32[]{:S(2)}) collective-permute-start(f32[4,96,512]{2,1,0:T(8,128)} %dynamic-slice_bitcast_fusion.1), channel_id=1, source_target_pairs={{0,16},{16,0},{1,17},{17,1},{2,18},{18,2},{3,19},{19,3},{4,20},{20... | collective-permute-start | bytes 2359304 | tf_op jit(solution)/shard_map/ppermute | solution.py:41
  179.8 3.7 %collective-permute-start.20 = (f32[4,96,512]{2,1,0:T(8,128)}, f32[4,96,512]{2,1,0:T(8,128)}, u32[]{:S(2)}, u32[]{:S(2)}) collective-permute-start(f32[4,96,512]{2,1,0:T(8,128)} %dynamic-slice_bitcast_fusion), channel_id=1, source_target_pairs={{0,16},{16,0},{1,17},{17,1},{2,18},{18,2},{3,19},{19,3},{4,20},{20... | collective-permute-start | bytes 2359304 | tf_op jit(solution)/shard_map/ppermute | solution.py:41
  186.2 0.9 copy-start.2
  187.1 13.3 %collective-permute-start.21 = (f32[96,512]{1,0:T(8,128)S(1)}, f32[96,512]{1,0:T(8,128)S(1)}, u32[]{:S(2)}, u32[]{:S(2)}) collective-permute-start(f32[96,512]{1,0:T(8,128)S(1)} %get-tuple-element.14), channel_id=1, source_target_pairs={{0,32},{32,64},{64,96},{96,0},{1,33},{33,65},{65,97},{97,1},{2,34}... | collective-permute-start | bytes 589832 | tf_op jit(solution)/shard_map/ppermute | solution.py:45
  187.2 13.2 %collective-permute-start.23 = (f32[96,512]{1,0:T(8,128)S(1)}, f32[96,512]{1,0:T(8,128)S(1)}, u32[]{:S(2)}, u32[]{:S(2)}) collective-permute-start(f32[96,512]{1,0:T(8,128)S(1)} %get-tuple-element.15), channel_id=1, source_target_pairs={{0,96},{32,0},{64,32},{96,64},{1,97},{33,1},{65,33},{97,65},{2,98}... | collective-permute-start | bytes 589832 | tf_op jit(solution)/shard_map/ppermute | solution.py:45
  190.4 10.0 %collective-permute-start.22 = (f32[96,512]{1,0:T(8,128)S(1)}, f32[96,512]{1,0:T(8,128)S(1)}, u32[]{:S(2)}, u32[]{:S(2)}) collective-permute-start(f32[96,512]{1,0:T(8,128)S(1)} %get-tuple-element.16), channel_id=1, source_target_pairs={{0,64},{32,96},{64,0},{96,32},{1,65},{33,97},{65,1},{97,33},{2,66}... | collective-permute-start | bytes 589832 | tf_op jit(solution)/shard_map/ppermute | solution.py:45
  191.8 16.2 %collective-permute-start.13 = (f32[96,512]{1,0:T(8,128)S(1)}, f32[96,512]{1,0:T(8,128)S(1)}, u32[]{:S(2)}, u32[]{:S(2)}) collective-permute-start(f32[96,512]{1,0:T(8,128)S(1)} %get-tuple-element.11), channel_id=1, source_target_pairs={{0,32},{32,64},{64,96},{96,0},{1,33},{33,65},{65,97},{97,1},{2,34}... | collective-permute-start | bytes 589832 | tf_op jit(solution)/shard_map/ppermute | solution.py:45
  192.5 15.5 %collective-permute-start.15 = (f32[96,512]{1,0:T(8,128)S(1)}, f32[96,512]{1,0:T(8,128)S(1)}, u32[]{:S(2)}, u32[]{:S(2)}) collective-permute-start(f32[96,512]{1,0:T(8,128)S(1)} %get-tuple-element.12), channel_id=1, source_target_pairs={{0,96},{32,0},{64,32},{96,64},{1,97},{33,1},{65,33},{97,65},{2,98}... | collective-permute-start | bytes 589832 | tf_op jit(solution)/shard_map/ppermute | solution.py:45
  200.4 7.6 %collective-permute-start.14 = (f32[96,512]{1,0:T(8,128)S(1)}, f32[96,512]{1,0:T(8,128)S(1)}, u32[]{:S(2)}, u32[]{:S(2)}) collective-permute-start(f32[96,512]{1,0:T(8,128)S(1)} %get-tuple-element.13), channel_id=1, source_target_pairs={{0,64},{32,96},{64,0},{96,32},{1,65},{33,97},{65,1},{97,33},{2,66}... | collective-permute-start | bytes 589832 | tf_op jit(solution)/shard_map/ppermute | solution.py:45
  201.4 7.7 %collective-permute-start.24 = (f32[512]{0:T(512)S(1)}, f32[512]{0:T(512)S(1)}, u32[]{:S(2)}, u32[]{:S(2)}) collective-permute-start(f32[512]{0:T(512)S(1)} %get-tuple-element.9), channel_id=1, source_target_pairs={{0,16},{16,0},{1,17},{17,1},{2,18},{18,2},{3,19},{19,3},{4,20},{20... | collective-permute-start | bytes 6152 | tf_op jit(solution)/shard_map/ppermute | solution.py:20
  209.0 4.1 %collective-permute-start.16 = (f32[512]{0:T(512)S(1)}, f32[512]{0:T(512)S(1)}, u32[]{:S(2)}, u32[]{:S(2)}) collective-permute-start(f32[512]{0:T(512)S(1)} %get-tuple-element.7), channel_id=1, source_target_pairs={{0,16},{16,0},{1,17},{17,1},{2,18},{18,2},{3,19},{19,3},{4,20},{20... | collective-permute-start | bytes 6152 | tf_op jit(solution)/shard_map/ppermute | solution.py:20
  209.1 8.6 %collective-permute-start.27 = (f32[512]{0:T(512)S(1)}, f32[512]{0:T(512)S(1)}, u32[]{:S(2)}, u32[]{:S(2)}) collective-permute-start(f32[512]{0:T(512)S(1)} %add.212), channel_id=1, source_target_pairs={{0,96},{32,0},{64,32},{96,64},{1,97},{33,1},{65,33},{97,65},{2,98}... | collective-permute-start | bytes 6152 | tf_op jit(solution)/shard_map/ppermute | solution.py:20
  212.1 5.6 %collective-permute-start.26 = (f32[512]{0:T(512)S(1)}, f32[512]{0:T(512)S(1)}, u32[]{:S(2)}, u32[]{:S(2)}) collective-permute-start(f32[512]{0:T(512)S(1)} %add.212), channel_id=1, source_target_pairs={{0,64},{32,96},{64,0},{96,32},{1,65},{33,97},{65,1},{97,33},{2,66}... | collective-permute-start | bytes 6152 | tf_op jit(solution)/shard_map/ppermute | solution.py:20
  212.2 5.6 %collective-permute-start.25 = (f32[512]{0:T(512)S(1)}, f32[512]{0:T(512)S(1)}, u32[]{:S(2)}, u32[]{:S(2)}) collective-permute-start(f32[512]{0:T(512)S(1)} %add.212), channel_id=1, source_target_pairs={{0,32},{32,64},{64,96},{96,0},{1,33},{33,65},{65,97},{97,1},{2,34}... | collective-permute-start | bytes 6152 | tf_op jit(solution)/shard_map/ppermute | solution.py:20
  213.1 4.7 %collective-permute-start.19 = (f32[512]{0:T(512)S(1)}, f32[512]{0:T(512)S(1)}, u32[]{:S(2)}, u32[]{:S(2)}) collective-permute-start(f32[512]{0:T(512)S(1)} %add.203), channel_id=1, source_target_pairs={{0,96},{32,0},{64,32},{96,64},{1,97},{33,1},{65,33},{97,65},{2,98}... | collective-permute-start | bytes 6152 | tf_op jit(solution)/shard_map/ppermute | solution.py:20
  215.4 5.1 %collective-permute-start.18 = (f32[512]{0:T(512)S(1)}, f32[512]{0:T(512)S(1)}, u32[]{:S(2)}, u32[]{:S(2)}) collective-permute-start(f32[512]{0:T(512)S(1)} %add.203), channel_id=1, source_target_pairs={{0,64},{32,96},{64,0},{96,32},{1,65},{33,97},{65,1},{97,33},{2,66}... | collective-permute-start | bytes 6152 | tf_op jit(solution)/shard_map/ppermute | solution.py:20
  217.7 4.8 %collective-permute-start.17 = (f32[512]{0:T(512)S(1)}, f32[512]{0:T(512)S(1)}, u32[]{:S(2)}, u32[]{:S(2)}) collective-permute-start(f32[512]{0:T(512)S(1)} %add.203), channel_id=1, source_target_pairs={{0,32},{32,64},{64,96},{96,0},{1,33},{33,65},{65,97},{97,1},{2,34}... | collective-permute-start | bytes 6152 | tf_op jit(solution)/shard_map/ppermute | solution.py:20
Sparse Core Ops, SparseCore 0:
  10.2 50.4 all-gather.1

commit v6 on v4

--- a/solution.py
+++ b/solution.py
@@ -28,7 +28,9 @@
 
 
 def reduce_row(x):
-    return shifted_sum(shifted_sum(x, "rc"), "rx")
+    n = lax.axis_size(ROW)
+    copies = lax.all_to_all(jnp.broadcast_to(x, (n, *x.shape)), ROW, 0, 0, tiled=False)
+    return jnp.sum(copies, axis=0)
 
 
 def scatter_row(x):
@@ -39,11 +41,7 @@
     for k in range(1, cores):
         piece = lax.dynamic_index_in_dim(blocks, (rc + k) % cores, 1, keepdims=False)
         half = half + lax.ppermute(piece, "rc", [(i, (i + k) % cores) for i in range(cores)])
-    total = lax.dynamic_index_in_dim(half, rx, 0, keepdims=False)
-    for k in range(1, chips):
-        piece = lax.dynamic_index_in_dim(half, (rx + k) % chips, 0, keepdims=False)
-        total = total + lax.ppermute(piece, "rx", [(i, (i + k) % chips) for i in range(chips)])
-    return total
+    return jnp.sum(lax.all_to_all(half, "rx", 0, 0, tiled=False), axis=0)
 
 
 def row_step(kernel, col_scale, weights):

time: 215 us -> 220 us (1.023)
  blocking collectives: 34.4 us -> 91.1 us
  waiting for transfers between devices: 99 us -> 62.7 us
  starting transfers between devices: 24.7 us -> 3.84 us
  other arithmetic: 23.9 us -> 28.6 us
    all_to_all x0 -> x5, blocking collectives: none -> 56.7 us  [the longest x4 33 us: reduce_row(): lax.all_to_all(jnp.broadcast_to(x, (n, *x.shape)), ROW, 0, 0, tiled=False)]
    ppermute x19 -> x0, waiting for transfers between devices: 36.2 us -> none  [the longest x3 18.3 us: scatter_row(): lax.ppermute(piece, 'rx', [(i, (i + k) % chips) for i in range(chips)])]
    ppermute x19 -> x0, starting transfers between devices: 21 us -> none  [the longest x16 17.7 us: shifted_sum(): total = total + lax.ppermute(x, axis, [(i, (i + k) % n) for i in range(n)])]
    reduce_sum x3, other arithmetic: 2.66 us -> 9.22 us  [row_step(): jnp.sum(kernel.astype(jnp.float32) * col_scale[None, :], axis=1)]
  transfers between devices with their start and end apart: 22 -> 3, of which waited for: 19 -> 3; matrix products, arithmetic and copies ran while one was open for 1% -> 1% of each run, Pallas kernels for 0% -> 0%
where the time goes in v6:
time: 220 us; the launch traced here: 218 us
  blocking collectives  91.1 us (41%)
  waiting for transfers between devices  62.7 us (28%)
  other arithmetic  28.6 us (13%)
  between operations  14.9 us (7%)
  matrix products  13.6 us (6%)
  starting transfers between devices  3.84 us (2%)
  local copies, waits for them, and re-layouts  3.36 us (2%)
    all_gather x1, waiting for transfers between devices, per_device(): full_rows = lax.all_gather(vectors, CENT, axis=1, tiled=True)  51 us
    all_to_all x3, blocking collectives, reduce_cent(): lax.all_to_all(jnp.broadcast_to(x, (n, *x.shape)), CENT, 0, 0, tiled=False)  34.4 us
    all_to_all x4, blocking collectives, reduce_row(): lax.all_to_all(jnp.broadcast_to(x, (n, *x.shape)), ROW, 0, 0, tiled=False)  33 us
    all_to_all x1, blocking collectives, scatter_row(): return jnp.sum(lax.all_to_all(half, 'rx', 0, 0, tiled=False), axis=0)  23.7 us
    reduce_sum x3, other arithmetic, per_device(): jnp.sum(kernel.astype(jnp.float32) * row_scale[:, None], axis=0)  9.37 us
    reduce_sum x3, other arithmetic, row_step(): jnp.sum(kernel.astype(jnp.float32) * col_scale[None, :], axis=1)  9.22 us
    dot_general x1, matrix products, per_device(): jnp.dot(full_rows, centroids.T, preferred_element_type=jnp.float32)  7.88 us
    all_to_all x1, waiting for transfers between devices, reduce_cent(): lax.all_to_all(jnp.broadcast_to(x, (n, *x.shape)), CENT, 0, 0, tiled=False)  7.71 us
  transfers between devices with their start and end apart: 3, of which 3 were waited for; matrix products, arithmetic and copies ran while one was open for 1% of the time, Pallas kernels for 0%

profile of v6, /device:TPU:0, one launch (start us, length us, event | category | flops | bytes accessed | tf_op | source)
XLA Modules:
  0.0 218.1 jit_solution(16297788457096156357)
XLA Ops:
  7.2 0.0 copy-start.2
  7.2 0.0 all-gather.2.cloned.1.call-start
  7.2 0.7 all-gather.2.cloned.1.call-update
  7.9 1.8 multiply_reduce_fusion.1
  9.7 51.0 %all-gather.2.cloned.1.call-done = bf16[2048,768]{0,1:T(8,128)(2,1)} async-done(((bf16[2048,48]{0,1:T(8,128)(2,1)}), bf16[2048,768]{0,1:T(8,128)(2,1)}) %all-gather.2.cloned.1.call-update) | async-done | bytes 3145744 | tf_op jit(solution)/shard_map/all_gather | solution.py:54
  60.7 2.6 %multiply_reduce_fusion = f32[2048]{0:T(1024)S(1)} fusion(bf16[2048,768]{0,1:T(8,128)(2,1)} %all-gather.2.cloned.1.call-done), kind=kLoop, calls=%fused_computation.18 | loop fusion | flops 4716544 | bytes 3153920 | tf_op jit(solution)/shard_map/reduce_sum | solution.py:60
  63.2 0.0 copy-done.2
  63.2 0.0 copy-start.3
  63.2 7.9 %fusion = (f32[2048]{0:T(1024)S(1)}, bf16[2048,1024]{0,1:T(8,128)(2,1)}) fusion(f32[1024]{0:T(1024)S(1)} %add_rsqrt_fusion.2, f32[2048]{0:T(1024)S(1)} %add_rsqrt_fusion, bf16[1024,768]{1,0:T(8,128)(2,1)S(1)} %copy-done.2, bf16[2048,768]{0,1:T(8,128)(2,1)} %all-gather.2.cloned.1.call-done), kind=kOutput, calls=%fused_computation.8 | convolution fusion | flops 3235903488 | bytes 8933376 | tf_op jit(solution)/shard_map/dot_general | solution.py:65
  71.1 0.1 broadcast_in_dim.18
  71.2 12.0 %all_to_all.53 = f32[16,1,2048]{2,1,0:T(1,128)S(1)} all-to-all(f32[16,1,2048]{2,1,0:T(1,128)S(1)} %broadcast_in_dim.18), channel_id=1, replica_groups=mesh['rx'=4,'rc'=2,'cy'=4,'cz'=4] {'cy','cz'}, dimensions={0} | all-to-all | bytes 262144 | tf_op jit(solution)/shard_map/all_to_all | solution.py:26
  83.2 0.1 reduce_sum.183
  83.2 0.0 copy-done.3
  83.3 0.6 fusion.14
  83.9 3.1 %fusion.1 = f32[1024]{0:T(1024)S(1)} fusion(bf16[2048,1024]{0,1:T(8,128)(2,1)} %get-tuple-element.10, f32[2048]{0:T(1024)S(1)} %get-tuple-element.7), kind=kLoop, calls=%fused_computation.9 | loop fusion | flops 6290432 | bytes 4206592 | tf_op jit(solution)/shard_map/reduce_sum | solution.py:77
  86.9 0.7 pad_maximum_fusion
  87.6 9.5 %all_to_all.54 = f32[8,1,1025]{2,1,0:T(1,128)S(1)} all-to-all(f32[8,1,1025]{2,1,0:T(1,128)S(1)} %broadcast_in_dim.40), channel_id=1, replica_groups=mesh['rx'=4,'rc'=2,'cy'=4,'cz'=4] {'rx','rc'}, dimensions={0} | all-to-all | bytes 65600 | tf_op jit(solution)/shard_map/all_to_all | solution.py:32
  97.2 0.5 slice.8
  98.4 3.1 %fusion.2 = f32[2048]{0:T(1024)S(1)} fusion(bf16[2048,1024]{0,1:T(8,128)(2,1)} %get-tuple-element.10, f32[1024]{0:T(1024)S(1)} %slice_divide_fusion), kind=kLoop, calls=%fused_computation.10 | loop fusion | flops 6289408 | bytes 4206592 | tf_op jit(solution)/shard_map/reduce_sum | solution.py:48
  101.4 0.1 broadcast_in_dim.41
  101.5 11.2 %all_to_all.55 = f32[16,1,2048]{2,1,0:T(1,128)S(1)} all-to-all(f32[16,1,2048]{2,1,0:T(1,128)S(1)} %broadcast_in_dim.41), channel_id=1, replica_groups=mesh['rx'=4,'rc'=2,'cy'=4,'cz'=4] {'cy','cz'}, dimensions={0} | all-to-all | bytes 262144 | tf_op jit(solution)/shard_map/all_to_all | solution.py:26
  112.8 0.1 reduce_sum.188
  112.9 3.1 %fusion.3 = f32[1024]{0:T(1024)S(1)} fusion(bf16[2048,1024]{0,1:T(8,128)(2,1)} %get-tuple-element.10, f32[2048]{0:T(1024)S(1)} %div.69), kind=kLoop, calls=%fused_computation.11 | loop fusion | flops 6290432 | bytes 4206592 | tf_op jit(solution)/shard_map/reduce_sum | solution.py:77
  116.0 7.8 %all_to_all.56 = f32[8,1,1024]{2,1,0:T(1,128)S(1)} all-to-all(f32[8,1,1024]{2,1,0:T(1,128)S(1)} %broadcast_in_dim.42), channel_id=1, replica_groups=mesh['rx'=4,'rc'=2,'cy'=4,'cz'=4] {'rx','rc'}, dimensions={0} | all-to-all | bytes 65536 | tf_op jit(solution)/shard_map/all_to_all | solution.py:32
  123.8 3.1 %fusion.4 = f32[2048]{0:T(1024)S(1)} fusion(bf16[2048,1024]{0,1:T(8,128)(2,1)} %get-tuple-element.10, f32[1024]{0:T(1024)S(1)} %broadcast_divide_fusion.1), kind=kLoop, calls=%fused_computation.12 | loop fusion | flops 6289408 | bytes 4206592 | tf_op jit(solution)/shard_map/reduce_sum | solution.py:48
  126.9 0.1 broadcast_in_dim.43
  127.0 11.2 %all_to_all.57 = f32[16,1,2048]{2,1,0:T(1,128)S(1)} all-to-all(f32[16,1,2048]{2,1,0:T(1,128)S(1)} %broadcast_in_dim.43), channel_id=1, replica_groups=mesh['rx'=4,'rc'=2,'cy'=4,'cz'=4] {'cy','cz'}, dimensions={0} | all-to-all | bytes 262144 | tf_op jit(solution)/shard_map/all_to_all | solution.py:26
  138.2 0.1 reduce_sum.192
  138.3 0.0 copy-start
  138.3 3.2 %fusion.5 = f32[1024]{0:T(1024)S(1)} fusion(bf16[2048,1024]{0,1:T(8,128)(2,1)} %get-tuple-element.10, f32[2048]{0:T(1024)S(1)} %div.71), kind=kLoop, calls=%fused_computation.13 | loop fusion | flops 6290432 | bytes 4206592 | tf_op jit(solution)/shard_map/reduce_sum | solution.py:77
  141.6 7.8 %all_to_all.58 = f32[8,1,1024]{2,1,0:T(1,128)S(1)} all-to-all(f32[8,1,1024]{2,1,0:T(1,128)S(1)} %broadcast_in_dim.44), channel_id=1, replica_groups=mesh['rx'=4,'rc'=2,'cy'=4,'cz'=4] {'rx','rc'}, dimensions={0} | all-to-all | bytes 65536 | tf_op jit(solution)/shard_map/all_to_all | solution.py:32
  149.4 0.6 multiply_log_fusion
  150.1 3.1 %fusion.6 = f32[2048]{0:T(1024)S(1)} fusion(bf16[2048,1024]{0,1:T(8,128)(2,1)} %get-tuple-element.10, f32[1024]{0:T(1024)S(1)} %get-tuple-element.4), kind=kLoop, calls=%fused_computation.14 | loop fusion | flops 6289408 | bytes 4206592 | tf_op jit(solution)/shard_map/reduce_sum | solution.py:48
  153.1 0.7 broadcast_in_dim.45
  153.9 3.7 %all-to-all-start.6 = ((f32[16,1,2048]{2,1,0:T(1,128)}), f32[16,1,2048]{2,1,0:T(1,128)S(1)}, u32[]{:S(2)}, u32[]{:S(2)}) async-start(f32[16,1,2048]{2,1,0:T(1,128)} %broadcast_in_dim.45), calls=%async_computation.6 | async-start | bytes 262144 | tf_op jit(solution)/shard_map/all_to_all | solution.py:26
  157.6 7.7 %all-to-all-done.6 = f32[16,1,2048]{2,1,0:T(1,128)S(1)} async-done(((f32[16,1,2048]{2,1,0:T(1,128)}), f32[16,1,2048]{2,1,0:T(1,128)S(1)}, u32[]{:S(2)}, u32[]{:S(2)}) %all-to-all-start.6) | async-done | bytes 131104 | tf_op jit(solution)/shard_map/all_to_all | solution.py:26
  165.3 0.1 reduce_sum.196
  165.4 0.6 fusion.13
  166.0 0.0 copy-done
  166.0 5.7 %fusion.9 = f32[1024,768]{0,1:T(8,128)S(1)} fusion(bf16[2048,768]{0,1:T(8,128)(2,1)S(1)} %copy-done, bf16[2048,1024]{0,1:T(8,128)(2,1)} %get-tuple-element.10, f32[2048]{0:T(1024)S(1)} %get-tuple-element.6, f32[1024]{0:T(1024)S(1)} %get-tuple-element.4), kind=kOutput, calls=%fused_computation.19 | convolution fusion | flops 3229614080 | bytes 10498048 | tf_op jit(solution)/shard_map/dot_general | solution.py:88
  171.7 0.0 copy-start.1
  171.7 1.7 copy-done.1
  173.4 0.2 dynamic-slice_bitcast_fusion
  173.5 0.1 collective-permute-start
  173.6 3.4 %collective-permute-done = f32[4,96,1024]{2,1,0:T(8,128)S(1)} collective-permute-done((f32[4,96,1024]{2,1,0:T(8,128)S(1)}, f32[4,96,1024]{2,1,0:T(8,128)S(1)}, u32[]{:S(2)}, u32[]{:S(2)}) %collective-permute-start) | collective-permute-done | bytes 1572896 | tf_op jit(solution)/shard_map/ppermute | solution.py:43
  177.0 1.7 bitcast_add_fusion
  178.7 23.7 %all_to_all.59 = f32[4,96,1024]{2,1,0:T(8,128)S(1)} all-to-all(f32[4,96,1024]{2,1,0:T(8,128)S(1)} %bitcast_add_fusion), channel_id=1, replica_groups=mesh['rx'=4,'rc'=2,'cy'=4,'cz'=4] {'rx'}, dimensions={0} | all-to-all | bytes 3145728 | tf_op jit(solution)/shard_map/all_to_all | solution.py:44
  202.4 0.1 reduce_sum.197
  202.7 7.8 %all_to_all.60 = f32[8,1,1024]{2,1,0:T(1,128)S(1)} all-to-all(f32[8,1,1024]{2,1,0:T(1,128)S(1)} %broadcast_in_dim.46), channel_id=1, replica_groups=mesh['rx'=4,'rc'=2,'cy'=4,'cz'=4] {'rx','rc'}, dimensions={0} | all-to-all | bytes 65536 | tf_op jit(solution)/shard_map/all_to_all | solution.py:32
  210.5 0.8 broadcast_multiply_fusion
  (16 shorter events, 0.3 us)
Async XLA Ops:
  7.2 56.1 %copy-start.2 = (bf16[1024,768]{1,0:T(8,128)(2,1)S(1)}, bf16[1024,768]{1,0:T(8,128)(2,1)}, u32[]{:S(2)}) copy-start(bf16[1024,768]{1,0:T(8,128)(2,1)} %param.4) | copy-start | bytes 4718596
  7.2 53.5 %all-gather.2.cloned.1.call-start = ((), (), s32[]{:S(2)}) async-start(), calls=%async_computation.9 | async-start | bytes 3342336 | tf_op jit(solution)/shard_map/all_gather | solution.py:54
  63.2 20.0 %copy-start.3 = (f32[2048]{0:T(1024)S(1)}, f32[2048]{0:T(1024)}, u32[]{:S(2)}) copy-start(f32[2048]{0:T(1024)} %param.5) | copy-start | bytes 24580
  138.3 27.7 %copy-start = (bf16[2048,768]{0,1:T(8,128)(2,1)S(1)}, bf16[2048,768]{0,1:T(8,128)(2,1)}, u32[]{:S(2)}) copy-start(bf16[2048,768]{0,1:T(8,128)(2,1)} %all-gather.2.cloned.1.call-done) | copy-start | bytes 9437188
  153.9 11.4 %all-to-all-start.6 = ((f32[16,1,2048]{2,1,0:T(1,128)}), f32[16,1,2048]{2,1,0:T(1,128)S(1)}, u32[]{:S(2)}, u32[]{:S(2)}) async-start(f32[16,1,2048]{2,1,0:T(1,128)} %broadcast_in_dim.45), calls=%async_computation.6 | async-start | bytes 262144 | tf_op jit(solution)/shard_map/all_to_all | solution.py:26
  171.7 1.7 copy-start.1
  173.5 3.5 %collective-permute-start = (f32[4,96,1024]{2,1,0:T(8,128)S(1)}, f32[4,96,1024]{2,1,0:T(8,128)S(1)}, u32[]{:S(2)}, u32[]{:S(2)}) collective-permute-start(f32[4,96,1024]{2,1,0:T(8,128)S(1)} %dynamic-slice_bitcast_fusion), channel_id=1, source_target_pairs={{0,16},{16,0},{1,17},{17,1},{2,18},{18,2},{3,19},{19,3},{4,20},{20... | collective-permute-start | bytes 4718600 | tf_op jit(solution)/shard_map/ppermute | solution.py:43
Sparse Core Ops, SparseCore 0:
  10.2 50.4 all-gather.1

commit v7 on v4

--- a/solution.py
+++ b/solution.py
@@ -28,7 +28,9 @@
 
 
 def reduce_row(x):
-    return shifted_sum(shifted_sum(x, "rc"), "rx")
+    n = lax.axis_size(ROW)
+    copies = lax.all_to_all(jnp.broadcast_to(x, (n, *x.shape)), ROW, 0, 0, tiled=False)
+    return jnp.sum(copies, axis=0)
 
 
 def scatter_row(x):
@@ -49,7 +51,7 @@
 def row_step(kernel, col_scale, weights):
     partial_mass = jnp.sum(kernel.astype(jnp.float32) * col_scale[None, :], axis=1)
     masses = reduce_cent(partial_mass)
-    return weights / masses
+    return lax.optimization_barrier(weights / masses)
 
 
 def per_device(vectors, centroids, weights):
@@ -82,7 +84,7 @@
             col_mass, weight_sum = both[:local_centres], both[local_centres]
         else:
             col_mass = reduce_row(partial_cols)
-        col_scale = weight_sum / centre_total / col_mass
+        col_scale = lax.optimization_barrier(weight_sum / centre_total / col_mass)
         row_scale = row_step(kernel, col_scale, weights)
     transport = (row_scale[:, None] * kernel.astype(jnp.float32) * col_scale[None, :]).astype(
         jnp.bfloat16

time: 215 us -> 219 us (1.019)
  blocking collectives: 34.4 us -> 59.6 us
  waiting for transfers between devices: 99 us -> 84.7 us
  starting transfers between devices: 24.7 us -> 11.4 us
  other arithmetic: 23.9 us -> 28.9 us
    all_to_all x0 -> x3, blocking collectives: none -> 25.2 us  [reduce_row(): lax.all_to_all(jnp.broadcast_to(x, (n, *x.shape)), ROW, 0, 0, tiled=False)]
    ppermute x16 -> x0, waiting for transfers between devices: 17.9 us -> none  [shifted_sum(): total = total + lax.ppermute(x, axis, [(i, (i + k) % n) for i in range(n)])]
    ppermute x16 -> x0, starting transfers between devices: 17.7 us -> none  [shifted_sum(): total = total + lax.ppermute(x, axis, [(i, (i + k) % n) for i in range(n)])]
    reduce_sum x3, other arithmetic: 2.66 us -> 9.22 us  [row_step(): jnp.sum(kernel.astype(jnp.float32) * col_scale[None, :], axis=1)]
    all_to_all x0 -> x1, waiting for transfers between devices: none -> 4.24 us  [reduce_row(): lax.all_to_all(jnp.broadcast_to(x, (n, *x.shape)), ROW, 0, 0, tiled=False)]
    all_to_all x0 -> x1, starting transfers between devices: none -> 3.81 us  [reduce_row(): lax.all_to_all(jnp.broadcast_to(x, (n, *x.shape)), ROW, 0, 0, tiled=False)]
  transfers between devices with their start and end apart: 22 -> 7, of which waited for: 19 -> 6; matrix products, arithmetic and copies ran while one was open for 1% -> 1% of each run, Pallas kernels for 0% -> 0%
where the time goes in v7:
time: 219 us; the launch traced here: 218 us
  waiting for transfers between devices  84.7 us (39%)
  blocking collectives  59.6 us (27%)
  other arithmetic  28.9 us (13%)
  between operations  15 us (7%)
  matrix products  13.6 us (6%)
  starting transfers between devices  11.4 us (5%)
  local copies, waits for them, and re-layouts  4.7 us (2%)
    all_gather x1, waiting for transfers between devices, per_device(): full_rows = lax.all_gather(vectors, CENT, axis=1, tiled=True)  51 us
    all_to_all x3, blocking collectives, reduce_cent(): lax.all_to_all(jnp.broadcast_to(x, (n, *x.shape)), CENT, 0, 0, tiled=False)  34.4 us
    all_to_all x3, blocking collectives, reduce_row(): lax.all_to_all(jnp.broadcast_to(x, (n, *x.shape)), ROW, 0, 0, tiled=False)  25.2 us
    ppermute x3, waiting for transfers between devices, scatter_row(): lax.ppermute(piece, 'rx', [(i, (i + k) % chips) for i in range(chips)])  17.8 us
    reduce_sum x3, other arithmetic, per_device(): jnp.sum(kernel.astype(jnp.float32) * row_scale[:, None], axis=0)  9.37 us
    reduce_sum x3, other arithmetic, row_step(): jnp.sum(kernel.astype(jnp.float32) * col_scale[None, :], axis=1)  9.22 us
    dot_general x1, matrix products, per_device(): jnp.dot(full_rows, centroids.T, preferred_element_type=jnp.float32)  7.88 us
    all_to_all x1, waiting for transfers between devices, reduce_cent(): lax.all_to_all(jnp.broadcast_to(x, (n, *x.shape)), CENT, 0, 0, tiled=False)  7.71 us
  transfers between devices with their start and end apart: 7, of which 6 were waited for; matrix products, arithmetic and copies ran while one was open for 1% of the time, Pallas kernels for 0%

profile of v7, /device:TPU:0, one launch (start us, length us, event | category | flops | bytes accessed | tf_op | source)
XLA Modules:
  0.0 217.9 jit_solution(18013426678735376517)
XLA Ops:
  7.2 0.0 copy-start.2
  7.2 0.0 all-gather.2.cloned.1.call-start
  7.2 0.7 all-gather.2.cloned.1.call-update
  7.9 1.8 multiply_reduce_fusion.1
  9.7 51.0 %all-gather.2.cloned.1.call-done = bf16[2048,768]{0,1:T(8,128)(2,1)} async-done(((bf16[2048,48]{0,1:T(8,128)(2,1)}), bf16[2048,768]{0,1:T(8,128)(2,1)}) %all-gather.2.cloned.1.call-update) | async-done | bytes 3145744 | tf_op jit(solution)/shard_map/all_gather | solution.py:58
  60.7 2.6 %multiply_reduce_fusion = f32[2048]{0:T(1024)S(1)} fusion(bf16[2048,768]{0,1:T(8,128)(2,1)} %all-gather.2.cloned.1.call-done), kind=kLoop, calls=%fused_computation.18 | loop fusion | flops 4716544 | bytes 3153920 | tf_op jit(solution)/shard_map/reduce_sum | solution.py:64
  63.2 0.0 copy-done.2
  63.2 0.0 copy-start.3
  63.2 7.9 %fusion = (f32[2048]{0:T(1024)S(1)}, bf16[2048,1024]{0,1:T(8,128)(2,1)}) fusion(f32[1024]{0:T(1024)S(1)} %add_rsqrt_fusion.2, f32[2048]{0:T(1024)S(1)} %add_rsqrt_fusion, bf16[1024,768]{1,0:T(8,128)(2,1)S(1)} %copy-done.2, bf16[2048,768]{0,1:T(8,128)(2,1)} %all-gather.2.cloned.1.call-done), kind=kOutput, calls=%fused_computation.8 | convolution fusion | flops 3235903488 | bytes 8933376 | tf_op jit(solution)/shard_map/dot_general | solution.py:69
  71.1 0.1 broadcast_in_dim.18
  71.2 12.0 %all_to_all.48 = f32[16,1,2048]{2,1,0:T(1,128)S(1)} all-to-all(f32[16,1,2048]{2,1,0:T(1,128)S(1)} %broadcast_in_dim.18), channel_id=1, replica_groups=mesh['rx'=4,'rc'=2,'cy'=4,'cz'=4] {'cy','cz'}, dimensions={0} | all-to-all | bytes 262144 | tf_op jit(solution)/shard_map/all_to_all | solution.py:26
  83.2 0.1 reduce_sum.174
  83.2 0.0 copy-done.3
  83.3 0.6 fusion.16
  83.9 3.1 %fusion.1 = f32[1024]{0:T(1024)S(1)} fusion(bf16[2048,1024]{0,1:T(8,128)(2,1)} %get-tuple-element.11, f32[2048]{0:T(1024)S(1)} %get-tuple-element.8), kind=kLoop, calls=%fused_computation.9 | loop fusion | flops 6290432 | bytes 4206592 | tf_op jit(solution)/shard_map/reduce_sum | solution.py:81
  86.9 0.7 pad_maximum_fusion
  87.6 9.5 %all_to_all.49 = f32[8,1,1025]{2,1,0:T(1,128)S(1)} all-to-all(f32[8,1,1025]{2,1,0:T(1,128)S(1)} %broadcast_in_dim.40), channel_id=1, replica_groups=mesh['rx'=4,'rc'=2,'cy'=4,'cz'=4] {'rx','rc'}, dimensions={0} | all-to-all | bytes 65600 | tf_op jit(solution)/shard_map/all_to_all | solution.py:32
  97.2 0.5 slice.8
  98.4 3.1 %fusion.2 = f32[2048]{0:T(1024)S(1)} fusion(bf16[2048,1024]{0,1:T(8,128)(2,1)} %get-tuple-element.11, f32[1024]{0:T(1024)S(1)} %slice_divide_fusion), kind=kLoop, calls=%fused_computation.10 | loop fusion | flops 6289408 | bytes 4206592 | tf_op jit(solution)/shard_map/reduce_sum | solution.py:52
  101.4 0.1 broadcast_in_dim.41
  101.5 11.2 %all_to_all.50 = f32[16,1,2048]{2,1,0:T(1,128)S(1)} all-to-all(f32[16,1,2048]{2,1,0:T(1,128)S(1)} %broadcast_in_dim.41), channel_id=1, replica_groups=mesh['rx'=4,'rc'=2,'cy'=4,'cz'=4] {'cy','cz'}, dimensions={0} | all-to-all | bytes 262144 | tf_op jit(solution)/shard_map/all_to_all | solution.py:26
  112.8 0.1 reduce_sum.179
  112.9 3.1 %fusion.3 = f32[1024]{0:T(1024)S(1)} fusion(bf16[2048,1024]{0,1:T(8,128)(2,1)} %get-tuple-element.11, f32[2048]{0:T(1024)S(1)} %div.61), kind=kLoop, calls=%fused_computation.11 | loop fusion | flops 6290432 | bytes 4206592 | tf_op jit(solution)/shard_map/reduce_sum | solution.py:81
  116.0 7.8 %all_to_all.51 = f32[8,1,1024]{2,1,0:T(1,128)S(1)} all-to-all(f32[8,1,1024]{2,1,0:T(1,128)S(1)} %broadcast_in_dim.42), channel_id=1, replica_groups=mesh['rx'=4,'rc'=2,'cy'=4,'cz'=4] {'rx','rc'}, dimensions={0} | all-to-all | bytes 65536 | tf_op jit(solution)/shard_map/all_to_all | solution.py:32
  123.8 3.1 %fusion.4 = f32[2048]{0:T(1024)S(1)} fusion(bf16[2048,1024]{0,1:T(8,128)(2,1)} %get-tuple-element.11, f32[1024]{0:T(1024)S(1)} %broadcast_divide_fusion.1), kind=kLoop, calls=%fused_computation.12 | loop fusion | flops 6289408 | bytes 4206592 | tf_op jit(solution)/shard_map/reduce_sum | solution.py:52
  126.9 0.1 broadcast_in_dim.43
  127.0 11.2 %all_to_all.52 = f32[16,1,2048]{2,1,0:T(1,128)S(1)} all-to-all(f32[16,1,2048]{2,1,0:T(1,128)S(1)} %broadcast_in_dim.43), channel_id=1, replica_groups=mesh['rx'=4,'rc'=2,'cy'=4,'cz'=4] {'cy','cz'}, dimensions={0} | all-to-all | bytes 262144 | tf_op jit(solution)/shard_map/all_to_all | solution.py:26
  138.2 0.1 reduce_sum.183
  138.3 0.0 copy-start
  138.3 3.2 %fusion.5 = f32[1024]{0:T(1024)S(1)} fusion(bf16[2048,1024]{0,1:T(8,128)(2,1)} %get-tuple-element.11, f32[2048]{0:T(1024)S(1)} %div.63), kind=kLoop, calls=%fused_computation.13 | loop fusion | flops 6290432 | bytes 4206592 | tf_op jit(solution)/shard_map/reduce_sum | solution.py:81
  141.6 7.8 %all_to_all.53 = f32[8,1,1024]{2,1,0:T(1,128)S(1)} all-to-all(f32[8,1,1024]{2,1,0:T(1,128)S(1)} %broadcast_in_dim.44), channel_id=1, replica_groups=mesh['rx'=4,'rc'=2,'cy'=4,'cz'=4] {'rx','rc'}, dimensions={0} | all-to-all | bytes 65536 | tf_op jit(solution)/shard_map/all_to_all | solution.py:32
  149.5 3.1 %fusion.6 = f32[2048]{0:T(1024)S(1)} fusion(bf16[2048,1024]{0,1:T(8,128)(2,1)} %get-tuple-element.11, f32[1024]{0:T(1024)S(1)} %broadcast_divide_fusion), kind=kLoop, calls=%fused_computation.14 | loop fusion | flops 6289408 | bytes 4206592 | tf_op jit(solution)/shard_map/reduce_sum | solution.py:52
  152.5 0.7 broadcast_in_dim.45
  153.3 3.7 %all-to-all-start.6 = ((f32[16,1,2048]{2,1,0:T(1,128)}), f32[16,1,2048]{2,1,0:T(1,128)S(1)}, u32[]{:S(2)}, u32[]{:S(2)}) async-start(f32[16,1,2048]{2,1,0:T(1,128)} %broadcast_in_dim.45), calls=%async_computation.6 | async-start | bytes 262144 | tf_op jit(solution)/shard_map/all_to_all | solution.py:26
  157.0 7.7 %all-to-all-done.6 = f32[16,1,2048]{2,1,0:T(1,128)S(1)} async-done(((f32[16,1,2048]{2,1,0:T(1,128)}), f32[16,1,2048]{2,1,0:T(1,128)S(1)}, u32[]{:S(2)}, u32[]{:S(2)}) %all-to-all-start.6) | async-done | bytes 131104 | tf_op jit(solution)/shard_map/all_to_all | solution.py:26
  164.7 0.1 reduce_sum.187
  164.8 0.0 copy-done
  164.8 5.7 %fusion.9 = f32[1024,768]{0,1:T(8,128)S(1)} fusion(bf16[2048,768]{0,1:T(8,128)(2,1)S(1)} %copy-done, bf16[2048,1024]{0,1:T(8,128)(2,1)} %get-tuple-element.11, f32[2048]{0:T(1024)S(1)} %div.65, f32[1024]{0:T(1024)S(1)} %broadcast_divide_fusion), kind=kOutput, calls=%fused_computation.19 | convolution fusion | flops 3229614080 | bytes 10498048 | tf_op jit(solution)/shard_map/dot_general | solution.py:92
  170.5 0.0 copy-start.1
  170.5 1.7 copy-done.1
  172.2 0.2 dynamic-slice_bitcast_fusion
  172.4 0.1 collective-permute-start
  172.5 3.4 %collective-permute-done = f32[4,96,1024]{2,1,0:T(8,128)S(1)} collective-permute-done((f32[4,96,1024]{2,1,0:T(8,128)S(1)}, f32[4,96,1024]{2,1,0:T(8,128)S(1)}, u32[]{:S(2)}, u32[]{:S(2)}) %collective-permute-start) | collective-permute-done | bytes 1572896 | tf_op jit(solution)/shard_map/ppermute | solution.py:43
  175.8 1.7 bitcast_add_fusion
  177.5 0.1 dynamic-slice_bitcast_fusion.3
  177.6 0.6 collective-permute-start.1
  178.3 2.1 collective-permute-start.2
  180.3 1.1 collective-permute-start.3
  181.4 17.1 %collective-permute-done.1 = f32[96,1024]{1,0:T(8,128)S(1)} collective-permute-done((f32[96,1024]{1,0:T(8,128)S(1)}, f32[96,1024]{1,0:T(8,128)S(1)}, u32[]{:S(2)}, u32[]{:S(2)}) %collective-permute-start.1) | collective-permute-done | bytes 393248 | tf_op jit(solution)/shard_map/ppermute | solution.py:47
  198.5 0.0 collective-permute-done.2
  198.5 0.7 collective-permute-done.3
  199.2 1.1 multiply_reduce_fusion.2
  200.4 0.6 broadcast_in_dim.46
  201.0 3.8 %all-to-all-start.7 = ((f32[8,1,1024]{2,1,0:T(1,128)}), f32[8,1,1024]{2,1,0:T(1,128)S(1)}, u32[]{:S(2)}, u32[]{:S(2)}) async-start(f32[8,1,1024]{2,1,0:T(1,128)} %broadcast_in_dim.46), calls=%async_computation.7 | async-start | bytes 65536 | tf_op jit(solution)/shard_map/all_to_all | solution.py:32
  204.8 0.6 multiply_log_fusion
  205.4 0.6 log.6
  206.0 4.2 %all-to-all-done.7 = f32[8,1,1024]{2,1,0:T(1,128)S(1)} async-done(((f32[8,1,1024]{2,1,0:T(1,128)}), f32[8,1,1024]{2,1,0:T(1,128)S(1)}, u32[]{:S(2)}, u32[]{:S(2)}) %all-to-all-start.7) | async-done | bytes 32800 | tf_op jit(solution)/shard_map/all_to_all | solution.py:32
  210.3 0.8 broadcast_multiply_fusion
  (16 shorter events, 0.2 us)
Async XLA Ops:
  7.2 56.1 %copy-start.2 = (bf16[1024,768]{1,0:T(8,128)(2,1)S(1)}, bf16[1024,768]{1,0:T(8,128)(2,1)}, u32[]{:S(2)}) copy-start(bf16[1024,768]{1,0:T(8,128)(2,1)} %param.4) | copy-start | bytes 4718596
  7.2 53.5 %all-gather.2.cloned.1.call-start = ((), (), s32[]{:S(2)}) async-start(), calls=%async_computation.8 | async-start | bytes 3342336 | tf_op jit(solution)/shard_map/all_gather | solution.py:58
  63.2 20.0 %copy-start.3 = (f32[2048]{0:T(1024)S(1)}, f32[2048]{0:T(1024)}, u32[]{:S(2)}) copy-start(f32[2048]{0:T(1024)} %param.5) | copy-start | bytes 24580
  138.3 26.5 %copy-start = (bf16[2048,768]{0,1:T(8,128)(2,1)S(1)}, bf16[2048,768]{0,1:T(8,128)(2,1)}, u32[]{:S(2)}) copy-start(bf16[2048,768]{0,1:T(8,128)(2,1)} %all-gather.2.cloned.1.call-done) | copy-start | bytes 9437188
  153.3 11.4 %all-to-all-start.6 = ((f32[16,1,2048]{2,1,0:T(1,128)}), f32[16,1,2048]{2,1,0:T(1,128)S(1)}, u32[]{:S(2)}, u32[]{:S(2)}) async-start(f32[16,1,2048]{2,1,0:T(1,128)} %broadcast_in_dim.45), calls=%async_computation.6 | async-start | bytes 262144 | tf_op jit(solution)/shard_map/all_to_all | solution.py:26
  170.5 1.7 copy-start.1
  172.4 3.5 %collective-permute-start = (f32[4,96,1024]{2,1,0:T(8,128)S(1)}, f32[4,96,1024]{2,1,0:T(8,128)S(1)}, u32[]{:S(2)}, u32[]{:S(2)}) collective-permute-start(f32[4,96,1024]{2,1,0:T(8,128)S(1)} %dynamic-slice_bitcast_fusion), channel_id=1, source_target_pairs={{0,16},{16,0},{1,17},{17,1},{2,18},{18,2},{3,19},{19,3},{4,20},{20... | collective-permute-start | bytes 4718600 | tf_op jit(solution)/shard_map/ppermute | solution.py:43
  177.6 20.9 %collective-permute-start.1 = (f32[96,1024]{1,0:T(8,128)S(1)}, f32[96,1024]{1,0:T(8,128)S(1)}, u32[]{:S(2)}, u32[]{:S(2)}) collective-permute-start(f32[96,1024]{1,0:T(8,128)S(1)} %get-tuple-element.5), channel_id=1, source_target_pairs={{0,32},{32,64},{64,96},{96,0},{1,33},{33,65},{65,97},{97,1},{2,34}... | collective-permute-start | bytes 1179656 | tf_op jit(solution)/shard_map/ppermute | solution.py:47
  178.3 20.2 %collective-permute-start.2 = (f32[96,1024]{1,0:T(8,128)S(1)}, f32[96,1024]{1,0:T(8,128)S(1)}, u32[]{:S(2)}, u32[]{:S(2)}) collective-permute-start(f32[96,1024]{1,0:T(8,128)S(1)} %get-tuple-element.7), channel_id=1, source_target_pairs={{0,64},{32,96},{64,0},{96,32},{1,65},{33,97},{65,1},{97,33},{2,66}... | collective-permute-start | bytes 1179656 | tf_op jit(solution)/shard_map/ppermute | solution.py:47
  180.3 18.9 %collective-permute-start.3 = (f32[96,1024]{1,0:T(8,128)S(1)}, f32[96,1024]{1,0:T(8,128)}, u32[]{:S(2)}, u32[]{:S(2)}) collective-permute-start(f32[96,1024]{1,0:T(8,128)S(1)} %get-tuple-element.6), channel_id=1, source_target_pairs={{0,96},{32,0},{64,32},{96,64},{1,97},{33,1},{65,33},{97,65},{2,98}... | collective-permute-start | bytes 1179656 | tf_op jit(solution)/shard_map/ppermute | solution.py:47
  201.0 9.3 %all-to-all-start.7 = ((f32[8,1,1024]{2,1,0:T(1,128)}), f32[8,1,1024]{2,1,0:T(1,128)S(1)}, u32[]{:S(2)}, u32[]{:S(2)}) async-start(f32[8,1,1024]{2,1,0:T(1,128)} %broadcast_in_dim.46), calls=%async_computation.7 | async-start | bytes 65536 | tf_op jit(solution)/shard_map/all_to_all | solution.py:32
Sparse Core Ops, SparseCore 0:
  10.2 50.4 all-gather.1

commit v8 on v4

--- a/solution.py
+++ b/solution.py
@@ -46,6 +46,15 @@
     return total
 
 
+def column_mass(kernel, row_scale):
+    high = row_scale.astype(jnp.bfloat16)
+    rest = row_scale - high.astype(jnp.float32)
+    middle = rest.astype(jnp.bfloat16)
+    low = (rest - middle.astype(jnp.float32)).astype(jnp.bfloat16)
+    parts = jnp.stack([high, middle, low])
+    return jnp.sum(jnp.dot(parts, kernel, preferred_element_type=jnp.float32), axis=0)
+
+
 def row_step(kernel, col_scale, weights):
     partial_mass = jnp.sum(kernel.astype(jnp.float32) * col_scale[None, :], axis=1)
     masses = reduce_cent(partial_mass)
@@ -76,7 +85,7 @@
     row_scale = row_step(kernel, col_scale, weights)
     weight_sum = None
     for sweep in range(ITERS):
-        partial_cols = jnp.sum(kernel.astype(jnp.float32) * row_scale[:, None], axis=0)
+        partial_cols = column_mass(kernel, row_scale)
         if weight_sum is None:
             both = reduce_row(jnp.concatenate([partial_cols, jnp.sum(weights)[None]]))
             col_mass, weight_sum = both[:local_centres], both[local_centres]

time: 215 us -> 216 us (level)
  matrix products: 13.6 us -> 24.4 us
  other arithmetic: 23.9 us -> 14.1 us
    dot_general x0 -> x3, matrix products: none -> 10.8 us  [column_mass(): jnp.dot(parts, kernel, preferred_element_type=jnp.float32)]
    reduce_sum x3 -> x0, other arithmetic: 9.83 us -> none  [per_device(): jnp.sum(kernel.astype(jnp.float32) * row_scale[:, None], axis=0)]
where the time goes in v8:
time: 216 us; the launch traced here: 215 us
  waiting for transfers between devices  99 us (46%)
  blocking collectives  34.4 us (16%)
  starting transfers between devices  24.7 us (11%)
  matrix products  24.4 us (11%)
  between operations  15.1 us (7%)
  other arithmetic  14.1 us (7%)
  local copies, waits for them, and re-layouts  3.49 us (2%)
    all_gather x1, waiting for transfers between devices, per_device(): full_rows = lax.all_gather(vectors, CENT, axis=1, tiled=True)  51 us
    all_to_all x3, blocking collectives, reduce_cent(): lax.all_to_all(jnp.broadcast_to(x, (n, *x.shape)), CENT, 0, 0, tiled=False)  34.4 us
    ppermute x3, waiting for transfers between devices, scatter_row(): lax.ppermute(piece, 'rx', [(i, (i + k) % chips) for i in range(chips)])  18.3 us
    ppermute x16, waiting for transfers between devices, shifted_sum(): total = total + lax.ppermute(x, axis, [(i, (i + k) % n) for i in range(n)])  17.9 us
    ppermute x16, starting transfers between devices, shifted_sum(): total = total + lax.ppermute(x, axis, [(i, (i + k) % n) for i in range(n)])  17.7 us
    dot_general x3, matrix products, column_mass(): jnp.dot(parts, kernel, preferred_element_type=jnp.float32)  10.8 us
    dot_general x1, matrix products, per_device(): jnp.dot(full_rows, centroids.T, preferred_element_type=jnp.float32)  7.88 us
    all_to_all x1, waiting for transfers between devices, reduce_cent(): lax.all_to_all(jnp.broadcast_to(x, (n, *x.shape)), CENT, 0, 0, tiled=False)  7.82 us
  transfers between devices with their start and end apart: 22, of which 19 were waited for; matrix products, arithmetic and copies ran while one was open for 1% of the time, Pallas kernels for 0%

profile of v8, /device:TPU:0, one launch (start us, length us, event | category | flops | bytes accessed | tf_op | source)
XLA Modules:
  0.0 215.2 jit_solution(7882133475098811992)
XLA Ops:
  7.2 0.7 all-gather.2.cloned.1.call-update
  7.9 1.8 multiply_reduce_fusion.1
  9.7 51.0 %all-gather.2.cloned.1.call-done = bf16[2048,768]{0,1:T(8,128)(2,1)} async-done(((bf16[2048,48]{0,1:T(8,128)(2,1)}), bf16[2048,768]{0,1:T(8,128)(2,1)}) %all-gather.2.cloned.1.call-update) | async-done | bytes 3145744 | tf_op jit(solution)/shard_map/all_gather | solution.py:65
  60.7 2.6 %multiply_reduce_fusion = f32[2048]{0:T(1024)S(1)} fusion(bf16[2048,768]{0,1:T(8,128)(2,1)} %all-gather.2.cloned.1.call-done), kind=kLoop, calls=%fused_computation.12 | loop fusion | flops 4716544 | bytes 3153920 | tf_op jit(solution)/shard_map/reduce_sum | solution.py:71
  63.2 7.9 %fusion = (f32[2048]{0:T(1024)S(1)}, bf16[2048,1024]{0,1:T(8,128)(2,1)}) fusion(f32[1024]{0:T(1024)S(1)} %add_rsqrt_fusion.2, f32[2048]{0:T(1024)S(1)} %add_rsqrt_fusion, bf16[1024,768]{1,0:T(8,128)(2,1)S(1)} %copy-done.5, bf16[2048,768]{0,1:T(8,128)(2,1)} %all-gather.2.cloned.1.call-done), kind=kOutput, calls=%fused_computation.5 | convolution fusion | flops 3235903488 | bytes 8933376 | tf_op jit(solution)/shard_map/dot_general | solution.py:76
  71.2 12.0 %all_to_all.24 = f32[16,1,2048]{2,1,0:T(1,128)S(1)} all-to-all(f32[16,1,2048]{2,1,0:T(1,128)S(1)} %broadcast_in_dim.10), channel_id=1, replica_groups=mesh['rx'=4,'rc'=2,'cy'=4,'cz'=4] {'cy','cz'}, dimensions={0} | all-to-all | bytes 262144 | tf_op jit(solution)/shard_map/all_to_all | solution.py:26
  83.2 0.1 reduce_sum.138
  83.3 0.6 divide_convert_fusion.2
  83.9 3.7 %convolution_reduce_fusion.2 = f32[1024]{0:T(1024)S(1)} fusion(bf16[2048,1024]{0,1:T(8,128)(2,1)} %get-tuple-element.23, bf16[1,2048]{1,0:T(2,128)(2,1)S(1)} %stack.38, bf16[1,2048]{1,0:T(2,128)(2,1)S(1)} %stack.37, bf16[1,2048]{1,0:T(2,128)(2,1)S(1)} %stack.36), kind=kOutput, calls=%fused_computation.21 | convolution fusion | flops 12621824 | bytes 4210688 | tf_op jit(solution)/shard_map/dot_general | solution.py:55
  87.6 0.7 pad_maximum_fusion
  88.4 1.2 collective-permute-done
  89.5 0.7 fusion.30
  90.2 1.5 collective-permute-start.1
  91.7 2.7 %collective-permute-start.2 = (f32[1025]{0:T(1024)S(1)}, f32[1025]{0:T(1024)S(1)}, u32[]{:S(2)}, u32[]{:S(2)}) collective-permute-start(f32[1025]{0:T(1024)S(1)} %fusion.30), channel_id=1, source_target_pairs={{0,64},{32,96},{64,0},{96,32},{1,65},{33,97},{65,1},{97,33},{2,66}... | collective-permute-start | bytes 12308 | tf_op jit(solution)/shard_map/ppermute | solution.py:20
  94.4 1.5 collective-permute-start.3
  95.9 1.0 collective-permute-done.2
  96.9 1.2 collective-permute-done.3
  98.1 0.5 slice.8
  99.3 0.9 fusion.1
  100.2 11.2 %all_to_all.25 = f32[16,1,2048]{2,1,0:T(1,128)S(1)} all-to-all(f32[16,1,2048]{2,1,0:T(1,128)S(1)} %broadcast_in_dim.12), channel_id=1, replica_groups=mesh['rx'=4,'rc'=2,'cy'=4,'cz'=4] {'cy','cz'}, dimensions={0} | all-to-all | bytes 262144 | tf_op jit(solution)/shard_map/all_to_all | solution.py:26
  111.5 0.1 reduce_sum.142
  111.6 3.5 %convolution_reduce_fusion.1 = f32[1024]{0:T(1024)S(1)} fusion(bf16[2048,1024]{0,1:T(8,128)(2,1)} %get-tuple-element.23, bf16[1,2048]{1,0:T(2,128)(2,1)S(1)} %stack.42, bf16[1,2048]{1,0:T(2,128)(2,1)S(1)} %stack.41, bf16[1,2048]{1,0:T(2,128)(2,1)S(1)} %stack.40), kind=kOutput, calls=%fused_computation.20 | convolution fusion | flops 12621824 | bytes 4210688 | tf_op jit(solution)/shard_map/dot_general | solution.py:55
  115.3 1.2 collective-permute-done.4
  116.4 0.3 collective-permute-start.5
  116.7 3.8 %collective-permute-start.6 = (f32[1024]{0:T(1024)S(1)}, f32[1024]{0:T(1024)S(1)}, u32[]{:S(2)}, u32[]{:S(2)}) collective-permute-start(f32[1024]{0:T(1024)S(1)} %add.132), channel_id=1, source_target_pairs={{0,64},{32,96},{64,0},{96,32},{1,65},{33,97},{65,1},{97,33},{2,66}... | collective-permute-start | bytes 12296 | tf_op jit(solution)/shard_map/ppermute | solution.py:20
  120.6 0.7 collective-permute-done.5
  121.3 0.9 collective-permute-done.6
  122.2 2.0 collective-permute-done.7
  124.2 0.9 fusion.2
  125.2 11.2 %all_to_all.26 = f32[16,1,2048]{2,1,0:T(1,128)S(1)} all-to-all(f32[16,1,2048]{2,1,0:T(1,128)S(1)} %broadcast_in_dim.26), channel_id=1, replica_groups=mesh['rx'=4,'rc'=2,'cy'=4,'cz'=4] {'cy','cz'}, dimensions={0} | all-to-all | bytes 262144 | tf_op jit(solution)/shard_map/all_to_all | solution.py:26
  136.4 0.1 reduce_sum.145
  136.6 3.5 %convolution_reduce_fusion = f32[1024]{0:T(1024)S(1)} fusion(bf16[2048,1024]{0,1:T(8,128)(2,1)} %get-tuple-element.23, bf16[1,2048]{1,0:T(2,128)(2,1)S(1)} %stack.46, bf16[1,2048]{1,0:T(2,128)(2,1)S(1)} %stack.45, bf16[1,2048]{1,0:T(2,128)(2,1)S(1)} %stack.44), kind=kOutput, calls=%fused_computation.19 | convolution fusion | flops 12621824 | bytes 4210688 | tf_op jit(solution)/shard_map/dot_general | solution.py:55
  140.1 0.3 collective-permute-start.8
  140.4 1.2 collective-permute-done.8
  141.6 1.5 collective-permute-start.10
  143.1 1.1 collective-permute-start.11
  144.2 0.9 collective-permute-start.9
  145.1 1.6 collective-permute-done.10
  146.7 2.3 %collective-permute-done.9 = f32[1024]{0:T(1024)S(1)} collective-permute-done((f32[1024]{0:T(1024)S(1)}, f32[1024]{0:T(1024)S(1)}, u32[]{:S(2)}, u32[]{:S(2)}) %collective-permute-start.9) | collective-permute-done | bytes 4128 | tf_op jit(solution)/shard_map/ppermute | solution.py:20
  149.0 0.6 multiply_log_fusion
  149.6 0.9 fusion.3
  150.5 0.7 broadcast_in_dim.27
  151.2 3.6 %all-to-all-start.3 = ((f32[16,1,2048]{2,1,0:T(1,128)}), f32[16,1,2048]{2,1,0:T(1,128)S(1)}, u32[]{:S(2)}, u32[]{:S(2)}) async-start(f32[16,1,2048]{2,1,0:T(1,128)} %broadcast_in_dim.27), calls=%async_computation.3 | async-start | bytes 262144 | tf_op jit(solution)/shard_map/all_to_all | solution.py:26
  154.9 7.8 %all-to-all-done.3 = f32[16,1,2048]{2,1,0:T(1,128)S(1)} async-done(((f32[16,1,2048]{2,1,0:T(1,128)}), f32[16,1,2048]{2,1,0:T(1,128)S(1)}, u32[]{:S(2)}, u32[]{:S(2)}) %all-to-all-start.3) | async-done | bytes 131104 | tf_op jit(solution)/shard_map/all_to_all | solution.py:26
  162.7 0.1 reduce_sum.148
  162.8 0.6 fusion.34
  163.4 5.7 %fusion.6 = f32[1024,768]{0,1:T(8,128)S(1)} fusion(bf16[2048,768]{0,1:T(8,128)(2,1)S(1)} %copy-done.3, bf16[2048,1024]{0,1:T(8,128)(2,1)} %get-tuple-element.23, f32[2048]{0:T(1024)S(1)} %get-tuple-element.6, f32[1024]{0:T(1024)S(1)} %get-tuple-element.4), kind=kOutput, calls=%fused_computation.13 | convolution fusion | flops 3229614080 | bytes 10498048 | tf_op jit(solution)/shard_map/dot_general | solution.py:99
  169.1 1.7 copy-done.4
  170.8 0.2 dynamic-slice_bitcast_fusion
  171.1 3.4 %collective-permute-done.12 = f32[4,96,1024]{2,1,0:T(8,128)S(1)} collective-permute-done((f32[4,96,1024]{2,1,0:T(8,128)S(1)}, f32[4,96,1024]{2,1,0:T(8,128)S(1)}, u32[]{:S(2)}, u32[]{:S(2)}) %collective-permute-start.12) | collective-permute-done | bytes 1572896 | tf_op jit(solution)/shard_map/ppermute | solution.py:41
  174.4 1.7 bitcast_add_fusion
  176.1 0.1 dynamic-slice_bitcast_fusion.3
  176.3 1.7 collective-permute-start.14
  178.0 1.5 collective-permute-start.15
  179.5 17.6 %collective-permute-done.13 = f32[96,1024]{1,0:T(8,128)S(1)} collective-permute-done((f32[96,1024]{1,0:T(8,128)S(1)}, f32[96,1024]{1,0:T(8,128)S(1)}, u32[]{:S(2)}, u32[]{:S(2)}) %collective-permute-start.13) | collective-permute-done | bytes 393248 | tf_op jit(solution)/shard_map/ppermute | solution.py:45
  197.1 0.7 collective-permute-done.15
  197.8 1.1 multiply_reduce_fusion.2
  199.0 1.2 collective-permute-done.16
  200.2 0.2 collective-permute-start.17
  200.4 3.6 %collective-permute-start.18 = (f32[1024]{0:T(1024)S(1)}, f32[1024]{0:T(1024)S(1)}, u32[]{:S(2)}, u32[]{:S(2)}) collective-permute-start(f32[1024]{0:T(1024)S(1)} %add.158), channel_id=1, source_target_pairs={{0,64},{32,96},{64,0},{96,32},{1,65},{33,97},{65,1},{97,33},{2,66}... | collective-permute-start | bytes 12296 | tf_op jit(solution)/shard_map/ppermute | solution.py:20
  204.0 1.0 collective-permute-done.17
  205.0 0.6 collective-permute-done.18
  205.6 2.0 collective-permute-done.19
  207.6 0.8 broadcast_multiply_fusion
  (47 shorter events, 0.8 us)
Async XLA Ops:
  7.2 56.1 %copy-start.5 = (bf16[1024,768]{1,0:T(8,128)(2,1)S(1)}, bf16[1024,768]{1,0:T(8,128)(2,1)}, u32[]{:S(2)}) copy-start(bf16[1024,768]{1,0:T(8,128)(2,1)} %param.4) | copy-start | bytes 4718596
  7.2 53.5 %all-gather.2.cloned.1.call-start = ((), (), s32[]{:S(2)}) async-start(), calls=%async_computation.4 | async-start | bytes 3342336 | tf_op jit(solution)/shard_map/all_gather | solution.py:65
  63.2 20.0 %copy-start.6 = (f32[2048]{0:T(1024)S(1)}, f32[2048]{0:T(1024)}, u32[]{:S(2)}) copy-start(f32[2048]{0:T(1024)} %param.5) | copy-start | bytes 24580
  83.3 16.0 %copy-start = (bf16[2048,1024]{0,1:T(8,128)(2,1)S(1)}, bf16[2048,1024]{0,1:T(8,128)(2,1)}, u32[]{:S(2)}) copy-start(bf16[2048,1024]{0,1:T(8,128)(2,1)} %get-tuple-element.23) | copy-start | bytes 12582916
  88.3 1.3 collective-permute-start
  90.2 5.7 %collective-permute-start.1 = (f32[1025]{0:T(1024)S(1)}, f32[1025]{0:T(1024)S(1)}, u32[]{:S(2)}, u32[]{:S(2)}) collective-permute-start(f32[1025]{0:T(1024)S(1)} %fusion.30), channel_id=1, source_target_pairs={{0,32},{32,64},{64,96},{96,0},{1,33},{33,65},{65,97},{97,1},{2,34}... | collective-permute-start | bytes 12308 | tf_op jit(solution)/shard_map/ppermute | solution.py:20
  91.7 5.2 %collective-permute-start.2 = (f32[1025]{0:T(1024)S(1)}, f32[1025]{0:T(1024)S(1)}, u32[]{:S(2)}, u32[]{:S(2)}) collective-permute-start(f32[1025]{0:T(1024)S(1)} %fusion.30), channel_id=1, source_target_pairs={{0,64},{32,96},{64,0},{96,32},{1,65},{33,97},{65,1},{97,33},{2,66}... | collective-permute-start | bytes 12308 | tf_op jit(solution)/shard_map/ppermute | solution.py:20
  94.4 3.7 %collective-permute-start.3 = (f32[1025]{0:T(1024)S(1)}, f32[1025]{0:T(1024)S(1)}, u32[]{:S(2)}, u32[]{:S(2)}) collective-permute-start(f32[1025]{0:T(1024)S(1)} %fusion.30), channel_id=1, source_target_pairs={{0,96},{32,0},{64,32},{96,64},{1,97},{33,1},{65,33},{97,65},{2,98}... | collective-permute-start | bytes 12308 | tf_op jit(solution)/shard_map/ppermute | solution.py:20
  111.6 12.6 %copy-start.1 = (bf16[2048,1024]{0,1:T(8,128)(2,1)S(1)}, bf16[2048,1024]{0,1:T(8,128)(2,1)}, u32[]{:S(2)}) copy-start(bf16[2048,1024]{0,1:T(8,128)(2,1)} %get-tuple-element.23) | copy-start | bytes 12582916
  115.2 1.2 collective-permute-start.4
  116.4 4.8 %collective-permute-start.5 = (f32[1024]{0:T(1024)S(1)}, f32[1024]{0:T(1024)S(1)}, u32[]{:S(2)}, u32[]{:S(2)}) collective-permute-start(f32[1024]{0:T(1024)S(1)} %add.132), channel_id=1, source_target_pairs={{0,32},{32,64},{64,96},{96,0},{1,33},{33,65},{65,97},{97,1},{2,34}... | collective-permute-start | bytes 12296 | tf_op jit(solution)/shard_map/ppermute | solution.py:20
  116.7 5.5 %collective-permute-start.6 = (f32[1024]{0:T(1024)S(1)}, f32[1024]{0:T(1024)S(1)}, u32[]{:S(2)}, u32[]{:S(2)}) collective-permute-start(f32[1024]{0:T(1024)S(1)} %add.132), channel_id=1, source_target_pairs={{0,64},{32,96},{64,0},{96,32},{1,65},{33,97},{65,1},{97,33},{2,66}... | collective-permute-start | bytes 12296 | tf_op jit(solution)/shard_map/ppermute | solution.py:20
  120.6 3.6 %collective-permute-start.7 = (f32[1024]{0:T(1024)S(1)}, f32[1024]{0:T(1024)S(1)}, u32[]{:S(2)}, u32[]{:S(2)}) collective-permute-start(f32[1024]{0:T(1024)S(1)} %add.132), channel_id=1, source_target_pairs={{0,96},{32,0},{64,32},{96,64},{1,97},{33,1},{65,33},{97,65},{2,98}... | collective-permute-start | bytes 12296 | tf_op jit(solution)/shard_map/ppermute | solution.py:20
  136.5 13.1 %copy-start.2 = (bf16[2048,1024]{0,1:T(8,128)(2,1)S(1)}, bf16[2048,1024]{0,1:T(8,128)(2,1)}, u32[]{:S(2)}) copy-start(bf16[2048,1024]{0,1:T(8,128)(2,1)} %get-tuple-element.23) | copy-start | bytes 12582916
  136.6 26.8 %copy-start.3 = (bf16[2048,768]{0,1:T(8,128)(2,1)S(1)}, bf16[2048,768]{0,1:T(8,128)(2,1)}, u32[]{:S(2)}) copy-start(bf16[2048,768]{0,1:T(8,128)(2,1)} %all-gather.2.cloned.1.call-done) | copy-start | bytes 9437188
  140.1 1.4 collective-permute-start.8
  141.6 5.1 %collective-permute-start.10 = (f32[1024]{0:T(1024)S(1)}, f32[1024]{0:T(1024)S(1)}, u32[]{:S(2)}, u32[]{:S(2)}) collective-permute-start(f32[1024]{0:T(1024)S(1)} %add.136), channel_id=1, source_target_pairs={{0,64},{32,96},{64,0},{96,32},{1,65},{33,97},{65,1},{97,33},{2,66}... | collective-permute-start | bytes 12296 | tf_op jit(solution)/shard_map/ppermute | solution.py:20
  143.1 3.6 %collective-permute-start.11 = (f32[1024]{0:T(1024)S(1)}, f32[1024]{0:T(1024)S(1)}, u32[]{:S(2)}, u32[]{:S(2)}) collective-permute-start(f32[1024]{0:T(1024)S(1)} %add.136), channel_id=1, source_target_pairs={{0,96},{32,0},{64,32},{96,64},{1,97},{33,1},{65,33},{97,65},{2,98}... | collective-permute-start | bytes 12296 | tf_op jit(solution)/shard_map/ppermute | solution.py:20
  144.2 4.8 %collective-permute-start.9 = (f32[1024]{0:T(1024)S(1)}, f32[1024]{0:T(1024)S(1)}, u32[]{:S(2)}, u32[]{:S(2)}) collective-permute-start(f32[1024]{0:T(1024)S(1)} %add.136), channel_id=1, source_target_pairs={{0,32},{32,64},{64,96},{96,0},{1,33},{33,65},{65,97},{97,1},{2,34}... | collective-permute-start | bytes 12296 | tf_op jit(solution)/shard_map/ppermute | solution.py:20
  151.2 11.4 %all-to-all-start.3 = ((f32[16,1,2048]{2,1,0:T(1,128)}), f32[16,1,2048]{2,1,0:T(1,128)S(1)}, u32[]{:S(2)}, u32[]{:S(2)}) async-start(f32[16,1,2048]{2,1,0:T(1,128)} %broadcast_in_dim.27), calls=%async_computation.3 | async-start | bytes 262144 | tf_op jit(solution)/shard_map/all_to_all | solution.py:26
  169.1 1.7 copy-start.4
  170.9 3.5 %collective-permute-start.12 = (f32[4,96,1024]{2,1,0:T(8,128)S(1)}, f32[4,96,1024]{2,1,0:T(8,128)S(1)}, u32[]{:S(2)}, u32[]{:S(2)}) collective-permute-start(f32[4,96,1024]{2,1,0:T(8,128)S(1)} %dynamic-slice_bitcast_fusion), channel_id=1, source_target_pairs={{0,16},{16,0},{1,17},{17,1},{2,18},{18,2},{3,19},{19,3},{4,20},{20... | collective-permute-start | bytes 4718600 | tf_op jit(solution)/shard_map/ppermute | solution.py:41
  176.2 20.9 %collective-permute-start.13 = (f32[96,1024]{1,0:T(8,128)S(1)}, f32[96,1024]{1,0:T(8,128)S(1)}, u32[]{:S(2)}, u32[]{:S(2)}) collective-permute-start(f32[96,1024]{1,0:T(8,128)S(1)} %get-tuple-element.9), channel_id=1, source_target_pairs={{0,32},{32,64},{64,96},{96,0},{1,33},{33,65},{65,97},{97,1},{2,34}... | collective-permute-start | bytes 1179656 | tf_op jit(solution)/shard_map/ppermute | solution.py:45
  176.3 20.8 %collective-permute-start.14 = (f32[96,1024]{1,0:T(8,128)S(1)}, f32[96,1024]{1,0:T(8,128)S(1)}, u32[]{:S(2)}, u32[]{:S(2)}) collective-permute-start(f32[96,1024]{1,0:T(8,128)S(1)} %get-tuple-element.11), channel_id=1, source_target_pairs={{0,64},{32,96},{64,0},{96,32},{1,65},{33,97},{65,1},{97,33},{2,66}... | collective-permute-start | bytes 1179656 | tf_op jit(solution)/shard_map/ppermute | solution.py:45
  178.0 19.8 %collective-permute-start.15 = (f32[96,1024]{1,0:T(8,128)S(1)}, f32[96,1024]{1,0:T(8,128)}, u32[]{:S(2)}, u32[]{:S(2)}) collective-permute-start(f32[96,1024]{1,0:T(8,128)S(1)} %get-tuple-element.10), channel_id=1, source_target_pairs={{0,96},{32,0},{64,32},{96,64},{1,97},{33,1},{65,33},{97,65},{2,98}... | collective-permute-start | bytes 1179656 | tf_op jit(solution)/shard_map/ppermute | solution.py:45
  198.9 1.2 collective-permute-start.16
  200.2 4.8 %collective-permute-start.17 = (f32[1024]{0:T(1024)S(1)}, f32[1024]{0:T(1024)S(1)}, u32[]{:S(2)}, u32[]{:S(2)}) collective-permute-start(f32[1024]{0:T(1024)S(1)} %add.158), channel_id=1, source_target_pairs={{0,32},{32,64},{64,96},{96,0},{1,33},{33,65},{65,97},{97,1},{2,34}... | collective-permute-start | bytes 12296 | tf_op jit(solution)/shard_map/ppermute | solution.py:20
  200.4 5.2 %collective-permute-start.18 = (f32[1024]{0:T(1024)S(1)}, f32[1024]{0:T(1024)S(1)}, u32[]{:S(2)}, u32[]{:S(2)}) collective-permute-start(f32[1024]{0:T(1024)S(1)} %add.158), channel_id=1, source_target_pairs={{0,64},{32,96},{64,0},{96,32},{1,65},{33,97},{65,1},{97,33},{2,66}... | collective-permute-start | bytes 12296 | tf_op jit(solution)/shard_map/ppermute | solution.py:20
  204.0 3.6 %collective-permute-start.19 = (f32[1024]{0:T(1024)S(1)}, f32[1024]{0:T(1024)S(1)}, u32[]{:S(2)}, u32[]{:S(2)}) collective-permute-start(f32[1024]{0:T(1024)S(1)} %add.158), channel_id=1, source_target_pairs={{0,96},{32,0},{64,32},{96,64},{1,97},{33,1},{65,33},{97,65},{2,98}... | collective-permute-start | bytes 12296 | tf_op jit(solution)/shard_map/ppermute | solution.py:20
Sparse Core Ops, SparseCore 0:
  10.2 50.4 all-gather.1

commit v9 on v4

--- a/solution.py
+++ b/solution.py
@@ -46,6 +46,14 @@
     return total
 
 
+def gather_features(vectors):
+    n = lax.axis_size(CENT)
+    blocks = lax.all_to_all(
+        jnp.broadcast_to(vectors, (n, *vectors.shape)), CENT, 0, 0, tiled=False
+    )
+    return jnp.transpose(blocks, (1, 0, 2)).reshape(vectors.shape[0], -1)
+
+
 def row_step(kernel, col_scale, weights):
     partial_mass = jnp.sum(kernel.astype(jnp.float32) * col_scale[None, :], axis=1)
     masses = reduce_cent(partial_mass)
@@ -53,7 +61,7 @@
 
 
 def per_device(vectors, centroids, weights):
-    full_rows = lax.all_gather(vectors, CENT, axis=1, tiled=True)
+    full_rows = gather_features(vectors)
     local_rows = full_rows.shape[0]
     feature_dimension = full_rows.shape[1]
     local_centres = centroids.shape[0]

time: 215 us -> 202 us (0.940)
  between operations: 15 us -> 1.63 us
  waiting for transfers between devices: 99 us -> 88 us
  starting transfers between devices: 24.7 us -> 32.7 us
  blocking collectives: 34.4 us -> 38 us
  local copies, waits for them, and re-layouts: 3.42 us -> 6.39 us
    all_gather x1 -> x0, waiting for transfers between devices: 51 us -> none  [per_device(): full_rows = lax.all_gather(vectors, CENT, axis=1, tiled=True)]
    all_to_all x0 -> x1, waiting for transfers between devices: none -> 40.6 us  [gather_features(): lax.all_to_all(jnp.broadcast_to(vectors, (n, *vectors.shape)), CENT, 0, 0...]
    all_to_all x0 -> x1, starting transfers between devices: none -> 8.16 us  [gather_features(): lax.all_to_all(jnp.broadcast_to(vectors, (n, *vectors.shape)), CENT, 0, 0...]
    all_to_all x3, blocking collectives: 34.4 us -> 38 us  [reduce_cent(): lax.all_to_all(jnp.broadcast_to(x, (n, *x.shape)), CENT, 0, 0, tiled=False)]
    broadcast_in_dim x0 -> x1, local copies, waits for them, and re-layouts: none -> 2.98 us  [gather_features(): jnp.broadcast_to(vectors, (n, *vectors.shape))]
where the time goes in v9:
time: 202 us
  waiting for transfers between devices  88 us (44%)
  blocking collectives  38 us (19%)
  starting transfers between devices  32.7 us (16%)
  other arithmetic  22.1 us (11%)
  matrix products  12.9 us (6%)
  local copies, waits for them, and re-layouts  6.39 us (3%)
    all_to_all x1, waiting for transfers between devices, gather_features(): lax.all_to_all(jnp.broadcast_to(vectors, (n, *vectors.shape)), CENT, 0, 0...  40.6 us
    all_to_all x3, blocking collectives, reduce_cent(): lax.all_to_all(jnp.broadcast_to(x, (n, *x.shape)), CENT, 0, 0, tiled=False)  38 us
    ppermute x3, waiting for transfers between devices, scatter_row(): lax.ppermute(piece, 'rx', [(i, (i + k) % chips) for i in range(chips)])  18.3 us
    ppermute x16, waiting for transfers between devices, shifted_sum(): total = total + lax.ppermute(x, axis, [(i, (i + k) % n) for i in range(n)])  17.9 us
    ppermute x16, starting transfers between devices, shifted_sum(): total = total + lax.ppermute(x, axis, [(i, (i + k) % n) for i in range(n)])  17.5 us
    reduce_sum x3, other arithmetic, per_device(): jnp.sum(kernel.astype(jnp.float32) * row_scale[:, None], axis=0)  9.83 us
    all_to_all x1, starting transfers between devices, gather_features(): lax.all_to_all(jnp.broadcast_to(vectors, (n, *vectors.shape)), CENT, 0, 0...  8.16 us
    all_to_all x1, waiting for transfers between devices, reduce_cent(): lax.all_to_all(jnp.broadcast_to(x, (n, *x.shape)), CENT, 0, 0, tiled=False)  7.82 us
  transfers between devices with their start and end apart: 22, of which 19 were waited for; matrix products, arithmetic and copies ran while one was open for 1% of the time, Pallas kernels for 0%

profile of v9, /device:TPU:0, one launch (start us, length us, event | category | flops | bytes accessed | tf_op | source)
XLA Modules:
  0.0 201.6 jit_solution(14099598243596317166)
XLA Ops:
  0.6 3.0 %broadcast_in_dim.12 = bf16[16,2048,48]{1,2,0:T(8,128)(2,1)} broadcast(bf16[2048,48]{0,1:T(8,128)(2,1)} %param.3), dimensions={1,2} | broadcast | bytes 3342336 | tf_op jit(solution)/shard_map/broadcast_in_dim | solution.py:52
  3.6 8.2 %all-to-all-start = ((bf16[16,2048,48]{1,2,0:T(8,128)(2,1)}), bf16[16,2048,48]{1,2,0:T(8,128)(2,1)S(1)}, u32[]{:S(2)}, u32[]{:S(2)}) async-start(bf16[16,2048,48]{1,2,0:T(8,128)(2,1)} %broadcast_in_dim.12), calls=%async_computation | async-start | bytes 6291456 | tf_op jit(solution)/shard_map/all_to_all | solution.py:51
  11.8 1.8 multiply_reduce_fusion.1
  13.6 40.6 %all-to-all-done = bf16[16,2048,48]{1,2,0:T(8,128)(2,1)S(1)} async-done(((bf16[16,2048,48]{1,2,0:T(8,128)(2,1)}), bf16[16,2048,48]{1,2,0:T(8,128)(2,1)S(1)}, u32[]{:S(2)}, u32[]{:S(2)}) %all-to-all-start) | async-done | bytes 3145760 | tf_op jit(solution)/shard_map/all_to_all | solution.py:51
  54.2 0.7 multiply_reduce_fusion
  54.9 7.2 %fusion = (f32[2048]{0:T(1024)S(1)}, bf16[2048,1024]{0,1:T(8,128)(2,1)}) fusion(f32[1024]{0:T(1024)S(1)} %add_rsqrt_fusion.2, f32[2048]{0:T(1024)S(1)} %add_rsqrt_fusion, bf16[1024,768]{1,0:T(8,128)(2,1)} %param.4, bf16[2048,768]{0,1:T(8,128)(2,1)S(1)} %bitcast.29), kind=kOutput, calls=%fused_computation.8 | convolution fusion | flops 3235903488 | bytes 8933376 | tf_op jit(solution)/shard_map/dot_general | solution.py:75
  62.1 15.5 %all_to_all.29 = f32[16,1,2048]{2,1,0:T(1,128)S(1)} all-to-all(f32[16,1,2048]{2,1,0:T(1,128)S(1)} %broadcast_in_dim.13), channel_id=1, replica_groups=mesh['rx'=4,'rc'=2,'cy'=4,'cz'=4] {'cy','cz'}, dimensions={0} | all-to-all | bytes 262144 | tf_op jit(solution)/shard_map/all_to_all | solution.py:26
  77.6 0.1 reduce_sum.138
  77.7 0.6 fusion.18
  78.3 3.4 %fusion.1 = f32[1024]{0:T(1024)S(1)} fusion(bf16[2048,1024]{0,1:T(8,128)(2,1)} %get-tuple-element.15, f32[2048]{0:T(1024)S(1)} %get-tuple-element.12), kind=kLoop, calls=%fused_computation.9 | loop fusion | flops 6290432 | bytes 4206592 | tf_op jit(solution)/shard_map/reduce_sum | solution.py:87
  81.7 0.7 pad_maximum_fusion
  82.5 1.2 collective-permute-done
  83.6 0.7 fusion.15
  84.3 1.6 collective-permute-start.1
  85.8 2.7 %collective-permute-start.2 = (f32[1025]{0:T(1024)S(1)}, f32[1025]{0:T(1024)S(1)}, u32[]{:S(2)}, u32[]{:S(2)}) collective-permute-start(f32[1025]{0:T(1024)S(1)} %fusion.15), channel_id=1, source_target_pairs={{0,64},{32,96},{64,0},{96,32},{1,65},{33,97},{65,1},{97,33},{2,66}... | collective-permute-start | bytes 12308 | tf_op jit(solution)/shard_map/ppermute | solution.py:20
  88.6 1.4 collective-permute-start.3
  90.0 1.0 collective-permute-done.2
  91.0 1.2 collective-permute-done.3
  92.2 0.5 slice.8
  93.4 0.9 fusion.2
  94.4 11.2 %all_to_all.30 = f32[16,1,2048]{2,1,0:T(1,128)S(1)} all-to-all(f32[16,1,2048]{2,1,0:T(1,128)S(1)} %broadcast_in_dim.15), channel_id=1, replica_groups=mesh['rx'=4,'rc'=2,'cy'=4,'cz'=4] {'cy','cz'}, dimensions={0} | all-to-all | bytes 262144 | tf_op jit(solution)/shard_map/all_to_all | solution.py:26
  105.6 0.1 reduce_sum.142
  105.8 3.2 %fusion.3 = f32[1024]{0:T(1024)S(1)} fusion(bf16[2048,1024]{0,1:T(8,128)(2,1)} %get-tuple-element.15, f32[2048]{0:T(1024)S(1)} %div.61), kind=kLoop, calls=%fused_computation.11 | loop fusion | flops 6290432 | bytes 4206592 | tf_op jit(solution)/shard_map/reduce_sum | solution.py:87
  109.1 1.2 collective-permute-done.4
  110.2 0.3 collective-permute-start.5
  110.5 3.8 %collective-permute-start.6 = (f32[1024]{0:T(1024)S(1)}, f32[1024]{0:T(1024)S(1)}, u32[]{:S(2)}, u32[]{:S(2)}) collective-permute-start(f32[1024]{0:T(1024)S(1)} %add.132), channel_id=1, source_target_pairs={{0,64},{32,96},{64,0},{96,32},{1,65},{33,97},{65,1},{97,33},{2,66}... | collective-permute-start | bytes 12296 | tf_op jit(solution)/shard_map/ppermute | solution.py:20
  114.4 0.7 collective-permute-done.5
  115.0 0.9 collective-permute-done.6
  116.0 2.0 collective-permute-done.7
  118.0 0.9 fusion.4
  118.9 11.2 %all_to_all.31 = f32[16,1,2048]{2,1,0:T(1,128)S(1)} all-to-all(f32[16,1,2048]{2,1,0:T(1,128)S(1)} %broadcast_in_dim.16), channel_id=1, replica_groups=mesh['rx'=4,'rc'=2,'cy'=4,'cz'=4] {'cy','cz'}, dimensions={0} | all-to-all | bytes 262144 | tf_op jit(solution)/shard_map/all_to_all | solution.py:26
  130.2 0.1 reduce_sum.145
  130.3 3.2 %fusion.5 = f32[1024]{0:T(1024)S(1)} fusion(bf16[2048,1024]{0,1:T(8,128)(2,1)} %get-tuple-element.15, f32[2048]{0:T(1024)S(1)} %div.63), kind=kLoop, calls=%fused_computation.13 | loop fusion | flops 6290432 | bytes 4206592 | tf_op jit(solution)/shard_map/reduce_sum | solution.py:87
  133.6 1.2 collective-permute-done.8
  134.8 1.5 collective-permute-start.10
  136.3 1.1 collective-permute-start.11
  137.4 0.9 collective-permute-start.9
  138.3 1.6 collective-permute-done.10
  139.9 2.4 %collective-permute-done.9 = f32[1024]{0:T(1024)S(1)} collective-permute-done((f32[1024]{0:T(1024)S(1)}, f32[1024]{0:T(1024)S(1)}, u32[]{:S(2)}, u32[]{:S(2)}) %collective-permute-start.9) | collective-permute-done | bytes 4128 | tf_op jit(solution)/shard_map/ppermute | solution.py:20
  142.2 0.6 multiply_log_fusion
  142.9 0.9 fusion.6
  143.7 0.7 broadcast_in_dim.34
  144.5 3.6 %all-to-all-start.4 = ((f32[16,1,2048]{2,1,0:T(1,128)}), f32[16,1,2048]{2,1,0:T(1,128)S(1)}, u32[]{:S(2)}, u32[]{:S(2)}) async-start(f32[16,1,2048]{2,1,0:T(1,128)} %broadcast_in_dim.34), calls=%async_computation.4 | async-start | bytes 262144 | tf_op jit(solution)/shard_map/all_to_all | solution.py:26
  148.1 7.8 %all-to-all-done.4 = f32[16,1,2048]{2,1,0:T(1,128)S(1)} async-done(((f32[16,1,2048]{2,1,0:T(1,128)}), f32[16,1,2048]{2,1,0:T(1,128)S(1)}, u32[]{:S(2)}, u32[]{:S(2)}) %all-to-all-start.4) | async-done | bytes 131104 | tf_op jit(solution)/shard_map/all_to_all | solution.py:26
  155.9 0.1 reduce_sum.148
  156.0 0.6 fusion.16
  156.6 5.7 %fusion.9 = f32[1024,768]{0,1:T(8,128)S(1)} fusion(bf16[2048,768]{0,1:T(8,128)(2,1)S(1)} %bitcast.30, bf16[2048,1024]{0,1:T(8,128)(2,1)} %get-tuple-element.15, f32[2048]{0:T(1024)S(1)} %get-tuple-element.6, f32[1024]{0:T(1024)S(1)} %get-tuple-element.4), kind=kOutput, calls=%fused_computation.19 | convolution fusion | flops 3229614080 | bytes 10498048 | tf_op jit(solution)/shard_map/dot_general | solution.py:98
  162.3 1.7 copy-done.3
  164.0 0.2 dynamic-slice_bitcast_fusion
  164.3 3.4 %collective-permute-done.12 = f32[4,96,1024]{2,1,0:T(8,128)S(1)} collective-permute-done((f32[4,96,1024]{2,1,0:T(8,128)S(1)}, f32[4,96,1024]{2,1,0:T(8,128)S(1)}, u32[]{:S(2)}, u32[]{:S(2)}) %collective-permute-start.12) | collective-permute-done | bytes 1572896 | tf_op jit(solution)/shard_map/ppermute | solution.py:41
  167.6 1.7 bitcast_add_fusion
  169.3 0.1 dynamic-slice_bitcast_fusion.3
  169.5 1.7 collective-permute-start.14
  171.2 1.6 collective-permute-start.15
  172.8 17.6 %collective-permute-done.13 = f32[96,1024]{1,0:T(8,128)S(1)} collective-permute-done((f32[96,1024]{1,0:T(8,128)S(1)}, f32[96,1024]{1,0:T(8,128)S(1)}, u32[]{:S(2)}, u32[]{:S(2)}) %collective-permute-start.13) | collective-permute-done | bytes 393248 | tf_op jit(solution)/shard_map/ppermute | solution.py:45
  190.3 0.7 collective-permute-done.15
  191.0 1.1 multiply_reduce_fusion.2
  192.2 1.2 collective-permute-done.16
  193.4 0.2 collective-permute-start.17
  193.6 3.6 %collective-permute-start.18 = (f32[1024]{0:T(1024)S(1)}, f32[1024]{0:T(1024)S(1)}, u32[]{:S(2)}, u32[]{:S(2)}) collective-permute-start(f32[1024]{0:T(1024)S(1)} %add.158), channel_id=1, source_target_pairs={{0,64},{32,96},{64,0},{96,32},{1,65},{33,97},{65,1},{97,33},{2,66}... | collective-permute-start | bytes 12296 | tf_op jit(solution)/shard_map/ppermute | solution.py:20
  197.2 1.0 collective-permute-done.17
  198.2 0.6 collective-permute-done.18
  198.8 2.0 collective-permute-done.19
  200.8 0.8 broadcast_multiply_fusion
  (34 shorter events, 0.8 us)
Async XLA Ops:
  3.6 50.6 %all-to-all-start = ((bf16[16,2048,48]{1,2,0:T(8,128)(2,1)}), bf16[16,2048,48]{1,2,0:T(8,128)(2,1)S(1)}, u32[]{:S(2)}, u32[]{:S(2)}) async-start(bf16[16,2048,48]{1,2,0:T(8,128)(2,1)} %broadcast_in_dim.12), calls=%async_computation | async-start | bytes 6291456 | tf_op jit(solution)/shard_map/all_to_all | solution.py:51
  54.9 22.9 %copy-start.4 = (f32[2048]{0:T(1024)S(1)}, f32[2048]{0:T(1024)}, u32[]{:S(2)}) copy-start(f32[2048]{0:T(1024)} %param.5) | copy-start | bytes 24580
  77.7 15.7 %copy-start = (bf16[2048,1024]{0,1:T(8,128)(2,1)S(1)}, bf16[2048,1024]{0,1:T(8,128)(2,1)}, u32[]{:S(2)}) copy-start(bf16[2048,1024]{0,1:T(8,128)(2,1)} %get-tuple-element.15) | copy-start | bytes 12582916
  82.4 1.3 collective-permute-start
  84.3 5.7 %collective-permute-start.1 = (f32[1025]{0:T(1024)S(1)}, f32[1025]{0:T(1024)S(1)}, u32[]{:S(2)}, u32[]{:S(2)}) collective-permute-start(f32[1025]{0:T(1024)S(1)} %fusion.15), channel_id=1, source_target_pairs={{0,32},{32,64},{64,96},{96,0},{1,33},{33,65},{65,97},{97,1},{2,34}... | collective-permute-start | bytes 12308 | tf_op jit(solution)/shard_map/ppermute | solution.py:20
  85.8 5.2 %collective-permute-start.2 = (f32[1025]{0:T(1024)S(1)}, f32[1025]{0:T(1024)S(1)}, u32[]{:S(2)}, u32[]{:S(2)}) collective-permute-start(f32[1025]{0:T(1024)S(1)} %fusion.15), channel_id=1, source_target_pairs={{0,64},{32,96},{64,0},{96,32},{1,65},{33,97},{65,1},{97,33},{2,66}... | collective-permute-start | bytes 12308 | tf_op jit(solution)/shard_map/ppermute | solution.py:20
  88.6 3.7 %collective-permute-start.3 = (f32[1025]{0:T(1024)S(1)}, f32[1025]{0:T(1024)S(1)}, u32[]{:S(2)}, u32[]{:S(2)}) collective-permute-start(f32[1025]{0:T(1024)S(1)} %fusion.15), channel_id=1, source_target_pairs={{0,96},{32,0},{64,32},{96,64},{1,97},{33,1},{65,33},{97,65},{2,98}... | collective-permute-start | bytes 12308 | tf_op jit(solution)/shard_map/ppermute | solution.py:20
  105.7 12.2 %copy-start.1 = (bf16[2048,1024]{0,1:T(8,128)(2,1)S(1)}, bf16[2048,1024]{0,1:T(8,128)(2,1)}, u32[]{:S(2)}) copy-start(bf16[2048,1024]{0,1:T(8,128)(2,1)} %get-tuple-element.15) | copy-start | bytes 12582916
  109.0 1.2 collective-permute-start.4
  110.2 4.8 %collective-permute-start.5 = (f32[1024]{0:T(1024)S(1)}, f32[1024]{0:T(1024)S(1)}, u32[]{:S(2)}, u32[]{:S(2)}) collective-permute-start(f32[1024]{0:T(1024)S(1)} %add.132), channel_id=1, source_target_pairs={{0,32},{32,64},{64,96},{96,0},{1,33},{33,65},{65,97},{97,1},{2,34}... | collective-permute-start | bytes 12296 | tf_op jit(solution)/shard_map/ppermute | solution.py:20
  110.5 5.5 %collective-permute-start.6 = (f32[1024]{0:T(1024)S(1)}, f32[1024]{0:T(1024)S(1)}, u32[]{:S(2)}, u32[]{:S(2)}) collective-permute-start(f32[1024]{0:T(1024)S(1)} %add.132), channel_id=1, source_target_pairs={{0,64},{32,96},{64,0},{96,32},{1,65},{33,97},{65,1},{97,33},{2,66}... | collective-permute-start | bytes 12296 | tf_op jit(solution)/shard_map/ppermute | solution.py:20
  114.3 3.6 %collective-permute-start.7 = (f32[1024]{0:T(1024)S(1)}, f32[1024]{0:T(1024)S(1)}, u32[]{:S(2)}, u32[]{:S(2)}) collective-permute-start(f32[1024]{0:T(1024)S(1)} %add.132), channel_id=1, source_target_pairs={{0,96},{32,0},{64,32},{96,64},{1,97},{33,1},{65,33},{97,65},{2,98}... | collective-permute-start | bytes 12296 | tf_op jit(solution)/shard_map/ppermute | solution.py:20
  130.3 12.6 %copy-start.2 = (bf16[2048,1024]{0,1:T(8,128)(2,1)S(1)}, bf16[2048,1024]{0,1:T(8,128)(2,1)}, u32[]{:S(2)}) copy-start(bf16[2048,1024]{0,1:T(8,128)(2,1)} %get-tuple-element.15) | copy-start | bytes 12582916
  133.5 1.2 collective-permute-start.8
  134.8 5.1 %collective-permute-start.10 = (f32[1024]{0:T(1024)S(1)}, f32[1024]{0:T(1024)S(1)}, u32[]{:S(2)}, u32[]{:S(2)}) collective-permute-start(f32[1024]{0:T(1024)S(1)} %add.136), channel_id=1, source_target_pairs={{0,64},{32,96},{64,0},{96,32},{1,65},{33,97},{65,1},{97,33},{2,66}... | collective-permute-start | bytes 12296 | tf_op jit(solution)/shard_map/ppermute | solution.py:20
  136.3 3.6 %collective-permute-start.11 = (f32[1024]{0:T(1024)S(1)}, f32[1024]{0:T(1024)S(1)}, u32[]{:S(2)}, u32[]{:S(2)}) collective-permute-start(f32[1024]{0:T(1024)S(1)} %add.136), channel_id=1, source_target_pairs={{0,96},{32,0},{64,32},{96,64},{1,97},{33,1},{65,33},{97,65},{2,98}... | collective-permute-start | bytes 12296 | tf_op jit(solution)/shard_map/ppermute | solution.py:20
  137.4 4.8 %collective-permute-start.9 = (f32[1024]{0:T(1024)S(1)}, f32[1024]{0:T(1024)S(1)}, u32[]{:S(2)}, u32[]{:S(2)}) collective-permute-start(f32[1024]{0:T(1024)S(1)} %add.136), channel_id=1, source_target_pairs={{0,32},{32,64},{64,96},{96,0},{1,33},{33,65},{65,97},{97,1},{2,34}... | collective-permute-start | bytes 12296 | tf_op jit(solution)/shard_map/ppermute | solution.py:20
  144.5 11.4 %all-to-all-start.4 = ((f32[16,1,2048]{2,1,0:T(1,128)}), f32[16,1,2048]{2,1,0:T(1,128)S(1)}, u32[]{:S(2)}, u32[]{:S(2)}) async-start(f32[16,1,2048]{2,1,0:T(1,128)} %broadcast_in_dim.34), calls=%async_computation.4 | async-start | bytes 262144 | tf_op jit(solution)/shard_map/all_to_all | solution.py:26
  162.3 1.7 copy-start.3
  164.2 3.5 %collective-permute-start.12 = (f32[4,96,1024]{2,1,0:T(8,128)S(1)}, f32[4,96,1024]{2,1,0:T(8,128)S(1)}, u32[]{:S(2)}, u32[]{:S(2)}) collective-permute-start(f32[4,96,1024]{2,1,0:T(8,128)S(1)} %dynamic-slice_bitcast_fusion), channel_id=1, source_target_pairs={{0,16},{16,0},{1,17},{17,1},{2,18},{18,2},{3,19},{19,3},{4,20},{20... | collective-permute-start | bytes 4718600 | tf_op jit(solution)/shard_map/ppermute | solution.py:41
  169.5 20.9 %collective-permute-start.13 = (f32[96,1024]{1,0:T(8,128)S(1)}, f32[96,1024]{1,0:T(8,128)S(1)}, u32[]{:S(2)}, u32[]{:S(2)}) collective-permute-start(f32[96,1024]{1,0:T(8,128)S(1)} %get-tuple-element.9), channel_id=1, source_target_pairs={{0,32},{32,64},{64,96},{96,0},{1,33},{33,65},{65,97},{97,1},{2,34}... | collective-permute-start | bytes 1179656 | tf_op jit(solution)/shard_map/ppermute | solution.py:45
  169.5 20.8 %collective-permute-start.14 = (f32[96,1024]{1,0:T(8,128)S(1)}, f32[96,1024]{1,0:T(8,128)S(1)}, u32[]{:S(2)}, u32[]{:S(2)}) collective-permute-start(f32[96,1024]{1,0:T(8,128)S(1)} %get-tuple-element.11), channel_id=1, source_target_pairs={{0,64},{32,96},{64,0},{96,32},{1,65},{33,97},{65,1},{97,33},{2,66}... | collective-permute-start | bytes 1179656 | tf_op jit(solution)/shard_map/ppermute | solution.py:45
  171.2 19.8 %collective-permute-start.15 = (f32[96,1024]{1,0:T(8,128)S(1)}, f32[96,1024]{1,0:T(8,128)}, u32[]{:S(2)}, u32[]{:S(2)}) collective-permute-start(f32[96,1024]{1,0:T(8,128)S(1)} %get-tuple-element.10), channel_id=1, source_target_pairs={{0,96},{32,0},{64,32},{96,64},{1,97},{33,1},{65,33},{97,65},{2,98}... | collective-permute-start | bytes 1179656 | tf_op jit(solution)/shard_map/ppermute | solution.py:45
  192.2 1.2 collective-permute-start.16
  193.4 4.8 %collective-permute-start.17 = (f32[1024]{0:T(1024)S(1)}, f32[1024]{0:T(1024)S(1)}, u32[]{:S(2)}, u32[]{:S(2)}) collective-permute-start(f32[1024]{0:T(1024)S(1)} %add.158), channel_id=1, source_target_pairs={{0,32},{32,64},{64,96},{96,0},{1,33},{33,65},{65,97},{97,1},{2,34}... | collective-permute-start | bytes 12296 | tf_op jit(solution)/shard_map/ppermute | solution.py:20
  193.6 5.2 %collective-permute-start.18 = (f32[1024]{0:T(1024)S(1)}, f32[1024]{0:T(1024)S(1)}, u32[]{:S(2)}, u32[]{:S(2)}) collective-permute-start(f32[1024]{0:T(1024)S(1)} %add.158), channel_id=1, source_target_pairs={{0,64},{32,96},{64,0},{96,32},{1,65},{33,97},{65,1},{97,33},{2,66}... | collective-permute-start | bytes 12296 | tf_op jit(solution)/shard_map/ppermute | solution.py:20
  197.2 3.6 %collective-permute-start.19 = (f32[1024]{0:T(1024)S(1)}, f32[1024]{0:T(1024)S(1)}, u32[]{:S(2)}, u32[]{:S(2)}) collective-permute-start(f32[1024]{0:T(1024)S(1)} %add.158), channel_id=1, source_target_pairs={{0,96},{32,0},{64,32},{96,64},{1,97},{33,1},{65,33},{97,65},{2,98}... | collective-permute-start | bytes 12296 | tf_op jit(solution)/shard_map/ppermute | solution.py:20

commit v10 on v9

--- a/solution.py
+++ b/solution.py
@@ -31,14 +31,22 @@
     return shifted_sum(shifted_sum(x, "rc"), "rx")
 
 
-def scatter_row(x):
+def summed_block(full_rows, transport):
     chips, cores = lax.axis_size("rx"), lax.axis_size("rc")
     rx, rc = lax.axis_index("rx"), lax.axis_index("rc")
-    blocks = x.reshape(chips, cores, x.shape[0] // (chips * cores), *x.shape[1:])
-    half = lax.dynamic_index_in_dim(blocks, rc, 1, keepdims=False)
-    for k in range(1, cores):
-        piece = lax.dynamic_index_in_dim(blocks, (rc + k) % cores, 1, keepdims=False)
-        half = half + lax.ppermute(piece, "rc", [(i, (i + k) % cores) for i in range(cores)])
+    rows, features = full_rows.shape
+    block = features // (chips * cores)
+    by_core = full_rows.reshape(rows, chips, cores, block)
+
+    def product(core):
+        part = lax.dynamic_index_in_dim(by_core, core, 2, keepdims=False)
+        return lax.dot_general(
+            part, transport, (((0,), (0,)), ((), ())), preferred_element_type=jnp.float32
+        )
+
+    sent = product((rc + 1) % cores)
+    received = lax.ppermute(sent, "rc", [(i, (i + 1) % cores) for i in range(cores)])
+    half = lax.optimization_barrier(product(rc)) + received
     total = lax.dynamic_index_in_dim(half, rx, 0, keepdims=False)
     for k in range(1, chips):
         piece = lax.dynamic_index_in_dim(half, (rx + k) % chips, 0, keepdims=False)
@@ -95,10 +103,7 @@
     transport = (row_scale[:, None] * kernel.astype(jnp.float32) * col_scale[None, :]).astype(
         jnp.bfloat16
     )
-    term = lax.dot_general(
-        full_rows, transport, (((0,), (0,)), ((), ())), preferred_element_type=jnp.float32
-    )
-    own_summed = scatter_row(term)
+    own_summed = summed_block(full_rows, transport)
     square_sum = reduce_row(jnp.sum(own_summed * own_summed, axis=0))
     new_centroids = own_summed * lax.rsqrt(square_sum / feature_dimension + 1e-06)[None, :]
     return (new_centroids, jnp.log(row_scale), jnp.log(centre_total * col_scale))

time: 202 us -> 200 us (0.990)
  starting transfers between devices: 32.7 us -> 27.5 us
  matrix products: 12.9 us -> 16.5 us
    ppermute x16, starting transfers between devices: 17.5 us -> 12.8 us  [shifted_sum(): total = total + lax.ppermute(x, axis, [(i, (i + k) % n) for i in range(n)])]
    dot_general x1 -> x2, matrix products: 5.69 us -> 9.33 us  [product(): lax.dot_general(part, transport, (((0,), (0,)), ((), ())), preferred_elem...]
    ppermute x16, waiting for transfers between devices: 17.9 us -> 21 us  [shifted_sum(): total = total + lax.ppermute(x, axis, [(i, (i + k) % n) for i in range(n)])]
    ppermute x4, waiting for transfers between devices: 21.6 us -> 19.3 us  [the longest x3 19.3 us: summed_block(): lax.ppermute(piece, 'rx', [(i, (i + k) % chips) for i in range(chips)])]
  transfers between devices with their start and end apart: 22 -> 22, of which waited for: 19 -> 20; matrix products, arithmetic and copies ran while one was open for 1% -> 3% of each run, Pallas kernels for 0% -> 0%
where the time goes in v10:
time: 200 us; the launch traced here: 199 us
  waiting for transfers between devices  88.7 us (44%)
  blocking collectives  38 us (19%)
  starting transfers between devices  27.5 us (14%)
  other arithmetic  22.2 us (11%)
  matrix products  16.5 us (8%)
  local copies, waits for them, and re-layouts  4.57 us (2%)
    all_to_all x1, waiting for transfers between devices, gather_features(): lax.all_to_all(jnp.broadcast_to(vectors, (n, *vectors.shape)), CENT, 0, 0...  40.6 us
    all_to_all x3, blocking collectives, reduce_cent(): lax.all_to_all(jnp.broadcast_to(x, (n, *x.shape)), CENT, 0, 0, tiled=False)  38 us
    ppermute x16, waiting for transfers between devices, shifted_sum(): total = total + lax.ppermute(x, axis, [(i, (i + k) % n) for i in range(n)])  21 us
    ppermute x3, waiting for transfers between devices, summed_block(): lax.ppermute(piece, 'rx', [(i, (i + k) % chips) for i in range(chips)])  19.3 us
    ppermute x16, starting transfers between devices, shifted_sum(): total = total + lax.ppermute(x, axis, [(i, (i + k) % n) for i in range(n)])  12.8 us
    reduce_sum x3, other arithmetic, per_device(): jnp.sum(kernel.astype(jnp.float32) * row_scale[:, None], axis=0)  9.83 us
    dot_general x2, matrix products, product(): lax.dot_general(part, transport, (((0,), (0,)), ((), ())), preferred_elem...  9.33 us
    all_to_all x1, starting transfers between devices, gather_features(): lax.all_to_all(jnp.broadcast_to(vectors, (n, *vectors.shape)), CENT, 0, 0...  8.16 us
  transfers between devices with their start and end apart: 22, of which 20 were waited for; matrix products, arithmetic and copies ran while one was open for 3% of the time, Pallas kernels for 0%

profile of v10, /device:TPU:0, one launch (start us, length us, event | category | flops | bytes accessed | tf_op | source)
XLA Modules:
  0.0 199.0 jit_solution(12434602511333616571)
XLA Ops:
  0.6 3.0 %broadcast_in_dim.12 = bf16[16,2048,48]{1,2,0:T(8,128)(2,1)} broadcast(bf16[2048,48]{0,1:T(8,128)(2,1)} %param.3), dimensions={1,2} | broadcast | bytes 3342336 | tf_op jit(solution)/shard_map/broadcast_in_dim | solution.py:60
  3.6 8.2 %all-to-all-start = ((bf16[16,2048,48]{1,2,0:T(8,128)(2,1)}), bf16[16,2048,48]{1,2,0:T(8,128)(2,1)S(1)}, u32[]{:S(2)}, u32[]{:S(2)}) async-start(bf16[16,2048,48]{1,2,0:T(8,128)(2,1)} %broadcast_in_dim.12), calls=%async_computation | async-start | bytes 6291456 | tf_op jit(solution)/shard_map/all_to_all | solution.py:59
  11.8 1.8 multiply_reduce_fusion.1
  13.6 40.6 %all-to-all-done = bf16[16,2048,48]{1,2,0:T(8,128)(2,1)S(1)} async-done(((bf16[16,2048,48]{1,2,0:T(8,128)(2,1)}), bf16[16,2048,48]{1,2,0:T(8,128)(2,1)S(1)}, u32[]{:S(2)}, u32[]{:S(2)}) %all-to-all-start) | async-done | bytes 3145760 | tf_op jit(solution)/shard_map/all_to_all | solution.py:59
  54.2 0.7 multiply_reduce_fusion
  54.9 7.2 %fusion = (f32[2048]{0:T(1024)S(1)}, bf16[2048,1024]{0,1:T(8,128)(2,1)}) fusion(f32[1024]{0:T(1024)S(1)} %add_rsqrt_fusion.2, f32[2048]{0:T(1024)S(1)} %add_rsqrt_fusion, bf16[1024,768]{1,0:T(8,128)(2,1)} %param.4, bf16[2048,768]{0,1:T(8,128)(2,1)S(1)} %bitcast.34), kind=kOutput, calls=%fused_computation.8 | convolution fusion | flops 3235903488 | bytes 8933376 | tf_op jit(solution)/shard_map/dot_general | solution.py:83
  62.1 15.5 %all_to_all.29 = f32[16,1,2048]{2,1,0:T(1,128)S(1)} all-to-all(f32[16,1,2048]{2,1,0:T(1,128)S(1)} %broadcast_in_dim.13), channel_id=1, replica_groups=mesh['rx'=4,'rc'=2,'cy'=4,'cz'=4] {'cy','cz'}, dimensions={0} | all-to-all | bytes 262144 | tf_op jit(solution)/shard_map/all_to_all | solution.py:26
  77.6 0.1 reduce_sum.138
  77.7 0.6 fusion.25
  78.3 3.4 %fusion.1 = f32[1024]{0:T(1024)S(1)} fusion(bf16[2048,1024]{0,1:T(8,128)(2,1)} %get-tuple-element.15, f32[2048]{0:T(1024)S(1)} %get-tuple-element.12), kind=kLoop, calls=%fused_computation.9 | loop fusion | flops 6290432 | bytes 4206592 | tf_op jit(solution)/shard_map/reduce_sum | solution.py:95
  81.7 0.7 pad_maximum_fusion
  82.5 1.2 collective-permute-done
  83.6 0.7 fusion.22
  84.3 2.8 %collective-permute-start.3 = (f32[1025]{0:T(1024)S(1)}, f32[1025]{0:T(1024)S(1)}, u32[]{:S(2)}, u32[]{:S(2)}) collective-permute-start(f32[1025]{0:T(1024)S(1)} %fusion.22), channel_id=1, source_target_pairs={{0,96},{32,0},{64,32},{96,64},{1,97},{33,1},{65,33},{97,65},{2,98}... | collective-permute-start | bytes 12308 | tf_op jit(solution)/shard_map/ppermute | solution.py:20
  87.1 0.8 collective-permute-start.2
  87.9 0.9 collective-permute-start.1
  88.8 3.5 %collective-permute-done.2 = f32[1025]{0:T(1024)S(1)} collective-permute-done((f32[1025]{0:T(1024)S(1)}, f32[1025]{0:T(1024)S(1)}, u32[]{:S(2)}, u32[]{:S(2)}) %collective-permute-start.2) | collective-permute-done | bytes 4132 | tf_op jit(solution)/shard_map/ppermute | solution.py:20
  92.3 0.5 collective-permute-done.1
  92.8 0.5 slice.8
  94.0 0.9 fusion.2
  94.9 11.2 %all_to_all.30 = f32[16,1,2048]{2,1,0:T(1,128)S(1)} all-to-all(f32[16,1,2048]{2,1,0:T(1,128)S(1)} %broadcast_in_dim.15), channel_id=1, replica_groups=mesh['rx'=4,'rc'=2,'cy'=4,'cz'=4] {'cy','cz'}, dimensions={0} | all-to-all | bytes 262144 | tf_op jit(solution)/shard_map/all_to_all | solution.py:26
  106.3 3.2 %fusion.3 = f32[1024]{0:T(1024)S(1)} fusion(bf16[2048,1024]{0,1:T(8,128)(2,1)} %get-tuple-element.15, f32[2048]{0:T(1024)S(1)} %div.61), kind=kLoop, calls=%fused_computation.11 | loop fusion | flops 6290432 | bytes 4206592 | tf_op jit(solution)/shard_map/reduce_sum | solution.py:95
  109.6 1.2 collective-permute-done.4
  110.8 0.3 collective-permute-start.7
  111.1 1.4 collective-permute-start.6
  112.5 1.2 collective-permute-start.5
  113.7 0.7 collective-permute-done.7
  114.4 1.8 collective-permute-done.6
  116.2 1.1 collective-permute-done.5
  117.4 0.9 fusion.4
  118.3 11.2 %all_to_all.31 = f32[16,1,2048]{2,1,0:T(1,128)S(1)} all-to-all(f32[16,1,2048]{2,1,0:T(1,128)S(1)} %broadcast_in_dim.16), channel_id=1, replica_groups=mesh['rx'=4,'rc'=2,'cy'=4,'cz'=4] {'cy','cz'}, dimensions={0} | all-to-all | bytes 262144 | tf_op jit(solution)/shard_map/all_to_all | solution.py:26
  129.7 3.2 %fusion.5 = f32[1024]{0:T(1024)S(1)} fusion(bf16[2048,1024]{0,1:T(8,128)(2,1)} %get-tuple-element.15, f32[2048]{0:T(1024)S(1)} %div.63), kind=kLoop, calls=%fused_computation.13 | loop fusion | flops 6290432 | bytes 4206592 | tf_op jit(solution)/shard_map/reduce_sum | solution.py:95
  133.0 1.2 collective-permute-done.8
  134.2 1.7 collective-permute-start.11
  135.9 0.9 collective-permute-start.10
  136.8 1.0 collective-permute-done.11
  137.8 3.2 %collective-permute-done.10 = f32[1024]{0:T(1024)S(1)} collective-permute-done((f32[1024]{0:T(1024)S(1)}, f32[1024]{0:T(1024)S(1)}, u32[]{:S(2)}, u32[]{:S(2)}) %collective-permute-start.10) | collective-permute-done | bytes 4128 | tf_op jit(solution)/shard_map/ppermute | solution.py:20
  141.0 0.6 collective-permute-done.9
  141.6 0.6 multiply_log_fusion
  142.2 0.9 fusion.6
  143.1 0.7 broadcast_in_dim.34
  143.9 3.6 %all-to-all-start.4 = ((f32[16,1,2048]{2,1,0:T(1,128)}), f32[16,1,2048]{2,1,0:T(1,128)S(1)}, u32[]{:S(2)}, u32[]{:S(2)}) async-start(f32[16,1,2048]{2,1,0:T(1,128)} %broadcast_in_dim.34), calls=%async_computation.4 | async-start | bytes 262144 | tf_op jit(solution)/shard_map/all_to_all | solution.py:26
  147.5 7.8 %all-to-all-done.4 = f32[16,1,2048]{2,1,0:T(1,128)S(1)} async-done(((f32[16,1,2048]{2,1,0:T(1,128)}), f32[16,1,2048]{2,1,0:T(1,128)S(1)}, u32[]{:S(2)}, u32[]{:S(2)}) %all-to-all-start.4) | async-done | bytes 131104 | tf_op jit(solution)/shard_map/all_to_all | solution.py:26
  155.4 0.6 fusion.23
  156.0 5.3 %fusion.10 = f32[4,96,1024]{2,1,0:T(8,128)} fusion(bf16[2048,1024]{0,1:T(8,128)(2,1)} %get-tuple-element.15, f32[2048]{0:T(1024)S(1)} %get-tuple-element.6, f32[1024]{0:T(1024)S(1)} %get-tuple-element.4, bf16[2048,4,2,96]{0,3,2,1:T(8,128)(2,1)S(1)} %bitcast.35, s32[]{:T(128)S(6)} %select_n.41), kind=kOutput, calls=%fused_computation.21 | convolution fusion | flops 1619001344 | bytes 7352324 | tf_op jit(solution)/shard_map/dot_general | solution.py:43
  161.3 4.1 %fusion.12 = f32[4,96,1024]{2,1,0:T(8,128)S(1)} fusion(bf16[2048,1024]{0,1:T(8,128)(2,1)} %get-tuple-element.15, f32[2048]{0:T(1024)S(1)} %get-tuple-element.6, f32[1024]{0:T(1024)S(1)} %get-tuple-element.4, bf16[2048,4,2,96]{0,3,2,1:T(8,128)(2,1)S(1)} %bitcast.36, s32[]{:T(128)S(6)} %select_n.39), kind=kOutput, calls=%fused_computation.22 | convolution fusion | flops 1619001344 | bytes 7352324 | tf_op jit(solution)/shard_map/dot_general | solution.py:43
  165.4 1.8 add.144
  167.1 0.1 dynamic-slice_bitcast_fusion.2
  167.3 0.9 collective-permute-start.15
  168.2 0.9 collective-permute-start.14
  169.1 1.1 collective-permute-start.13
  170.2 9.2 %collective-permute-done.15 = f32[96,1024]{1,0:T(8,128)S(1)} collective-permute-done((f32[96,1024]{1,0:T(8,128)S(1)}, f32[96,1024]{1,0:T(8,128)S(1)}, u32[]{:S(2)}, u32[]{:S(2)}) %collective-permute-start.15) | collective-permute-done | bytes 393248 | tf_op jit(solution)/shard_map/ppermute | solution.py:53
  179.3 2.4 %collective-permute-done.14 = f32[96,1024]{1,0:T(8,128)S(1)} collective-permute-done((f32[96,1024]{1,0:T(8,128)S(1)}, f32[96,1024]{1,0:T(8,128)S(1)}, u32[]{:S(2)}, u32[]{:S(2)}) %collective-permute-start.14) | collective-permute-done | bytes 393248 | tf_op jit(solution)/shard_map/ppermute | solution.py:53
  181.7 7.7 %collective-permute-done.13 = f32[96,1024]{1,0:T(8,128)} collective-permute-done((f32[96,1024]{1,0:T(8,128)S(1)}, f32[96,1024]{1,0:T(8,128)}, u32[]{:S(2)}, u32[]{:S(2)}) %collective-permute-start.13) | collective-permute-done | bytes 393248 | tf_op jit(solution)/shard_map/ppermute | solution.py:53
  189.5 1.1 multiply_reduce_fusion.2
  190.6 0.1 collective-permute-start.16
  190.7 1.1 collective-permute-done.16
  191.8 0.6 collective-permute-start.19
  192.4 0.9 collective-permute-start.18
  193.4 0.8 collective-permute-start.17
  194.2 1.2 collective-permute-done.19
  195.4 2.1 %collective-permute-done.18 = f32[1024]{0:T(1024)S(1)} collective-permute-done((f32[1024]{0:T(1024)S(1)}, f32[1024]{0:T(1024)S(1)}, u32[]{:S(2)}, u32[]{:S(2)}) %collective-permute-start.18) | collective-permute-done | bytes 4128 | tf_op jit(solution)/shard_map/ppermute | solution.py:20
  197.5 0.7 collective-permute-done.17
  198.2 0.8 broadcast_multiply_fusion
  (32 shorter events, 0.8 us)
Async XLA Ops:
  3.6 50.6 %all-to-all-start = ((bf16[16,2048,48]{1,2,0:T(8,128)(2,1)}), bf16[16,2048,48]{1,2,0:T(8,128)(2,1)S(1)}, u32[]{:S(2)}, u32[]{:S(2)}) async-start(bf16[16,2048,48]{1,2,0:T(8,128)(2,1)} %broadcast_in_dim.12), calls=%async_computation | async-start | bytes 6291456 | tf_op jit(solution)/shard_map/all_to_all | solution.py:59
  54.9 22.9 %copy-start.3 = (f32[2048]{0:T(1024)S(1)}, f32[2048]{0:T(1024)}, u32[]{:S(2)}) copy-start(f32[2048]{0:T(1024)} %param.5) | copy-start | bytes 24580
  77.7 16.2 %copy-start = (bf16[2048,1024]{0,1:T(8,128)(2,1)S(1)}, bf16[2048,1024]{0,1:T(8,128)(2,1)}, u32[]{:S(2)}) copy-start(bf16[2048,1024]{0,1:T(8,128)(2,1)} %get-tuple-element.15) | copy-start | bytes 12582916
  82.4 1.3 collective-permute-start
  84.3 4.5 %collective-permute-start.3 = (f32[1025]{0:T(1024)S(1)}, f32[1025]{0:T(1024)S(1)}, u32[]{:S(2)}, u32[]{:S(2)}) collective-permute-start(f32[1025]{0:T(1024)S(1)} %fusion.22), channel_id=1, source_target_pairs={{0,96},{32,0},{64,32},{96,64},{1,97},{33,1},{65,33},{97,65},{2,98}... | collective-permute-start | bytes 12308 | tf_op jit(solution)/shard_map/ppermute | solution.py:20
  87.1 5.2 %collective-permute-start.2 = (f32[1025]{0:T(1024)S(1)}, f32[1025]{0:T(1024)S(1)}, u32[]{:S(2)}, u32[]{:S(2)}) collective-permute-start(f32[1025]{0:T(1024)S(1)} %fusion.22), channel_id=1, source_target_pairs={{0,64},{32,96},{64,0},{96,32},{1,65},{33,97},{65,1},{97,33},{2,66}... | collective-permute-start | bytes 12308 | tf_op jit(solution)/shard_map/ppermute | solution.py:20
  87.9 4.9 %collective-permute-start.1 = (f32[1025]{0:T(1024)S(1)}, f32[1025]{0:T(1024)S(1)}, u32[]{:S(2)}, u32[]{:S(2)}) collective-permute-start(f32[1025]{0:T(1024)S(1)} %fusion.22), channel_id=1, source_target_pairs={{0,32},{32,64},{64,96},{96,0},{1,33},{33,65},{65,97},{97,1},{2,34}... | collective-permute-start | bytes 12308 | tf_op jit(solution)/shard_map/ppermute | solution.py:20
  106.3 11.1 %copy-start.1 = (bf16[2048,1024]{0,1:T(8,128)(2,1)S(1)}, bf16[2048,1024]{0,1:T(8,128)(2,1)}, u32[]{:S(2)}) copy-start(bf16[2048,1024]{0,1:T(8,128)(2,1)} %get-tuple-element.15) | copy-start | bytes 12582916
  109.5 1.2 collective-permute-start.4
  110.8 3.6 %collective-permute-start.7 = (f32[1024]{0:T(1024)S(1)}, f32[1024]{0:T(1024)S(1)}, u32[]{:S(2)}, u32[]{:S(2)}) collective-permute-start(f32[1024]{0:T(1024)S(1)} %add.133), channel_id=1, source_target_pairs={{0,96},{32,0},{64,32},{96,64},{1,97},{33,1},{65,33},{97,65},{2,98}... | collective-permute-start | bytes 12296 | tf_op jit(solution)/shard_map/ppermute | solution.py:20
  111.1 5.1 %collective-permute-start.6 = (f32[1024]{0:T(1024)S(1)}, f32[1024]{0:T(1024)S(1)}, u32[]{:S(2)}, u32[]{:S(2)}) collective-permute-start(f32[1024]{0:T(1024)S(1)} %add.133), channel_id=1, source_target_pairs={{0,64},{32,96},{64,0},{96,32},{1,65},{33,97},{65,1},{97,33},{2,66}... | collective-permute-start | bytes 12296 | tf_op jit(solution)/shard_map/ppermute | solution.py:20
  112.5 4.8 %collective-permute-start.5 = (f32[1024]{0:T(1024)S(1)}, f32[1024]{0:T(1024)S(1)}, u32[]{:S(2)}, u32[]{:S(2)}) collective-permute-start(f32[1024]{0:T(1024)S(1)} %add.133), channel_id=1, source_target_pairs={{0,32},{32,64},{64,96},{96,0},{1,33},{33,65},{65,97},{97,1},{2,34}... | collective-permute-start | bytes 12296 | tf_op jit(solution)/shard_map/ppermute | solution.py:20
  129.7 12.6 %copy-start.2 = (bf16[2048,1024]{0,1:T(8,128)(2,1)S(1)}, bf16[2048,1024]{0,1:T(8,128)(2,1)}, u32[]{:S(2)}) copy-start(bf16[2048,1024]{0,1:T(8,128)(2,1)} %get-tuple-element.15) | copy-start | bytes 12582916
  132.9 1.2 collective-permute-start.8
  134.2 3.6 %collective-permute-start.11 = (f32[1024]{0:T(1024)S(1)}, f32[1024]{0:T(1024)S(1)}, u32[]{:S(2)}, u32[]{:S(2)}) collective-permute-start(f32[1024]{0:T(1024)S(1)} %add.137), channel_id=1, source_target_pairs={{0,96},{32,0},{64,32},{96,64},{1,97},{33,1},{65,33},{97,65},{2,98}... | collective-permute-start | bytes 12296 | tf_op jit(solution)/shard_map/ppermute | solution.py:20
  135.9 5.1 %collective-permute-start.10 = (f32[1024]{0:T(1024)S(1)}, f32[1024]{0:T(1024)S(1)}, u32[]{:S(2)}, u32[]{:S(2)}) collective-permute-start(f32[1024]{0:T(1024)S(1)} %add.137), channel_id=1, source_target_pairs={{0,64},{32,96},{64,0},{96,32},{1,65},{33,97},{65,1},{97,33},{2,66}... | collective-permute-start | bytes 12296 | tf_op jit(solution)/shard_map/ppermute | solution.py:20
  136.8 4.8 %collective-permute-start.9 = (f32[1024]{0:T(1024)S(1)}, f32[1024]{0:T(1024)S(1)}, u32[]{:S(2)}, u32[]{:S(2)}) collective-permute-start(f32[1024]{0:T(1024)S(1)} %add.137), channel_id=1, source_target_pairs={{0,32},{32,64},{64,96},{96,0},{1,33},{33,65},{65,97},{97,1},{2,34}... | collective-permute-start | bytes 12296 | tf_op jit(solution)/shard_map/ppermute | solution.py:20
  143.9 11.4 %all-to-all-start.4 = ((f32[16,1,2048]{2,1,0:T(1,128)}), f32[16,1,2048]{2,1,0:T(1,128)S(1)}, u32[]{:S(2)}, u32[]{:S(2)}) async-start(f32[16,1,2048]{2,1,0:T(1,128)} %broadcast_in_dim.34), calls=%async_computation.4 | async-start | bytes 262144 | tf_op jit(solution)/shard_map/all_to_all | solution.py:26
  161.3 4.1 %collective-permute-start.12 = (f32[4,96,1024]{2,1,0:T(8,128)}, f32[4,96,1024]{2,1,0:T(8,128)}, u32[]{:S(2)}, u32[]{:S(2)}) collective-permute-start(f32[4,96,1024]{2,1,0:T(8,128)} %fusion.10), channel_id=1, source_target_pairs={{0,16},{16,0},{1,17},{17,1},{2,18},{18,2},{3,19},{19,3},{4,20},{20... | collective-permute-start | bytes 4718600 | tf_op jit(solution)/shard_map/ppermute | solution.py:48
  167.3 12.1 %collective-permute-start.15 = (f32[96,1024]{1,0:T(8,128)S(1)}, f32[96,1024]{1,0:T(8,128)S(1)}, u32[]{:S(2)}, u32[]{:S(2)}) collective-permute-start(f32[96,1024]{1,0:T(8,128)S(1)} %get-tuple-element.10), channel_id=1, source_target_pairs={{0,96},{32,0},{64,32},{96,64},{1,97},{33,1},{65,33},{97,65},{2,98}... | collective-permute-start | bytes 1179656 | tf_op jit(solution)/shard_map/ppermute | solution.py:53
  168.2 13.5 %collective-permute-start.14 = (f32[96,1024]{1,0:T(8,128)S(1)}, f32[96,1024]{1,0:T(8,128)S(1)}, u32[]{:S(2)}, u32[]{:S(2)}) collective-permute-start(f32[96,1024]{1,0:T(8,128)S(1)} %get-tuple-element.11), channel_id=1, source_target_pairs={{0,64},{32,96},{64,0},{96,32},{1,65},{33,97},{65,1},{97,33},{2,66}... | collective-permute-start | bytes 1179656 | tf_op jit(solution)/shard_map/ppermute | solution.py:53
  169.1 20.4 %collective-permute-start.13 = (f32[96,1024]{1,0:T(8,128)S(1)}, f32[96,1024]{1,0:T(8,128)}, u32[]{:S(2)}, u32[]{:S(2)}) collective-permute-start(f32[96,1024]{1,0:T(8,128)S(1)} %get-tuple-element.9), channel_id=1, source_target_pairs={{0,32},{32,64},{64,96},{96,0},{1,33},{33,65},{65,97},{97,1},{2,34}... | collective-permute-start | bytes 1179656 | tf_op jit(solution)/shard_map/ppermute | solution.py:53
  190.6 1.2 collective-permute-start.16
  191.8 3.6 %collective-permute-start.19 = (f32[1024]{0:T(1024)S(1)}, f32[1024]{0:T(1024)S(1)}, u32[]{:S(2)}, u32[]{:S(2)}) collective-permute-start(f32[1024]{0:T(1024)S(1)} %add.158), channel_id=1, source_target_pairs={{0,96},{32,0},{64,32},{96,64},{1,97},{33,1},{65,33},{97,65},{2,98}... | collective-permute-start | bytes 12296 | tf_op jit(solution)/shard_map/ppermute | solution.py:20
  192.4 5.1 %collective-permute-start.18 = (f32[1024]{0:T(1024)S(1)}, f32[1024]{0:T(1024)S(1)}, u32[]{:S(2)}, u32[]{:S(2)}) collective-permute-start(f32[1024]{0:T(1024)S(1)} %add.158), channel_id=1, source_target_pairs={{0,64},{32,96},{64,0},{96,32},{1,65},{33,97},{65,1},{97,33},{2,66}... | collective-permute-start | bytes 12296 | tf_op jit(solution)/shard_map/ppermute | solution.py:20
  193.4 4.8 %collective-permute-start.17 = (f32[1024]{0:T(1024)S(1)}, f32[1024]{0:T(1024)S(1)}, u32[]{:S(2)}, u32[]{:S(2)}) collective-permute-start(f32[1024]{0:T(1024)S(1)} %add.158), channel_id=1, source_target_pairs={{0,32},{32,64},{64,96},{96,0},{1,33},{33,65},{65,97},{97,1},{2,34}... | collective-permute-start | bytes 12296 | tf_op jit(solution)/shard_map/ppermute | solution.py:20

commit v11 on v10

--- a/solution.py
+++ b/solution.py
@@ -103,7 +103,7 @@
     transport = (row_scale[:, None] * kernel.astype(jnp.float32) * col_scale[None, :]).astype(
         jnp.bfloat16
     )
-    own_summed = summed_block(full_rows, transport)
+    own_summed = summed_block(full_rows, lax.optimization_barrier(transport))
     square_sum = reduce_row(jnp.sum(own_summed * own_summed, axis=0))
     new_centroids = own_summed * lax.rsqrt(square_sum / feature_dimension + 1e-06)[None, :]
     return (new_centroids, jnp.log(row_scale), jnp.log(centre_total * col_scale))

time: 200 us -> 202 us (1.010)
  starting transfers between devices: 27.5 us -> 32.6 us
  waiting for transfers between devices: 88.7 us -> 85 us
  other arithmetic: 22.2 us -> 25.2 us
  matrix products: 16.5 us -> 14.2 us
    ppermute x16, starting transfers between devices: 12.8 us -> 17.5 us  [shifted_sum(): total = total + lax.ppermute(x, axis, [(i, (i + k) % n) for i in range(n)])]
    convert_element_type x0 -> x1, other arithmetic: none -> 3.17 us  [per_device(): (row_scale[:, None] * kernel.astype(jnp.float32) * col_scale[None, :]).as...]
    ppermute x16, waiting for transfers between devices: 21 us -> 18 us  [shifted_sum(): total = total + lax.ppermute(x, axis, [(i, (i + k) % n) for i in range(n)])]
    dot_general x2, matrix products: 9.33 us -> 7.01 us  [product(): lax.dot_general(part, transport, (((0,), (0,)), ((), ())), preferred_elem...]
  transfers between devices with their start and end apart: 22 -> 22, of which waited for: 20 -> 18; matrix products, arithmetic and copies ran while one was open for 3% -> 3% of each run, Pallas kernels for 0% -> 0%
where the time goes in v11:
time: 202 us; the launch traced here: 201 us
  waiting for transfers between devices  85 us (42%)
  blocking collectives  38 us (19%)
  starting transfers between devices  32.6 us (16%)
  other arithmetic  25.2 us (12%)
  matrix products  14.2 us (7%)
  local copies, waits for them, and re-layouts  4.57 us (2%)
    all_to_all x1, waiting for transfers between devices, gather_features(): lax.all_to_all(jnp.broadcast_to(vectors, (n, *vectors.shape)), CENT, 0, 0...  40.6 us
    all_to_all x3, blocking collectives, reduce_cent(): lax.all_to_all(jnp.broadcast_to(x, (n, *x.shape)), CENT, 0, 0, tiled=False)  38 us
    ppermute x3, waiting for transfers between devices, summed_block(): lax.ppermute(piece, 'rx', [(i, (i + k) % chips) for i in range(chips)])  18.6 us
    ppermute x16, waiting for transfers between devices, shifted_sum(): total = total + lax.ppermute(x, axis, [(i, (i + k) % n) for i in range(n)])  18 us
    ppermute x16, starting transfers between devices, shifted_sum(): total = total + lax.ppermute(x, axis, [(i, (i + k) % n) for i in range(n)])  17.5 us
    reduce_sum x3, other arithmetic, per_device(): jnp.sum(kernel.astype(jnp.float32) * row_scale[:, None], axis=0)  9.83 us
    all_to_all x1, starting transfers between devices, gather_features(): lax.all_to_all(jnp.broadcast_to(vectors, (n, *vectors.shape)), CENT, 0, 0...  8.16 us
    all_to_all x1, waiting for transfers between devices, reduce_cent(): lax.all_to_all(jnp.broadcast_to(x, (n, *x.shape)), CENT, 0, 0, tiled=False)  7.82 us
  transfers between devices with their start and end apart: 22, of which 18 were waited for; matrix products, arithmetic and copies ran while one was open for 3% of the time, Pallas kernels for 0%

profile of v11, /device:TPU:0, one launch (start us, length us, event | category | flops | bytes accessed | tf_op | source)
XLA Modules:
  0.0 201.2 jit_solution(7190365883154966627)
XLA Ops:
  0.6 3.0 %broadcast_in_dim.12 = bf16[16,2048,48]{1,2,0:T(8,128)(2,1)} broadcast(bf16[2048,48]{0,1:T(8,128)(2,1)} %param.3), dimensions={1,2} | broadcast | bytes 3342336 | tf_op jit(solution)/shard_map/broadcast_in_dim | solution.py:60
  3.6 8.2 %all-to-all-start = ((bf16[16,2048,48]{1,2,0:T(8,128)(2,1)}), bf16[16,2048,48]{1,2,0:T(8,128)(2,1)S(1)}, u32[]{:S(2)}, u32[]{:S(2)}) async-start(bf16[16,2048,48]{1,2,0:T(8,128)(2,1)} %broadcast_in_dim.12), calls=%async_computation | async-start | bytes 6291456 | tf_op jit(solution)/shard_map/all_to_all | solution.py:59
  11.8 1.8 multiply_reduce_fusion.1
  13.6 40.6 %all-to-all-done = bf16[16,2048,48]{1,2,0:T(8,128)(2,1)S(1)} async-done(((bf16[16,2048,48]{1,2,0:T(8,128)(2,1)}), bf16[16,2048,48]{1,2,0:T(8,128)(2,1)S(1)}, u32[]{:S(2)}, u32[]{:S(2)}) %all-to-all-start) | async-done | bytes 3145760 | tf_op jit(solution)/shard_map/all_to_all | solution.py:59
  54.2 0.7 multiply_reduce_fusion
  54.9 7.2 %fusion = (f32[2048]{0:T(1024)S(1)}, bf16[2048,1024]{0,1:T(8,128)(2,1)}) fusion(f32[1024]{0:T(1024)S(1)} %add_rsqrt_fusion.2, f32[2048]{0:T(1024)S(1)} %add_rsqrt_fusion, bf16[1024,768]{1,0:T(8,128)(2,1)} %param.4, bf16[2048,768]{0,1:T(8,128)(2,1)S(1)} %bitcast.35), kind=kOutput, calls=%fused_computation.8 | convolution fusion | flops 3235903488 | bytes 8933376 | tf_op jit(solution)/shard_map/dot_general | solution.py:83
  62.1 15.5 %all_to_all.29 = f32[16,1,2048]{2,1,0:T(1,128)S(1)} all-to-all(f32[16,1,2048]{2,1,0:T(1,128)S(1)} %broadcast_in_dim.13), channel_id=1, replica_groups=mesh['rx'=4,'rc'=2,'cy'=4,'cz'=4] {'cy','cz'}, dimensions={0} | all-to-all | bytes 262144 | tf_op jit(solution)/shard_map/all_to_all | solution.py:26
  77.6 0.1 reduce_sum.138
  77.7 0.6 fusion.24
  78.3 3.4 %fusion.1 = f32[1024]{0:T(1024)S(1)} fusion(bf16[2048,1024]{0,1:T(8,128)(2,1)} %get-tuple-element.15, f32[2048]{0:T(1024)S(1)} %get-tuple-element.12), kind=kLoop, calls=%fused_computation.9 | loop fusion | flops 6290432 | bytes 4206592 | tf_op jit(solution)/shard_map/reduce_sum | solution.py:95
  81.7 0.7 pad_maximum_fusion
  82.4 0.1 collective-permute-start
  82.5 1.2 collective-permute-done
  83.6 0.7 fusion.21
  84.3 1.6 collective-permute-start.1
  85.8 2.7 %collective-permute-start.2 = (f32[1025]{0:T(1024)S(1)}, f32[1025]{0:T(1024)S(1)}, u32[]{:S(2)}, u32[]{:S(2)}) collective-permute-start(f32[1025]{0:T(1024)S(1)} %fusion.21), channel_id=1, source_target_pairs={{0,64},{32,96},{64,0},{96,32},{1,65},{33,97},{65,1},{97,33},{2,66}... | collective-permute-start | bytes 12308 | tf_op jit(solution)/shard_map/ppermute | solution.py:20
  88.6 1.4 collective-permute-start.3
  90.0 1.0 collective-permute-done.2
  91.0 1.2 collective-permute-done.3
  92.2 0.5 slice.8
  93.4 0.9 fusion.2
  94.4 11.2 %all_to_all.30 = f32[16,1,2048]{2,1,0:T(1,128)S(1)} all-to-all(f32[16,1,2048]{2,1,0:T(1,128)S(1)} %broadcast_in_dim.15), channel_id=1, replica_groups=mesh['rx'=4,'rc'=2,'cy'=4,'cz'=4] {'cy','cz'}, dimensions={0} | all-to-all | bytes 262144 | tf_op jit(solution)/shard_map/all_to_all | solution.py:26
  105.6 0.1 reduce_sum.142
  105.8 3.2 %fusion.3 = f32[1024]{0:T(1024)S(1)} fusion(bf16[2048,1024]{0,1:T(8,128)(2,1)} %get-tuple-element.15, f32[2048]{0:T(1024)S(1)} %div.61), kind=kLoop, calls=%fused_computation.11 | loop fusion | flops 6290432 | bytes 4206592 | tf_op jit(solution)/shard_map/reduce_sum | solution.py:95
  109.1 1.2 collective-permute-done.4
  110.2 0.3 collective-permute-start.5
  110.5 3.8 %collective-permute-start.6 = (f32[1024]{0:T(1024)S(1)}, f32[1024]{0:T(1024)S(1)}, u32[]{:S(2)}, u32[]{:S(2)}) collective-permute-start(f32[1024]{0:T(1024)S(1)} %add.133), channel_id=1, source_target_pairs={{0,64},{32,96},{64,0},{96,32},{1,65},{33,97},{65,1},{97,33},{2,66}... | collective-permute-start | bytes 12296 | tf_op jit(solution)/shard_map/ppermute | solution.py:20
  114.4 0.7 collective-permute-done.5
  115.1 0.9 collective-permute-done.6
  116.0 2.0 collective-permute-done.7
  118.0 0.9 fusion.4
  118.9 11.2 %all_to_all.31 = f32[16,1,2048]{2,1,0:T(1,128)S(1)} all-to-all(f32[16,1,2048]{2,1,0:T(1,128)S(1)} %broadcast_in_dim.16), channel_id=1, replica_groups=mesh['rx'=4,'rc'=2,'cy'=4,'cz'=4] {'cy','cz'}, dimensions={0} | all-to-all | bytes 262144 | tf_op jit(solution)/shard_map/all_to_all | solution.py:26
  130.2 0.1 reduce_sum.145
  130.3 3.2 %fusion.5 = f32[1024]{0:T(1024)S(1)} fusion(bf16[2048,1024]{0,1:T(8,128)(2,1)} %get-tuple-element.15, f32[2048]{0:T(1024)S(1)} %div.63), kind=kLoop, calls=%fused_computation.13 | loop fusion | flops 6290432 | bytes 4206592 | tf_op jit(solution)/shard_map/reduce_sum | solution.py:95
  133.6 1.2 collective-permute-done.8
  134.8 1.5 collective-permute-start.10
  136.3 1.2 collective-permute-start.11
  137.4 0.9 collective-permute-start.9
  138.3 1.6 collective-permute-done.10
  139.9 2.4 %collective-permute-done.9 = f32[1024]{0:T(1024)S(1)} collective-permute-done((f32[1024]{0:T(1024)S(1)}, f32[1024]{0:T(1024)S(1)}, u32[]{:S(2)}, u32[]{:S(2)}) %collective-permute-start.9) | collective-permute-done | bytes 4128 | tf_op jit(solution)/shard_map/ppermute | solution.py:20
  142.2 0.6 multiply_log_fusion
  142.9 0.9 fusion.6
  143.8 0.7 broadcast_in_dim.34
  144.5 3.6 %all-to-all-start.4 = ((f32[16,1,2048]{2,1,0:T(1,128)}), f32[16,1,2048]{2,1,0:T(1,128)S(1)}, u32[]{:S(2)}, u32[]{:S(2)}) async-start(f32[16,1,2048]{2,1,0:T(1,128)} %broadcast_in_dim.34), calls=%async_computation.4 | async-start | bytes 262144 | tf_op jit(solution)/shard_map/all_to_all | solution.py:26
  148.1 7.8 %all-to-all-done.4 = f32[16,1,2048]{2,1,0:T(1,128)S(1)} async-done(((f32[16,1,2048]{2,1,0:T(1,128)}), f32[16,1,2048]{2,1,0:T(1,128)S(1)}, u32[]{:S(2)}, u32[]{:S(2)}) %all-to-all-start.4) | async-done | bytes 131104 | tf_op jit(solution)/shard_map/all_to_all | solution.py:26
  155.9 0.1 reduce_sum.148
  156.0 0.6 fusion.22
  156.6 3.2 %fusion.8 = bf16[2048,1024]{0,1:T(8,128)(2,1)S(1)} fusion(bf16[2048,1024]{0,1:T(8,128)(2,1)} %get-tuple-element.15, f32[2048]{0:T(1024)S(1)} %get-tuple-element.6, f32[1024]{0:T(1024)S(1)} %get-tuple-element.4), kind=kLoop, calls=%fused_computation.16 | loop fusion | flops 8388608 | bytes 8400896 | tf_op jit(solution)/shard_map/convert_element_type | solution.py:103
  159.8 3.0 %fusion.9 = f32[4,96,1024]{2,1,0:T(8,128)} fusion(bf16[2048,1024]{0,1:T(8,128)(2,1)S(1)} %fusion.8, bf16[2048,4,2,96]{0,3,2,1:T(8,128)(2,1)S(1)} %bitcast.36, s32[]{:T(128)S(6)} %select_n.41), kind=kOutput, calls=%fused_computation.19 | convolution fusion | flops 1610612736 | bytes 7340036 | tf_op jit(solution)/shard_map/dot_general | solution.py:43
  162.8 4.0 %fusion.11 = f32[4,96,1024]{2,1,0:T(8,128)S(1)} fusion(bf16[2048,1024]{0,1:T(8,128)(2,1)} %copy-done.3, bf16[2048,4,2,96]{0,3,2,1:T(8,128)(2,1)S(1)} %bitcast.37, s32[]{:T(128)S(6)} %select_n.39), kind=kOutput, calls=%fused_computation.21 | convolution fusion | flops 1610612736 | bytes 7340036 | tf_op jit(solution)/shard_map/dot_general | solution.py:43
  166.9 1.7 add.144
  168.5 0.1 dynamic-slice_bitcast_fusion.2
  168.7 1.7 collective-permute-start.14
  170.4 1.6 collective-permute-start.15
  172.0 17.9 %collective-permute-done.13 = f32[96,1024]{1,0:T(8,128)S(1)} collective-permute-done((f32[96,1024]{1,0:T(8,128)S(1)}, f32[96,1024]{1,0:T(8,128)S(1)}, u32[]{:S(2)}, u32[]{:S(2)}) %collective-permute-start.13) | collective-permute-done | bytes 393248 | tf_op jit(solution)/shard_map/ppermute | solution.py:53
  189.9 0.7 collective-permute-done.15
  190.6 1.1 multiply_reduce_fusion.2
  191.8 1.2 collective-permute-done.16
  193.0 0.2 collective-permute-start.17
  193.2 3.6 %collective-permute-start.18 = (f32[1024]{0:T(1024)S(1)}, f32[1024]{0:T(1024)S(1)}, u32[]{:S(2)}, u32[]{:S(2)}) collective-permute-start(f32[1024]{0:T(1024)S(1)} %add.158), channel_id=1, source_target_pairs={{0,64},{32,96},{64,0},{96,32},{1,65},{33,97},{65,1},{97,33},{2,66}... | collective-permute-start | bytes 12296 | tf_op jit(solution)/shard_map/ppermute | solution.py:20
  196.8 1.0 collective-permute-done.17
  197.8 0.6 collective-permute-done.18
  198.4 2.0 collective-permute-done.19
  200.4 0.8 broadcast_multiply_fusion
  (35 shorter events, 0.7 us)
Async XLA Ops:
  3.6 50.6 %all-to-all-start = ((bf16[16,2048,48]{1,2,0:T(8,128)(2,1)}), bf16[16,2048,48]{1,2,0:T(8,128)(2,1)S(1)}, u32[]{:S(2)}, u32[]{:S(2)}) async-start(bf16[16,2048,48]{1,2,0:T(8,128)(2,1)} %broadcast_in_dim.12), calls=%async_computation | async-start | bytes 6291456 | tf_op jit(solution)/shard_map/all_to_all | solution.py:59
  54.9 22.9 %copy-start.4 = (f32[2048]{0:T(1024)S(1)}, f32[2048]{0:T(1024)}, u32[]{:S(2)}) copy-start(f32[2048]{0:T(1024)} %param.5) | copy-start | bytes 24580
  77.7 15.7 %copy-start = (bf16[2048,1024]{0,1:T(8,128)(2,1)S(1)}, bf16[2048,1024]{0,1:T(8,128)(2,1)}, u32[]{:S(2)}) copy-start(bf16[2048,1024]{0,1:T(8,128)(2,1)} %get-tuple-element.15) | copy-start | bytes 12582916
  82.4 1.3 collective-permute-start
  84.3 5.7 %collective-permute-start.1 = (f32[1025]{0:T(1024)S(1)}, f32[1025]{0:T(1024)S(1)}, u32[]{:S(2)}, u32[]{:S(2)}) collective-permute-start(f32[1025]{0:T(1024)S(1)} %fusion.21), channel_id=1, source_target_pairs={{0,32},{32,64},{64,96},{96,0},{1,33},{33,65},{65,97},{97,1},{2,34}... | collective-permute-start | bytes 12308 | tf_op jit(solution)/shard_map/ppermute | solution.py:20
  85.8 5.2 %collective-permute-start.2 = (f32[1025]{0:T(1024)S(1)}, f32[1025]{0:T(1024)S(1)}, u32[]{:S(2)}, u32[]{:S(2)}) collective-permute-start(f32[1025]{0:T(1024)S(1)} %fusion.21), channel_id=1, source_target_pairs={{0,64},{32,96},{64,0},{96,32},{1,65},{33,97},{65,1},{97,33},{2,66}... | collective-permute-start | bytes 12308 | tf_op jit(solution)/shard_map/ppermute | solution.py:20
  88.6 3.7 %collective-permute-start.3 = (f32[1025]{0:T(1024)S(1)}, f32[1025]{0:T(1024)S(1)}, u32[]{:S(2)}, u32[]{:S(2)}) collective-permute-start(f32[1025]{0:T(1024)S(1)} %fusion.21), channel_id=1, source_target_pairs={{0,96},{32,0},{64,32},{96,64},{1,97},{33,1},{65,33},{97,65},{2,98}... | collective-permute-start | bytes 12308 | tf_op jit(solution)/shard_map/ppermute | solution.py:20
  105.7 12.2 %copy-start.1 = (bf16[2048,1024]{0,1:T(8,128)(2,1)S(1)}, bf16[2048,1024]{0,1:T(8,128)(2,1)}, u32[]{:S(2)}) copy-start(bf16[2048,1024]{0,1:T(8,128)(2,1)} %get-tuple-element.15) | copy-start | bytes 12582916
  109.0 1.2 collective-permute-start.4
  110.2 4.8 %collective-permute-start.5 = (f32[1024]{0:T(1024)S(1)}, f32[1024]{0:T(1024)S(1)}, u32[]{:S(2)}, u32[]{:S(2)}) collective-permute-start(f32[1024]{0:T(1024)S(1)} %add.133), channel_id=1, source_target_pairs={{0,32},{32,64},{64,96},{96,0},{1,33},{33,65},{65,97},{97,1},{2,34}... | collective-permute-start | bytes 12296 | tf_op jit(solution)/shard_map/ppermute | solution.py:20
  110.5 5.5 %collective-permute-start.6 = (f32[1024]{0:T(1024)S(1)}, f32[1024]{0:T(1024)S(1)}, u32[]{:S(2)}, u32[]{:S(2)}) collective-permute-start(f32[1024]{0:T(1024)S(1)} %add.133), channel_id=1, source_target_pairs={{0,64},{32,96},{64,0},{96,32},{1,65},{33,97},{65,1},{97,33},{2,66}... | collective-permute-start | bytes 12296 | tf_op jit(solution)/shard_map/ppermute | solution.py:20
  114.3 3.6 %collective-permute-start.7 = (f32[1024]{0:T(1024)S(1)}, f32[1024]{0:T(1024)S(1)}, u32[]{:S(2)}, u32[]{:S(2)}) collective-permute-start(f32[1024]{0:T(1024)S(1)} %add.133), channel_id=1, source_target_pairs={{0,96},{32,0},{64,32},{96,64},{1,97},{33,1},{65,33},{97,65},{2,98}... | collective-permute-start | bytes 12296 | tf_op jit(solution)/shard_map/ppermute | solution.py:20
  130.3 12.6 %copy-start.2 = (bf16[2048,1024]{0,1:T(8,128)(2,1)S(1)}, bf16[2048,1024]{0,1:T(8,128)(2,1)}, u32[]{:S(2)}) copy-start(bf16[2048,1024]{0,1:T(8,128)(2,1)} %get-tuple-element.15) | copy-start | bytes 12582916
  133.5 1.2 collective-permute-start.8
  134.8 5.1 %collective-permute-start.10 = (f32[1024]{0:T(1024)S(1)}, f32[1024]{0:T(1024)S(1)}, u32[]{:S(2)}, u32[]{:S(2)}) collective-permute-start(f32[1024]{0:T(1024)S(1)} %add.137), channel_id=1, source_target_pairs={{0,64},{32,96},{64,0},{96,32},{1,65},{33,97},{65,1},{97,33},{2,66}... | collective-permute-start | bytes 12296 | tf_op jit(solution)/shard_map/ppermute | solution.py:20
  136.3 3.6 %collective-permute-start.11 = (f32[1024]{0:T(1024)S(1)}, f32[1024]{0:T(1024)S(1)}, u32[]{:S(2)}, u32[]{:S(2)}) collective-permute-start(f32[1024]{0:T(1024)S(1)} %add.137), channel_id=1, source_target_pairs={{0,96},{32,0},{64,32},{96,64},{1,97},{33,1},{65,33},{97,65},{2,98}... | collective-permute-start | bytes 12296 | tf_op jit(solution)/shard_map/ppermute | solution.py:20
  137.4 4.8 %collective-permute-start.9 = (f32[1024]{0:T(1024)S(1)}, f32[1024]{0:T(1024)S(1)}, u32[]{:S(2)}, u32[]{:S(2)}) collective-permute-start(f32[1024]{0:T(1024)S(1)} %add.137), channel_id=1, source_target_pairs={{0,32},{32,64},{64,96},{96,0},{1,33},{33,65},{65,97},{97,1},{2,34}... | collective-permute-start | bytes 12296 | tf_op jit(solution)/shard_map/ppermute | solution.py:20
  144.5 11.4 %all-to-all-start.4 = ((f32[16,1,2048]{2,1,0:T(1,128)}), f32[16,1,2048]{2,1,0:T(1,128)S(1)}, u32[]{:S(2)}, u32[]{:S(2)}) async-start(f32[16,1,2048]{2,1,0:T(1,128)} %broadcast_in_dim.34), calls=%async_computation.4 | async-start | bytes 262144 | tf_op jit(solution)/shard_map/all_to_all | solution.py:26
  159.8 3.0 %copy-start.3 = (bf16[2048,1024]{0,1:T(8,128)(2,1)}, bf16[2048,1024]{0,1:T(8,128)(2,1)S(1)}, u32[]{:S(2)}) copy-start(bf16[2048,1024]{0,1:T(8,128)(2,1)S(1)} %fusion.8) | copy-start | bytes 12582916
  162.8 4.0 %collective-permute-start.12 = (f32[4,96,1024]{2,1,0:T(8,128)}, f32[4,96,1024]{2,1,0:T(8,128)}, u32[]{:S(2)}, u32[]{:S(2)}) collective-permute-start(f32[4,96,1024]{2,1,0:T(8,128)} %fusion.9), channel_id=1, source_target_pairs={{0,16},{16,0},{1,17},{17,1},{2,18},{18,2},{3,19},{19,3},{4,20},{20... | collective-permute-start | bytes 4718600 | tf_op jit(solution)/shard_map/ppermute | solution.py:48
  168.7 21.2 %collective-permute-start.13 = (f32[96,1024]{1,0:T(8,128)S(1)}, f32[96,1024]{1,0:T(8,128)S(1)}, u32[]{:S(2)}, u32[]{:S(2)}) collective-permute-start(f32[96,1024]{1,0:T(8,128)S(1)} %get-tuple-element.9), channel_id=1, source_target_pairs={{0,32},{32,64},{64,96},{96,0},{1,33},{33,65},{65,97},{97,1},{2,34}... | collective-permute-start | bytes 1179656 | tf_op jit(solution)/shard_map/ppermute | solution.py:53
  168.7 21.2 %collective-permute-start.14 = (f32[96,1024]{1,0:T(8,128)S(1)}, f32[96,1024]{1,0:T(8,128)S(1)}, u32[]{:S(2)}, u32[]{:S(2)}) collective-permute-start(f32[96,1024]{1,0:T(8,128)S(1)} %get-tuple-element.11), channel_id=1, source_target_pairs={{0,64},{32,96},{64,0},{96,32},{1,65},{33,97},{65,1},{97,33},{2,66}... | collective-permute-start | bytes 1179656 | tf_op jit(solution)/shard_map/ppermute | solution.py:53
  170.4 20.2 %collective-permute-start.15 = (f32[96,1024]{1,0:T(8,128)S(1)}, f32[96,1024]{1,0:T(8,128)}, u32[]{:S(2)}, u32[]{:S(2)}) collective-permute-start(f32[96,1024]{1,0:T(8,128)S(1)} %get-tuple-element.10), channel_id=1, source_target_pairs={{0,96},{32,0},{64,32},{96,64},{1,97},{33,1},{65,33},{97,65},{2,98}... | collective-permute-start | bytes 1179656 | tf_op jit(solution)/shard_map/ppermute | solution.py:53
  191.7 1.2 collective-permute-start.16
  193.0 4.8 %collective-permute-start.17 = (f32[1024]{0:T(1024)S(1)}, f32[1024]{0:T(1024)S(1)}, u32[]{:S(2)}, u32[]{:S(2)}) collective-permute-start(f32[1024]{0:T(1024)S(1)} %add.158), channel_id=1, source_target_pairs={{0,32},{32,64},{64,96},{96,0},{1,33},{33,65},{65,97},{97,1},{2,34}... | collective-permute-start | bytes 12296 | tf_op jit(solution)/shard_map/ppermute | solution.py:20
  193.2 5.2 %collective-permute-start.18 = (f32[1024]{0:T(1024)S(1)}, f32[1024]{0:T(1024)S(1)}, u32[]{:S(2)}, u32[]{:S(2)}) collective-permute-start(f32[1024]{0:T(1024)S(1)} %add.158), channel_id=1, source_target_pairs={{0,64},{32,96},{64,0},{96,32},{1,65},{33,97},{65,1},{97,33},{2,66}... | collective-permute-start | bytes 12296 | tf_op jit(solution)/shard_map/ppermute | solution.py:20
  196.8 3.6 %collective-permute-start.19 = (f32[1024]{0:T(1024)S(1)}, f32[1024]{0:T(1024)S(1)}, u32[]{:S(2)}, u32[]{:S(2)}) collective-permute-start(f32[1024]{0:T(1024)S(1)} %add.158), channel_id=1, source_target_pairs={{0,96},{32,0},{64,32},{96,64},{1,97},{33,1},{65,33},{97,65},{2,98}... | collective-permute-start | bytes 12296 | tf_op jit(solution)/shard_map/ppermute | solution.py:20

commit v12 on v10

--- a/solution.py
+++ b/solution.py
@@ -47,10 +47,19 @@
     sent = product((rc + 1) % cores)
     received = lax.ppermute(sent, "rc", [(i, (i + 1) % cores) for i in range(cores)])
     half = lax.optimization_barrier(product(rc)) + received
-    total = lax.dynamic_index_in_dim(half, rx, 0, keepdims=False)
-    for k in range(1, chips):
-        piece = lax.dynamic_index_in_dim(half, (rx + k) % chips, 0, keepdims=False)
-        total = total + lax.ppermute(piece, "rx", [(i, (i + k) % chips) for i in range(chips)])
+    split = block // 2
+    clockwise = ring_sum(half[:, :split], rx, chips, 1)
+    counter = ring_sum(half[:, split:], rx, chips, -1)
+    return jnp.concatenate([clockwise, counter], axis=0)
+
+
+def ring_sum(blocks, me, n, step):
+    neighbour = [(i, (i + step) % n) for i in range(n)]
+    total = lax.dynamic_index_in_dim(blocks, (me - step) % n, 0, keepdims=False)
+    for s in range(1, n):
+        arrived = lax.ppermute(total, "rx", neighbour)
+        own = lax.dynamic_index_in_dim(blocks, (me - step * (1 + s)) % n, 0, keepdims=False)
+        total = arrived + own
     return total
 
 

time: 200 us -> 200 us (level)
  starting transfers between devices: 27.5 us -> 32 us
  waiting for transfers between devices: 88.7 us -> 86 us
    ppermute x3 -> x6, starting transfers between devices: 2.9 us -> 7.76 us  [ring_sum(): arrived = lax.ppermute(total, 'rx', neighbour)]
    ppermute x3 -> x6, waiting for transfers between devices: 19.3 us -> 16.3 us  [ring_sum(): arrived = lax.ppermute(total, 'rx', neighbour)]
  transfers between devices with their start and end apart: 22 -> 25, of which waited for: 20 -> 21; matrix products, arithmetic and copies ran while one was open for 3% -> 3% of each run, Pallas kernels for 0% -> 0%
where the time goes in v12:
time: 200 us
  waiting for transfers between devices  86 us (43%)
  blocking collectives  38 us (19%)
  starting transfers between devices  32 us (16%)
  other arithmetic  21.1 us (11%)
  matrix products  16.5 us (8%)
  local copies, waits for them, and re-layouts  4.65 us (2%)
    all_to_all x1, waiting for transfers between devices, gather_features(): lax.all_to_all(jnp.broadcast_to(vectors, (n, *vectors.shape)), CENT, 0, 0...  40.6 us
    all_to_all x3, blocking collectives, reduce_cent(): lax.all_to_all(jnp.broadcast_to(x, (n, *x.shape)), CENT, 0, 0, tiled=False)  38 us
    ppermute x16, waiting for transfers between devices, shifted_sum(): total = total + lax.ppermute(x, axis, [(i, (i + k) % n) for i in range(n)])  21.3 us
    ppermute x6, waiting for transfers between devices, ring_sum(): arrived = lax.ppermute(total, 'rx', neighbour)  16.3 us
    ppermute x16, starting transfers between devices, shifted_sum(): total = total + lax.ppermute(x, axis, [(i, (i + k) % n) for i in range(n)])  12.5 us
    reduce_sum x3, other arithmetic, per_device(): jnp.sum(kernel.astype(jnp.float32) * row_scale[:, None], axis=0)  9.83 us
    dot_general x2, matrix products, product(): lax.dot_general(part, transport, (((0,), (0,)), ((), ())), preferred_elem...  9.34 us
    all_to_all x1, starting transfers between devices, gather_features(): lax.all_to_all(jnp.broadcast_to(vectors, (n, *vectors.shape)), CENT, 0, 0...  8.16 us
  transfers between devices with their start and end apart: 25, of which 21 were waited for; matrix products, arithmetic and copies ran while one was open for 3% of the time, Pallas kernels for 0%

profile of v12, /device:TPU:0, one launch (start us, length us, event | category | flops | bytes accessed | tf_op | source)
XLA Modules:
  0.0 199.9 jit_solution(7005325713553978643)
XLA Ops:
  0.6 3.0 %broadcast_in_dim.12 = bf16[16,2048,48]{1,2,0:T(8,128)(2,1)} broadcast(bf16[2048,48]{0,1:T(8,128)(2,1)} %param.3), dimensions={1,2} | broadcast | bytes 3342336 | tf_op jit(solution)/shard_map/broadcast_in_dim | solution.py:69
  3.6 8.2 %all-to-all-start = ((bf16[16,2048,48]{1,2,0:T(8,128)(2,1)}), bf16[16,2048,48]{1,2,0:T(8,128)(2,1)S(1)}, u32[]{:S(2)}, u32[]{:S(2)}) async-start(bf16[16,2048,48]{1,2,0:T(8,128)(2,1)} %broadcast_in_dim.12), calls=%async_computation | async-start | bytes 6291456 | tf_op jit(solution)/shard_map/all_to_all | solution.py:68
  11.8 1.8 multiply_reduce_fusion.1
  13.6 40.6 %all-to-all-done = bf16[16,2048,48]{1,2,0:T(8,128)(2,1)S(1)} async-done(((bf16[16,2048,48]{1,2,0:T(8,128)(2,1)}), bf16[16,2048,48]{1,2,0:T(8,128)(2,1)S(1)}, u32[]{:S(2)}, u32[]{:S(2)}) %all-to-all-start) | async-done | bytes 3145760 | tf_op jit(solution)/shard_map/all_to_all | solution.py:68
  54.2 0.7 multiply_reduce_fusion
  54.9 7.2 %fusion = (f32[2048]{0:T(1024)S(1)}, bf16[2048,1024]{0,1:T(8,128)(2,1)}) fusion(f32[1024]{0:T(1024)S(1)} %add_rsqrt_fusion.2, f32[2048]{0:T(1024)S(1)} %add_rsqrt_fusion, bf16[1024,768]{1,0:T(8,128)(2,1)} %param.4, bf16[2048,768]{0,1:T(8,128)(2,1)S(1)} %bitcast.37), kind=kOutput, calls=%fused_computation.8 | convolution fusion | flops 3235903488 | bytes 8933376 | tf_op jit(solution)/shard_map/dot_general | solution.py:92
  62.1 15.5 %all_to_all.29 = f32[16,1,2048]{2,1,0:T(1,128)S(1)} all-to-all(f32[16,1,2048]{2,1,0:T(1,128)S(1)} %broadcast_in_dim.13), channel_id=1, replica_groups=mesh['rx'=4,'rc'=2,'cy'=4,'cz'=4] {'cy','cz'}, dimensions={0} | all-to-all | bytes 262144 | tf_op jit(solution)/shard_map/all_to_all | solution.py:26
  77.6 0.1 reduce_sum.138
  77.7 0.6 fusion.24
  78.3 3.4 %fusion.1 = f32[1024]{0:T(1024)S(1)} fusion(bf16[2048,1024]{0,1:T(8,128)(2,1)} %get-tuple-element.12, f32[2048]{0:T(1024)S(1)} %get-tuple-element.9), kind=kLoop, calls=%fused_computation.9 | loop fusion | flops 6290432 | bytes 4206592 | tf_op jit(solution)/shard_map/reduce_sum | solution.py:104
  81.7 0.7 pad_maximum_fusion.1
  82.5 1.2 collective-permute-done
  83.6 0.7 fusion.21
  84.3 2.8 %collective-permute-start.3 = (f32[1025]{0:T(1024)S(1)}, f32[1025]{0:T(1024)S(1)}, u32[]{:S(2)}, u32[]{:S(2)}) collective-permute-start(f32[1025]{0:T(1024)S(1)} %fusion.21), channel_id=1, source_target_pairs={{0,96},{32,0},{64,32},{96,64},{1,97},{33,1},{65,33},{97,65},{2,98}... | collective-permute-start | bytes 12308 | tf_op jit(solution)/shard_map/ppermute | solution.py:20
  87.1 0.8 collective-permute-start.2
  87.9 0.9 collective-permute-start.1
  88.8 3.5 %collective-permute-done.2 = f32[1025]{0:T(1024)S(1)} collective-permute-done((f32[1025]{0:T(1024)S(1)}, f32[1025]{0:T(1024)S(1)}, u32[]{:S(2)}, u32[]{:S(2)}) %collective-permute-start.2) | collective-permute-done | bytes 4132 | tf_op jit(solution)/shard_map/ppermute | solution.py:20
  92.3 0.5 collective-permute-done.1
  92.8 0.5 slice.16
  94.0 0.9 fusion.2
  94.9 11.2 %all_to_all.30 = f32[16,1,2048]{2,1,0:T(1,128)S(1)} all-to-all(f32[16,1,2048]{2,1,0:T(1,128)S(1)} %broadcast_in_dim.15), channel_id=1, replica_groups=mesh['rx'=4,'rc'=2,'cy'=4,'cz'=4] {'cy','cz'}, dimensions={0} | all-to-all | bytes 262144 | tf_op jit(solution)/shard_map/all_to_all | solution.py:26
  106.2 0.1 reduce_sum.142
  106.3 3.2 %fusion.3 = f32[1024]{0:T(1024)S(1)} fusion(bf16[2048,1024]{0,1:T(8,128)(2,1)} %get-tuple-element.12, f32[2048]{0:T(1024)S(1)} %div.61), kind=kLoop, calls=%fused_computation.11 | loop fusion | flops 6290432 | bytes 4206592 | tf_op jit(solution)/shard_map/reduce_sum | solution.py:104
  109.6 1.2 collective-permute-done.4
  110.8 0.3 collective-permute-start.7
  111.1 1.4 collective-permute-start.6
  112.5 1.2 collective-permute-start.5
  113.7 0.7 collective-permute-done.7
  114.4 1.8 collective-permute-done.6
  116.2 1.1 collective-permute-done.5
  117.3 0.9 fusion.4
  118.3 11.2 %all_to_all.31 = f32[16,1,2048]{2,1,0:T(1,128)S(1)} all-to-all(f32[16,1,2048]{2,1,0:T(1,128)S(1)} %broadcast_in_dim.16), channel_id=1, replica_groups=mesh['rx'=4,'rc'=2,'cy'=4,'cz'=4] {'cy','cz'}, dimensions={0} | all-to-all | bytes 262144 | tf_op jit(solution)/shard_map/all_to_all | solution.py:26
  129.7 3.2 %fusion.5 = f32[1024]{0:T(1024)S(1)} fusion(bf16[2048,1024]{0,1:T(8,128)(2,1)} %get-tuple-element.12, f32[2048]{0:T(1024)S(1)} %div.63), kind=kLoop, calls=%fused_computation.13 | loop fusion | flops 6290432 | bytes 4206592 | tf_op jit(solution)/shard_map/reduce_sum | solution.py:104
  133.0 1.2 collective-permute-done.8
  134.2 1.7 collective-permute-start.11
  135.9 0.9 collective-permute-start.10
  136.8 1.0 collective-permute-done.11
  137.8 3.2 %collective-permute-done.10 = f32[1024]{0:T(1024)S(1)} collective-permute-done((f32[1024]{0:T(1024)S(1)}, f32[1024]{0:T(1024)S(1)}, u32[]{:S(2)}, u32[]{:S(2)}) %collective-permute-start.10) | collective-permute-done | bytes 4128 | tf_op jit(solution)/shard_map/ppermute | solution.py:20
  141.0 0.6 collective-permute-done.9
  141.6 0.6 multiply_log_fusion
  142.2 0.9 fusion.6
  143.1 0.7 broadcast_in_dim.34
  143.9 3.6 %all-to-all-start.4 = ((f32[16,1,2048]{2,1,0:T(1,128)}), f32[16,1,2048]{2,1,0:T(1,128)S(1)}, u32[]{:S(2)}, u32[]{:S(2)}) async-start(f32[16,1,2048]{2,1,0:T(1,128)} %broadcast_in_dim.34), calls=%async_computation.4 | async-start | bytes 262144 | tf_op jit(solution)/shard_map/all_to_all | solution.py:26
  147.5 7.8 %all-to-all-done.4 = f32[16,1,2048]{2,1,0:T(1,128)S(1)} async-done(((f32[16,1,2048]{2,1,0:T(1,128)}), f32[16,1,2048]{2,1,0:T(1,128)S(1)}, u32[]{:S(2)}, u32[]{:S(2)}) %all-to-all-start.4) | async-done | bytes 131104 | tf_op jit(solution)/shard_map/all_to_all | solution.py:26
  155.4 0.6 fusion.22
  156.0 5.3 %fusion.10 = f32[4,96,1024]{2,1,0:T(8,128)} fusion(bf16[2048,1024]{0,1:T(8,128)(2,1)} %get-tuple-element.12, f32[2048]{0:T(1024)S(1)} %get-tuple-element.6, f32[1024]{0:T(1024)S(1)} %get-tuple-element.4, bf16[2048,4,2,96]{0,3,2,1:T(8,128)(2,1)S(1)} %bitcast.38, s32[]{:T(128)S(6)} %select_n.73), kind=kOutput, calls=%fused_computation.21 | convolution fusion | flops 1619001344 | bytes 7352324 | tf_op jit(solution)/shard_map/dot_general | solution.py:43
  161.3 4.1 %fusion.12 = f32[4,96,1024]{2,1,0:T(8,128)S(1)} fusion(bf16[2048,1024]{0,1:T(8,128)(2,1)} %get-tuple-element.12, f32[2048]{0:T(1024)S(1)} %get-tuple-element.6, f32[1024]{0:T(1024)S(1)} %get-tuple-element.4, bf16[2048,4,2,96]{0,3,2,1:T(8,128)(2,1)S(1)} %bitcast.39, s32[]{:T(128)S(6)} %select_n.71), kind=kOutput, calls=%fused_computation.22 | convolution fusion | flops 1619001344 | bytes 7352324 | tf_op jit(solution)/shard_map/dot_general | solution.py:43
  165.4 1.7 add.179
  167.0 0.2 fusion.23
  167.2 0.9 collective-permute-start.16
  168.2 1.3 collective-permute-start.13
  169.4 5.2 %collective-permute-done.16 = f32[48,1024]{1,0:T(8,128)S(1)} collective-permute-done((f32[48,1024]{1,0:T(8,128)S(1)}, f32[48,1024]{1,0:T(8,128)S(1)}, u32[]{:S(2)}, u32[]{:S(2)}) %collective-permute-start.16) | collective-permute-done | bytes 196640 | tf_op jit(solution)/shard_map/ppermute | solution.py:60
  174.7 2.1 %collective-permute-start.17 = (f32[48,1024]{1,0:T(8,128)S(1)}, f32[48,1024]{1,0:T(8,128)S(1)}, u32[]{:S(2)}, u32[]{:S(2)}) collective-permute-start(f32[48,1024]{1,0:T(8,128)S(1)} %bitcast_add_fusion.2), channel_id=1, source_target_pairs={{0,96},{32,0},{64,32},{96,64},{1,97},{33,1},{65,33},{97,65},{2,98}... | collective-permute-start | bytes 589832 | tf_op jit(solution)/shard_map/ppermute | solution.py:60
  176.9 4.3 %collective-permute-done.17 = f32[48,1024]{1,0:T(8,128)S(1)} collective-permute-done((f32[48,1024]{1,0:T(8,128)S(1)}, f32[48,1024]{1,0:T(8,128)S(1)}, u32[]{:S(2)}, u32[]{:S(2)}) %collective-permute-start.17) | collective-permute-done | bytes 196640 | tf_op jit(solution)/shard_map/ppermute | solution.py:60
  181.2 3.3 %collective-permute-start.18 = (f32[48,1024]{1,0:T(8,128)S(1)}, f32[48,1024]{1,0:T(8,128)S(1)}, u32[]{:S(2)}, u32[]{:S(2)}) collective-permute-start(f32[48,1024]{1,0:T(8,128)S(1)} %bitcast_add_fusion.1), channel_id=1, source_target_pairs={{0,96},{32,0},{64,32},{96,64},{1,97},{33,1},{65,33},{97,65},{2,98}... | collective-permute-start | bytes 589832 | tf_op jit(solution)/shard_map/ppermute | solution.py:60
  184.7 3.1 %collective-permute-done.18 = f32[48,1024]{1,0:T(8,128)S(1)} collective-permute-done((f32[48,1024]{1,0:T(8,128)S(1)}, f32[48,1024]{1,0:T(8,128)S(1)}, u32[]{:S(2)}, u32[]{:S(2)}) %collective-permute-start.18) | collective-permute-done | bytes 196640 | tf_op jit(solution)/shard_map/ppermute | solution.py:60
  187.8 3.8 %collective-permute-done.15 = f32[48,1024]{1,0:T(8,128)S(1)} collective-permute-done((f32[48,1024]{1,0:T(8,128)S(1)}, f32[48,1024]{1,0:T(8,128)S(1)}, u32[]{:S(2)}, u32[]{:S(2)}) %collective-permute-start.15) | collective-permute-done | bytes 196640 | tf_op jit(solution)/shard_map/ppermute | solution.py:60
  191.7 1.2 collective-permute-done.19
  192.9 0.9 collective-permute-start.21
  193.7 1.2 collective-permute-start.20
  194.9 1.6 collective-permute-done.22
  196.5 1.5 collective-permute-done.21
  198.0 1.2 collective-permute-done.20
  199.1 0.8 fusion.18
  (46 shorter events, 1.2 us)
Async XLA Ops:
  3.6 50.6 %all-to-all-start = ((bf16[16,2048,48]{1,2,0:T(8,128)(2,1)}), bf16[16,2048,48]{1,2,0:T(8,128)(2,1)S(1)}, u32[]{:S(2)}, u32[]{:S(2)}) async-start(bf16[16,2048,48]{1,2,0:T(8,128)(2,1)} %broadcast_in_dim.12), calls=%async_computation | async-start | bytes 6291456 | tf_op jit(solution)/shard_map/all_to_all | solution.py:68
  54.9 22.9 %copy-start.3 = (f32[2048]{0:T(1024)S(1)}, f32[2048]{0:T(1024)}, u32[]{:S(2)}) copy-start(f32[2048]{0:T(1024)} %param.5) | copy-start | bytes 24580
  77.7 16.2 %copy-start = (bf16[2048,1024]{0,1:T(8,128)(2,1)S(1)}, bf16[2048,1024]{0,1:T(8,128)(2,1)}, u32[]{:S(2)}) copy-start(bf16[2048,1024]{0,1:T(8,128)(2,1)} %get-tuple-element.12) | copy-start | bytes 12582916
  82.4 1.3 collective-permute-start
  84.3 4.5 %collective-permute-start.3 = (f32[1025]{0:T(1024)S(1)}, f32[1025]{0:T(1024)S(1)}, u32[]{:S(2)}, u32[]{:S(2)}) collective-permute-start(f32[1025]{0:T(1024)S(1)} %fusion.21), channel_id=1, source_target_pairs={{0,96},{32,0},{64,32},{96,64},{1,97},{33,1},{65,33},{97,65},{2,98}... | collective-permute-start | bytes 12308 | tf_op jit(solution)/shard_map/ppermute | solution.py:20
  87.1 5.2 %collective-permute-start.2 = (f32[1025]{0:T(1024)S(1)}, f32[1025]{0:T(1024)S(1)}, u32[]{:S(2)}, u32[]{:S(2)}) collective-permute-start(f32[1025]{0:T(1024)S(1)} %fusion.21), channel_id=1, source_target_pairs={{0,64},{32,96},{64,0},{96,32},{1,65},{33,97},{65,1},{97,33},{2,66}... | collective-permute-start | bytes 12308 | tf_op jit(solution)/shard_map/ppermute | solution.py:20
  87.9 4.9 %collective-permute-start.1 = (f32[1025]{0:T(1024)S(1)}, f32[1025]{0:T(1024)S(1)}, u32[]{:S(2)}, u32[]{:S(2)}) collective-permute-start(f32[1025]{0:T(1024)S(1)} %fusion.21), channel_id=1, source_target_pairs={{0,32},{32,64},{64,96},{96,0},{1,33},{33,65},{65,97},{97,1},{2,34}... | collective-permute-start | bytes 12308 | tf_op jit(solution)/shard_map/ppermute | solution.py:20
  106.3 11.1 %copy-start.1 = (bf16[2048,1024]{0,1:T(8,128)(2,1)S(1)}, bf16[2048,1024]{0,1:T(8,128)(2,1)}, u32[]{:S(2)}) copy-start(bf16[2048,1024]{0,1:T(8,128)(2,1)} %get-tuple-element.12) | copy-start | bytes 12582916
  109.5 1.2 collective-permute-start.4
  110.8 3.6 %collective-permute-start.7 = (f32[1024]{0:T(1024)S(1)}, f32[1024]{0:T(1024)S(1)}, u32[]{:S(2)}, u32[]{:S(2)}) collective-permute-start(f32[1024]{0:T(1024)S(1)} %add.168), channel_id=1, source_target_pairs={{0,96},{32,0},{64,32},{96,64},{1,97},{33,1},{65,33},{97,65},{2,98}... | collective-permute-start | bytes 12296 | tf_op jit(solution)/shard_map/ppermute | solution.py:20
  111.1 5.1 %collective-permute-start.6 = (f32[1024]{0:T(1024)S(1)}, f32[1024]{0:T(1024)S(1)}, u32[]{:S(2)}, u32[]{:S(2)}) collective-permute-start(f32[1024]{0:T(1024)S(1)} %add.168), channel_id=1, source_target_pairs={{0,64},{32,96},{64,0},{96,32},{1,65},{33,97},{65,1},{97,33},{2,66}... | collective-permute-start | bytes 12296 | tf_op jit(solution)/shard_map/ppermute | solution.py:20
  112.5 4.8 %collective-permute-start.5 = (f32[1024]{0:T(1024)S(1)}, f32[1024]{0:T(1024)S(1)}, u32[]{:S(2)}, u32[]{:S(2)}) collective-permute-start(f32[1024]{0:T(1024)S(1)} %add.168), channel_id=1, source_target_pairs={{0,32},{32,64},{64,96},{96,0},{1,33},{33,65},{65,97},{97,1},{2,34}... | collective-permute-start | bytes 12296 | tf_op jit(solution)/shard_map/ppermute | solution.py:20
  129.7 12.6 %copy-start.2 = (bf16[2048,1024]{0,1:T(8,128)(2,1)S(1)}, bf16[2048,1024]{0,1:T(8,128)(2,1)}, u32[]{:S(2)}) copy-start(bf16[2048,1024]{0,1:T(8,128)(2,1)} %get-tuple-element.12) | copy-start | bytes 12582916
  132.9 1.2 collective-permute-start.8
  134.2 3.6 %collective-permute-start.11 = (f32[1024]{0:T(1024)S(1)}, f32[1024]{0:T(1024)S(1)}, u32[]{:S(2)}, u32[]{:S(2)}) collective-permute-start(f32[1024]{0:T(1024)S(1)} %add.172), channel_id=1, source_target_pairs={{0,96},{32,0},{64,32},{96,64},{1,97},{33,1},{65,33},{97,65},{2,98}... | collective-permute-start | bytes 12296 | tf_op jit(solution)/shard_map/ppermute | solution.py:20
  135.9 5.1 %collective-permute-start.10 = (f32[1024]{0:T(1024)S(1)}, f32[1024]{0:T(1024)S(1)}, u32[]{:S(2)}, u32[]{:S(2)}) collective-permute-start(f32[1024]{0:T(1024)S(1)} %add.172), channel_id=1, source_target_pairs={{0,64},{32,96},{64,0},{96,32},{1,65},{33,97},{65,1},{97,33},{2,66}... | collective-permute-start | bytes 12296 | tf_op jit(solution)/shard_map/ppermute | solution.py:20
  136.8 4.8 %collective-permute-start.9 = (f32[1024]{0:T(1024)S(1)}, f32[1024]{0:T(1024)S(1)}, u32[]{:S(2)}, u32[]{:S(2)}) collective-permute-start(f32[1024]{0:T(1024)S(1)} %add.172), channel_id=1, source_target_pairs={{0,32},{32,64},{64,96},{96,0},{1,33},{33,65},{65,97},{97,1},{2,34}... | collective-permute-start | bytes 12296 | tf_op jit(solution)/shard_map/ppermute | solution.py:20
  143.9 11.4 %all-to-all-start.4 = ((f32[16,1,2048]{2,1,0:T(1,128)}), f32[16,1,2048]{2,1,0:T(1,128)S(1)}, u32[]{:S(2)}, u32[]{:S(2)}) async-start(f32[16,1,2048]{2,1,0:T(1,128)} %broadcast_in_dim.34), calls=%async_computation.4 | async-start | bytes 262144 | tf_op jit(solution)/shard_map/all_to_all | solution.py:26
  161.3 4.1 %collective-permute-start.12 = (f32[4,96,1024]{2,1,0:T(8,128)}, f32[4,96,1024]{2,1,0:T(8,128)}, u32[]{:S(2)}, u32[]{:S(2)}) collective-permute-start(f32[4,96,1024]{2,1,0:T(8,128)} %fusion.10), channel_id=1, source_target_pairs={{0,16},{16,0},{1,17},{17,1},{2,18},{18,2},{3,19},{19,3},{4,20},{20... | collective-permute-start | bytes 4718600 | tf_op jit(solution)/shard_map/ppermute | solution.py:48
  167.2 7.4 %collective-permute-start.16 = (f32[48,1024]{1,0:T(8,128)S(1)}, f32[48,1024]{1,0:T(8,128)S(1)}, u32[]{:S(2)}, u32[]{:S(2)}) collective-permute-start(f32[48,1024]{1,0:T(8,128)S(1)} %dynamic-slice_bitcast_fusion), channel_id=1, source_target_pairs={{0,96},{32,0},{64,32},{96,64},{1,97},{33,1},{65,33},{97,65},{2,98}... | collective-permute-start | bytes 589832 | tf_op jit(solution)/shard_map/ppermute | solution.py:60
  168.2 8.6 %collective-permute-start.13 = (f32[48,1024]{1,0:T(8,128)S(1)}, f32[48,1024]{1,0:T(8,128)S(1)}, u32[]{:S(2)}, u32[]{:S(2)}) collective-permute-start(f32[48,1024]{1,0:T(8,128)S(1)} %dynamic-slice_bitcast_fusion.1), channel_id=1, source_target_pairs={{0,32},{32,64},{64,96},{96,0},{1,33},{33,65},{65,97},{97,1},{2,34}... | collective-permute-start | bytes 589832 | tf_op jit(solution)/shard_map/ppermute | solution.py:60
  174.7 6.5 %collective-permute-start.17 = (f32[48,1024]{1,0:T(8,128)S(1)}, f32[48,1024]{1,0:T(8,128)S(1)}, u32[]{:S(2)}, u32[]{:S(2)}) collective-permute-start(f32[48,1024]{1,0:T(8,128)S(1)} %bitcast_add_fusion.2), channel_id=1, source_target_pairs={{0,96},{32,0},{64,32},{96,64},{1,97},{33,1},{65,33},{97,65},{2,98}... | collective-permute-start | bytes 589832 | tf_op jit(solution)/shard_map/ppermute | solution.py:60
  176.8 7.7 %collective-permute-start.14 = (f32[48,1024]{1,0:T(8,128)S(1)}, f32[48,1024]{1,0:T(8,128)S(1)}, u32[]{:S(2)}, u32[]{:S(2)}) collective-permute-start(f32[48,1024]{1,0:T(8,128)S(1)} %bitcast_add_fusion.5), channel_id=1, source_target_pairs={{0,32},{32,64},{64,96},{96,0},{1,33},{33,65},{65,97},{97,1},{2,34}... | collective-permute-start | bytes 589832 | tf_op jit(solution)/shard_map/ppermute | solution.py:60
  181.2 6.5 %collective-permute-start.18 = (f32[48,1024]{1,0:T(8,128)S(1)}, f32[48,1024]{1,0:T(8,128)S(1)}, u32[]{:S(2)}, u32[]{:S(2)}) collective-permute-start(f32[48,1024]{1,0:T(8,128)S(1)} %bitcast_add_fusion.1), channel_id=1, source_target_pairs={{0,96},{32,0},{64,32},{96,64},{1,97},{33,1},{65,33},{97,65},{2,98}... | collective-permute-start | bytes 589832 | tf_op jit(solution)/shard_map/ppermute | solution.py:60
  184.6 6.9 %collective-permute-start.15 = (f32[48,1024]{1,0:T(8,128)S(1)}, f32[48,1024]{1,0:T(8,128)S(1)}, u32[]{:S(2)}, u32[]{:S(2)}) collective-permute-start(f32[48,1024]{1,0:T(8,128)S(1)} %bitcast_add_fusion.4), channel_id=1, source_target_pairs={{0,32},{32,64},{64,96},{96,0},{1,33},{33,65},{65,97},{97,1},{2,34}... | collective-permute-start | bytes 589832 | tf_op jit(solution)/shard_map/ppermute | solution.py:60
  191.6 1.2 collective-permute-start.19
  192.8 3.6 %collective-permute-start.22 = (f32[1024]{0:T(1024)S(1)}, f32[1024]{0:T(1024)S(1)}, u32[]{:S(2)}, u32[]{:S(2)}) collective-permute-start(f32[1024]{0:T(1024)S(1)} %add.202), channel_id=1, source_target_pairs={{0,96},{32,0},{64,32},{96,64},{1,97},{33,1},{65,33},{97,65},{2,98}... | collective-permute-start | bytes 12296 | tf_op jit(solution)/shard_map/ppermute | solution.py:20
  192.9 5.1 %collective-permute-start.21 = (f32[1024]{0:T(1024)S(1)}, f32[1024]{0:T(1024)S(1)}, u32[]{:S(2)}, u32[]{:S(2)}) collective-permute-start(f32[1024]{0:T(1024)S(1)} %add.202), channel_id=1, source_target_pairs={{0,64},{32,96},{64,0},{96,32},{1,65},{33,97},{65,1},{97,33},{2,66}... | collective-permute-start | bytes 12296 | tf_op jit(solution)/shard_map/ppermute | solution.py:20
  193.7 5.4 %collective-permute-start.20 = (f32[1024]{0:T(1024)S(1)}, f32[1024]{0:T(1024)S(1)}, u32[]{:S(2)}, u32[]{:S(2)}) collective-permute-start(f32[1024]{0:T(1024)S(1)} %add.202), channel_id=1, source_target_pairs={{0,32},{32,64},{64,96},{96,0},{1,33},{33,65},{65,97},{97,1},{2,34}... | collective-permute-start | bytes 12296 | tf_op jit(solution)/shard_map/ppermute | solution.py:20

commit v13 on v10

--- a/solution.py
+++ b/solution.py
@@ -29,6 +29,12 @@
 
 def reduce_row(x):
     return shifted_sum(shifted_sum(x, "rc"), "rx")
+
+
+def gather_sum_row(x):
+    n = lax.axis_size(ROW)
+    copies = lax.all_to_all(jnp.broadcast_to(x, (n, *x.shape)), ROW, 0, 0, tiled=False)
+    return jnp.sum(copies, axis=0)
 
 
 def summed_block(full_rows, transport):
@@ -104,7 +110,7 @@
         jnp.bfloat16
     )
     own_summed = summed_block(full_rows, transport)
-    square_sum = reduce_row(jnp.sum(own_summed * own_summed, axis=0))
+    square_sum = gather_sum_row(jnp.sum(own_summed * own_summed, axis=0))
     new_centroids = own_summed * lax.rsqrt(square_sum / feature_dimension + 1e-06)[None, :]
     return (new_centroids, jnp.log(row_scale), jnp.log(centre_total * col_scale))
 

time: 200 us -> 201 us (level)
  blocking collectives: 38 us -> 45.8 us
  waiting for transfers between devices: 88.7 us -> 83.6 us
  starting transfers between devices: 27.5 us -> 25 us
    all_to_all x0 -> x1, blocking collectives: none -> 7.82 us  [gather_sum_row(): lax.all_to_all(jnp.broadcast_to(x, (n, *x.shape)), ROW, 0, 0, tiled=False)]
    ppermute x16 -> x12, waiting for transfers between devices: 21 us -> 15.9 us  [shifted_sum(): total = total + lax.ppermute(x, axis, [(i, (i + k) % n) for i in range(n)])]
    ppermute x16 -> x12, starting transfers between devices: 12.8 us -> 10.4 us  [shifted_sum(): total = total + lax.ppermute(x, axis, [(i, (i + k) % n) for i in range(n)])]
  transfers between devices with their start and end apart: 22 -> 18, of which waited for: 20 -> 16; matrix products, arithmetic and copies ran while one was open for 3% -> 3% of each run, Pallas kernels for 0% -> 0%
where the time goes in v13:
time: 201 us; the launch traced here: 199 us
  waiting for transfers between devices  83.6 us (42%)
  blocking collectives  45.8 us (23%)
  starting transfers between devices  25 us (12%)
  other arithmetic  22.2 us (11%)
  matrix products  16.5 us (8%)
  local copies, waits for them, and re-layouts  4.59 us (2%)
    all_to_all x1, waiting for transfers between devices, gather_features(): lax.all_to_all(jnp.broadcast_to(vectors, (n, *vectors.shape)), CENT, 0, 0...  40.6 us
    all_to_all x3, blocking collectives, reduce_cent(): lax.all_to_all(jnp.broadcast_to(x, (n, *x.shape)), CENT, 0, 0, tiled=False)  38 us
    ppermute x3, waiting for transfers between devices, summed_block(): lax.ppermute(piece, 'rx', [(i, (i + k) % chips) for i in range(chips)])  19.3 us
    ppermute x12, waiting for transfers between devices, shifted_sum(): total = total + lax.ppermute(x, axis, [(i, (i + k) % n) for i in range(n)])  15.9 us
    ppermute x12, starting transfers between devices, shifted_sum(): total = total + lax.ppermute(x, axis, [(i, (i + k) % n) for i in range(n)])  10.4 us
    reduce_sum x3, other arithmetic, per_device(): jnp.sum(kernel.astype(jnp.float32) * row_scale[:, None], axis=0)  9.83 us
    dot_general x2, matrix products, product(): lax.dot_general(part, transport, (((0,), (0,)), ((), ())), preferred_elem...  9.33 us
    all_to_all x1, starting transfers between devices, gather_features(): lax.all_to_all(jnp.broadcast_to(vectors, (n, *vectors.shape)), CENT, 0, 0...  8.16 us
  transfers between devices with their start and end apart: 18, of which 16 were waited for; matrix products, arithmetic and copies ran while one was open for 3% of the time, Pallas kernels for 0%

profile of v13, /device:TPU:0, one launch (start us, length us, event | category | flops | bytes accessed | tf_op | source)
XLA Modules:
  0.0 199.2 jit_solution(17880748165031873700)
XLA Ops:
  0.6 3.0 %broadcast_in_dim.14 = bf16[16,2048,48]{1,2,0:T(8,128)(2,1)} broadcast(bf16[2048,48]{0,1:T(8,128)(2,1)} %param.3), dimensions={1,2} | broadcast | bytes 3342336 | tf_op jit(solution)/shard_map/broadcast_in_dim | solution.py:66
  3.6 8.2 %all-to-all-start = ((bf16[16,2048,48]{1,2,0:T(8,128)(2,1)}), bf16[16,2048,48]{1,2,0:T(8,128)(2,1)S(1)}, u32[]{:S(2)}, u32[]{:S(2)}) async-start(bf16[16,2048,48]{1,2,0:T(8,128)(2,1)} %broadcast_in_dim.14), calls=%async_computation | async-start | bytes 6291456 | tf_op jit(solution)/shard_map/all_to_all | solution.py:65
  11.8 1.8 multiply_reduce_fusion.1
  13.6 40.6 %all-to-all-done = bf16[16,2048,48]{1,2,0:T(8,128)(2,1)S(1)} async-done(((bf16[16,2048,48]{1,2,0:T(8,128)(2,1)}), bf16[16,2048,48]{1,2,0:T(8,128)(2,1)S(1)}, u32[]{:S(2)}, u32[]{:S(2)}) %all-to-all-start) | async-done | bytes 3145760 | tf_op jit(solution)/shard_map/all_to_all | solution.py:65
  54.2 0.7 multiply_reduce_fusion
  54.9 7.2 %fusion = (f32[2048]{0:T(1024)S(1)}, bf16[2048,1024]{0,1:T(8,128)(2,1)}) fusion(f32[1024]{0:T(1024)S(1)} %add_rsqrt_fusion.2, f32[2048]{0:T(1024)S(1)} %add_rsqrt_fusion, bf16[1024,768]{1,0:T(8,128)(2,1)} %param.4, bf16[2048,768]{0,1:T(8,128)(2,1)S(1)} %bitcast.34), kind=kOutput, calls=%fused_computation.8 | convolution fusion | flops 3235903488 | bytes 8933376 | tf_op jit(solution)/shard_map/dot_general | solution.py:89
  62.1 15.5 %all_to_all.35 = f32[16,1,2048]{2,1,0:T(1,128)S(1)} all-to-all(f32[16,1,2048]{2,1,0:T(1,128)S(1)} %broadcast_in_dim.15), channel_id=1, replica_groups=mesh['rx'=4,'rc'=2,'cy'=4,'cz'=4] {'cy','cz'}, dimensions={0} | all-to-all | bytes 262144 | tf_op jit(solution)/shard_map/all_to_all | solution.py:26
  77.6 0.1 reduce_sum.147
  77.7 0.6 fusion.25
  78.3 3.4 %fusion.1 = f32[1024]{0:T(1024)S(1)} fusion(bf16[2048,1024]{0,1:T(8,128)(2,1)} %get-tuple-element.15, f32[2048]{0:T(1024)S(1)} %get-tuple-element.12), kind=kLoop, calls=%fused_computation.9 | loop fusion | flops 6290432 | bytes 4206592 | tf_op jit(solution)/shard_map/reduce_sum | solution.py:101
  81.7 0.7 pad_maximum_fusion
  82.4 0.1 collective-permute-start
  82.5 1.2 collective-permute-done
  83.6 0.7 fusion.22
  84.3 2.8 %collective-permute-start.3 = (f32[1025]{0:T(1024)S(1)}, f32[1025]{0:T(1024)S(1)}, u32[]{:S(2)}, u32[]{:S(2)}) collective-permute-start(f32[1025]{0:T(1024)S(1)} %fusion.22), channel_id=1, source_target_pairs={{0,96},{32,0},{64,32},{96,64},{1,97},{33,1},{65,33},{97,65},{2,98}... | collective-permute-start | bytes 12308 | tf_op jit(solution)/shard_map/ppermute | solution.py:20
  87.1 0.8 collective-permute-start.2
  87.9 0.9 collective-permute-start.1
  88.8 3.5 %collective-permute-done.2 = f32[1025]{0:T(1024)S(1)} collective-permute-done((f32[1025]{0:T(1024)S(1)}, f32[1025]{0:T(1024)S(1)}, u32[]{:S(2)}, u32[]{:S(2)}) %collective-permute-start.2) | collective-permute-done | bytes 4132 | tf_op jit(solution)/shard_map/ppermute | solution.py:20
  92.3 0.5 collective-permute-done.1
  92.8 0.5 slice.8
  94.0 0.9 fusion.2
  94.9 0.1 broadcast_in_dim.17
  94.9 11.2 %all_to_all.36 = f32[16,1,2048]{2,1,0:T(1,128)S(1)} all-to-all(f32[16,1,2048]{2,1,0:T(1,128)S(1)} %broadcast_in_dim.17), channel_id=1, replica_groups=mesh['rx'=4,'rc'=2,'cy'=4,'cz'=4] {'cy','cz'}, dimensions={0} | all-to-all | bytes 262144 | tf_op jit(solution)/shard_map/all_to_all | solution.py:26
  106.2 0.1 reduce_sum.151
  106.3 3.2 %fusion.3 = f32[1024]{0:T(1024)S(1)} fusion(bf16[2048,1024]{0,1:T(8,128)(2,1)} %get-tuple-element.15, f32[2048]{0:T(1024)S(1)} %div.61), kind=kLoop, calls=%fused_computation.11 | loop fusion | flops 6290432 | bytes 4206592 | tf_op jit(solution)/shard_map/reduce_sum | solution.py:101
  109.5 0.1 collective-permute-start.4
  109.6 1.2 collective-permute-done.4
  110.8 0.3 collective-permute-start.7
  111.1 1.4 collective-permute-start.6
  112.5 1.2 collective-permute-start.5
  113.7 0.7 collective-permute-done.7
  114.4 1.8 collective-permute-done.6
  116.2 1.1 collective-permute-done.5
  117.4 0.9 fusion.4
  118.3 11.2 %all_to_all.37 = f32[16,1,2048]{2,1,0:T(1,128)S(1)} all-to-all(f32[16,1,2048]{2,1,0:T(1,128)S(1)} %broadcast_in_dim.36), channel_id=1, replica_groups=mesh['rx'=4,'rc'=2,'cy'=4,'cz'=4] {'cy','cz'}, dimensions={0} | all-to-all | bytes 262144 | tf_op jit(solution)/shard_map/all_to_all | solution.py:26
  129.6 0.1 reduce_sum.154
  129.7 3.2 %fusion.5 = f32[1024]{0:T(1024)S(1)} fusion(bf16[2048,1024]{0,1:T(8,128)(2,1)} %get-tuple-element.15, f32[2048]{0:T(1024)S(1)} %div.63), kind=kLoop, calls=%fused_computation.13 | loop fusion | flops 6290432 | bytes 4206592 | tf_op jit(solution)/shard_map/reduce_sum | solution.py:101
  132.9 0.1 collective-permute-start.8
  133.0 1.2 collective-permute-done.8
  134.2 1.7 collective-permute-start.11
  135.9 0.9 collective-permute-start.10
  136.8 1.0 collective-permute-done.11
  137.8 3.2 %collective-permute-done.10 = f32[1024]{0:T(1024)S(1)} collective-permute-done((f32[1024]{0:T(1024)S(1)}, f32[1024]{0:T(1024)S(1)}, u32[]{:S(2)}, u32[]{:S(2)}) %collective-permute-start.10) | collective-permute-done | bytes 4128 | tf_op jit(solution)/shard_map/ppermute | solution.py:20
  141.0 0.6 collective-permute-done.9
  141.6 0.6 multiply_log_fusion
  142.2 0.9 fusion.6
  143.1 0.7 broadcast_in_dim.37
  143.9 3.6 %all-to-all-start.4 = ((f32[16,1,2048]{2,1,0:T(1,128)}), f32[16,1,2048]{2,1,0:T(1,128)S(1)}, u32[]{:S(2)}, u32[]{:S(2)}) async-start(f32[16,1,2048]{2,1,0:T(1,128)} %broadcast_in_dim.37), calls=%async_computation.4 | async-start | bytes 262144 | tf_op jit(solution)/shard_map/all_to_all | solution.py:26
  147.5 7.8 %all-to-all-done.4 = f32[16,1,2048]{2,1,0:T(1,128)S(1)} async-done(((f32[16,1,2048]{2,1,0:T(1,128)}), f32[16,1,2048]{2,1,0:T(1,128)S(1)}, u32[]{:S(2)}, u32[]{:S(2)}) %all-to-all-start.4) | async-done | bytes 131104 | tf_op jit(solution)/shard_map/all_to_all | solution.py:26
  155.3 0.1 reduce_sum.157
  155.4 0.6 fusion.23
  156.0 5.3 %fusion.10 = f32[4,96,1024]{2,1,0:T(8,128)} fusion(bf16[2048,1024]{0,1:T(8,128)(2,1)} %get-tuple-element.15, f32[2048]{0:T(1024)S(1)} %get-tuple-element.6, f32[1024]{0:T(1024)S(1)} %get-tuple-element.4, bf16[2048,4,2,96]{0,3,2,1:T(8,128)(2,1)S(1)} %bitcast.35, s32[]{:T(128)S(6)} %select_n.41), kind=kOutput, calls=%fused_computation.21 | convolution fusion | flops 1619001344 | bytes 7352324 | tf_op jit(solution)/shard_map/dot_general | solution.py:49
  161.3 4.1 %fusion.12 = f32[4,96,1024]{2,1,0:T(8,128)S(1)} fusion(bf16[2048,1024]{0,1:T(8,128)(2,1)} %get-tuple-element.15, f32[2048]{0:T(1024)S(1)} %get-tuple-element.6, f32[1024]{0:T(1024)S(1)} %get-tuple-element.4, bf16[2048,4,2,96]{0,3,2,1:T(8,128)(2,1)S(1)} %bitcast.36, s32[]{:T(128)S(6)} %select_n.39), kind=kOutput, calls=%fused_computation.22 | convolution fusion | flops 1619001344 | bytes 7352324 | tf_op jit(solution)/shard_map/dot_general | solution.py:49
  165.4 1.8 add.136
  167.1 0.1 dynamic-slice_bitcast_fusion.2
  167.3 0.9 collective-permute-start.15
  168.2 0.9 collective-permute-start.14
  169.1 1.1 collective-permute-start.13
  170.2 9.2 %collective-permute-done.15 = f32[96,1024]{1,0:T(8,128)S(1)} collective-permute-done((f32[96,1024]{1,0:T(8,128)S(1)}, f32[96,1024]{1,0:T(8,128)S(1)}, u32[]{:S(2)}, u32[]{:S(2)}) %collective-permute-start.15) | collective-permute-done | bytes 393248 | tf_op jit(solution)/shard_map/ppermute | solution.py:59
  179.3 2.4 %collective-permute-done.14 = f32[96,1024]{1,0:T(8,128)S(1)} collective-permute-done((f32[96,1024]{1,0:T(8,128)S(1)}, f32[96,1024]{1,0:T(8,128)S(1)}, u32[]{:S(2)}, u32[]{:S(2)}) %collective-permute-start.14) | collective-permute-done | bytes 393248 | tf_op jit(solution)/shard_map/ppermute | solution.py:59
  181.7 7.7 %collective-permute-done.13 = f32[96,1024]{1,0:T(8,128)} collective-permute-done((f32[96,1024]{1,0:T(8,128)S(1)}, f32[96,1024]{1,0:T(8,128)}, u32[]{:S(2)}, u32[]{:S(2)}) %collective-permute-start.13) | collective-permute-done | bytes 393248 | tf_op jit(solution)/shard_map/ppermute | solution.py:59
  189.5 1.1 multiply_reduce_fusion.2
  190.6 7.8 %all_to_all.38 = f32[8,1,1024]{2,1,0:T(1,128)S(1)} all-to-all(f32[8,1,1024]{2,1,0:T(1,128)S(1)} %broadcast_in_dim.38), channel_id=1, replica_groups=mesh['rx'=4,'rc'=2,'cy'=4,'cz'=4] {'rx','rc'}, dimensions={0} | all-to-all | bytes 65536 | tf_op jit(solution)/shard_map/all_to_all | solution.py:36
  198.5 0.8 broadcast_multiply_fusion
  (26 shorter events, 0.3 us)
Async XLA Ops:
  3.6 50.6 %all-to-all-start = ((bf16[16,2048,48]{1,2,0:T(8,128)(2,1)}), bf16[16,2048,48]{1,2,0:T(8,128)(2,1)S(1)}, u32[]{:S(2)}, u32[]{:S(2)}) async-start(bf16[16,2048,48]{1,2,0:T(8,128)(2,1)} %broadcast_in_dim.14), calls=%async_computation | async-start | bytes 6291456 | tf_op jit(solution)/shard_map/all_to_all | solution.py:65
  54.9 22.9 %copy-start.3 = (f32[2048]{0:T(1024)S(1)}, f32[2048]{0:T(1024)}, u32[]{:S(2)}) copy-start(f32[2048]{0:T(1024)} %param.5) | copy-start | bytes 24580
  77.7 16.2 %copy-start = (bf16[2048,1024]{0,1:T(8,128)(2,1)S(1)}, bf16[2048,1024]{0,1:T(8,128)(2,1)}, u32[]{:S(2)}) copy-start(bf16[2048,1024]{0,1:T(8,128)(2,1)} %get-tuple-element.15) | copy-start | bytes 12582916
  82.4 1.3 collective-permute-start
  84.3 4.5 %collective-permute-start.3 = (f32[1025]{0:T(1024)S(1)}, f32[1025]{0:T(1024)S(1)}, u32[]{:S(2)}, u32[]{:S(2)}) collective-permute-start(f32[1025]{0:T(1024)S(1)} %fusion.22), channel_id=1, source_target_pairs={{0,96},{32,0},{64,32},{96,64},{1,97},{33,1},{65,33},{97,65},{2,98}... | collective-permute-start | bytes 12308 | tf_op jit(solution)/shard_map/ppermute | solution.py:20
  87.1 5.2 %collective-permute-start.2 = (f32[1025]{0:T(1024)S(1)}, f32[1025]{0:T(1024)S(1)}, u32[]{:S(2)}, u32[]{:S(2)}) collective-permute-start(f32[1025]{0:T(1024)S(1)} %fusion.22), channel_id=1, source_target_pairs={{0,64},{32,96},{64,0},{96,32},{1,65},{33,97},{65,1},{97,33},{2,66}... | collective-permute-start | bytes 12308 | tf_op jit(solution)/shard_map/ppermute | solution.py:20
  87.9 4.9 %collective-permute-start.1 = (f32[1025]{0:T(1024)S(1)}, f32[1025]{0:T(1024)S(1)}, u32[]{:S(2)}, u32[]{:S(2)}) collective-permute-start(f32[1025]{0:T(1024)S(1)} %fusion.22), channel_id=1, source_target_pairs={{0,32},{32,64},{64,96},{96,0},{1,33},{33,65},{65,97},{97,1},{2,34}... | collective-permute-start | bytes 12308 | tf_op jit(solution)/shard_map/ppermute | solution.py:20
  106.3 11.1 %copy-start.1 = (bf16[2048,1024]{0,1:T(8,128)(2,1)S(1)}, bf16[2048,1024]{0,1:T(8,128)(2,1)}, u32[]{:S(2)}) copy-start(bf16[2048,1024]{0,1:T(8,128)(2,1)} %get-tuple-element.15) | copy-start | bytes 12582916
  109.5 1.2 collective-permute-start.4
  110.8 3.6 %collective-permute-start.7 = (f32[1024]{0:T(1024)S(1)}, f32[1024]{0:T(1024)S(1)}, u32[]{:S(2)}, u32[]{:S(2)}) collective-permute-start(f32[1024]{0:T(1024)S(1)} %add.125), channel_id=1, source_target_pairs={{0,96},{32,0},{64,32},{96,64},{1,97},{33,1},{65,33},{97,65},{2,98}... | collective-permute-start | bytes 12296 | tf_op jit(solution)/shard_map/ppermute | solution.py:20
  111.1 5.1 %collective-permute-start.6 = (f32[1024]{0:T(1024)S(1)}, f32[1024]{0:T(1024)S(1)}, u32[]{:S(2)}, u32[]{:S(2)}) collective-permute-start(f32[1024]{0:T(1024)S(1)} %add.125), channel_id=1, source_target_pairs={{0,64},{32,96},{64,0},{96,32},{1,65},{33,97},{65,1},{97,33},{2,66}... | collective-permute-start | bytes 12296 | tf_op jit(solution)/shard_map/ppermute | solution.py:20
  112.5 4.8 %collective-permute-start.5 = (f32[1024]{0:T(1024)S(1)}, f32[1024]{0:T(1024)S(1)}, u32[]{:S(2)}, u32[]{:S(2)}) collective-permute-start(f32[1024]{0:T(1024)S(1)} %add.125), channel_id=1, source_target_pairs={{0,32},{32,64},{64,96},{96,0},{1,33},{33,65},{65,97},{97,1},{2,34}... | collective-permute-start | bytes 12296 | tf_op jit(solution)/shard_map/ppermute | solution.py:20
  129.7 12.6 %copy-start.2 = (bf16[2048,1024]{0,1:T(8,128)(2,1)S(1)}, bf16[2048,1024]{0,1:T(8,128)(2,1)}, u32[]{:S(2)}) copy-start(bf16[2048,1024]{0,1:T(8,128)(2,1)} %get-tuple-element.15) | copy-start | bytes 12582916
  132.9 1.2 collective-permute-start.8
  134.2 3.6 %collective-permute-start.11 = (f32[1024]{0:T(1024)S(1)}, f32[1024]{0:T(1024)S(1)}, u32[]{:S(2)}, u32[]{:S(2)}) collective-permute-start(f32[1024]{0:T(1024)S(1)} %add.129), channel_id=1, source_target_pairs={{0,96},{32,0},{64,32},{96,64},{1,97},{33,1},{65,33},{97,65},{2,98}... | collective-permute-start | bytes 12296 | tf_op jit(solution)/shard_map/ppermute | solution.py:20
  135.9 5.1 %collective-permute-start.10 = (f32[1024]{0:T(1024)S(1)}, f32[1024]{0:T(1024)S(1)}, u32[]{:S(2)}, u32[]{:S(2)}) collective-permute-start(f32[1024]{0:T(1024)S(1)} %add.129), channel_id=1, source_target_pairs={{0,64},{32,96},{64,0},{96,32},{1,65},{33,97},{65,1},{97,33},{2,66}... | collective-permute-start | bytes 12296 | tf_op jit(solution)/shard_map/ppermute | solution.py:20
  136.8 4.8 %collective-permute-start.9 = (f32[1024]{0:T(1024)S(1)}, f32[1024]{0:T(1024)S(1)}, u32[]{:S(2)}, u32[]{:S(2)}) collective-permute-start(f32[1024]{0:T(1024)S(1)} %add.129), channel_id=1, source_target_pairs={{0,32},{32,64},{64,96},{96,0},{1,33},{33,65},{65,97},{97,1},{2,34}... | collective-permute-start | bytes 12296 | tf_op jit(solution)/shard_map/ppermute | solution.py:20
  143.9 11.4 %all-to-all-start.4 = ((f32[16,1,2048]{2,1,0:T(1,128)}), f32[16,1,2048]{2,1,0:T(1,128)S(1)}, u32[]{:S(2)}, u32[]{:S(2)}) async-start(f32[16,1,2048]{2,1,0:T(1,128)} %broadcast_in_dim.37), calls=%async_computation.4 | async-start | bytes 262144 | tf_op jit(solution)/shard_map/all_to_all | solution.py:26
  161.3 4.1 %collective-permute-start.12 = (f32[4,96,1024]{2,1,0:T(8,128)}, f32[4,96,1024]{2,1,0:T(8,128)}, u32[]{:S(2)}, u32[]{:S(2)}) collective-permute-start(f32[4,96,1024]{2,1,0:T(8,128)} %fusion.10), channel_id=1, source_target_pairs={{0,16},{16,0},{1,17},{17,1},{2,18},{18,2},{3,19},{19,3},{4,20},{20... | collective-permute-start | bytes 4718600 | tf_op jit(solution)/shard_map/ppermute | solution.py:54
  167.3 12.1 %collective-permute-start.15 = (f32[96,1024]{1,0:T(8,128)S(1)}, f32[96,1024]{1,0:T(8,128)S(1)}, u32[]{:S(2)}, u32[]{:S(2)}) collective-permute-start(f32[96,1024]{1,0:T(8,128)S(1)} %get-tuple-element.10), channel_id=1, source_target_pairs={{0,96},{32,0},{64,32},{96,64},{1,97},{33,1},{65,33},{97,65},{2,98}... | collective-permute-start | bytes 1179656 | tf_op jit(solution)/shard_map/ppermute | solution.py:59
  168.2 13.5 %collective-permute-start.14 = (f32[96,1024]{1,0:T(8,128)S(1)}, f32[96,1024]{1,0:T(8,128)S(1)}, u32[]{:S(2)}, u32[]{:S(2)}) collective-permute-start(f32[96,1024]{1,0:T(8,128)S(1)} %get-tuple-element.11), channel_id=1, source_target_pairs={{0,64},{32,96},{64,0},{96,32},{1,65},{33,97},{65,1},{97,33},{2,66}... | collective-permute-start | bytes 1179656 | tf_op jit(solution)/shard_map/ppermute | solution.py:59
  169.1 20.4 %collective-permute-start.13 = (f32[96,1024]{1,0:T(8,128)S(1)}, f32[96,1024]{1,0:T(8,128)}, u32[]{:S(2)}, u32[]{:S(2)}) collective-permute-start(f32[96,1024]{1,0:T(8,128)S(1)} %get-tuple-element.9), channel_id=1, source_target_pairs={{0,32},{32,64},{64,96},{96,0},{1,33},{33,65},{65,97},{97,1},{2,34}... | collective-permute-start | bytes 1179656 | tf_op jit(solution)/shard_map/ppermute | solution.py:59

commit v14 on v10

--- a/solution.py
+++ b/solution.py
@@ -80,6 +80,9 @@
     reciprocal_centroid_magnitudes = lax.rsqrt(
         jnp.mean(jnp.square(centroids.astype(jnp.float32)), axis=1) + 1e-06
     )
+    weight_sum, reciprocal_centroid_magnitudes = lax.optimization_barrier(
+        (reduce_row(jnp.sum(weights)), reciprocal_centroid_magnitudes)
+    )
     similarity_matrix = jnp.dot(full_rows, centroids.T, preferred_element_type=jnp.float32)
     sharpened_similarity = (
         similarity_matrix
@@ -90,14 +93,9 @@
     kernel = jnp.exp(sharpened_similarity).astype(jnp.bfloat16)
     col_scale = jnp.full((local_centres,), 1.0, jnp.float32) / centre_total
     row_scale = row_step(kernel, col_scale, weights)
-    weight_sum = None
     for sweep in range(ITERS):
         partial_cols = jnp.sum(kernel.astype(jnp.float32) * row_scale[:, None], axis=0)
-        if weight_sum is None:
-            both = reduce_row(jnp.concatenate([partial_cols, jnp.sum(weights)[None]]))
-            col_mass, weight_sum = both[:local_centres], both[local_centres]
-        else:
-            col_mass = reduce_row(partial_cols)
+        col_mass = reduce_row(partial_cols)
         col_scale = weight_sum / centre_total / col_mass
         row_scale = row_step(kernel, col_scale, weights)
     transport = (row_scale[:, None] * kernel.astype(jnp.float32) * col_scale[None, :]).astype(

time: 200 us -> 198 us (0.990)
  waiting for transfers between devices: 88.7 us -> 75.4 us
  starting transfers between devices: 27.5 us -> 37 us
  between operations: 1.56 us -> 3.95 us
    all_to_all x1, waiting for transfers between devices: 40.6 us -> 27.3 us  [gather_features(): lax.all_to_all(jnp.broadcast_to(vectors, (n, *vectors.shape)), CENT, 0, 0...]
    ppermute x16 -> x20, starting transfers between devices: 12.8 us -> 22.4 us  [shifted_sum(): total = total + lax.ppermute(x, axis, [(i, (i + k) % n) for i in range(n)])]
    reduce_sum x3, other arithmetic: 2.66 us -> 4.85 us  [row_step(): jnp.sum(kernel.astype(jnp.float32) * col_scale[None, :], axis=1)]
    ppermute x16 -> x20, waiting for transfers between devices: 21 us -> 21 us  [shifted_sum(): total = total + lax.ppermute(x, axis, [(i, (i + k) % n) for i in range(n)])]
  transfers between devices with their start and end apart: 22 -> 26, of which waited for: 20 -> 20; matrix products, arithmetic and copies ran while one was open for 3% -> 3% of each run, Pallas kernels for 0% -> 0%
where the time goes in v14:
time: 198 us
  waiting for transfers between devices  75.4 us (38%)
  blocking collectives  38 us (19%)
  starting transfers between devices  37 us (19%)
  other arithmetic  22.7 us (11%)
  matrix products  16.5 us (8%)
  local copies, waits for them, and re-layouts  4.05 us (2%)
  between operations  3.95 us (2%)
    all_to_all x3, blocking collectives, reduce_cent(): lax.all_to_all(jnp.broadcast_to(x, (n, *x.shape)), CENT, 0, 0, tiled=False)  38 us
    all_to_all x1, waiting for transfers between devices, gather_features(): lax.all_to_all(jnp.broadcast_to(vectors, (n, *vectors.shape)), CENT, 0, 0...  27.3 us
    ppermute x20, starting transfers between devices, shifted_sum(): total = total + lax.ppermute(x, axis, [(i, (i + k) % n) for i in range(n)])  22.4 us
    ppermute x20, waiting for transfers between devices, shifted_sum(): total = total + lax.ppermute(x, axis, [(i, (i + k) % n) for i in range(n)])  21 us
    ppermute x3, waiting for transfers between devices, summed_block(): lax.ppermute(piece, 'rx', [(i, (i + k) % chips) for i in range(chips)])  19.3 us
    reduce_sum x3, other arithmetic, per_device(): jnp.sum(kernel.astype(jnp.float32) * row_scale[:, None], axis=0)  9.52 us
    dot_general x2, matrix products, product(): lax.dot_general(part, transport, (((0,), (0,)), ((), ())), preferred_elem...  9.33 us
    all_to_all x1, starting transfers between devices, gather_features(): lax.all_to_all(jnp.broadcast_to(vectors, (n, *vectors.shape)), CENT, 0, 0...  8.16 us
  transfers between devices with their start and end apart: 26, of which 20 were waited for; matrix products, arithmetic and copies ran while one was open for 3% of the time, Pallas kernels for 0%

profile of v14, /device:TPU:0, one launch (start us, length us, event | category | flops | bytes accessed | tf_op | source)
XLA Modules:
  0.0 197.7 jit_solution(5180516931290393938)
XLA Ops:
  0.6 3.0 %broadcast_in_dim.10 = bf16[16,2048,48]{1,2,0:T(8,128)(2,1)} broadcast(bf16[2048,48]{0,1:T(8,128)(2,1)} %param.3), dimensions={1,2} | broadcast | bytes 3342336 | tf_op jit(solution)/shard_map/broadcast_in_dim | solution.py:60
  3.6 8.2 %all-to-all-start = ((bf16[16,2048,48]{1,2,0:T(8,128)(2,1)}), bf16[16,2048,48]{1,2,0:T(8,128)(2,1)S(1)}, u32[]{:S(2)}, u32[]{:S(2)}) async-start(bf16[16,2048,48]{1,2,0:T(8,128)(2,1)} %broadcast_in_dim.10), calls=%async_computation | async-start | bytes 6291456 | tf_op jit(solution)/shard_map/all_to_all | solution.py:59
  11.8 0.6 reduce_sum.136
  12.4 1.8 multiply_reduce_fusion.1
  15.4 2.9 %collective-permute-start.1 = (f32[]{:T(128)}, f32[]{:T(128)}, u32[]{:S(2)}, u32[]{:S(2)}) collective-permute-start(f32[]{:T(128)} %add.136), channel_id=1, source_target_pairs={{0,32},{32,64},{64,96},{96,0},{1,33},{33,65},{65,97},{97,1},{2,34}... | collective-permute-start | bytes 20 | tf_op jit(solution)/shard_map/ppermute | solution.py:20
  18.3 4.0 %collective-permute-start.2 = (f32[]{:T(128)}, f32[]{:T(128)}, u32[]{:S(2)}, u32[]{:S(2)}) collective-permute-start(f32[]{:T(128)} %add.136), channel_id=1, source_target_pairs={{0,64},{32,96},{64,0},{96,32},{1,65},{33,97},{65,1},{97,33},{2,66}... | collective-permute-start | bytes 20 | tf_op jit(solution)/shard_map/ppermute | solution.py:20
  22.3 2.7 %collective-permute-start.3 = (f32[]{:T(128)}, f32[]{:T(128)}, u32[]{:S(2)}, u32[]{:S(2)}) collective-permute-start(f32[]{:T(128)} %add.136), channel_id=1, source_target_pairs={{0,96},{32,0},{64,32},{96,64},{1,97},{33,1},{65,33},{97,65},{2,98}... | collective-permute-start | bytes 20 | tf_op jit(solution)/shard_map/ppermute | solution.py:20
  26.9 27.3 %all-to-all-done = bf16[16,2048,48]{1,2,0:T(8,128)(2,1)S(1)} async-done(((bf16[16,2048,48]{1,2,0:T(8,128)(2,1)}), bf16[16,2048,48]{1,2,0:T(8,128)(2,1)S(1)}, u32[]{:S(2)}, u32[]{:S(2)}) %all-to-all-start) | async-done | bytes 3145760 | tf_op jit(solution)/shard_map/all_to_all | solution.py:59
  54.2 0.7 multiply_reduce_fusion
  54.9 7.2 %fusion = (f32[2048]{0:T(1024)S(1)}, bf16[2048,1024]{0,1:T(8,128)(2,1)}) fusion(f32[1024]{0:T(1024)S(1)} %add_rsqrt_fusion.2, f32[2048]{0:T(1024)S(1)} %add_rsqrt_fusion, bf16[1024,768]{1,0:T(8,128)(2,1)} %param.4, bf16[2048,768]{0,1:T(8,128)(2,1)S(1)} %bitcast.32), kind=kOutput, calls=%fused_computation.8 | convolution fusion | flops 3235903488 | bytes 8933376 | tf_op jit(solution)/shard_map/dot_general | solution.py:86
  62.1 15.5 %all_to_all.29 = f32[16,1,2048]{2,1,0:T(1,128)S(1)} all-to-all(f32[16,1,2048]{2,1,0:T(1,128)S(1)} %broadcast_in_dim.11), channel_id=1, replica_groups=mesh['rx'=4,'rc'=2,'cy'=4,'cz'=4] {'cy','cz'}, dimensions={0} | all-to-all | bytes 262144 | tf_op jit(solution)/shard_map/all_to_all | solution.py:26
  77.6 0.1 reduce_sum.139
  77.7 3.1 %fusion.1 = f32[1024]{0:T(1024)S(1)} fusion(bf16[2048,1024]{0,1:T(8,128)(2,1)} %get-tuple-element.14, f32[2048]{0:T(1024)S(1)} %div.56), kind=kLoop, calls=%fused_computation.9 | loop fusion | flops 6290432 | bytes 4206592 | tf_op jit(solution)/shard_map/reduce_sum | solution.py:97
  80.9 1.2 collective-permute-done.4
  82.1 2.8 %collective-permute-start.7 = (f32[1024]{0:T(1024)S(1)}, f32[1024]{0:T(1024)S(1)}, u32[]{:S(2)}, u32[]{:S(2)}) collective-permute-start(f32[1024]{0:T(1024)S(1)} %add.141), channel_id=1, source_target_pairs={{0,96},{32,0},{64,32},{96,64},{1,97},{33,1},{65,33},{97,65},{2,98}... | collective-permute-start | bytes 12296 | tf_op jit(solution)/shard_map/ppermute | solution.py:20
  84.8 0.8 collective-permute-start.6
  85.6 0.9 collective-permute-start.5
  86.5 3.4 %collective-permute-done.6 = f32[1024]{0:T(1024)S(1)} collective-permute-done((f32[1024]{0:T(1024)S(1)}, f32[1024]{0:T(1024)S(1)}, u32[]{:S(2)}, u32[]{:S(2)}) %collective-permute-start.6) | collective-permute-done | bytes 4128 | tf_op jit(solution)/shard_map/ppermute | solution.py:20
  89.9 0.5 collective-permute-done.5
  90.4 3.1 %fusion.2 = f32[2048]{0:T(1024)S(1)} fusion(bf16[2048,1024]{0,1:T(8,128)(2,1)} %get-tuple-element.14, f32[1024]{0:T(1024)S(1)} %add_divide_fusion.2), kind=kLoop, calls=%fused_computation.10 | loop fusion | flops 6289408 | bytes 4206592 | tf_op jit(solution)/shard_map/reduce_sum | solution.py:66
  93.6 11.2 %all_to_all.30 = f32[16,1,2048]{2,1,0:T(1,128)S(1)} all-to-all(f32[16,1,2048]{2,1,0:T(1,128)S(1)} %broadcast_in_dim.12), channel_id=1, replica_groups=mesh['rx'=4,'rc'=2,'cy'=4,'cz'=4] {'cy','cz'}, dimensions={0} | all-to-all | bytes 262144 | tf_op jit(solution)/shard_map/all_to_all | solution.py:26
  105.0 3.2 %fusion.3 = f32[1024]{0:T(1024)S(1)} fusion(bf16[2048,1024]{0,1:T(8,128)(2,1)} %get-tuple-element.14, f32[2048]{0:T(1024)S(1)} %div.58), kind=kLoop, calls=%fused_computation.11 | loop fusion | flops 6290432 | bytes 4206592 | tf_op jit(solution)/shard_map/reduce_sum | solution.py:97
  108.3 1.2 collective-permute-done.8
  109.4 0.3 collective-permute-start.11
  109.8 1.4 collective-permute-start.10
  111.2 1.2 collective-permute-start.9
  112.4 0.7 collective-permute-done.11
  113.0 1.8 collective-permute-done.10
  114.9 1.1 collective-permute-done.9
  116.0 0.9 fusion.4
  117.0 11.2 %all_to_all.31 = f32[16,1,2048]{2,1,0:T(1,128)S(1)} all-to-all(f32[16,1,2048]{2,1,0:T(1,128)S(1)} %broadcast_in_dim.13), channel_id=1, replica_groups=mesh['rx'=4,'rc'=2,'cy'=4,'cz'=4] {'cy','cz'}, dimensions={0} | all-to-all | bytes 262144 | tf_op jit(solution)/shard_map/all_to_all | solution.py:26
  128.3 3.2 %fusion.5 = f32[1024]{0:T(1024)S(1)} fusion(bf16[2048,1024]{0,1:T(8,128)(2,1)} %get-tuple-element.14, f32[2048]{0:T(1024)S(1)} %div.60), kind=kLoop, calls=%fused_computation.13 | loop fusion | flops 6290432 | bytes 4206592 | tf_op jit(solution)/shard_map/reduce_sum | solution.py:97
  131.7 1.2 collective-permute-done.12
  132.8 1.7 collective-permute-start.15
  134.6 0.9 collective-permute-start.14
  135.5 1.0 collective-permute-done.15
  136.4 3.2 %collective-permute-done.14 = f32[1024]{0:T(1024)S(1)} collective-permute-done((f32[1024]{0:T(1024)S(1)}, f32[1024]{0:T(1024)S(1)}, u32[]{:S(2)}, u32[]{:S(2)}) %collective-permute-start.14) | collective-permute-done | bytes 4128 | tf_op jit(solution)/shard_map/ppermute | solution.py:20
  139.7 0.6 collective-permute-done.13
  140.3 0.6 multiply_log_fusion
  140.9 0.9 fusion.6
  141.8 0.7 broadcast_in_dim.14
  142.5 3.6 %all-to-all-start.4 = ((f32[16,1,2048]{2,1,0:T(1,128)}), f32[16,1,2048]{2,1,0:T(1,128)S(1)}, u32[]{:S(2)}, u32[]{:S(2)}) async-start(f32[16,1,2048]{2,1,0:T(1,128)} %broadcast_in_dim.14), calls=%async_computation.4 | async-start | bytes 262144 | tf_op jit(solution)/shard_map/all_to_all | solution.py:26
  146.1 7.8 %all-to-all-done.4 = f32[16,1,2048]{2,1,0:T(1,128)S(1)} async-done(((f32[16,1,2048]{2,1,0:T(1,128)}), f32[16,1,2048]{2,1,0:T(1,128)S(1)}, u32[]{:S(2)}, u32[]{:S(2)}) %all-to-all-start.4) | async-done | bytes 131104 | tf_op jit(solution)/shard_map/all_to_all | solution.py:26
  154.1 0.6 fusion.22
  154.7 5.3 %fusion.10 = f32[4,96,1024]{2,1,0:T(8,128)} fusion(bf16[2048,1024]{0,1:T(8,128)(2,1)} %get-tuple-element.14, f32[2048]{0:T(1024)S(1)} %get-tuple-element.10, f32[1024]{0:T(1024)S(1)} %get-tuple-element.8, bf16[2048,4,2,96]{0,3,2,1:T(8,128)(2,1)S(1)} %bitcast.33, s32[]{:T(128)S(6)} %select_n.41), kind=kOutput, calls=%fused_computation.21 | convolution fusion | flops 1619001344 | bytes 7352324 | tf_op jit(solution)/shard_map/dot_general | solution.py:43
  159.9 4.1 %fusion.12 = f32[4,96,1024]{2,1,0:T(8,128)S(1)} fusion(bf16[2048,1024]{0,1:T(8,128)(2,1)} %get-tuple-element.14, f32[2048]{0:T(1024)S(1)} %get-tuple-element.10, f32[1024]{0:T(1024)S(1)} %get-tuple-element.8, bf16[2048,4,2,96]{0,3,2,1:T(8,128)(2,1)S(1)} %bitcast.34, s32[]{:T(128)S(6)} %select_n.39), kind=kOutput, calls=%fused_computation.22 | convolution fusion | flops 1619001344 | bytes 7352324 | tf_op jit(solution)/shard_map/dot_general | solution.py:43
  164.0 1.8 add.156
  165.8 0.1 dynamic-slice_bitcast_fusion.2
  165.9 0.9 collective-permute-start.19
  166.8 0.9 collective-permute-start.18
  167.7 1.1 collective-permute-start.17
  168.8 9.2 %collective-permute-done.19 = f32[96,1024]{1,0:T(8,128)S(1)} collective-permute-done((f32[96,1024]{1,0:T(8,128)S(1)}, f32[96,1024]{1,0:T(8,128)S(1)}, u32[]{:S(2)}, u32[]{:S(2)}) %collective-permute-start.19) | collective-permute-done | bytes 393248 | tf_op jit(solution)/shard_map/ppermute | solution.py:53
  178.0 2.4 %collective-permute-done.18 = f32[96,1024]{1,0:T(8,128)S(1)} collective-permute-done((f32[96,1024]{1,0:T(8,128)S(1)}, f32[96,1024]{1,0:T(8,128)S(1)}, u32[]{:S(2)}, u32[]{:S(2)}) %collective-permute-start.18) | collective-permute-done | bytes 393248 | tf_op jit(solution)/shard_map/ppermute | solution.py:53
  180.4 7.7 %collective-permute-done.17 = f32[96,1024]{1,0:T(8,128)} collective-permute-done((f32[96,1024]{1,0:T(8,128)S(1)}, f32[96,1024]{1,0:T(8,128)}, u32[]{:S(2)}, u32[]{:S(2)}) %collective-permute-start.17) | collective-permute-done | bytes 393248 | tf_op jit(solution)/shard_map/ppermute | solution.py:53
  188.1 1.1 multiply_reduce_fusion.2
  189.2 0.1 collective-permute-start.20
  189.3 1.1 collective-permute-done.20
  190.5 0.6 collective-permute-start.23
  191.1 0.9 collective-permute-start.22
  192.0 0.8 collective-permute-start.21
  192.9 1.2 collective-permute-done.23
  194.1 2.1 %collective-permute-done.22 = f32[1024]{0:T(1024)S(1)} collective-permute-done((f32[1024]{0:T(1024)S(1)}, f32[1024]{0:T(1024)S(1)}, u32[]{:S(2)}, u32[]{:S(2)}) %collective-permute-start.22) | collective-permute-done | bytes 4128 | tf_op jit(solution)/shard_map/ppermute | solution.py:20
  196.2 0.6 collective-permute-done.21
  196.9 0.8 broadcast_multiply_fusion
  (36 shorter events, 0.8 us)
Async XLA Ops:
  0.6 11.2 %copy-start.2 = (f32[2048]{0:T(1024)S(1)}, f32[2048]{0:T(1024)}, u32[]{:S(2)}) copy-start(f32[2048]{0:T(1024)} %param.5) | copy-start | bytes 24580
  3.6 50.6 %all-to-all-start = ((bf16[16,2048,48]{1,2,0:T(8,128)(2,1)}), bf16[16,2048,48]{1,2,0:T(8,128)(2,1)S(1)}, u32[]{:S(2)}, u32[]{:S(2)}) async-start(bf16[16,2048,48]{1,2,0:T(8,128)(2,1)} %broadcast_in_dim.10), calls=%async_computation | async-start | bytes 6291456 | tf_op jit(solution)/shard_map/all_to_all | solution.py:59
  12.4 1.8 collective-permute-start
  15.4 9.6 %collective-permute-start.1 = (f32[]{:T(128)}, f32[]{:T(128)}, u32[]{:S(2)}, u32[]{:S(2)}) collective-permute-start(f32[]{:T(128)} %add.136), channel_id=1, source_target_pairs={{0,32},{32,64},{64,96},{96,0},{1,33},{33,65},{65,97},{97,1},{2,34}... | collective-permute-start | bytes 20 | tf_op jit(solution)/shard_map/ppermute | solution.py:20
  18.3 7.3 %collective-permute-start.2 = (f32[]{:T(128)}, f32[]{:T(128)}, u32[]{:S(2)}, u32[]{:S(2)}) collective-permute-start(f32[]{:T(128)} %add.136), channel_id=1, source_target_pairs={{0,64},{32,96},{64,0},{96,32},{1,65},{33,97},{65,1},{97,33},{2,66}... | collective-permute-start | bytes 20 | tf_op jit(solution)/shard_map/ppermute | solution.py:20
  22.3 3.9 %collective-permute-start.3 = (f32[]{:T(128)}, f32[]{:T(128)}, u32[]{:S(2)}, u32[]{:S(2)}) collective-permute-start(f32[]{:T(128)} %add.136), channel_id=1, source_target_pairs={{0,96},{32,0},{64,32},{96,64},{1,97},{33,1},{65,33},{97,65},{2,98}... | collective-permute-start | bytes 20 | tf_op jit(solution)/shard_map/ppermute | solution.py:20
  80.8 1.2 collective-permute-start.4
  82.1 4.4 %collective-permute-start.7 = (f32[1024]{0:T(1024)S(1)}, f32[1024]{0:T(1024)S(1)}, u32[]{:S(2)}, u32[]{:S(2)}) collective-permute-start(f32[1024]{0:T(1024)S(1)} %add.141), channel_id=1, source_target_pairs={{0,96},{32,0},{64,32},{96,64},{1,97},{33,1},{65,33},{97,65},{2,98}... | collective-permute-start | bytes 12296 | tf_op jit(solution)/shard_map/ppermute | solution.py:20
  84.8 5.1 %collective-permute-start.6 = (f32[1024]{0:T(1024)S(1)}, f32[1024]{0:T(1024)S(1)}, u32[]{:S(2)}, u32[]{:S(2)}) collective-permute-start(f32[1024]{0:T(1024)S(1)} %add.141), channel_id=1, source_target_pairs={{0,64},{32,96},{64,0},{96,32},{1,65},{33,97},{65,1},{97,33},{2,66}... | collective-permute-start | bytes 12296 | tf_op jit(solution)/shard_map/ppermute | solution.py:20
  85.6 4.8 %collective-permute-start.5 = (f32[1024]{0:T(1024)S(1)}, f32[1024]{0:T(1024)S(1)}, u32[]{:S(2)}, u32[]{:S(2)}) collective-permute-start(f32[1024]{0:T(1024)S(1)} %add.141), channel_id=1, source_target_pairs={{0,32},{32,64},{64,96},{96,0},{1,33},{33,65},{65,97},{97,1},{2,34}... | collective-permute-start | bytes 12296 | tf_op jit(solution)/shard_map/ppermute | solution.py:20
  104.9 11.1 %copy-start = (bf16[2048,1024]{0,1:T(8,128)(2,1)S(1)}, bf16[2048,1024]{0,1:T(8,128)(2,1)}, u32[]{:S(2)}) copy-start(bf16[2048,1024]{0,1:T(8,128)(2,1)} %get-tuple-element.14) | copy-start | bytes 12582916
  108.2 1.2 collective-permute-start.8
  109.4 3.6 %collective-permute-start.11 = (f32[1024]{0:T(1024)S(1)}, f32[1024]{0:T(1024)S(1)}, u32[]{:S(2)}, u32[]{:S(2)}) collective-permute-start(f32[1024]{0:T(1024)S(1)} %add.145), channel_id=1, source_target_pairs={{0,96},{32,0},{64,32},{96,64},{1,97},{33,1},{65,33},{97,65},{2,98}... | collective-permute-start | bytes 12296 | tf_op jit(solution)/shard_map/ppermute | solution.py:20
  109.8 5.1 %collective-permute-start.10 = (f32[1024]{0:T(1024)S(1)}, f32[1024]{0:T(1024)S(1)}, u32[]{:S(2)}, u32[]{:S(2)}) collective-permute-start(f32[1024]{0:T(1024)S(1)} %add.145), channel_id=1, source_target_pairs={{0,64},{32,96},{64,0},{96,32},{1,65},{33,97},{65,1},{97,33},{2,66}... | collective-permute-start | bytes 12296 | tf_op jit(solution)/shard_map/ppermute | solution.py:20
  111.2 4.8 %collective-permute-start.9 = (f32[1024]{0:T(1024)S(1)}, f32[1024]{0:T(1024)S(1)}, u32[]{:S(2)}, u32[]{:S(2)}) collective-permute-start(f32[1024]{0:T(1024)S(1)} %add.145), channel_id=1, source_target_pairs={{0,32},{32,64},{64,96},{96,0},{1,33},{33,65},{65,97},{97,1},{2,34}... | collective-permute-start | bytes 12296 | tf_op jit(solution)/shard_map/ppermute | solution.py:20
  128.3 12.6 %copy-start.1 = (bf16[2048,1024]{0,1:T(8,128)(2,1)S(1)}, bf16[2048,1024]{0,1:T(8,128)(2,1)}, u32[]{:S(2)}) copy-start(bf16[2048,1024]{0,1:T(8,128)(2,1)} %get-tuple-element.14) | copy-start | bytes 12582916
  131.6 1.2 collective-permute-start.12
  132.8 3.6 %collective-permute-start.15 = (f32[1024]{0:T(1024)S(1)}, f32[1024]{0:T(1024)S(1)}, u32[]{:S(2)}, u32[]{:S(2)}) collective-permute-start(f32[1024]{0:T(1024)S(1)} %add.149), channel_id=1, source_target_pairs={{0,96},{32,0},{64,32},{96,64},{1,97},{33,1},{65,33},{97,65},{2,98}... | collective-permute-start | bytes 12296 | tf_op jit(solution)/shard_map/ppermute | solution.py:20
  134.6 5.1 %collective-permute-start.14 = (f32[1024]{0:T(1024)S(1)}, f32[1024]{0:T(1024)S(1)}, u32[]{:S(2)}, u32[]{:S(2)}) collective-permute-start(f32[1024]{0:T(1024)S(1)} %add.149), channel_id=1, source_target_pairs={{0,64},{32,96},{64,0},{96,32},{1,65},{33,97},{65,1},{97,33},{2,66}... | collective-permute-start | bytes 12296 | tf_op jit(solution)/shard_map/ppermute | solution.py:20
  135.5 4.8 %collective-permute-start.13 = (f32[1024]{0:T(1024)S(1)}, f32[1024]{0:T(1024)S(1)}, u32[]{:S(2)}, u32[]{:S(2)}) collective-permute-start(f32[1024]{0:T(1024)S(1)} %add.149), channel_id=1, source_target_pairs={{0,32},{32,64},{64,96},{96,0},{1,33},{33,65},{65,97},{97,1},{2,34}... | collective-permute-start | bytes 12296 | tf_op jit(solution)/shard_map/ppermute | solution.py:20
  142.5 11.4 %all-to-all-start.4 = ((f32[16,1,2048]{2,1,0:T(1,128)}), f32[16,1,2048]{2,1,0:T(1,128)S(1)}, u32[]{:S(2)}, u32[]{:S(2)}) async-start(f32[16,1,2048]{2,1,0:T(1,128)} %broadcast_in_dim.14), calls=%async_computation.4 | async-start | bytes 262144 | tf_op jit(solution)/shard_map/all_to_all | solution.py:26
  159.9 4.1 %collective-permute-start.16 = (f32[4,96,1024]{2,1,0:T(8,128)}, f32[4,96,1024]{2,1,0:T(8,128)}, u32[]{:S(2)}, u32[]{:S(2)}) collective-permute-start(f32[4,96,1024]{2,1,0:T(8,128)} %fusion.10), channel_id=1, source_target_pairs={{0,16},{16,0},{1,17},{17,1},{2,18},{18,2},{3,19},{19,3},{4,20},{20... | collective-permute-start | bytes 4718600 | tf_op jit(solution)/shard_map/ppermute | solution.py:48
  165.9 12.1 %collective-permute-start.19 = (f32[96,1024]{1,0:T(8,128)S(1)}, f32[96,1024]{1,0:T(8,128)S(1)}, u32[]{:S(2)}, u32[]{:S(2)}) collective-permute-start(f32[96,1024]{1,0:T(8,128)S(1)} %get-tuple-element.16), channel_id=1, source_target_pairs={{0,96},{32,0},{64,32},{96,64},{1,97},{33,1},{65,33},{97,65},{2,98}... | collective-permute-start | bytes 1179656 | tf_op jit(solution)/shard_map/ppermute | solution.py:53
  166.8 13.5 %collective-permute-start.18 = (f32[96,1024]{1,0:T(8,128)S(1)}, f32[96,1024]{1,0:T(8,128)S(1)}, u32[]{:S(2)}, u32[]{:S(2)}) collective-permute-start(f32[96,1024]{1,0:T(8,128)S(1)} %get-tuple-element.17), channel_id=1, source_target_pairs={{0,64},{32,96},{64,0},{96,32},{1,65},{33,97},{65,1},{97,33},{2,66}... | collective-permute-start | bytes 1179656 | tf_op jit(solution)/shard_map/ppermute | solution.py:53
  167.7 20.4 %collective-permute-start.17 = (f32[96,1024]{1,0:T(8,128)S(1)}, f32[96,1024]{1,0:T(8,128)}, u32[]{:S(2)}, u32[]{:S(2)}) collective-permute-start(f32[96,1024]{1,0:T(8,128)S(1)} %get-tuple-element.15), channel_id=1, source_target_pairs={{0,32},{32,64},{64,96},{96,0},{1,33},{33,65},{65,97},{97,1},{2,34}... | collective-permute-start | bytes 1179656 | tf_op jit(solution)/shard_map/ppermute | solution.py:53
  189.2 1.2 collective-permute-start.20
  190.5 3.6 %collective-permute-start.23 = (f32[1024]{0:T(1024)S(1)}, f32[1024]{0:T(1024)S(1)}, u32[]{:S(2)}, u32[]{:S(2)}) collective-permute-start(f32[1024]{0:T(1024)S(1)} %add.170), channel_id=1, source_target_pairs={{0,96},{32,0},{64,32},{96,64},{1,97},{33,1},{65,33},{97,65},{2,98}... | collective-permute-start | bytes 12296 | tf_op jit(solution)/shard_map/ppermute | solution.py:20
  191.1 5.1 %collective-permute-start.22 = (f32[1024]{0:T(1024)S(1)}, f32[1024]{0:T(1024)S(1)}, u32[]{:S(2)}, u32[]{:S(2)}) collective-permute-start(f32[1024]{0:T(1024)S(1)} %add.170), channel_id=1, source_target_pairs={{0,64},{32,96},{64,0},{96,32},{1,65},{33,97},{65,1},{97,33},{2,66}... | collective-permute-start | bytes 12296 | tf_op jit(solution)/shard_map/ppermute | solution.py:20
  192.0 4.8 %collective-permute-start.21 = (f32[1024]{0:T(1024)S(1)}, f32[1024]{0:T(1024)S(1)}, u32[]{:S(2)}, u32[]{:S(2)}) collective-permute-start(f32[1024]{0:T(1024)S(1)} %add.170), channel_id=1, source_target_pairs={{0,32},{32,64},{64,96},{96,0},{1,33},{33,65},{65,97},{97,1},{2,34}... | collective-permute-start | bytes 12296 | tf_op jit(solution)/shard_map/ppermute | solution.py:20

commit v15 on v14

--- a/solution.py
+++ b/solution.py
@@ -62,6 +62,13 @@
     return jnp.transpose(blocks, (1, 0, 2)).reshape(vectors.shape[0], -1)
 
 
+def column_mass(kernel, row_scale):
+    rows, cols = kernel.shape
+    grouped = kernel.reshape(rows // 128, 128, cols).astype(jnp.float32)
+    lanes = jnp.sum(grouped * row_scale.reshape(rows // 128, 128, 1), axis=0)
+    return jnp.sum(lax.optimization_barrier(lanes), axis=0)
+
+
 def row_step(kernel, col_scale, weights):
     partial_mass = jnp.sum(kernel.astype(jnp.float32) * col_scale[None, :], axis=1)
     masses = reduce_cent(partial_mass)
@@ -94,7 +101,7 @@
     col_scale = jnp.full((local_centres,), 1.0, jnp.float32) / centre_total
     row_scale = row_step(kernel, col_scale, weights)
     for sweep in range(ITERS):
-        partial_cols = jnp.sum(kernel.astype(jnp.float32) * row_scale[:, None], axis=0)
+        partial_cols = column_mass(kernel, row_scale)
         col_mass = reduce_row(partial_cols)
         col_scale = weight_sum / centre_total / col_mass
         row_scale = row_step(kernel, col_scale, weights)

time: 198 us -> 214 us (1.081)
  other arithmetic: 22.7 us -> 36.7 us
  starting transfers between devices: 37 us -> 44.2 us
  waiting for transfers between devices: 75.4 us -> 68.5 us
    reduce_sum x3 -> x6, other arithmetic: 9.52 us -> 19.2 us  [the longest x3 15.9 us: column_mass(): lanes = jnp.sum(grouped * row_scale.reshape(rows // 128, 128, 1), axis=0)]
    ppermute x20, waiting for transfers between devices: 21 us -> 15.6 us  [shifted_sum(): total = total + lax.ppermute(x, axis, [(i, (i + k) % n) for i in range(n)])]
    ppermute x20, starting transfers between devices: 22.4 us -> 27.6 us  [shifted_sum(): total = total + lax.ppermute(x, axis, [(i, (i + k) % n) for i in range(n)])]
    reduce_sum x3, other arithmetic: 4.85 us -> 9.25 us  [row_step(): jnp.sum(kernel.astype(jnp.float32) * col_scale[None, :], axis=1)]
  transfers between devices with their start and end apart: 26 -> 26, of which waited for: 20 -> 18; matrix products, arithmetic and copies ran while one was open for 3% -> 3% of each run, Pallas kernels for 0% -> 0%
where the time goes in v15:
time: 214 us; the launch traced here: 213 us
  waiting for transfers between devices  68.5 us (32%)
  starting transfers between devices  44.2 us (21%)
  blocking collectives  38 us (18%)
  other arithmetic  36.7 us (17%)
  matrix products  17.7 us (8%)
  local copies, waits for them, and re-layouts  4.05 us (2%)
  between operations  3.93 us (2%)
    all_to_all x3, blocking collectives, reduce_cent(): lax.all_to_all(jnp.broadcast_to(x, (n, *x.shape)), CENT, 0, 0, tiled=False)  38 us
    ppermute x20, starting transfers between devices, shifted_sum(): total = total + lax.ppermute(x, axis, [(i, (i + k) % n) for i in range(n)])  27.6 us
    all_to_all x1, waiting for transfers between devices, gather_features(): lax.all_to_all(jnp.broadcast_to(vectors, (n, *vectors.shape)), CENT, 0, 0...  27.3 us
    ppermute x3, waiting for transfers between devices, summed_block(): lax.ppermute(piece, 'rx', [(i, (i + k) % chips) for i in range(chips)])  17.8 us
    reduce_sum x3, other arithmetic, column_mass(): lanes = jnp.sum(grouped * row_scale.reshape(rows // 128, 128, 1), axis=0)  15.9 us
    ppermute x20, waiting for transfers between devices, shifted_sum(): total = total + lax.ppermute(x, axis, [(i, (i + k) % n) for i in range(n)])  15.6 us
    dot_general x2, matrix products, product(): lax.dot_general(part, transport, (((0,), (0,)), ((), ())), preferred_elem...  9.36 us
    reduce_sum x3, other arithmetic, row_step(): jnp.sum(kernel.astype(jnp.float32) * col_scale[None, :], axis=1)  9.25 us
  transfers between devices with their start and end apart: 26, of which 18 were waited for; matrix products, arithmetic and copies ran while one was open for 3% of the time, Pallas kernels for 0%

profile of v15, /device:TPU:0, one launch (start us, length us, event | category | flops | bytes accessed | tf_op | source)
XLA Modules:
  0.0 213.0 jit_solution(5451602479970952325)
XLA Ops:
  0.6 3.0 %broadcast_in_dim.10 = bf16[16,2048,48]{1,2,0:T(8,128)(2,1)} broadcast(bf16[2048,48]{0,1:T(8,128)(2,1)} %param.3), dimensions={1,2} | broadcast | bytes 3342336 | tf_op jit(solution)/shard_map/broadcast_in_dim | solution.py:60
  3.6 8.2 %all-to-all-start = ((bf16[16,2048,48]{1,2,0:T(8,128)(2,1)}), bf16[16,2048,48]{1,2,0:T(8,128)(2,1)S(1)}, u32[]{:S(2)}, u32[]{:S(2)}) async-start(bf16[16,2048,48]{1,2,0:T(8,128)(2,1)} %broadcast_in_dim.10), calls=%async_computation | async-start | bytes 6291456 | tf_op jit(solution)/shard_map/all_to_all | solution.py:59
  11.8 0.6 reduce_sum.163
  12.4 1.8 multiply_reduce_fusion.4
  15.4 2.9 %collective-permute-start.1 = (f32[]{:T(128)}, f32[]{:T(128)}, u32[]{:S(2)}, u32[]{:S(2)}) collective-permute-start(f32[]{:T(128)} %add.136), channel_id=1, source_target_pairs={{0,32},{32,64},{64,96},{96,0},{1,33},{33,65},{65,97},{97,1},{2,34}... | collective-permute-start | bytes 20 | tf_op jit(solution)/shard_map/ppermute | solution.py:20
  18.3 4.0 %collective-permute-start.2 = (f32[]{:T(128)}, f32[]{:T(128)}, u32[]{:S(2)}, u32[]{:S(2)}) collective-permute-start(f32[]{:T(128)} %add.136), channel_id=1, source_target_pairs={{0,64},{32,96},{64,0},{96,32},{1,65},{33,97},{65,1},{97,33},{2,66}... | collective-permute-start | bytes 20 | tf_op jit(solution)/shard_map/ppermute | solution.py:20
  22.3 2.7 %collective-permute-start.3 = (f32[]{:T(128)}, f32[]{:T(128)}, u32[]{:S(2)}, u32[]{:S(2)}) collective-permute-start(f32[]{:T(128)} %add.136), channel_id=1, source_target_pairs={{0,96},{32,0},{64,32},{96,64},{1,97},{33,1},{65,33},{97,65},{2,98}... | collective-permute-start | bytes 20 | tf_op jit(solution)/shard_map/ppermute | solution.py:20
  26.9 27.3 %all-to-all-done = bf16[16,2048,48]{1,2,0:T(8,128)(2,1)S(1)} async-done(((bf16[16,2048,48]{1,2,0:T(8,128)(2,1)}), bf16[16,2048,48]{1,2,0:T(8,128)(2,1)S(1)}, u32[]{:S(2)}, u32[]{:S(2)}) %all-to-all-start) | async-done | bytes 3145760 | tf_op jit(solution)/shard_map/all_to_all | solution.py:59
  54.2 0.7 multiply_reduce_fusion.3
  54.9 8.3 %fusion = (f32[2048]{0:T(1024)S(1)}, bf16[2048,1024]{1,0:T(8,128)(2,1)}) fusion(f32[1024]{0:T(1024)S(1)} %add_rsqrt_fusion.2, f32[2048]{0:T(1024)S(1)} %add_rsqrt_fusion, bf16[2048,768]{0,1:T(8,128)(2,1)S(1)} %bitcast.40, bf16[1024,768]{1,0:T(8,128)(2,1)} %param.4), kind=kOutput, calls=%fused_computation.5 | convolution fusion | flops 3235903488 | bytes 8933376 | tf_op jit(solution)/shard_map/dot_general | solution.py:93
  63.3 15.5 %all_to_all.29 = f32[16,1,2048]{2,1,0:T(1,128)S(1)} all-to-all(f32[16,1,2048]{2,1,0:T(1,128)S(1)} %broadcast_in_dim.11), channel_id=1, replica_groups=mesh['rx'=4,'rc'=2,'cy'=4,'cz'=4] {'cy','cz'}, dimensions={0} | all-to-all | bytes 262144 | tf_op jit(solution)/shard_map/all_to_all | solution.py:26
  78.8 0.1 reduce_sum.166
  78.9 6.1 %multiply_reduce_fusion.2 = (f32[128,1024]{1,0:T(8,128)}, f32[16,128,1024]{2,1,0:T(8,128)}) fusion(f32[16,128]{1,0:T(8,128)S(1)} %divide_bitcast_fusion.2, bf16[16,128,1024]{2,1,0:T(8,128)(2,1)} %bitcast.39), kind=kLoop, calls=%fused_computation.13 | loop fusion | flops 6160384 | bytes 13115392 | tf_op jit(solution)/shard_map/reduce_sum | solution.py:68
  85.0 1.1 reduce_sum.168
  86.2 1.2 collective-permute-done.4
  87.4 1.5 collective-permute-start.5
  88.9 2.7 %collective-permute-start.6 = (f32[1024]{0:T(1024)S(1)}, f32[1024]{0:T(1024)S(1)}, u32[]{:S(2)}, u32[]{:S(2)}) collective-permute-start(f32[1024]{0:T(1024)S(1)} %add.141), channel_id=1, source_target_pairs={{0,64},{32,96},{64,0},{96,32},{1,65},{33,97},{65,1},{97,33},{2,66}... | collective-permute-start | bytes 12296 | tf_op jit(solution)/shard_map/ppermute | solution.py:20
  91.6 1.4 collective-permute-start.7
  93.0 0.9 collective-permute-done.6
  94.0 1.2 collective-permute-done.7
  95.2 3.1 %fusion.1 = f32[2048]{0:T(1024)S(1)} fusion(bf16[2048,1024]{1,0:T(8,128)(2,1)} %get-tuple-element.16, f32[1024]{0:T(1024)S(1)} %add_divide_fusion.2), kind=kLoop, calls=%fused_computation.6 | loop fusion | flops 6289408 | bytes 4206592 | tf_op jit(solution)/shard_map/reduce_sum | solution.py:73
  98.4 11.2 %all_to_all.30 = f32[16,1,2048]{2,1,0:T(1,128)S(1)} all-to-all(f32[16,1,2048]{2,1,0:T(1,128)S(1)} %broadcast_in_dim.12), channel_id=1, replica_groups=mesh['rx'=4,'rc'=2,'cy'=4,'cz'=4] {'cy','cz'}, dimensions={0} | all-to-all | bytes 262144 | tf_op jit(solution)/shard_map/all_to_all | solution.py:26
  109.7 4.9 %multiply_reduce_fusion.1 = f32[128,1024]{1,0:T(8,128)} fusion(f32[16,128,1024]{2,1,0:T(8,128)} %get-tuple-element.14, f32[16,128]{1,0:T(8,128)S(1)} %divide_bitcast_fusion.1), kind=kLoop, calls=%fused_computation.12 | loop fusion | flops 4063232 | bytes 8921088 | tf_op jit(solution)/shard_map/reduce_sum | solution.py:68
  114.6 1.1 reduce_sum.172
  115.8 1.2 collective-permute-done.8
  116.9 1.5 collective-permute-start.10
  118.4 1.4 collective-permute-start.11
  119.9 0.6 collective-permute-start.9
  120.5 1.6 collective-permute-done.10
  122.1 2.6 %collective-permute-done.9 = f32[1024]{0:T(1024)S(1)} collective-permute-done((f32[1024]{0:T(1024)S(1)}, f32[1024]{0:T(1024)S(1)}, u32[]{:S(2)}, u32[]{:S(2)}) %collective-permute-start.9) | collective-permute-done | bytes 4128 | tf_op jit(solution)/shard_map/ppermute | solution.py:20
  124.7 3.1 %fusion.2 = f32[2048]{0:T(1024)S(1)} fusion(bf16[2048,1024]{1,0:T(8,128)(2,1)} %get-tuple-element.16, f32[1024]{0:T(1024)S(1)} %add_divide_fusion.1), kind=kLoop, calls=%fused_computation.7 | loop fusion | flops 6289408 | bytes 4206592 | tf_op jit(solution)/shard_map/reduce_sum | solution.py:73
  127.9 11.2 %all_to_all.31 = f32[16,1,2048]{2,1,0:T(1,128)S(1)} all-to-all(f32[16,1,2048]{2,1,0:T(1,128)S(1)} %broadcast_in_dim.26), channel_id=1, replica_groups=mesh['rx'=4,'rc'=2,'cy'=4,'cz'=4] {'cy','cz'}, dimensions={0} | all-to-all | bytes 262144 | tf_op jit(solution)/shard_map/all_to_all | solution.py:26
  139.2 4.9 %multiply_reduce_fusion = f32[128,1024]{1,0:T(8,128)} fusion(f32[16,128,1024]{2,1,0:T(8,128)} %get-tuple-element.14, f32[16,128]{1,0:T(8,128)S(1)} %divide_bitcast_fusion), kind=kLoop, calls=%fused_computation.11 | loop fusion | flops 4063232 | bytes 8921088 | tf_op jit(solution)/shard_map/reduce_sum | solution.py:68
  144.1 1.1 reduce_sum.176
  145.3 1.2 collective-permute-done.12
  146.4 1.5 collective-permute-start.14
  147.9 2.5 %collective-permute-start.15 = (f32[1024]{0:T(1024)S(1)}, f32[1024]{0:T(1024)S(1)}, u32[]{:S(2)}, u32[]{:S(2)}) collective-permute-start(f32[1024]{0:T(1024)S(1)} %add.149), channel_id=1, source_target_pairs={{0,96},{32,0},{64,32},{96,64},{1,97},{33,1},{65,33},{97,65},{2,98}... | collective-permute-start | bytes 12296 | tf_op jit(solution)/shard_map/ppermute | solution.py:20
  150.5 0.8 collective-permute-done.13
  151.2 0.3 collective-permute-done.14
  151.5 0.6 collective-permute-done.15
  152.1 0.6 multiply_log_fusion
  152.8 3.1 %fusion.3 = f32[2048]{0:T(1024)S(1)} fusion(bf16[2048,1024]{1,0:T(8,128)(2,1)} %get-tuple-element.16, f32[1024]{0:T(1024)S(1)} %get-tuple-element.8), kind=kLoop, calls=%fused_computation.8 | loop fusion | flops 6289408 | bytes 4206592 | tf_op jit(solution)/shard_map/reduce_sum | solution.py:73
  155.8 0.7 broadcast_in_dim.27
  156.6 3.6 %all-to-all-start.4 = ((f32[16,1,2048]{2,1,0:T(1,128)}), f32[16,1,2048]{2,1,0:T(1,128)S(1)}, u32[]{:S(2)}, u32[]{:S(2)}) async-start(f32[16,1,2048]{2,1,0:T(1,128)} %broadcast_in_dim.27), calls=%async_computation.4 | async-start | bytes 262144 | tf_op jit(solution)/shard_map/all_to_all | solution.py:26
  160.2 7.8 %all-to-all-done.4 = f32[16,1,2048]{2,1,0:T(1,128)S(1)} async-done(((f32[16,1,2048]{2,1,0:T(1,128)}), f32[16,1,2048]{2,1,0:T(1,128)S(1)}, u32[]{:S(2)}, u32[]{:S(2)}) %all-to-all-start.4) | async-done | bytes 131104 | tf_op jit(solution)/shard_map/all_to_all | solution.py:26
  168.1 0.6 fusion.19
  168.7 5.3 %fusion.7 = f32[4,96,1024]{2,1,0:T(8,128)} fusion(bf16[2048,1024]{1,0:T(8,128)(2,1)} %get-tuple-element.16, f32[2048]{0:T(1024)S(1)} %get-tuple-element.10, f32[1024]{0:T(1024)S(1)} %get-tuple-element.8, bf16[2048,4,2,96]{0,3,2,1:T(8,128)(2,1)S(1)} %bitcast.41, s32[]{:T(128)S(6)} %select_n.41), kind=kOutput, calls=%fused_computation.18 | convolution fusion | flops 1619001344 | bytes 7352324 | tf_op jit(solution)/shard_map/dot_general | solution.py:43
  174.0 4.1 %fusion.9 = f32[4,96,1024]{2,1,0:T(8,128)S(1)} fusion(bf16[2048,1024]{1,0:T(8,128)(2,1)} %get-tuple-element.16, f32[2048]{0:T(1024)S(1)} %get-tuple-element.10, f32[1024]{0:T(1024)S(1)} %get-tuple-element.8, bf16[2048,4,2,96]{0,3,2,1:T(8,128)(2,1)S(1)} %bitcast.42, s32[]{:T(128)S(6)} %select_n.39), kind=kOutput, calls=%fused_computation.19 | convolution fusion | flops 1619001344 | bytes 7352324 | tf_op jit(solution)/shard_map/dot_general | solution.py:43
  178.1 1.7 add.156
  179.8 0.1 dynamic-slice_bitcast_fusion.2
  179.9 2.1 collective-permute-start.17
  182.0 2.6 %collective-permute-start.18 = (f32[96,1024]{1,0:T(8,128)S(1)}, f32[96,1024]{1,0:T(8,128)S(1)}, u32[]{:S(2)}, u32[]{:S(2)}) collective-permute-start(f32[96,1024]{1,0:T(8,128)S(1)} %get-tuple-element.19), channel_id=1, source_target_pairs={{0,64},{32,96},{64,0},{96,32},{1,65},{33,97},{65,1},{97,33},{2,66}... | collective-permute-start | bytes 1179656 | tf_op jit(solution)/shard_map/ppermute | solution.py:53
  184.6 0.2 collective-permute-start.19
  184.7 8.2 %collective-permute-done.17 = f32[96,1024]{1,0:T(8,128)S(1)} collective-permute-done((f32[96,1024]{1,0:T(8,128)S(1)}, f32[96,1024]{1,0:T(8,128)S(1)}, u32[]{:S(2)}, u32[]{:S(2)}) %collective-permute-start.17) | collective-permute-done | bytes 393248 | tf_op jit(solution)/shard_map/ppermute | solution.py:53
  192.9 9.6 %collective-permute-done.18 = f32[96,1024]{1,0:T(8,128)S(1)} collective-permute-done((f32[96,1024]{1,0:T(8,128)S(1)}, f32[96,1024]{1,0:T(8,128)S(1)}, u32[]{:S(2)}, u32[]{:S(2)}) %collective-permute-start.18) | collective-permute-done | bytes 393248 | tf_op jit(solution)/shard_map/ppermute | solution.py:53
  202.5 1.1 multiply_reduce_fusion.5
  203.7 1.2 collective-permute-done.20
  204.9 1.1 collective-permute-start.21
  206.0 2.6 %collective-permute-start.22 = (f32[1024]{0:T(1024)S(1)}, f32[1024]{0:T(1024)S(1)}, u32[]{:S(2)}, u32[]{:S(2)}) collective-permute-start(f32[1024]{0:T(1024)S(1)} %add.170), channel_id=1, source_target_pairs={{0,64},{32,96},{64,0},{96,32},{1,65},{33,97},{65,1},{97,33},{2,66}... | collective-permute-start | bytes 12296 | tf_op jit(solution)/shard_map/ppermute | solution.py:20
  208.6 0.7 collective-permute-start.23
  209.3 0.4 collective-permute-done.21
  209.7 1.4 collective-permute-done.22
  211.1 1.1 collective-permute-done.23
  212.2 0.8 broadcast_multiply_fusion
  (35 shorter events, 0.9 us)
Async XLA Ops:
  0.6 11.2 %copy-start = (f32[2048]{0:T(1024)S(1)}, f32[2048]{0:T(1024)}, u32[]{:S(2)}) copy-start(f32[2048]{0:T(1024)} %param.5) | copy-start | bytes 24580
  3.6 50.6 %all-to-all-start = ((bf16[16,2048,48]{1,2,0:T(8,128)(2,1)}), bf16[16,2048,48]{1,2,0:T(8,128)(2,1)S(1)}, u32[]{:S(2)}, u32[]{:S(2)}) async-start(bf16[16,2048,48]{1,2,0:T(8,128)(2,1)} %broadcast_in_dim.10), calls=%async_computation | async-start | bytes 6291456 | tf_op jit(solution)/shard_map/all_to_all | solution.py:59
  12.4 1.8 collective-permute-start
  15.4 9.6 %collective-permute-start.1 = (f32[]{:T(128)}, f32[]{:T(128)}, u32[]{:S(2)}, u32[]{:S(2)}) collective-permute-start(f32[]{:T(128)} %add.136), channel_id=1, source_target_pairs={{0,32},{32,64},{64,96},{96,0},{1,33},{33,65},{65,97},{97,1},{2,34}... | collective-permute-start | bytes 20 | tf_op jit(solution)/shard_map/ppermute | solution.py:20
  18.3 7.3 %collective-permute-start.2 = (f32[]{:T(128)}, f32[]{:T(128)}, u32[]{:S(2)}, u32[]{:S(2)}) collective-permute-start(f32[]{:T(128)} %add.136), channel_id=1, source_target_pairs={{0,64},{32,96},{64,0},{96,32},{1,65},{33,97},{65,1},{97,33},{2,66}... | collective-permute-start | bytes 20 | tf_op jit(solution)/shard_map/ppermute | solution.py:20
  22.3 3.9 %collective-permute-start.3 = (f32[]{:T(128)}, f32[]{:T(128)}, u32[]{:S(2)}, u32[]{:S(2)}) collective-permute-start(f32[]{:T(128)} %add.136), channel_id=1, source_target_pairs={{0,96},{32,0},{64,32},{96,64},{1,97},{33,1},{65,33},{97,65},{2,98}... | collective-permute-start | bytes 20 | tf_op jit(solution)/shard_map/ppermute | solution.py:20
  86.1 1.2 collective-permute-start.4
  87.4 5.7 %collective-permute-start.5 = (f32[1024]{0:T(1024)S(1)}, f32[1024]{0:T(1024)S(1)}, u32[]{:S(2)}, u32[]{:S(2)}) collective-permute-start(f32[1024]{0:T(1024)S(1)} %add.141), channel_id=1, source_target_pairs={{0,32},{32,64},{64,96},{96,0},{1,33},{33,65},{65,97},{97,1},{2,34}... | collective-permute-start | bytes 12296 | tf_op jit(solution)/shard_map/ppermute | solution.py:20
  88.9 5.1 %collective-permute-start.6 = (f32[1024]{0:T(1024)S(1)}, f32[1024]{0:T(1024)S(1)}, u32[]{:S(2)}, u32[]{:S(2)}) collective-permute-start(f32[1024]{0:T(1024)S(1)} %add.141), channel_id=1, source_target_pairs={{0,64},{32,96},{64,0},{96,32},{1,65},{33,97},{65,1},{97,33},{2,66}... | collective-permute-start | bytes 12296 | tf_op jit(solution)/shard_map/ppermute | solution.py:20
  91.6 3.6 %collective-permute-start.7 = (f32[1024]{0:T(1024)S(1)}, f32[1024]{0:T(1024)S(1)}, u32[]{:S(2)}, u32[]{:S(2)}) collective-permute-start(f32[1024]{0:T(1024)S(1)} %add.141), channel_id=1, source_target_pairs={{0,96},{32,0},{64,32},{96,64},{1,97},{33,1},{65,33},{97,65},{2,98}... | collective-permute-start | bytes 12296 | tf_op jit(solution)/shard_map/ppermute | solution.py:20
  115.7 1.2 collective-permute-start.8
  116.9 5.1 %collective-permute-start.10 = (f32[1024]{0:T(1024)S(1)}, f32[1024]{0:T(1024)S(1)}, u32[]{:S(2)}, u32[]{:S(2)}) collective-permute-start(f32[1024]{0:T(1024)S(1)} %add.145), channel_id=1, source_target_pairs={{0,64},{32,96},{64,0},{96,32},{1,65},{33,97},{65,1},{97,33},{2,66}... | collective-permute-start | bytes 12296 | tf_op jit(solution)/shard_map/ppermute | solution.py:20
  118.4 3.6 %collective-permute-start.11 = (f32[1024]{0:T(1024)S(1)}, f32[1024]{0:T(1024)S(1)}, u32[]{:S(2)}, u32[]{:S(2)}) collective-permute-start(f32[1024]{0:T(1024)S(1)} %add.145), channel_id=1, source_target_pairs={{0,96},{32,0},{64,32},{96,64},{1,97},{33,1},{65,33},{97,65},{2,98}... | collective-permute-start | bytes 12296 | tf_op jit(solution)/shard_map/ppermute | solution.py:20
  119.9 4.8 %collective-permute-start.9 = (f32[1024]{0:T(1024)S(1)}, f32[1024]{0:T(1024)S(1)}, u32[]{:S(2)}, u32[]{:S(2)}) collective-permute-start(f32[1024]{0:T(1024)S(1)} %add.145), channel_id=1, source_target_pairs={{0,32},{32,64},{64,96},{96,0},{1,33},{33,65},{65,97},{97,1},{2,34}... | collective-permute-start | bytes 12296 | tf_op jit(solution)/shard_map/ppermute | solution.py:20
  145.2 1.2 collective-permute-start.12
  146.4 4.8 %collective-permute-start.13 = (f32[1024]{0:T(1024)S(1)}, f32[1024]{0:T(1024)S(1)}, u32[]{:S(2)}, u32[]{:S(2)}) collective-permute-start(f32[1024]{0:T(1024)S(1)} %add.149), channel_id=1, source_target_pairs={{0,32},{32,64},{64,96},{96,0},{1,33},{33,65},{65,97},{97,1},{2,34}... | collective-permute-start | bytes 12296 | tf_op jit(solution)/shard_map/ppermute | solution.py:20
  146.4 5.1 %collective-permute-start.14 = (f32[1024]{0:T(1024)S(1)}, f32[1024]{0:T(1024)S(1)}, u32[]{:S(2)}, u32[]{:S(2)}) collective-permute-start(f32[1024]{0:T(1024)S(1)} %add.149), channel_id=1, source_target_pairs={{0,64},{32,96},{64,0},{96,32},{1,65},{33,97},{65,1},{97,33},{2,66}... | collective-permute-start | bytes 12296 | tf_op jit(solution)/shard_map/ppermute | solution.py:20
  147.9 4.2 %collective-permute-start.15 = (f32[1024]{0:T(1024)S(1)}, f32[1024]{0:T(1024)S(1)}, u32[]{:S(2)}, u32[]{:S(2)}) collective-permute-start(f32[1024]{0:T(1024)S(1)} %add.149), channel_id=1, source_target_pairs={{0,96},{32,0},{64,32},{96,64},{1,97},{33,1},{65,33},{97,65},{2,98}... | collective-permute-start | bytes 12296 | tf_op jit(solution)/shard_map/ppermute | solution.py:20
  156.6 11.4 %all-to-all-start.4 = ((f32[16,1,2048]{2,1,0:T(1,128)}), f32[16,1,2048]{2,1,0:T(1,128)S(1)}, u32[]{:S(2)}, u32[]{:S(2)}) async-start(f32[16,1,2048]{2,1,0:T(1,128)} %broadcast_in_dim.27), calls=%async_computation.4 | async-start | bytes 262144 | tf_op jit(solution)/shard_map/all_to_all | solution.py:26
  174.0 4.1 %collective-permute-start.16 = (f32[4,96,1024]{2,1,0:T(8,128)}, f32[4,96,1024]{2,1,0:T(8,128)}, u32[]{:S(2)}, u32[]{:S(2)}) collective-permute-start(f32[4,96,1024]{2,1,0:T(8,128)} %fusion.7), channel_id=1, source_target_pairs={{0,16},{16,0},{1,17},{17,1},{2,18},{18,2},{3,19},{19,3},{4,20},{20... | collective-permute-start | bytes 4718600 | tf_op jit(solution)/shard_map/ppermute | solution.py:48
  179.9 13.0 %collective-permute-start.17 = (f32[96,1024]{1,0:T(8,128)S(1)}, f32[96,1024]{1,0:T(8,128)S(1)}, u32[]{:S(2)}, u32[]{:S(2)}) collective-permute-start(f32[96,1024]{1,0:T(8,128)S(1)} %get-tuple-element.17), channel_id=1, source_target_pairs={{0,32},{32,64},{64,96},{96,0},{1,33},{33,65},{65,97},{97,1},{2,34}... | collective-permute-start | bytes 1179656 | tf_op jit(solution)/shard_map/ppermute | solution.py:53
  182.0 20.6 %collective-permute-start.18 = (f32[96,1024]{1,0:T(8,128)S(1)}, f32[96,1024]{1,0:T(8,128)S(1)}, u32[]{:S(2)}, u32[]{:S(2)}) collective-permute-start(f32[96,1024]{1,0:T(8,128)S(1)} %get-tuple-element.19), channel_id=1, source_target_pairs={{0,64},{32,96},{64,0},{96,32},{1,65},{33,97},{65,1},{97,33},{2,66}... | collective-permute-start | bytes 1179656 | tf_op jit(solution)/shard_map/ppermute | solution.py:53
  184.6 17.9 %collective-permute-start.19 = (f32[96,1024]{1,0:T(8,128)S(1)}, f32[96,1024]{1,0:T(8,128)}, u32[]{:S(2)}, u32[]{:S(2)}) collective-permute-start(f32[96,1024]{1,0:T(8,128)S(1)} %get-tuple-element.18), channel_id=1, source_target_pairs={{0,96},{32,0},{64,32},{96,64},{1,97},{33,1},{65,33},{97,65},{2,98}... | collective-permute-start | bytes 1179656 | tf_op jit(solution)/shard_map/ppermute | solution.py:53
  203.6 1.2 collective-permute-start.20
  204.9 4.8 %collective-permute-start.21 = (f32[1024]{0:T(1024)S(1)}, f32[1024]{0:T(1024)S(1)}, u32[]{:S(2)}, u32[]{:S(2)}) collective-permute-start(f32[1024]{0:T(1024)S(1)} %add.170), channel_id=1, source_target_pairs={{0,32},{32,64},{64,96},{96,0},{1,33},{33,65},{65,97},{97,1},{2,34}... | collective-permute-start | bytes 12296 | tf_op jit(solution)/shard_map/ppermute | solution.py:20
  206.0 5.1 %collective-permute-start.22 = (f32[1024]{0:T(1024)S(1)}, f32[1024]{0:T(1024)S(1)}, u32[]{:S(2)}, u32[]{:S(2)}) collective-permute-start(f32[1024]{0:T(1024)S(1)} %add.170), channel_id=1, source_target_pairs={{0,64},{32,96},{64,0},{96,32},{1,65},{33,97},{65,1},{97,33},{2,66}... | collective-permute-start | bytes 12296 | tf_op jit(solution)/shard_map/ppermute | solution.py:20
  208.6 3.6 %collective-permute-start.23 = (f32[1024]{0:T(1024)S(1)}, f32[1024]{0:T(1024)S(1)}, u32[]{:S(2)}, u32[]{:S(2)}) collective-permute-start(f32[1024]{0:T(1024)S(1)} %add.170), channel_id=1, source_target_pairs={{0,96},{32,0},{64,32},{96,64},{1,97},{33,1},{65,33},{97,65},{2,98}... | collective-permute-start | bytes 12296 | tf_op jit(solution)/shard_map/ppermute | solution.py:20

commit v16 on v14

--- a/solution.py
+++ b/solution.py
@@ -46,10 +46,16 @@
 
     sent = product((rc + 1) % cores)
     received = lax.ppermute(sent, "rc", [(i, (i + 1) % cores) for i in range(cores)])
-    half = lax.optimization_barrier(product(rc)) + received
-    total = lax.dynamic_index_in_dim(half, rx, 0, keepdims=False)
+    kept = lax.optimization_barrier(product(rc))
+
+    def half_block(chip):
+        return lax.dynamic_index_in_dim(kept, chip, 0, keepdims=False) + (
+            lax.dynamic_index_in_dim(received, chip, 0, keepdims=False)
+        )
+
+    total = half_block(rx)
     for k in range(1, chips):
-        piece = lax.dynamic_index_in_dim(half, (rx + k) % chips, 0, keepdims=False)
+        piece = half_block((rx + k) % chips)
         total = total + lax.ppermute(piece, "rx", [(i, (i + k) % chips) for i in range(chips)])
     return total
 

time: 198 us -> 199 us (level)
  starting transfers between devices: 37 us -> 44 us
  waiting for transfers between devices: 75.4 us -> 68.5 us
    ppermute x20, waiting for transfers between devices: 21 us -> 15.6 us  [shifted_sum(): total = total + lax.ppermute(x, axis, [(i, (i + k) % n) for i in range(n)])]
    ppermute x20, starting transfers between devices: 22.4 us -> 27.5 us  [shifted_sum(): total = total + lax.ppermute(x, axis, [(i, (i + k) % n) for i in range(n)])]
  transfers between devices with their start and end apart: 26 -> 26, of which waited for: 20 -> 18; matrix products, arithmetic and copies ran while one was open for 3% -> 3% of each run, Pallas kernels for 0% -> 0%
where the time goes in v16:
time: 199 us
  waiting for transfers between devices  68.5 us (34%)
  starting transfers between devices  44 us (22%)
  blocking collectives  38 us (19%)
  other arithmetic  22.6 us (11%)
  matrix products  16.5 us (8%)
  local copies, waits for them, and re-layouts  5.07 us (3%)
  between operations  3.96 us (2%)
    all_to_all x3, blocking collectives, reduce_cent(): lax.all_to_all(jnp.broadcast_to(x, (n, *x.shape)), CENT, 0, 0, tiled=False)  38 us
    ppermute x20, starting transfers between devices, shifted_sum(): total = total + lax.ppermute(x, axis, [(i, (i + k) % n) for i in range(n)])  27.5 us
    all_to_all x1, waiting for transfers between devices, gather_features(): lax.all_to_all(jnp.broadcast_to(vectors, (n, *vectors.shape)), CENT, 0, 0...  27.3 us
    ppermute x3, waiting for transfers between devices, summed_block(): lax.ppermute(piece, 'rx', [(i, (i + k) % chips) for i in range(chips)])  17.8 us
    ppermute x20, waiting for transfers between devices, shifted_sum(): total = total + lax.ppermute(x, axis, [(i, (i + k) % n) for i in range(n)])  15.6 us
    reduce_sum x3, other arithmetic, per_device(): jnp.sum(kernel.astype(jnp.float32) * row_scale[:, None], axis=0)  9.52 us
    dot_general x2, matrix products, product(): lax.dot_general(part, transport, (((0,), (0,)), ((), ())), preferred_elem...  9.34 us
    all_to_all x1, starting transfers between devices, gather_features(): lax.all_to_all(jnp.broadcast_to(vectors, (n, *vectors.shape)), CENT, 0, 0...  8.16 us
  transfers between devices with their start and end apart: 26, of which 18 were waited for; matrix products, arithmetic and copies ran while one was open for 3% of the time, Pallas kernels for 0%

profile of v16, /device:TPU:0, one launch (start us, length us, event | category | flops | bytes accessed | tf_op | source)
XLA Modules:
  0.0 198.7 jit_solution(4914157051914401505)
XLA Ops:
  0.6 3.0 %broadcast_in_dim.10 = bf16[16,2048,48]{1,2,0:T(8,128)(2,1)} broadcast(bf16[2048,48]{0,1:T(8,128)(2,1)} %param.3), dimensions={1,2} | broadcast | bytes 3342336 | tf_op jit(solution)/shard_map/broadcast_in_dim | solution.py:66
  3.6 8.2 %all-to-all-start = ((bf16[16,2048,48]{1,2,0:T(8,128)(2,1)}), bf16[16,2048,48]{1,2,0:T(8,128)(2,1)S(1)}, u32[]{:S(2)}, u32[]{:S(2)}) async-start(bf16[16,2048,48]{1,2,0:T(8,128)(2,1)} %broadcast_in_dim.10), calls=%async_computation | async-start | bytes 6291456 | tf_op jit(solution)/shard_map/all_to_all | solution.py:65
  11.8 0.6 reduce_sum.136
  12.4 1.8 multiply_reduce_fusion.1
  15.4 2.9 %collective-permute-start.1 = (f32[]{:T(128)}, f32[]{:T(128)}, u32[]{:S(2)}, u32[]{:S(2)}) collective-permute-start(f32[]{:T(128)} %add.161), channel_id=1, source_target_pairs={{0,32},{32,64},{64,96},{96,0},{1,33},{33,65},{65,97},{97,1},{2,34}... | collective-permute-start | bytes 20 | tf_op jit(solution)/shard_map/ppermute | solution.py:20
  18.3 4.0 %collective-permute-start.2 = (f32[]{:T(128)}, f32[]{:T(128)}, u32[]{:S(2)}, u32[]{:S(2)}) collective-permute-start(f32[]{:T(128)} %add.161), channel_id=1, source_target_pairs={{0,64},{32,96},{64,0},{96,32},{1,65},{33,97},{65,1},{97,33},{2,66}... | collective-permute-start | bytes 20 | tf_op jit(solution)/shard_map/ppermute | solution.py:20
  22.3 2.7 %collective-permute-start.3 = (f32[]{:T(128)}, f32[]{:T(128)}, u32[]{:S(2)}, u32[]{:S(2)}) collective-permute-start(f32[]{:T(128)} %add.161), channel_id=1, source_target_pairs={{0,96},{32,0},{64,32},{96,64},{1,97},{33,1},{65,33},{97,65},{2,98}... | collective-permute-start | bytes 20 | tf_op jit(solution)/shard_map/ppermute | solution.py:20
  26.9 27.3 %all-to-all-done = bf16[16,2048,48]{1,2,0:T(8,128)(2,1)S(1)} async-done(((bf16[16,2048,48]{1,2,0:T(8,128)(2,1)}), bf16[16,2048,48]{1,2,0:T(8,128)(2,1)S(1)}, u32[]{:S(2)}, u32[]{:S(2)}) %all-to-all-start) | async-done | bytes 3145760 | tf_op jit(solution)/shard_map/all_to_all | solution.py:65
  54.2 0.7 multiply_reduce_fusion
  54.9 7.2 %fusion = (f32[2048]{0:T(1024)S(1)}, bf16[2048,1024]{0,1:T(8,128)(2,1)}) fusion(f32[1024]{0:T(1024)S(1)} %add_rsqrt_fusion.2, f32[2048]{0:T(1024)S(1)} %add_rsqrt_fusion, bf16[1024,768]{1,0:T(8,128)(2,1)} %param.4, bf16[2048,768]{0,1:T(8,128)(2,1)S(1)} %bitcast.32), kind=kOutput, calls=%fused_computation.8 | convolution fusion | flops 3235903488 | bytes 8933376 | tf_op jit(solution)/shard_map/dot_general | solution.py:92
  62.1 15.5 %all_to_all.29 = f32[16,1,2048]{2,1,0:T(1,128)S(1)} all-to-all(f32[16,1,2048]{2,1,0:T(1,128)S(1)} %broadcast_in_dim.11), channel_id=1, replica_groups=mesh['rx'=4,'rc'=2,'cy'=4,'cz'=4] {'cy','cz'}, dimensions={0} | all-to-all | bytes 262144 | tf_op jit(solution)/shard_map/all_to_all | solution.py:26
  77.6 0.1 reduce_sum.139
  77.7 3.1 %fusion.1 = f32[1024]{0:T(1024)S(1)} fusion(bf16[2048,1024]{0,1:T(8,128)(2,1)} %get-tuple-element.14, f32[2048]{0:T(1024)S(1)} %div.56), kind=kLoop, calls=%fused_computation.9 | loop fusion | flops 6290432 | bytes 4206592 | tf_op jit(solution)/shard_map/reduce_sum | solution.py:103
  80.9 1.2 collective-permute-done.4
  82.1 1.5 collective-permute-start.5
  83.5 2.7 %collective-permute-start.6 = (f32[1024]{0:T(1024)S(1)}, f32[1024]{0:T(1024)S(1)}, u32[]{:S(2)}, u32[]{:S(2)}) collective-permute-start(f32[1024]{0:T(1024)S(1)} %add.166), channel_id=1, source_target_pairs={{0,64},{32,96},{64,0},{96,32},{1,65},{33,97},{65,1},{97,33},{2,66}... | collective-permute-start | bytes 12296 | tf_op jit(solution)/shard_map/ppermute | solution.py:20
  86.3 1.4 collective-permute-start.7
  87.7 0.9 collective-permute-done.6
  88.7 1.2 collective-permute-done.7
  89.9 3.1 %fusion.2 = f32[2048]{0:T(1024)S(1)} fusion(bf16[2048,1024]{0,1:T(8,128)(2,1)} %get-tuple-element.14, f32[1024]{0:T(1024)S(1)} %add_divide_fusion.2), kind=kLoop, calls=%fused_computation.10 | loop fusion | flops 6289408 | bytes 4206592 | tf_op jit(solution)/shard_map/reduce_sum | solution.py:72
  93.1 11.2 %all_to_all.30 = f32[16,1,2048]{2,1,0:T(1,128)S(1)} all-to-all(f32[16,1,2048]{2,1,0:T(1,128)S(1)} %broadcast_in_dim.12), channel_id=1, replica_groups=mesh['rx'=4,'rc'=2,'cy'=4,'cz'=4] {'cy','cz'}, dimensions={0} | all-to-all | bytes 262144 | tf_op jit(solution)/shard_map/all_to_all | solution.py:26
  104.3 0.1 reduce_sum.142
  104.4 3.2 %fusion.3 = f32[1024]{0:T(1024)S(1)} fusion(bf16[2048,1024]{0,1:T(8,128)(2,1)} %get-tuple-element.14, f32[2048]{0:T(1024)S(1)} %div.58), kind=kLoop, calls=%fused_computation.11 | loop fusion | flops 6290432 | bytes 4206592 | tf_op jit(solution)/shard_map/reduce_sum | solution.py:103
  107.7 1.2 collective-permute-done.8
  108.9 1.5 collective-permute-start.10
  110.4 1.4 collective-permute-start.11
  111.8 0.6 collective-permute-start.9
  112.4 1.6 collective-permute-done.10
  114.0 2.6 %collective-permute-done.9 = f32[1024]{0:T(1024)S(1)} collective-permute-done((f32[1024]{0:T(1024)S(1)}, f32[1024]{0:T(1024)S(1)}, u32[]{:S(2)}, u32[]{:S(2)}) %collective-permute-start.9) | collective-permute-done | bytes 4128 | tf_op jit(solution)/shard_map/ppermute | solution.py:20
  116.7 0.9 fusion.4
  117.6 11.2 %all_to_all.31 = f32[16,1,2048]{2,1,0:T(1,128)S(1)} all-to-all(f32[16,1,2048]{2,1,0:T(1,128)S(1)} %broadcast_in_dim.13), channel_id=1, replica_groups=mesh['rx'=4,'rc'=2,'cy'=4,'cz'=4] {'cy','cz'}, dimensions={0} | all-to-all | bytes 262144 | tf_op jit(solution)/shard_map/all_to_all | solution.py:26
  128.9 0.1 reduce_sum.145
  129.0 3.2 %fusion.5 = f32[1024]{0:T(1024)S(1)} fusion(bf16[2048,1024]{0,1:T(8,128)(2,1)} %get-tuple-element.14, f32[2048]{0:T(1024)S(1)} %div.60), kind=kLoop, calls=%fused_computation.13 | loop fusion | flops 6290432 | bytes 4206592 | tf_op jit(solution)/shard_map/reduce_sum | solution.py:103
  132.3 1.2 collective-permute-done.12
  133.5 1.5 collective-permute-start.14
  135.0 2.5 %collective-permute-start.15 = (f32[1024]{0:T(1024)S(1)}, f32[1024]{0:T(1024)S(1)}, u32[]{:S(2)}, u32[]{:S(2)}) collective-permute-start(f32[1024]{0:T(1024)S(1)} %add.174), channel_id=1, source_target_pairs={{0,96},{32,0},{64,32},{96,64},{1,97},{33,1},{65,33},{97,65},{2,98}... | collective-permute-start | bytes 12296 | tf_op jit(solution)/shard_map/ppermute | solution.py:20
  137.5 0.8 collective-permute-done.13
  138.3 0.3 collective-permute-done.14
  138.6 0.6 collective-permute-done.15
  139.2 0.6 multiply_log_fusion
  139.8 0.9 fusion.6
  140.7 0.7 broadcast_in_dim.14
  141.4 3.6 %all-to-all-start.4 = ((f32[16,1,2048]{2,1,0:T(1,128)}), f32[16,1,2048]{2,1,0:T(1,128)S(1)}, u32[]{:S(2)}, u32[]{:S(2)}) async-start(f32[16,1,2048]{2,1,0:T(1,128)} %broadcast_in_dim.14), calls=%async_computation.4 | async-start | bytes 262144 | tf_op jit(solution)/shard_map/all_to_all | solution.py:26
  145.0 7.8 %all-to-all-done.4 = f32[16,1,2048]{2,1,0:T(1,128)S(1)} async-done(((f32[16,1,2048]{2,1,0:T(1,128)}), f32[16,1,2048]{2,1,0:T(1,128)S(1)}, u32[]{:S(2)}, u32[]{:S(2)}) %all-to-all-start.4) | async-done | bytes 131104 | tf_op jit(solution)/shard_map/all_to_all | solution.py:26
  152.9 0.1 reduce_sum.148
  153.0 0.6 fusion.22
  153.6 5.3 %fusion.10 = f32[4,96,1024]{2,1,0:T(8,128)} fusion(bf16[2048,1024]{0,1:T(8,128)(2,1)} %get-tuple-element.14, f32[2048]{0:T(1024)S(1)} %get-tuple-element.10, f32[1024]{0:T(1024)S(1)} %get-tuple-element.8, bf16[2048,4,2,96]{0,3,2,1:T(8,128)(2,1)S(1)} %bitcast.33, s32[]{:T(128)S(6)} %select_n.46), kind=kOutput, calls=%fused_computation.21 | convolution fusion | flops 1619001344 | bytes 7352324 | tf_op jit(solution)/shard_map/dot_general | solution.py:43
  158.8 4.1 %fusion.12 = f32[4,96,1024]{2,1,0:T(8,128)S(1)} fusion(bf16[2048,1024]{0,1:T(8,128)(2,1)} %get-tuple-element.14, f32[2048]{0:T(1024)S(1)} %get-tuple-element.10, f32[1024]{0:T(1024)S(1)} %get-tuple-element.8, bf16[2048,4,2,96]{0,3,2,1:T(8,128)(2,1)S(1)} %bitcast.34, s32[]{:T(128)S(6)} %select_n.43), kind=kOutput, calls=%fused_computation.22 | convolution fusion | flops 1619001344 | bytes 7352324 | tf_op jit(solution)/shard_map/dot_general | solution.py:43
  162.9 1.1 copy-done.2
  164.1 1.4 add_bitcast_fusion.2
  165.5 2.1 %collective-permute-start.17 = (f32[96,1024]{1,0:T(8,128)S(1)}, f32[96,1024]{1,0:T(8,128)S(1)}, u32[]{:S(2)}, u32[]{:S(2)}) collective-permute-start(f32[96,1024]{1,0:T(8,128)S(1)} %get-tuple-element.15), channel_id=1, source_target_pairs={{0,32},{32,64},{64,96},{96,0},{1,33},{33,65},{65,97},{97,1},{2,34}... | collective-permute-start | bytes 1179656 | tf_op jit(solution)/shard_map/ppermute | solution.py:59
  167.6 2.6 %collective-permute-start.18 = (f32[96,1024]{1,0:T(8,128)S(1)}, f32[96,1024]{1,0:T(8,128)S(1)}, u32[]{:S(2)}, u32[]{:S(2)}) collective-permute-start(f32[96,1024]{1,0:T(8,128)S(1)} %get-tuple-element.17), channel_id=1, source_target_pairs={{0,64},{32,96},{64,0},{96,32},{1,65},{33,97},{65,1},{97,33},{2,66}... | collective-permute-start | bytes 1179656 | tf_op jit(solution)/shard_map/ppermute | solution.py:59
  170.2 0.1 collective-permute-start.19
  170.4 8.2 %collective-permute-done.17 = f32[96,1024]{1,0:T(8,128)S(1)} collective-permute-done((f32[96,1024]{1,0:T(8,128)S(1)}, f32[96,1024]{1,0:T(8,128)S(1)}, u32[]{:S(2)}, u32[]{:S(2)}) %collective-permute-start.17) | collective-permute-done | bytes 393248 | tf_op jit(solution)/shard_map/ppermute | solution.py:59
  178.5 9.6 %collective-permute-done.18 = f32[96,1024]{1,0:T(8,128)S(1)} collective-permute-done((f32[96,1024]{1,0:T(8,128)S(1)}, f32[96,1024]{1,0:T(8,128)S(1)}, u32[]{:S(2)}, u32[]{:S(2)}) %collective-permute-start.18) | collective-permute-done | bytes 393248 | tf_op jit(solution)/shard_map/ppermute | solution.py:59
  188.1 1.3 multiply_reduce_fusion.2
  189.5 1.2 collective-permute-done.20
  190.7 1.0 collective-permute-start.21
  191.7 2.6 %collective-permute-start.22 = (f32[1024]{0:T(1024)S(1)}, f32[1024]{0:T(1024)S(1)}, u32[]{:S(2)}, u32[]{:S(2)}) collective-permute-start(f32[1024]{0:T(1024)S(1)} %add.202), channel_id=1, source_target_pairs={{0,64},{32,96},{64,0},{96,32},{1,65},{33,97},{65,1},{97,33},{2,66}... | collective-permute-start | bytes 12296 | tf_op jit(solution)/shard_map/ppermute | solution.py:20
  194.3 0.7 collective-permute-start.23
  194.9 0.5 collective-permute-done.21
  195.5 1.3 collective-permute-done.22
  196.8 1.1 collective-permute-done.23
  197.9 0.8 broadcast_multiply_fusion
  (37 shorter events, 0.7 us)
Async XLA Ops:
  0.6 11.2 %copy-start.3 = (f32[2048]{0:T(1024)S(1)}, f32[2048]{0:T(1024)}, u32[]{:S(2)}) copy-start(f32[2048]{0:T(1024)} %param.5) | copy-start | bytes 24580
  3.6 50.6 %all-to-all-start = ((bf16[16,2048,48]{1,2,0:T(8,128)(2,1)}), bf16[16,2048,48]{1,2,0:T(8,128)(2,1)S(1)}, u32[]{:S(2)}, u32[]{:S(2)}) async-start(bf16[16,2048,48]{1,2,0:T(8,128)(2,1)} %broadcast_in_dim.10), calls=%async_computation | async-start | bytes 6291456 | tf_op jit(solution)/shard_map/all_to_all | solution.py:65
  12.4 1.8 collective-permute-start
  15.4 9.6 %collective-permute-start.1 = (f32[]{:T(128)}, f32[]{:T(128)}, u32[]{:S(2)}, u32[]{:S(2)}) collective-permute-start(f32[]{:T(128)} %add.161), channel_id=1, source_target_pairs={{0,32},{32,64},{64,96},{96,0},{1,33},{33,65},{65,97},{97,1},{2,34}... | collective-permute-start | bytes 20 | tf_op jit(solution)/shard_map/ppermute | solution.py:20
  18.3 7.3 %collective-permute-start.2 = (f32[]{:T(128)}, f32[]{:T(128)}, u32[]{:S(2)}, u32[]{:S(2)}) collective-permute-start(f32[]{:T(128)} %add.161), channel_id=1, source_target_pairs={{0,64},{32,96},{64,0},{96,32},{1,65},{33,97},{65,1},{97,33},{2,66}... | collective-permute-start | bytes 20 | tf_op jit(solution)/shard_map/ppermute | solution.py:20
  22.3 3.9 %collective-permute-start.3 = (f32[]{:T(128)}, f32[]{:T(128)}, u32[]{:S(2)}, u32[]{:S(2)}) collective-permute-start(f32[]{:T(128)} %add.161), channel_id=1, source_target_pairs={{0,96},{32,0},{64,32},{96,64},{1,97},{33,1},{65,33},{97,65},{2,98}... | collective-permute-start | bytes 20 | tf_op jit(solution)/shard_map/ppermute | solution.py:20
  80.8 1.2 collective-permute-start.4
  82.1 5.7 %collective-permute-start.5 = (f32[1024]{0:T(1024)S(1)}, f32[1024]{0:T(1024)S(1)}, u32[]{:S(2)}, u32[]{:S(2)}) collective-permute-start(f32[1024]{0:T(1024)S(1)} %add.166), channel_id=1, source_target_pairs={{0,32},{32,64},{64,96},{96,0},{1,33},{33,65},{65,97},{97,1},{2,34}... | collective-permute-start | bytes 12296 | tf_op jit(solution)/shard_map/ppermute | solution.py:20
  83.5 5.1 %collective-permute-start.6 = (f32[1024]{0:T(1024)S(1)}, f32[1024]{0:T(1024)S(1)}, u32[]{:S(2)}, u32[]{:S(2)}) collective-permute-start(f32[1024]{0:T(1024)S(1)} %add.166), channel_id=1, source_target_pairs={{0,64},{32,96},{64,0},{96,32},{1,65},{33,97},{65,1},{97,33},{2,66}... | collective-permute-start | bytes 12296 | tf_op jit(solution)/shard_map/ppermute | solution.py:20
  86.3 3.6 %collective-permute-start.7 = (f32[1024]{0:T(1024)S(1)}, f32[1024]{0:T(1024)S(1)}, u32[]{:S(2)}, u32[]{:S(2)}) collective-permute-start(f32[1024]{0:T(1024)S(1)} %add.166), channel_id=1, source_target_pairs={{0,96},{32,0},{64,32},{96,64},{1,97},{33,1},{65,33},{97,65},{2,98}... | collective-permute-start | bytes 12296 | tf_op jit(solution)/shard_map/ppermute | solution.py:20
  104.4 12.3 %copy-start = (bf16[2048,1024]{0,1:T(8,128)(2,1)S(1)}, bf16[2048,1024]{0,1:T(8,128)(2,1)}, u32[]{:S(2)}) copy-start(bf16[2048,1024]{0,1:T(8,128)(2,1)} %get-tuple-element.14) | copy-start | bytes 12582916
  107.6 1.2 collective-permute-start.8
  108.9 5.1 %collective-permute-start.10 = (f32[1024]{0:T(1024)S(1)}, f32[1024]{0:T(1024)S(1)}, u32[]{:S(2)}, u32[]{:S(2)}) collective-permute-start(f32[1024]{0:T(1024)S(1)} %add.170), channel_id=1, source_target_pairs={{0,64},{32,96},{64,0},{96,32},{1,65},{33,97},{65,1},{97,33},{2,66}... | collective-permute-start | bytes 12296 | tf_op jit(solution)/shard_map/ppermute | solution.py:20
  110.4 3.6 %collective-permute-start.11 = (f32[1024]{0:T(1024)S(1)}, f32[1024]{0:T(1024)S(1)}, u32[]{:S(2)}, u32[]{:S(2)}) collective-permute-start(f32[1024]{0:T(1024)S(1)} %add.170), channel_id=1, source_target_pairs={{0,96},{32,0},{64,32},{96,64},{1,97},{33,1},{65,33},{97,65},{2,98}... | collective-permute-start | bytes 12296 | tf_op jit(solution)/shard_map/ppermute | solution.py:20
  111.8 4.8 %collective-permute-start.9 = (f32[1024]{0:T(1024)S(1)}, f32[1024]{0:T(1024)S(1)}, u32[]{:S(2)}, u32[]{:S(2)}) collective-permute-start(f32[1024]{0:T(1024)S(1)} %add.170), channel_id=1, source_target_pairs={{0,32},{32,64},{64,96},{96,0},{1,33},{33,65},{65,97},{97,1},{2,34}... | collective-permute-start | bytes 12296 | tf_op jit(solution)/shard_map/ppermute | solution.py:20
  129.0 10.8 %copy-start.1 = (bf16[2048,1024]{0,1:T(8,128)(2,1)S(1)}, bf16[2048,1024]{0,1:T(8,128)(2,1)}, u32[]{:S(2)}) copy-start(bf16[2048,1024]{0,1:T(8,128)(2,1)} %get-tuple-element.14) | copy-start | bytes 12582916
  132.2 1.2 collective-permute-start.12
  133.5 4.8 %collective-permute-start.13 = (f32[1024]{0:T(1024)S(1)}, f32[1024]{0:T(1024)S(1)}, u32[]{:S(2)}, u32[]{:S(2)}) collective-permute-start(f32[1024]{0:T(1024)S(1)} %add.174), channel_id=1, source_target_pairs={{0,32},{32,64},{64,96},{96,0},{1,33},{33,65},{65,97},{97,1},{2,34}... | collective-permute-start | bytes 12296 | tf_op jit(solution)/shard_map/ppermute | solution.py:20
  133.5 5.1 %collective-permute-start.14 = (f32[1024]{0:T(1024)S(1)}, f32[1024]{0:T(1024)S(1)}, u32[]{:S(2)}, u32[]{:S(2)}) collective-permute-start(f32[1024]{0:T(1024)S(1)} %add.174), channel_id=1, source_target_pairs={{0,64},{32,96},{64,0},{96,32},{1,65},{33,97},{65,1},{97,33},{2,66}... | collective-permute-start | bytes 12296 | tf_op jit(solution)/shard_map/ppermute | solution.py:20
  135.0 4.2 %collective-permute-start.15 = (f32[1024]{0:T(1024)S(1)}, f32[1024]{0:T(1024)S(1)}, u32[]{:S(2)}, u32[]{:S(2)}) collective-permute-start(f32[1024]{0:T(1024)S(1)} %add.174), channel_id=1, source_target_pairs={{0,96},{32,0},{64,32},{96,64},{1,97},{33,1},{65,33},{97,65},{2,98}... | collective-permute-start | bytes 12296 | tf_op jit(solution)/shard_map/ppermute | solution.py:20
  141.4 11.4 %all-to-all-start.4 = ((f32[16,1,2048]{2,1,0:T(1,128)}), f32[16,1,2048]{2,1,0:T(1,128)S(1)}, u32[]{:S(2)}, u32[]{:S(2)}) async-start(f32[16,1,2048]{2,1,0:T(1,128)} %broadcast_in_dim.14), calls=%async_computation.4 | async-start | bytes 262144 | tf_op jit(solution)/shard_map/all_to_all | solution.py:26
  158.8 4.1 %collective-permute-start.16 = (f32[4,96,1024]{2,1,0:T(8,128)}, f32[4,96,1024]{2,1,0:T(8,128)}, u32[]{:S(2)}, u32[]{:S(2)}) collective-permute-start(f32[4,96,1024]{2,1,0:T(8,128)} %fusion.10), channel_id=1, source_target_pairs={{0,16},{16,0},{1,17},{17,1},{2,18},{18,2},{3,19},{19,3},{4,20},{20... | collective-permute-start | bytes 4718600 | tf_op jit(solution)/shard_map/ppermute | solution.py:48
  162.9 1.2 copy-start.2
  165.5 13.0 %collective-permute-start.17 = (f32[96,1024]{1,0:T(8,128)S(1)}, f32[96,1024]{1,0:T(8,128)S(1)}, u32[]{:S(2)}, u32[]{:S(2)}) collective-permute-start(f32[96,1024]{1,0:T(8,128)S(1)} %get-tuple-element.15), channel_id=1, source_target_pairs={{0,32},{32,64},{64,96},{96,0},{1,33},{33,65},{65,97},{97,1},{2,34}... | collective-permute-start | bytes 1179656 | tf_op jit(solution)/shard_map/ppermute | solution.py:59
  167.6 20.6 %collective-permute-start.18 = (f32[96,1024]{1,0:T(8,128)S(1)}, f32[96,1024]{1,0:T(8,128)S(1)}, u32[]{:S(2)}, u32[]{:S(2)}) collective-permute-start(f32[96,1024]{1,0:T(8,128)S(1)} %get-tuple-element.17), channel_id=1, source_target_pairs={{0,64},{32,96},{64,0},{96,32},{1,65},{33,97},{65,1},{97,33},{2,66}... | collective-permute-start | bytes 1179656 | tf_op jit(solution)/shard_map/ppermute | solution.py:59
  170.2 17.9 %collective-permute-start.19 = (f32[96,1024]{1,0:T(8,128)S(1)}, f32[96,1024]{1,0:T(8,128)S(1)}, u32[]{:S(2)}, u32[]{:S(2)}) collective-permute-start(f32[96,1024]{1,0:T(8,128)S(1)} %get-tuple-element.16), channel_id=1, source_target_pairs={{0,96},{32,0},{64,32},{96,64},{1,97},{33,1},{65,33},{97,65},{2,98}... | collective-permute-start | bytes 1179656 | tf_op jit(solution)/shard_map/ppermute | solution.py:59
  189.4 1.2 collective-permute-start.20
  190.7 4.8 %collective-permute-start.21 = (f32[1024]{0:T(1024)S(1)}, f32[1024]{0:T(1024)S(1)}, u32[]{:S(2)}, u32[]{:S(2)}) collective-permute-start(f32[1024]{0:T(1024)S(1)} %add.202), channel_id=1, source_target_pairs={{0,32},{32,64},{64,96},{96,0},{1,33},{33,65},{65,97},{97,1},{2,34}... | collective-permute-start | bytes 12296 | tf_op jit(solution)/shard_map/ppermute | solution.py:20
  191.7 5.1 %collective-permute-start.22 = (f32[1024]{0:T(1024)S(1)}, f32[1024]{0:T(1024)S(1)}, u32[]{:S(2)}, u32[]{:S(2)}) collective-permute-start(f32[1024]{0:T(1024)S(1)} %add.202), channel_id=1, source_target_pairs={{0,64},{32,96},{64,0},{96,32},{1,65},{33,97},{65,1},{97,33},{2,66}... | collective-permute-start | bytes 12296 | tf_op jit(solution)/shard_map/ppermute | solution.py:20
  194.3 3.6 %collective-permute-start.23 = (f32[1024]{0:T(1024)S(1)}, f32[1024]{0:T(1024)S(1)}, u32[]{:S(2)}, u32[]{:S(2)}) collective-permute-start(f32[1024]{0:T(1024)S(1)} %add.202), channel_id=1, source_target_pairs={{0,96},{32,0},{64,32},{96,64},{1,97},{33,1},{65,33},{97,65},{2,98}... | collective-permute-start | bytes 12296 | tf_op jit(solution)/shard_map/ppermute | solution.py:20

commit v17 on v14

--- a/solution.py
+++ b/solution.py
@@ -74,15 +74,15 @@
     feature_dimension = full_rows.shape[1]
     local_centres = centroids.shape[0]
     centre_total = local_centres * lax.axis_size(CENT)
-    reciprocal_vector_magnitudes = lax.rsqrt(
-        jnp.mean(jnp.square(full_rows.astype(jnp.float32)), axis=1) + 1e-06
-    )
+    local_squares = jnp.sum(jnp.square(vectors.astype(jnp.float32)), axis=1)
+    square_norms = shifted_sum(shifted_sum(local_squares, "cz"), "cy")
     reciprocal_centroid_magnitudes = lax.rsqrt(
         jnp.mean(jnp.square(centroids.astype(jnp.float32)), axis=1) + 1e-06
     )
-    weight_sum, reciprocal_centroid_magnitudes = lax.optimization_barrier(
-        (reduce_row(jnp.sum(weights)), reciprocal_centroid_magnitudes)
+    weight_sum, square_norms, reciprocal_centroid_magnitudes = lax.optimization_barrier(
+        (reduce_row(jnp.sum(weights)), square_norms, reciprocal_centroid_magnitudes)
     )
+    reciprocal_vector_magnitudes = lax.rsqrt(square_norms / feature_dimension + 1e-06)
     similarity_matrix = jnp.dot(full_rows, centroids.T, preferred_element_type=jnp.float32)
     sharpened_similarity = (
         similarity_matrix

time: 198 us -> 211 us (1.066)
  starting transfers between devices: 37 us -> 57.5 us
  waiting for transfers between devices: 75.4 us -> 68 us
    all_to_all x1, waiting for transfers between devices: 27.3 us -> 0.01 us  [gather_features(): lax.all_to_all(jnp.broadcast_to(vectors, (n, *vectors.shape)), CENT, 0, 0...]
    ppermute x20 -> x26, starting transfers between devices: 22.4 us -> 42.8 us  [shifted_sum(): total = total + lax.ppermute(x, axis, [(i, (i + k) % n) for i in range(n)])]
    ppermute x20 -> x26, waiting for transfers between devices: 21 us -> 40.8 us  [shifted_sum(): total = total + lax.ppermute(x, axis, [(i, (i + k) % n) for i in range(n)])]
  transfers between devices with their start and end apart: 26 -> 32, of which waited for: 20 -> 21; matrix products, arithmetic and copies ran while one was open for 3% -> 3% of each run, Pallas kernels for 0% -> 0%
where the time goes in v17:
time: 211 us; the launch traced here: 210 us
  waiting for transfers between devices  68 us (32%)
  starting transfers between devices  57.5 us (27%)
  blocking collectives  37.6 us (18%)
  other arithmetic  22.1 us (10%)
  matrix products  16.5 us (8%)
  local copies, waits for them, and re-layouts  4.11 us (2%)
  between operations  4.01 us (2%)
    ppermute x26, starting transfers between devices, shifted_sum(): total = total + lax.ppermute(x, axis, [(i, (i + k) % n) for i in range(n)])  42.8 us
    ppermute x26, waiting for transfers between devices, shifted_sum(): total = total + lax.ppermute(x, axis, [(i, (i + k) % n) for i in range(n)])  40.8 us
    all_to_all x3, blocking collectives, reduce_cent(): lax.all_to_all(jnp.broadcast_to(x, (n, *x.shape)), CENT, 0, 0, tiled=False)  37.6 us
    ppermute x3, waiting for transfers between devices, summed_block(): lax.ppermute(piece, 'rx', [(i, (i + k) % chips) for i in range(chips)])  19.5 us
    reduce_sum x3, other arithmetic, per_device(): jnp.sum(kernel.astype(jnp.float32) * row_scale[:, None], axis=0)  9.52 us
    dot_general x2, matrix products, product(): lax.dot_general(part, transport, (((0,), (0,)), ((), ())), preferred_elem...  9.35 us
    all_to_all x1, starting transfers between devices, gather_features(): lax.all_to_all(jnp.broadcast_to(vectors, (n, *vectors.shape)), CENT, 0, 0...  8.16 us
    all_to_all x1, waiting for transfers between devices, reduce_cent(): lax.all_to_all(jnp.broadcast_to(x, (n, *x.shape)), CENT, 0, 0, tiled=False)  7.82 us
  transfers between devices with their start and end apart: 32, of which 21 were waited for; matrix products, arithmetic and copies ran while one was open for 3% of the time, Pallas kernels for 0%

profile of v17, /device:TPU:0, one launch (start us, length us, event | category | flops | bytes accessed | tf_op | source)
XLA Modules:
  0.0 209.9 jit_solution(11274225029632340058)
XLA Ops:
  0.6 3.0 %broadcast_in_dim.10 = bf16[16,2048,48]{1,2,0:T(8,128)(2,1)} broadcast(bf16[2048,48]{0,1:T(8,128)(2,1)} %param.3), dimensions={1,2} | broadcast | bytes 3342336 | tf_op jit(solution)/shard_map/broadcast_in_dim | solution.py:60
  3.7 8.2 %all-to-all-start = ((bf16[16,2048,48]{1,2,0:T(8,128)(2,1)}), bf16[16,2048,48]{1,2,0:T(8,128)(2,1)S(1)}, u32[]{:S(2)}, u32[]{:S(2)}) async-start(bf16[16,2048,48]{1,2,0:T(8,128)(2,1)} %broadcast_in_dim.10), calls=%async_computation | async-start | bytes 6291456 | tf_op jit(solution)/shard_map/all_to_all | solution.py:59
  11.9 3.2 %collective-permute-start.6 = (f32[2048]{0:T(1024)S(1)}, f32[2048]{0:T(1024)S(1)}, u32[]{:S(2)}, u32[]{:S(2)}) collective-permute-start(f32[2048]{0:T(1024)S(1)} %multiply_reduce_fusion.2), channel_id=1, source_target_pairs={{0,3},{1,0},{2,1},{3,2},{4,7},{5,4},{6,5},{7,6},{8,11},{9,8},{10,9... | collective-permute-start | bytes 24584 | tf_op jit(solution)/shard_map/ppermute | solution.py:20
  15.1 0.9 collective-permute-start.5
  16.0 0.9 collective-permute-start.4
  16.8 0.6 reduce_sum.135
  17.4 1.8 multiply_reduce_fusion
  19.2 19.7 %collective-permute-done.6 = f32[2048]{0:T(1024)S(1)} collective-permute-done((f32[2048]{0:T(1024)S(1)}, f32[2048]{0:T(1024)S(1)}, u32[]{:S(2)}, u32[]{:S(2)}) %collective-permute-start.6) | collective-permute-done | bytes 8224 | tf_op jit(solution)/shard_map/ppermute | solution.py:20
  39.0 15.6 %collective-permute-start.9 = (f32[2048]{0:T(1024)S(1)}, f32[2048]{0:T(1024)S(1)}, u32[]{:S(2)}, u32[]{:S(2)}) collective-permute-start(f32[2048]{0:T(1024)S(1)} %add_add_fusion.1), channel_id=1, source_target_pairs={{0,12},{4,0},{8,4},{12,8},{1,13},{5,1},{9,5},{13,9},{2,14},{6,2},{... | collective-permute-start | bytes 24584 | tf_op jit(solution)/shard_map/ppermute | solution.py:20
  54.5 0.6 collective-permute-start.8
  56.7 2.9 %collective-permute-start.1 = (f32[]{:T(128)}, f32[]{:T(128)}, u32[]{:S(2)}, u32[]{:S(2)}) collective-permute-start(f32[]{:T(128)} %add.148), channel_id=1, source_target_pairs={{0,32},{32,64},{64,96},{96,0},{1,33},{33,65},{65,97},{97,1},{2,34}... | collective-permute-start | bytes 20 | tf_op jit(solution)/shard_map/ppermute | solution.py:20
  59.5 4.0 %collective-permute-start.2 = (f32[]{:T(128)}, f32[]{:T(128)}, u32[]{:S(2)}, u32[]{:S(2)}) collective-permute-start(f32[]{:T(128)} %add.148), channel_id=1, source_target_pairs={{0,64},{32,96},{64,0},{96,32},{1,65},{33,97},{65,1},{97,33},{2,66}... | collective-permute-start | bytes 20 | tf_op jit(solution)/shard_map/ppermute | solution.py:20
  63.6 2.7 %collective-permute-start.3 = (f32[]{:T(128)}, f32[]{:T(128)}, u32[]{:S(2)}, u32[]{:S(2)}) collective-permute-start(f32[]{:T(128)} %add.148), channel_id=1, source_target_pairs={{0,96},{32,0},{64,32},{96,64},{1,97},{33,1},{65,33},{97,65},{2,98}... | collective-permute-start | bytes 20 | tf_op jit(solution)/shard_map/ppermute | solution.py:20
  68.2 7.2 %fusion = (f32[2048]{0:T(1024)S(1)}, bf16[2048,1024]{0,1:T(8,128)(2,1)}) fusion(f32[1024]{0:T(1024)S(1)} %add_rsqrt_fusion.2, f32[2048]{0:T(1024)S(1)} %add_rsqrt_fusion, bf16[1024,768]{1,0:T(8,128)(2,1)} %param.4, bf16[2048,768]{0,1:T(8,128)(2,1)S(1)} %bitcast.31), kind=kOutput, calls=%fused_computation.8 | convolution fusion | flops 3235903488 | bytes 8933376 | tf_op jit(solution)/shard_map/dot_general | solution.py:86
  75.5 15.2 %all_to_all.29 = f32[16,1,2048]{2,1,0:T(1,128)S(1)} all-to-all(f32[16,1,2048]{2,1,0:T(1,128)S(1)} %broadcast_in_dim.11), channel_id=1, replica_groups=mesh['rx'=4,'rc'=2,'cy'=4,'cz'=4] {'cy','cz'}, dimensions={0} | all-to-all | bytes 262144 | tf_op jit(solution)/shard_map/all_to_all | solution.py:26
  90.8 3.1 %fusion.1 = f32[1024]{0:T(1024)S(1)} fusion(bf16[2048,1024]{0,1:T(8,128)(2,1)} %get-tuple-element.16, f32[2048]{0:T(1024)S(1)} %div.56), kind=kLoop, calls=%fused_computation.9 | loop fusion | flops 6290432 | bytes 4206592 | tf_op jit(solution)/shard_map/reduce_sum | solution.py:97
  93.9 1.2 collective-permute-done.10
  95.1 2.3 %collective-permute-start.13 = (f32[1024]{0:T(1024)S(1)}, f32[1024]{0:T(1024)S(1)}, u32[]{:S(2)}, u32[]{:S(2)}) collective-permute-start(f32[1024]{0:T(1024)S(1)} %add.161), channel_id=1, source_target_pairs={{0,96},{32,0},{64,32},{96,64},{1,97},{33,1},{65,33},{97,65},{2,98}... | collective-permute-start | bytes 12296 | tf_op jit(solution)/shard_map/ppermute | solution.py:20
  97.3 0.4 collective-permute-start.12
  97.7 0.5 collective-permute-start.11
  98.2 0.5 collective-permute-done.13
  98.7 3.8 %collective-permute-done.12 = f32[1024]{0:T(1024)S(1)} collective-permute-done((f32[1024]{0:T(1024)S(1)}, f32[1024]{0:T(1024)S(1)}, u32[]{:S(2)}, u32[]{:S(2)}) %collective-permute-start.12) | collective-permute-done | bytes 4128 | tf_op jit(solution)/shard_map/ppermute | solution.py:20
  102.6 3.1 %fusion.2 = f32[2048]{0:T(1024)S(1)} fusion(bf16[2048,1024]{0,1:T(8,128)(2,1)} %get-tuple-element.16, f32[1024]{0:T(1024)S(1)} %add_divide_fusion.2), kind=kLoop, calls=%fused_computation.10 | loop fusion | flops 6289408 | bytes 4206592 | tf_op jit(solution)/shard_map/reduce_sum | solution.py:66
  105.7 11.2 %all_to_all.30 = f32[16,1,2048]{2,1,0:T(1,128)S(1)} all-to-all(f32[16,1,2048]{2,1,0:T(1,128)S(1)} %broadcast_in_dim.12), channel_id=1, replica_groups=mesh['rx'=4,'rc'=2,'cy'=4,'cz'=4] {'cy','cz'}, dimensions={0} | all-to-all | bytes 262144 | tf_op jit(solution)/shard_map/all_to_all | solution.py:26
  117.1 3.2 %fusion.3 = f32[1024]{0:T(1024)S(1)} fusion(bf16[2048,1024]{0,1:T(8,128)(2,1)} %get-tuple-element.16, f32[2048]{0:T(1024)S(1)} %div.58), kind=kLoop, calls=%fused_computation.11 | loop fusion | flops 6290432 | bytes 4206592 | tf_op jit(solution)/shard_map/reduce_sum | solution.py:97
  120.4 1.2 collective-permute-done.14
  121.6 0.8 collective-permute-start.17
  122.4 1.1 collective-permute-start.16
  123.5 1.4 collective-permute-start.15
  125.2 2.3 %collective-permute-done.16 = f32[1024]{0:T(1024)S(1)} collective-permute-done((f32[1024]{0:T(1024)S(1)}, f32[1024]{0:T(1024)S(1)}, u32[]{:S(2)}, u32[]{:S(2)}) %collective-permute-start.16) | collective-permute-done | bytes 4128 | tf_op jit(solution)/shard_map/ppermute | solution.py:20
  127.5 0.8 collective-permute-done.15
  128.3 0.9 fusion.4
  129.3 11.2 %all_to_all.31 = f32[16,1,2048]{2,1,0:T(1,128)S(1)} all-to-all(f32[16,1,2048]{2,1,0:T(1,128)S(1)} %broadcast_in_dim.13), channel_id=1, replica_groups=mesh['rx'=4,'rc'=2,'cy'=4,'cz'=4] {'cy','cz'}, dimensions={0} | all-to-all | bytes 262144 | tf_op jit(solution)/shard_map/all_to_all | solution.py:26
  140.6 3.2 %fusion.5 = f32[1024]{0:T(1024)S(1)} fusion(bf16[2048,1024]{0,1:T(8,128)(2,1)} %get-tuple-element.16, f32[2048]{0:T(1024)S(1)} %div.60), kind=kLoop, calls=%fused_computation.13 | loop fusion | flops 6290432 | bytes 4206592 | tf_op jit(solution)/shard_map/reduce_sum | solution.py:97
  144.0 1.2 collective-permute-done.18
  145.1 1.6 collective-permute-start.21
  146.7 0.9 collective-permute-start.20
  147.8 1.0 collective-permute-done.21
  148.7 3.1 %collective-permute-done.20 = f32[1024]{0:T(1024)S(1)} collective-permute-done((f32[1024]{0:T(1024)S(1)}, f32[1024]{0:T(1024)S(1)}, u32[]{:S(2)}, u32[]{:S(2)}) %collective-permute-start.20) | collective-permute-done | bytes 4128 | tf_op jit(solution)/shard_map/ppermute | solution.py:20
  151.8 0.6 collective-permute-done.19
  152.4 0.6 multiply_log_fusion
  153.0 0.9 fusion.6
  153.9 0.7 broadcast_in_dim.14
  154.6 3.6 %all-to-all-start.4 = ((f32[16,1,2048]{2,1,0:T(1,128)}), f32[16,1,2048]{2,1,0:T(1,128)S(1)}, u32[]{:S(2)}, u32[]{:S(2)}) async-start(f32[16,1,2048]{2,1,0:T(1,128)} %broadcast_in_dim.14), calls=%async_computation.4 | async-start | bytes 262144 | tf_op jit(solution)/shard_map/all_to_all | solution.py:26
  158.3 7.8 %all-to-all-done.4 = f32[16,1,2048]{2,1,0:T(1,128)S(1)} async-done(((f32[16,1,2048]{2,1,0:T(1,128)}), f32[16,1,2048]{2,1,0:T(1,128)S(1)}, u32[]{:S(2)}, u32[]{:S(2)}) %all-to-all-start.4) | async-done | bytes 131104 | tf_op jit(solution)/shard_map/all_to_all | solution.py:26
  166.2 0.6 fusion.22
  166.8 5.3 %fusion.10 = f32[4,96,1024]{2,1,0:T(8,128)} fusion(bf16[2048,1024]{0,1:T(8,128)(2,1)} %get-tuple-element.16, f32[2048]{0:T(1024)S(1)} %get-tuple-element.12, f32[1024]{0:T(1024)S(1)} %get-tuple-element.10, bf16[2048,4,2,96]{0,3,2,1:T(8,128)(2,1)S(1)} %bitcast.32, s32[]{:T(128)S(6)} %select_n.41), kind=kOutput, calls=%fused_computation.20 | convolution fusion | flops 1619001344 | bytes 7352324 | tf_op jit(solution)/shard_map/dot_general | solution.py:43
  172.1 4.1 %fusion.12 = f32[4,96,1024]{2,1,0:T(8,128)S(1)} fusion(bf16[2048,1024]{0,1:T(8,128)(2,1)} %get-tuple-element.16, f32[2048]{0:T(1024)S(1)} %get-tuple-element.12, f32[1024]{0:T(1024)S(1)} %get-tuple-element.10, bf16[2048,4,2,96]{0,3,2,1:T(8,128)(2,1)S(1)} %bitcast.33, s32[]{:T(128)S(6)} %select_n.39), kind=kOutput, calls=%fused_computation.21 | convolution fusion | flops 1619001344 | bytes 7352324 | tf_op jit(solution)/shard_map/dot_general | solution.py:43
  176.2 1.8 add.176
  178.1 1.1 collective-permute-start.25
  179.1 0.9 collective-permute-start.24
  180.0 0.9 collective-permute-start.23
  181.0 9.2 %collective-permute-done.25 = f32[96,1024]{1,0:T(8,128)S(1)} collective-permute-done((f32[96,1024]{1,0:T(8,128)S(1)}, f32[96,1024]{1,0:T(8,128)S(1)}, u32[]{:S(2)}, u32[]{:S(2)}) %collective-permute-start.25) | collective-permute-done | bytes 393248 | tf_op jit(solution)/shard_map/ppermute | solution.py:53
  190.1 2.6 %collective-permute-done.24 = f32[96,1024]{1,0:T(8,128)S(1)} collective-permute-done((f32[96,1024]{1,0:T(8,128)S(1)}, f32[96,1024]{1,0:T(8,128)S(1)}, u32[]{:S(2)}, u32[]{:S(2)}) %collective-permute-start.24) | collective-permute-done | bytes 393248 | tf_op jit(solution)/shard_map/ppermute | solution.py:53
  192.7 7.7 %collective-permute-done.23 = f32[96,1024]{1,0:T(8,128)} collective-permute-done((f32[96,1024]{1,0:T(8,128)S(1)}, f32[96,1024]{1,0:T(8,128)}, u32[]{:S(2)}, u32[]{:S(2)}) %collective-permute-start.23) | collective-permute-done | bytes 393248 | tf_op jit(solution)/shard_map/ppermute | solution.py:53
  200.4 1.1 multiply_reduce_fusion.1
  201.6 1.1 collective-permute-done.26
  202.8 0.6 collective-permute-start.29
  203.4 0.9 collective-permute-start.28
  204.3 0.8 collective-permute-start.27
  205.1 1.3 collective-permute-done.29
  206.4 2.1 %collective-permute-done.28 = f32[1024]{0:T(1024)S(1)} collective-permute-done((f32[1024]{0:T(1024)S(1)}, f32[1024]{0:T(1024)S(1)}, u32[]{:S(2)}, u32[]{:S(2)}) %collective-permute-start.28) | collective-permute-done | bytes 4128 | tf_op jit(solution)/shard_map/ppermute | solution.py:20
  208.5 0.6 collective-permute-done.27
  209.1 0.8 broadcast_multiply_fusion
  (52 shorter events, 2.1 us)
Async XLA Ops:
  0.6 11.2 %copy-start.2 = (bf16[2048,48]{0,1:T(8,128)(2,1)S(1)}, bf16[2048,48]{0,1:T(8,128)(2,1)}, u32[]{:S(2)}) copy-start(bf16[2048,48]{0,1:T(8,128)(2,1)} %param.3) | copy-start | bytes 589828
  0.6 16.2 %copy-start.3 = (f32[2048]{0:T(1024)S(1)}, f32[2048]{0:T(1024)}, u32[]{:S(2)}) copy-start(f32[2048]{0:T(1024)} %param.5) | copy-start | bytes 24580
  3.7 64.6 %all-to-all-start = ((bf16[16,2048,48]{1,2,0:T(8,128)(2,1)}), bf16[16,2048,48]{1,2,0:T(8,128)(2,1)S(1)}, u32[]{:S(2)}, u32[]{:S(2)}) async-start(bf16[16,2048,48]{1,2,0:T(8,128)(2,1)} %broadcast_in_dim.10), calls=%async_computation | async-start | bytes 6291456 | tf_op jit(solution)/shard_map/all_to_all | solution.py:59
  11.9 27.0 %collective-permute-start.6 = (f32[2048]{0:T(1024)S(1)}, f32[2048]{0:T(1024)S(1)}, u32[]{:S(2)}, u32[]{:S(2)}) collective-permute-start(f32[2048]{0:T(1024)S(1)} %multiply_reduce_fusion.2), channel_id=1, source_target_pairs={{0,3},{1,0},{2,1},{3,2},{4,7},{5,4},{6,5},{7,6},{8,11},{9,8},{10,9... | collective-permute-start | bytes 24584 | tf_op jit(solution)/shard_map/ppermute | solution.py:20
  15.1 23.8 %collective-permute-start.5 = (f32[2048]{0:T(1024)S(1)}, f32[2048]{0:T(1024)S(1)}, u32[]{:S(2)}, u32[]{:S(2)}) collective-permute-start(f32[2048]{0:T(1024)S(1)} %multiply_reduce_fusion.2), channel_id=1, source_target_pairs={{0,2},{1,3},{2,0},{3,1},{4,6},{5,7},{6,4},{7,5},{8,10},{9,11},{10,... | collective-permute-start | bytes 24584 | tf_op jit(solution)/shard_map/ppermute | solution.py:20
  16.0 23.0 %collective-permute-start.4 = (f32[2048]{0:T(1024)S(1)}, f32[2048]{0:T(1024)S(1)}, u32[]{:S(2)}, u32[]{:S(2)}) collective-permute-start(f32[2048]{0:T(1024)S(1)} %multiply_reduce_fusion.2), channel_id=1, source_target_pairs={{0,1},{1,2},{2,3},{3,0},{4,5},{5,6},{6,7},{7,4},{8,9},{9,10},{10,1... | collective-permute-start | bytes 24584 | tf_op jit(solution)/shard_map/ppermute | solution.py:20
  17.4 38.0 %collective-permute-start = (f32[]{:T(128)}, f32[]{:T(128)}, u32[]{:S(2)}, u32[]{:S(2)}) collective-permute-start(f32[]{:T(128)} %reduce_sum.135), channel_id=1, source_target_pairs={{0,16},{16,0},{1,17},{17,1},{2,18},{18,2},{3,19},{19,3},{4,20},{20... | collective-permute-start | bytes 20 | tf_op jit(solution)/shard_map/ppermute | solution.py:20
  39.0 29.2 %collective-permute-start.9 = (f32[2048]{0:T(1024)S(1)}, f32[2048]{0:T(1024)S(1)}, u32[]{:S(2)}, u32[]{:S(2)}) collective-permute-start(f32[2048]{0:T(1024)S(1)} %add_add_fusion.1), channel_id=1, source_target_pairs={{0,12},{4,0},{8,4},{12,8},{1,13},{5,1},{9,5},{13,9},{2,14},{6,2},{... | collective-permute-start | bytes 24584 | tf_op jit(solution)/shard_map/ppermute | solution.py:20
  54.5 13.7 %collective-permute-start.8 = (f32[2048]{0:T(1024)S(1)}, f32[2048]{0:T(1024)S(1)}, u32[]{:S(2)}, u32[]{:S(2)}) collective-permute-start(f32[2048]{0:T(1024)S(1)} %add_add_fusion.1), channel_id=1, source_target_pairs={{0,8},{4,12},{8,0},{12,4},{1,9},{5,13},{9,1},{13,5},{2,10},{6,14},... | collective-permute-start | bytes 24584 | tf_op jit(solution)/shard_map/ppermute | solution.py:20
  55.1 13.1 %collective-permute-start.7 = (f32[2048]{0:T(1024)S(1)}, f32[2048]{0:T(1024)S(1)}, u32[]{:S(2)}, u32[]{:S(2)}) collective-permute-start(f32[2048]{0:T(1024)S(1)} %add_add_fusion.1), channel_id=1, source_target_pairs={{0,4},{4,8},{8,12},{12,0},{1,5},{5,9},{9,13},{13,1},{2,6},{6,10},{... | collective-permute-start | bytes 24584 | tf_op jit(solution)/shard_map/ppermute | solution.py:20
  56.7 6.9 %collective-permute-start.1 = (f32[]{:T(128)}, f32[]{:T(128)}, u32[]{:S(2)}, u32[]{:S(2)}) collective-permute-start(f32[]{:T(128)} %add.148), channel_id=1, source_target_pairs={{0,32},{32,64},{64,96},{96,0},{1,33},{33,65},{65,97},{97,1},{2,34}... | collective-permute-start | bytes 20 | tf_op jit(solution)/shard_map/ppermute | solution.py:20
  59.5 7.3 %collective-permute-start.2 = (f32[]{:T(128)}, f32[]{:T(128)}, u32[]{:S(2)}, u32[]{:S(2)}) collective-permute-start(f32[]{:T(128)} %add.148), channel_id=1, source_target_pairs={{0,64},{32,96},{64,0},{96,32},{1,65},{33,97},{65,1},{97,33},{2,66}... | collective-permute-start | bytes 20 | tf_op jit(solution)/shard_map/ppermute | solution.py:20
  63.6 3.9 %collective-permute-start.3 = (f32[]{:T(128)}, f32[]{:T(128)}, u32[]{:S(2)}, u32[]{:S(2)}) collective-permute-start(f32[]{:T(128)} %add.148), channel_id=1, source_target_pairs={{0,96},{32,0},{64,32},{96,64},{1,97},{33,1},{65,33},{97,65},{2,98}... | collective-permute-start | bytes 20 | tf_op jit(solution)/shard_map/ppermute | solution.py:20
  93.8 1.2 collective-permute-start.10
  95.1 3.6 %collective-permute-start.13 = (f32[1024]{0:T(1024)S(1)}, f32[1024]{0:T(1024)S(1)}, u32[]{:S(2)}, u32[]{:S(2)}) collective-permute-start(f32[1024]{0:T(1024)S(1)} %add.161), channel_id=1, source_target_pairs={{0,96},{32,0},{64,32},{96,64},{1,97},{33,1},{65,33},{97,65},{2,98}... | collective-permute-start | bytes 12296 | tf_op jit(solution)/shard_map/ppermute | solution.py:20
  97.3 5.1 %collective-permute-start.12 = (f32[1024]{0:T(1024)S(1)}, f32[1024]{0:T(1024)S(1)}, u32[]{:S(2)}, u32[]{:S(2)}) collective-permute-start(f32[1024]{0:T(1024)S(1)} %add.161), channel_id=1, source_target_pairs={{0,64},{32,96},{64,0},{96,32},{1,65},{33,97},{65,1},{97,33},{2,66}... | collective-permute-start | bytes 12296 | tf_op jit(solution)/shard_map/ppermute | solution.py:20
  97.7 4.8 %collective-permute-start.11 = (f32[1024]{0:T(1024)S(1)}, f32[1024]{0:T(1024)S(1)}, u32[]{:S(2)}, u32[]{:S(2)}) collective-permute-start(f32[1024]{0:T(1024)S(1)} %add.161), channel_id=1, source_target_pairs={{0,32},{32,64},{64,96},{96,0},{1,33},{33,65},{65,97},{97,1},{2,34}... | collective-permute-start | bytes 12296 | tf_op jit(solution)/shard_map/ppermute | solution.py:20
  117.1 11.2 %copy-start = (bf16[2048,1024]{0,1:T(8,128)(2,1)S(1)}, bf16[2048,1024]{0,1:T(8,128)(2,1)}, u32[]{:S(2)}) copy-start(bf16[2048,1024]{0,1:T(8,128)(2,1)} %get-tuple-element.16) | copy-start | bytes 12582916
  120.3 1.2 collective-permute-start.14
  121.6 3.6 %collective-permute-start.17 = (f32[1024]{0:T(1024)S(1)}, f32[1024]{0:T(1024)S(1)}, u32[]{:S(2)}, u32[]{:S(2)}) collective-permute-start(f32[1024]{0:T(1024)S(1)} %add.165), channel_id=1, source_target_pairs={{0,96},{32,0},{64,32},{96,64},{1,97},{33,1},{65,33},{97,65},{2,98}... | collective-permute-start | bytes 12296 | tf_op jit(solution)/shard_map/ppermute | solution.py:20
  122.4 5.1 %collective-permute-start.16 = (f32[1024]{0:T(1024)S(1)}, f32[1024]{0:T(1024)S(1)}, u32[]{:S(2)}, u32[]{:S(2)}) collective-permute-start(f32[1024]{0:T(1024)S(1)} %add.165), channel_id=1, source_target_pairs={{0,64},{32,96},{64,0},{96,32},{1,65},{33,97},{65,1},{97,33},{2,66}... | collective-permute-start | bytes 12296 | tf_op jit(solution)/shard_map/ppermute | solution.py:20
  123.5 4.8 %collective-permute-start.15 = (f32[1024]{0:T(1024)S(1)}, f32[1024]{0:T(1024)S(1)}, u32[]{:S(2)}, u32[]{:S(2)}) collective-permute-start(f32[1024]{0:T(1024)S(1)} %add.165), channel_id=1, source_target_pairs={{0,32},{32,64},{64,96},{96,0},{1,33},{33,65},{65,97},{97,1},{2,34}... | collective-permute-start | bytes 12296 | tf_op jit(solution)/shard_map/ppermute | solution.py:20
  140.6 12.4 %copy-start.1 = (bf16[2048,1024]{0,1:T(8,128)(2,1)S(1)}, bf16[2048,1024]{0,1:T(8,128)(2,1)}, u32[]{:S(2)}) copy-start(bf16[2048,1024]{0,1:T(8,128)(2,1)} %get-tuple-element.16) | copy-start | bytes 12582916
  143.9 1.2 collective-permute-start.18
  145.1 3.6 %collective-permute-start.21 = (f32[1024]{0:T(1024)S(1)}, f32[1024]{0:T(1024)S(1)}, u32[]{:S(2)}, u32[]{:S(2)}) collective-permute-start(f32[1024]{0:T(1024)S(1)} %add.169), channel_id=1, source_target_pairs={{0,96},{32,0},{64,32},{96,64},{1,97},{33,1},{65,33},{97,65},{2,98}... | collective-permute-start | bytes 12296 | tf_op jit(solution)/shard_map/ppermute | solution.py:20
  146.7 5.1 %collective-permute-start.20 = (f32[1024]{0:T(1024)S(1)}, f32[1024]{0:T(1024)S(1)}, u32[]{:S(2)}, u32[]{:S(2)}) collective-permute-start(f32[1024]{0:T(1024)S(1)} %add.169), channel_id=1, source_target_pairs={{0,64},{32,96},{64,0},{96,32},{1,65},{33,97},{65,1},{97,33},{2,66}... | collective-permute-start | bytes 12296 | tf_op jit(solution)/shard_map/ppermute | solution.py:20
  147.6 4.8 %collective-permute-start.19 = (f32[1024]{0:T(1024)S(1)}, f32[1024]{0:T(1024)S(1)}, u32[]{:S(2)}, u32[]{:S(2)}) collective-permute-start(f32[1024]{0:T(1024)S(1)} %add.169), channel_id=1, source_target_pairs={{0,32},{32,64},{64,96},{96,0},{1,33},{33,65},{65,97},{97,1},{2,34}... | collective-permute-start | bytes 12296 | tf_op jit(solution)/shard_map/ppermute | solution.py:20
  154.6 11.4 %all-to-all-start.4 = ((f32[16,1,2048]{2,1,0:T(1,128)}), f32[16,1,2048]{2,1,0:T(1,128)S(1)}, u32[]{:S(2)}, u32[]{:S(2)}) async-start(f32[16,1,2048]{2,1,0:T(1,128)} %broadcast_in_dim.14), calls=%async_computation.4 | async-start | bytes 262144 | tf_op jit(solution)/shard_map/all_to_all | solution.py:26
  172.1 4.1 %collective-permute-start.22 = (f32[4,96,1024]{2,1,0:T(8,128)}, f32[4,96,1024]{2,1,0:T(8,128)}, u32[]{:S(2)}, u32[]{:S(2)}) collective-permute-start(f32[4,96,1024]{2,1,0:T(8,128)} %fusion.10), channel_id=1, source_target_pairs={{0,16},{16,0},{1,17},{17,1},{2,18},{18,2},{3,19},{19,3},{4,20},{20... | collective-permute-start | bytes 4718600 | tf_op jit(solution)/shard_map/ppermute | solution.py:48
  178.1 12.1 %collective-permute-start.25 = (f32[96,1024]{1,0:T(8,128)S(1)}, f32[96,1024]{1,0:T(8,128)S(1)}, u32[]{:S(2)}, u32[]{:S(2)}) collective-permute-start(f32[96,1024]{1,0:T(8,128)S(1)} %get-tuple-element.18), channel_id=1, source_target_pairs={{0,96},{32,0},{64,32},{96,64},{1,97},{33,1},{65,33},{97,65},{2,98}... | collective-permute-start | bytes 1179656 | tf_op jit(solution)/shard_map/ppermute | solution.py:53
  179.1 13.5 %collective-permute-start.24 = (f32[96,1024]{1,0:T(8,128)S(1)}, f32[96,1024]{1,0:T(8,128)S(1)}, u32[]{:S(2)}, u32[]{:S(2)}) collective-permute-start(f32[96,1024]{1,0:T(8,128)S(1)} %get-tuple-element.19), channel_id=1, source_target_pairs={{0,64},{32,96},{64,0},{96,32},{1,65},{33,97},{65,1},{97,33},{2,66}... | collective-permute-start | bytes 1179656 | tf_op jit(solution)/shard_map/ppermute | solution.py:53
  180.0 20.4 %collective-permute-start.23 = (f32[96,1024]{1,0:T(8,128)S(1)}, f32[96,1024]{1,0:T(8,128)}, u32[]{:S(2)}, u32[]{:S(2)}) collective-permute-start(f32[96,1024]{1,0:T(8,128)S(1)} %get-tuple-element.17), channel_id=1, source_target_pairs={{0,32},{32,64},{64,96},{96,0},{1,33},{33,65},{65,97},{97,1},{2,34}... | collective-permute-start | bytes 1179656 | tf_op jit(solution)/shard_map/ppermute | solution.py:53
  201.5 1.2 collective-permute-start.26
  202.8 3.6 %collective-permute-start.29 = (f32[1024]{0:T(1024)S(1)}, f32[1024]{0:T(1024)S(1)}, u32[]{:S(2)}, u32[]{:S(2)}) collective-permute-start(f32[1024]{0:T(1024)S(1)} %add.190), channel_id=1, source_target_pairs={{0,96},{32,0},{64,32},{96,64},{1,97},{33,1},{65,33},{97,65},{2,98}... | collective-permute-start | bytes 12296 | tf_op jit(solution)/shard_map/ppermute | solution.py:20
  203.4 5.1 %collective-permute-start.28 = (f32[1024]{0:T(1024)S(1)}, f32[1024]{0:T(1024)S(1)}, u32[]{:S(2)}, u32[]{:S(2)}) collective-permute-start(f32[1024]{0:T(1024)S(1)} %add.190), channel_id=1, source_target_pairs={{0,64},{32,96},{64,0},{96,32},{1,65},{33,97},{65,1},{97,33},{2,66}... | collective-permute-start | bytes 12296 | tf_op jit(solution)/shard_map/ppermute | solution.py:20
  204.3 4.8 %collective-permute-start.27 = (f32[1024]{0:T(1024)S(1)}, f32[1024]{0:T(1024)S(1)}, u32[]{:S(2)}, u32[]{:S(2)}) collective-permute-start(f32[1024]{0:T(1024)S(1)} %add.190), channel_id=1, source_target_pairs={{0,32},{32,64},{64,96},{96,0},{1,33},{33,65},{65,97},{97,1},{2,34}... | collective-permute-start | bytes 12296 | tf_op jit(solution)/shard_map/ppermute | solution.py:20
